TPU v7x, 256 devices: a whole 4x4x8 slice. The times are simulated.
256 devices in a mesh: seq: 64 (over x, z, core), head: 4 (over y).
Axes of the slice: x: 4, y: 4, z: 8, core: 2. Of those that a mesh axis runs over, the one named last changes fastest.
Arguments:
- features_in: bfloat16 [32768, 3072], P('seq', 'head'), may hold values from -66 to 66
- gate_in: bfloat16 [32768, 3072], P('seq', 'head'), may hold values from -6 to 6
- b_input: bfloat16 [32768, 128], P('seq'), may hold values from -0.0234375 to 0.0234375
- c_input: bfloat16 [32768, 128], P('seq'), may hold values from -6 to 6
- log_decay: bfloat16 [32768, 48], P('seq', 'head'), may hold values from -1 to 0, as said below
- row_target: int32 [32768], P('seq'), may hold values from 0 to 32767, as said below
- doc_lengths: int32 [4], replicated, may hold values from 1 to 16384, 32768 in all
- skip_gain: float32 [48], P('head'), may hold values from 0.5 to 1.5
- norm_gain: float32 [3072], P('head'), may hold values from 0.1 to 1.9
- out_weight: bfloat16 [3072, 1536], P('head'), may hold values from -0.109375 to 0.109375
Outputs:
- layer_out: bfloat16 [32768, 1536], P(('seq', 'head'))
Inputs may be any that keep to these rules, and one draw needn't show every extreme that they name: row_target is a permutation; the rows of one device go to every device along seq, exactly 8 rows to each. `doc_lengths`: the lengths sum to 32768. `log_decay`: every decay is below one.
All inputs are finite; a program needn't handle non-finite values.
Results may differ from a plain program's by a relative error of at most 0.022.
Values may be sent and summed in bfloat16 or wider, within the bound.
No kernel may reach another device: no remote copies, remote signals or barrier semaphores. Data moves between devices by JAX's collectives and lax.ppermute only.
A program may use at most 128 MiB of HBM per device.

v0:
```python
import jax
import jax.numpy as jnp
from jax import lax
from jax.sharding import PartitionSpec as P

ATTENTION_LANES = 48
HEAD_DIM = 64
BLOCK = 512


far_below = -1e30
norm_eps = 1e-05


def prefix(x, axis, combine, identity):
    length, here = (lax.axis_size(axis), lax.axis_index(axis))
    everything = jax.tree.map(
        lambda part, kind: lax.all_gather(part.astype(kind), axis), x, (jnp.bfloat16, jnp.bfloat16)
    )
    start = jax.tree.map(
        lambda part, zero: jnp.broadcast_to(jnp.asarray(zero, part.dtype), part.shape), x, identity
    )

    def hop(k, before):
        reached = k < here
        new = combine(
            before, jax.tree.map(lambda part, own: part[k].astype(own.dtype), everything, x)
        )
        return jax.tree.map(lambda a, b: jnp.where(reached, a, b), new, before)

    return lax.fori_loop(0, length, hop, start)


def doc_index(places, starts):
    return jnp.sum((starts[None, :] <= places[:, None]).astype(jnp.int32), axis=1) - 1


def state_terms(by_head, key_block, decay_block, doc_block, before):
    running = jnp.cumsum(decay_block.astype(jnp.float32), axis=0)
    same_doc = (doc_block == doc_block[-1]).astype(jnp.float32)
    closing_weight = jnp.exp(running[-1][None, :] - running) * same_doc[:, None]
    weighted = (key_block.astype(jnp.float32)[None, :, :] * closing_weight.T[:, :, None]).astype(
        jnp.bfloat16
    )
    block_state = jnp.einsum("hsn,shp->hpn", weighted, by_head, preferred_element_type=jnp.float32)
    through = jnp.exp(running[-1]) * (doc_block[-1] == before).astype(jnp.float32)
    return (block_state, through, running)


def inner_terms(by_head, key_block, query_block, running, doc_block):
    length = running.shape[0]
    later = lax.broadcasted_iota(jnp.int32, (length, length), 0)
    earlier = lax.broadcasted_iota(jnp.int32, (length, length), 1)
    allowed = (later >= earlier) & (doc_block[:, None] == doc_block[None, :])
    running_heads = running.T
    decay_gaps = jnp.where(
        allowed[None, :, :], running_heads[:, :, None] - running_heads[:, None, :], far_below
    )
    products = jnp.einsum("tn,sn->ts", query_block, key_block, preferred_element_type=jnp.float32)
    affinity_logits = (products[None, :, :] * jnp.exp(decay_gaps)).astype(jnp.bfloat16)
    return jnp.einsum("hts,shp->thp", affinity_logits, by_head, preferred_element_type=jnp.float32)


def entry_terms(query_block, carry_state, running, doc_block, before):
    entry_weight = jnp.exp(running) * (doc_block == before).astype(jnp.float32)[:, None]
    carried = jnp.einsum(
        "tn,hpn->thp", query_block.astype(jnp.float32), carry_state, precision=lax.Precision.HIGHEST
    )
    return carried * entry_weight[:, :, None]


def combine(earlier, later):
    return (earlier[0] * later[0], later[0][:, None, None] * earlier[1] + later[1])


def body(
    features_in,
    gate_in,
    b_input,
    c_input,
    log_decay,
    row_target,
    doc_lengths,
    skip_gain,
    norm_gain,
    out_weight,
):
    tok_dev = features_in.shape[0]
    heads_here = log_decay.shape[1]
    width = features_in.shape[1] // heads_here
    shards = lax.axis_size("seq")
    capacity = tok_dev // shards
    owner = row_target // tok_dev
    local_place = row_target - owner * tok_dev
    owner_hits = (owner[:, None] == lax.broadcasted_iota(jnp.int32, (tok_dev, shards), 1)).astype(
        jnp.int32
    )
    slot_rank = jnp.sum((jnp.cumsum(owner_hits, axis=0) - owner_hits) * owner_hits, axis=1)
    slot_index = owner * capacity + slot_rank

    def pack_rows(values):
        blank = jnp.zeros((shards * capacity,) + values.shape[1:], values.dtype)
        return blank.at[slot_index].set(values).reshape((shards, capacity) + values.shape[1:])

    slot_place = (
        jnp.full((shards * capacity,), tok_dev, jnp.int32)
        .at[slot_index]
        .set(local_place)
        .reshape(shards, capacity)
    )
    moved_inputs, gate_early, moved_keys, moved_queries, moved_decay, moved_place = (
        lax.all_to_all(pack_rows(features_in), "seq", split_axis=0, concat_axis=0, tiled=True),
        lax.all_to_all(pack_rows(gate_in), "seq", split_axis=0, concat_axis=0, tiled=True),
        lax.all_to_all(pack_rows(b_input), "seq", split_axis=0, concat_axis=0, tiled=True),
        lax.all_to_all(pack_rows(c_input), "seq", split_axis=0, concat_axis=0, tiled=True),
        lax.all_to_all(pack_rows(log_decay), "seq", split_axis=0, concat_axis=0, tiled=True),
        lax.all_to_all(slot_place, "seq", split_axis=0, concat_axis=0, tiled=True),
    )
    arrived = moved_place.reshape(shards * capacity)

    def unpack_rows(values):
        flattened = values.reshape((shards * capacity,) + values.shape[2:])
        blank = jnp.zeros((tok_dev,) + values.shape[2:], values.dtype)
        return blank.at[arrived].set(flattened, mode="drop")

    features = unpack_rows(moved_inputs)
    key_rows = unpack_rows(moved_keys)
    query_rows = unpack_rows(moved_queries)
    decays = unpack_rows(moved_decay)
    key_full, query_full = (key_rows, query_rows)
    doc_starts = jnp.cumsum(doc_lengths) - doc_lengths
    first_place = lax.axis_index("seq") * tok_dev
    blocks = tok_dev // BLOCK
    places = first_place + lax.broadcasted_iota(jnp.int32, (tok_dev,), 0)
    doc_ids = doc_index(places, doc_starts).reshape(blocks, BLOCK)
    doc_before = doc_index(
        first_place + lax.broadcasted_iota(jnp.int32, (blocks,), 0) * BLOCK - 1, doc_starts
    )
    inputs_blocks = features.reshape(blocks, BLOCK, heads_here, width)
    key_blocks = key_full.reshape(blocks, BLOCK, key_full.shape[1])
    query_blocks = query_full.reshape(blocks, BLOCK, query_full.shape[1])
    decay_blocks = decays.reshape(blocks, BLOCK, heads_here)

    def state_pass(carry, pieces):
        carry_state, kept_share = carry
        by_head, key_block, query_block, decay_block, doc_block, before = pieces
        block_state, through, running = state_terms(
            by_head, key_block, decay_block, doc_block, before
        )
        new_carry = (through[:, None, None] * carry_state + block_state, through * kept_share)
        return (new_carry, (block_state, through, running))

    zero_state = jnp.zeros((heads_here, width, key_full.shape[1]), jnp.float32)
    ones_here = jnp.ones((heads_here,), jnp.float32)
    local_carry, block_outputs = lax.scan(
        state_pass,
        (zero_state, ones_here),
        (inputs_blocks, key_blocks, query_blocks, decay_blocks, doc_ids, doc_before),
    )
    local_state, local_kept = local_carry
    block_states, throughs, runnings = (block_outputs[0], block_outputs[1], block_outputs[2])
    entry_kept, entry_state = prefix(
        (local_kept, local_state), "seq", combine, (ones_here, zero_state)
    )

    def mix_pass(carry_state, pieces):
        by_head, key_block, query_block, running, doc_block, before, block_state, through = pieces
        carried = entry_terms(query_block, carry_state, running, doc_block, before)
        mixed_block = (
            inner_terms(by_head, key_block, query_block, running, doc_block)
            + carried
            + skip_gain[None, :, None] * by_head.astype(jnp.float32)
        )
        return (through[:, None, None] * carry_state + block_state, mixed_block)

    final_state, mixed = lax.scan(
        mix_pass,
        entry_state,
        (
            inputs_blocks,
            key_blocks,
            query_blocks,
            runnings,
            doc_ids,
            doc_before,
            block_states,
            throughs,
        ),
    )
    mixed = mixed.reshape(tok_dev, heads_here * width)
    gate_rows = unpack_rows(gate_early)
    gated = mixed * jax.nn.silu(gate_rows.astype(jnp.float32))
    squares = lax.psum(jnp.sum(gated * gated, axis=1), "head")
    row_scale = lax.rsqrt(squares / (ATTENTION_LANES * HEAD_DIM) + norm_eps)
    normed = (gated * row_scale[:, None] * norm_gain[None, :]).astype(jnp.bfloat16)
    return lax.psum_scatter(
        jnp.dot(normed, out_weight, preferred_element_type=jnp.float32).astype(jnp.bfloat16),
        "head",
        scatter_dimension=0,
        tiled=True,
    )


def solution(mesh):
    in_specs = (
        P("seq", "head"),
        P("seq", "head"),
        P("seq", None),
        P("seq", None),
        P("seq", "head"),
        P("seq"),
        P(),
        P("head"),
        P("head"),
        P("head", None),
    )
    out_specs = P(("seq", "head"), None)
    return jax.shard_map(body, mesh=mesh, in_specs=in_specs, out_specs=out_specs, check_vma=False)
```

profile of v0, /device:TPU:1, one launch (start us, length us, event | category | flops | bytes accessed | tf_op | source)
XLA Modules:
  0.0 352.3 jit_solution(5628531493185967500)
XLA Ops:
  7.4 1.2 reduce-window.24
  9.0 2.4 scatter_custom_fusion
  12.2 13.0 %all-to-all-start = ((s32[64,1,8]{2,1,0:T(1,128)}), s32[64,1,8]{2,1,0:T(1,128)S(1)}, u32[]{:S(2)}, u32[]{:S(2)}) async-start(s32[64,1,8]{2,1,0:T(1,128)} %bitcast.2), calls=%async_computation | async-start | bytes 65536 | tf_op jit(solution)/shard_map/all_to_all | solution.py:117
  26.0 2.4 scatter_custom_fusion.7
  28.4 6.1 %all-to-all-done = s32[64,1,8]{2,1,0:T(1,128)S(1)} async-done(((s32[64,1,8]{2,1,0:T(1,128)}), s32[64,1,8]{2,1,0:T(1,128)S(1)}, u32[]{:S(2)}, u32[]{:S(2)}) %all-to-all-start) | async-done | bytes 2080 | tf_op jit(solution)/shard_map/all_to_all | solution.py:117
  34.4 4.7 %all-to-all-start.4 = ((bf16[64,8,12]{2,1,0:T(8,128)(2,1)}), bf16[64,8,12]{2,1,0:T(8,128)(2,1)S(1)}, u32[]{:S(2)}, u32[]{:S(2)}) async-start(bf16[64,8,12]{2,1,0:T(8,128)(2,1)} %bitcast.13), calls=%async_computation.4 | async-start | bytes 262144 | tf_op jit(solution)/shard_map/all_to_all | solution.py:116
  40.0 2.7 scatter_custom_fusion.5
  42.7 6.9 %all-to-all-done.4 = bf16[64,8,12]{2,1,0:T(8,128)(2,1)S(1)} async-done(((bf16[64,8,12]{2,1,0:T(8,128)(2,1)}), bf16[64,8,12]{2,1,0:T(8,128)(2,1)S(1)}, u32[]{:S(2)}, u32[]{:S(2)}) %all-to-all-start.4) | async-done | bytes 12320 | tf_op jit(solution)/shard_map/all_to_all | solution.py:116
  49.6 4.9 %all-to-all-start.3 = ((bf16[64,8,128]{2,1,0:T(8,128)(2,1)}), bf16[64,8,128]{2,1,0:T(8,128)(2,1)S(1)}, u32[]{:S(2)}, u32[]{:S(2)}) async-start(bf16[64,8,128]{2,1,0:T(8,128)(2,1)} %bitcast.9), calls=%async_computation.3 | async-start | bytes 262144 | tf_op jit(solution)/shard_map/all_to_all | solution.py:114
  55.2 4.1 %scatter_custom_fusion.1 = bf16[512,768]{1,0:T(8,128)(2,1)} fusion(s32[512]{0:T(512)S(1)} %compare_select_fusion.1, bf16[512,768]{1,0:T(8,128)(2,1)} %param.12, bf16[]{:T(256)} %constant.110.clone.1), kind=kCustom, calls=%fused_computation.46 | custom fusion | bytes 786944 | tf_op jit(solution)/shard_map/scatter | solution.py:103
  59.4 5.5 %all-to-all-done.3 = bf16[64,8,128]{2,1,0:T(8,128)(2,1)S(1)} async-done(((bf16[64,8,128]{2,1,0:T(8,128)(2,1)}), bf16[64,8,128]{2,1,0:T(8,128)(2,1)S(1)}, u32[]{:S(2)}, u32[]{:S(2)}) %all-to-all-start.3) | async-done | bytes 131104 | tf_op jit(solution)/shard_map/all_to_all | solution.py:114
  65.5 4.9 %all-to-all-start.1 = ((bf16[64,8,768]{2,1,0:T(8,128)(2,1)}), bf16[64,8,768]{2,1,0:T(8,128)(2,1)S(1)}, u32[]{:S(2)}, u32[]{:S(2)}) async-start(bf16[64,8,768]{2,1,0:T(8,128)(2,1)} %bitcast.4), calls=%async_computation.1 | async-start | bytes 1572864 | tf_op jit(solution)/shard_map/all_to_all | solution.py:112
  72.6 1.2 compare_convert_fusion
  75.0 1.8 scatter_custom_fusion.8
  76.9 1.1 reduce-window.32
  79.8 2.1 scatter_custom_fusion.6
  82.0 11.4 %all-to-all-done.1 = bf16[64,8,768]{2,1,0:T(8,128)(2,1)S(1)} async-done(((bf16[64,8,768]{2,1,0:T(8,128)(2,1)}), bf16[64,8,768]{2,1,0:T(8,128)(2,1)S(1)}, u32[]{:S(2)}, u32[]{:S(2)}) %all-to-all-start.1) | async-done | bytes 786464 | tf_op jit(solution)/shard_map/all_to_all | solution.py:112
  93.4 3.6 %scatter_custom_fusion.2 = bf16[512,768]{1,0:T(8,128)(2,1)} fusion(s32[512]{0:T(512)S(1)} %bitcast.105, bf16[64,8,768]{2,1,0:T(8,128)(2,1)S(1)} %all-to-all-done.1, bf16[]{:T(256)} %constant.110.clone.1), kind=kCustom, calls=%fused_computation.38 | custom fusion | bytes 1572866 | tf_op jit(solution)/shard_map/scatter | solution.py:124
  97.0 1.4 copy.45
  98.4 2.8 fusion.12
  101.2 2.7 scatter_custom_fusion.3
  103.9 6.2 %all-to-all-start.2 = ((bf16[64,8,128]{2,1,0:T(8,128)(2,1)}), bf16[64,8,128]{2,1,0:T(8,128)(2,1)S(1)}, u32[]{:S(2)}, u32[]{:S(2)}) async-start(bf16[64,8,128]{2,1,0:T(8,128)(2,1)} %bitcast.7), calls=%async_computation.2 | async-start | bytes 262144 | tf_op jit(solution)/shard_map/all_to_all | solution.py:115
  110.1 4.2 %scatter_custom_fusion.9 = bf16[512,768]{1,0:T(8,128)(2,1)} fusion(s32[512]{0:T(512)S(1)} %compare_select_fusion.1, bf16[512,768]{1,0:T(8,128)(2,1)} %param.13, bf16[]{:T(256)} %constant.110.clone.1), kind=kCustom, calls=%fused_computation.43 | custom fusion | bytes 786944 | tf_op jit(solution)/shard_map/scatter | solution.py:103
  114.2 6.2 %all-to-all-done.2 = bf16[64,8,128]{2,1,0:T(8,128)(2,1)S(1)} async-done(((bf16[64,8,128]{2,1,0:T(8,128)(2,1)}), bf16[64,8,128]{2,1,0:T(8,128)(2,1)S(1)}, u32[]{:S(2)}, u32[]{:S(2)}) %all-to-all-start.2) | async-done | bytes 131104 | tf_op jit(solution)/shard_map/all_to_all | solution.py:115
  120.5 5.9 %all-to-all-start.5 = ((bf16[64,8,768]{2,1,0:T(8,128)(2,1)}), bf16[64,8,768]{2,1,0:T(8,128)(2,1)}, u32[]{:S(2)}, u32[]{:S(2)}) async-start(bf16[64,8,768]{2,1,0:T(8,128)(2,1)} %bitcast.91), calls=%async_computation.5 | async-start | bytes 1572864 | tf_op jit(solution)/shard_map/all_to_all | solution.py:113
  128.3 54.1 %all-gather.1 = bf16[64,1,12]{2,1,0:T(2,128)(2,1)S(1)} all-gather(bf16[1,1,12]{2,1,0:T(2,128)(2,1)S(1)} %bitcast.102), channel_id=1, replica_groups=mesh['seq'=64,'head'=4] {'seq'}, dimensions={0}, use_global_device_ids=true | all-gather | bytes 1560 | tf_op jit(solution)/shard_map/all_gather | solution.py:18
  182.4 1.4 exponential_multiply_fusion
  183.8 2.7 scatter_custom_fusion.4
  186.5 2.2 fusion.54
  188.7 4.2 %scatter_custom_fusion.10 = bf16[512,768]{1,0:T(8,128)(2,1)} fusion(s32[512]{0:T(512)} %bitcast.107, bf16[64,8,768]{2,1,0:T(8,128)(2,1)} %all-to-all-done.5, bf16[]{:T(256)} %constant.110.clone.1), kind=kCustom, calls=%fused_computation.36 | custom fusion | bytes 1573376 | tf_op jit(solution)/shard_map/scatter | solution.py:124
  192.9 5.8 %fusion.1 = f32[12,64,512]{2,1,0:T(8,128)} fusion(bf16[512,12,64]{0,2,1:T(8,128)(2,1)S(1)} %bitcast.89, f32[12,512]{1,0:T(8,128)} %bitcast.97, f32[512,512]{1,0:T(8,128)} %fusion.54, pred[512,512]{1,0:T(8,128)(4,1)} %fusion.13), kind=kOutput, calls=%fused_computation.15 | convolution fusion | flops 415236096 | bytes 3694592 | tf_op jit(solution)/shard_map/while/body/eval_jaxpr/hts,shp->thp/dot_general | solution.py:61
  198.8 101.6 %while.9 = (s32[]{:T(128)}, f32[12,64,128]{2,1,0:T(8,128)S(1)}, s32[]{:T(128)}, bf16[64,12]{1,0:T(8,128)(2,1)S(1)}, bf16[64,12,64,128]{3,2,1,0:T(8,128)(2,1)}, /*index=5*/s32[]{:T(128)}, s32[]{:T(128)}) while((s32[]{:T(128)}, f32[12,64,128]{2,1,0:T(8,128)S(1)}, s32[]{:T(128)}, bf16[64,12]{1,0:T(8,128)(2,1)S(1)}, ...), condition=%wide.region_18.19_spmd.clone, body=%wide.region_17.18_spmd.clone.sunk | while | flops 491536 | bytes 983265 | solution.py:31
  199.3 1.0 fusion.62
  200.9 1.0 fusion.62
  202.4 1.0 fusion.62
  204.0 1.0 fusion.62
  215.2 1.0 fusion.62
  216.7 1.0 fusion.62
  218.3 1.0 fusion.62
  219.9 1.0 fusion.62
  221.5 1.0 fusion.62
  223.1 1.0 fusion.62
  224.7 1.0 fusion.62
  226.3 1.0 fusion.62
  227.9 1.0 fusion.62
  229.4 1.0 fusion.62
  231.0 1.0 fusion.62
  232.6 1.0 fusion.62
  234.2 1.0 fusion.62
  245.3 1.0 fusion.62
  246.9 1.0 fusion.62
  248.5 1.0 fusion.62
  250.1 1.0 fusion.62
  251.7 1.0 fusion.62
  253.3 1.0 fusion.62
  254.9 1.0 fusion.62
  256.5 1.0 fusion.62
  258.0 1.0 fusion.62
  300.4 3.6 %fusion.8 = f32[512,12,64]{0,2,1:T(8,128)} fusion(f32[12,64,512]{2,1,0:T(8,128)} %fusion.1, bf16[512,12,64]{0,2,1:T(8,128)(2,1)S(1)} %bitcast.90, f32[12,64,128]{2,1,0:T(8,128)S(1)} %get-tuple-element.168, f32[12]{0:T(128)} %param.19, f32[512,12]{0,1:T(8,128)} %exponential_multiply_fusion, bf16[512,128]{1,0:T(8,128)(2,1)} %scatter_custom_fusion.4), kind=kOutput, calls=%fused_computation.27 | convolution fusion | flops 605945856 | bytes 4481072 | tf_op jit(solution)/shard_map/while/body/eval_jaxpr/tn,hpn->thp/dot_general | solution.py:66
  304.0 3.1 copy.52
  307.1 2.0 multiply_reduce_fusion
  309.1 8.7 %psum.7 = f32[512]{0:T(512)S(1)} all-reduce(f32[512]{0:T(512)S(1)} %multiply_reduce_fusion), channel_id=1, replica_groups=mesh['seq'=64,'head'=4] {'head'}, use_global_device_ids=true, to_apply=%region_22.23 | all-reduce | flops 512 | bytes 4096 | tf_op jit(solution)/shard_map/psum | solution.py:193
  317.8 4.3 %convolution_convert_fusion = bf16[512,1536]{1,0:T(8,128)(2,1)} fusion(bf16[768,1536]{1,0:T(8,128)(2,1)S(1)} %copy-done, f32[768]{0:T(1024)S(1)} %copy-done.8, f32[512]{0:T(512)S(1)} %add_rsqrt_fusion, f32[512,768]{1,0:T(8,128)} %copy.52, bf16[512,768]{1,0:T(8,128)(2,1)S(1)} %copy-done.1), kind=kOutput, calls=%fused_computation.18 | convolution fusion | flops 1212284928 | bytes 6296576 | tf_op jit(solution)/shard_map/dot_general | solution.py:197
  322.1 23.3 %reduce-scatter.2.cloned.1.call-done = bf16[128,1536]{1,0:T(8,128)(2,1)} async-done(((bf16[512,1536]{1,0:T(8,128)(2,1)}), bf16[128,1536]{1,0:T(8,128)(2,1)}) %reduce-scatter.2.cloned.1.call-update) | async-done | bytes 393232 | tf_op jit(solution)/shard_map/reduce_scatter | solution.py:196
  (165 shorter events, 84.2 us)
Async XLA Ops:
  6.5 311.3 %copy-start = (bf16[768,1536]{1,0:T(8,128)(2,1)S(1)}, bf16[768,1536]{1,0:T(8,128)(2,1)}, u32[]{:S(2)}) copy-start(bf16[768,1536]{1,0:T(8,128)(2,1)} %param.21) | copy-start | bytes 7077892
  6.5 48.0 %copy-start.7 = (s32[4]{0:T(128)S(1)}, s32[4]{0:T(128)}, u32[]{:S(2)}) copy-start(s32[4]{0:T(128)} %param.18) | copy-start | bytes 52
  12.2 22.3 %all-to-all-start = ((s32[64,1,8]{2,1,0:T(1,128)}), s32[64,1,8]{2,1,0:T(1,128)S(1)}, u32[]{:S(2)}, u32[]{:S(2)}) async-start(s32[64,1,8]{2,1,0:T(1,128)} %bitcast.2), calls=%async_computation | async-start | bytes 65536 | tf_op jit(solution)/shard_map/all_to_all | solution.py:117
  34.4 15.2 %all-to-all-start.4 = ((bf16[64,8,12]{2,1,0:T(8,128)(2,1)}), bf16[64,8,12]{2,1,0:T(8,128)(2,1)S(1)}, u32[]{:S(2)}, u32[]{:S(2)}) async-start(bf16[64,8,12]{2,1,0:T(8,128)(2,1)} %bitcast.13), calls=%async_computation.4 | async-start | bytes 262144 | tf_op jit(solution)/shard_map/all_to_all | solution.py:116
  49.6 15.2 %all-to-all-start.3 = ((bf16[64,8,128]{2,1,0:T(8,128)(2,1)}), bf16[64,8,128]{2,1,0:T(8,128)(2,1)S(1)}, u32[]{:S(2)}, u32[]{:S(2)}) async-start(bf16[64,8,128]{2,1,0:T(8,128)(2,1)} %bitcast.9), calls=%async_computation.3 | async-start | bytes 262144 | tf_op jit(solution)/shard_map/all_to_all | solution.py:114
  64.9 0.7 copy-start.3
  65.5 27.9 %all-to-all-start.1 = ((bf16[64,8,768]{2,1,0:T(8,128)(2,1)}), bf16[64,8,768]{2,1,0:T(8,128)(2,1)S(1)}, u32[]{:S(2)}, u32[]{:S(2)}) async-start(bf16[64,8,768]{2,1,0:T(8,128)(2,1)} %bitcast.4), calls=%async_computation.1 | async-start | bytes 1572864 | tf_op jit(solution)/shard_map/all_to_all | solution.py:112
  70.4 128.3 %all-gather.4.cloned.1.call-start = ((), (), s32[]{:S(2)}) async-start(), calls=%async_computation.8 | async-start | bytes 12779520 | tf_op jit(solution)/shard_map/all_gather | solution.py:18
  75.0 22.0 %copy-start.6 = (s32[512,1]{0,1:T(1,128)}, s32[512,1]{0,1:T(1,128)S(1)}, u32[]{:S(2)}) copy-start(s32[512,1]{0,1:T(1,128)S(1)} %compare_select_fusion) | copy-start | bytes 6148
  78.4 0.7 copy-start.5
  81.9 16.4 %copy-start.2 = (bf16[512,128]{1,0:T(8,128)(2,1)}, bf16[512,128]{1,0:T(8,128)(2,1)S(1)}, u32[]{:S(2)}) copy-start(bf16[512,128]{1,0:T(8,128)(2,1)S(1)} %scatter_custom_fusion.6) | copy-start | bytes 393220
  82.0 16.4 %copy-start.9 = (f32[12]{0:T(128)S(1)}, f32[12]{0:T(128)}, u32[]{:S(2)}) copy-start(f32[12]{0:T(128)} %multiply_multiply_fusion) | copy-start | bytes 148
  103.9 16.6 %all-to-all-start.2 = ((bf16[64,8,128]{2,1,0:T(8,128)(2,1)}), bf16[64,8,128]{2,1,0:T(8,128)(2,1)S(1)}, u32[]{:S(2)}, u32[]{:S(2)}) async-start(bf16[64,8,128]{2,1,0:T(8,128)(2,1)} %bitcast.7), calls=%async_computation.2 | async-start | bytes 262144 | tf_op jit(solution)/shard_map/all_to_all | solution.py:115
  120.5 5.9 %copy-start.4 = (bf16[64,8,128]{2,1,0:T(8,128)(2,1)}, bf16[64,8,128]{2,1,0:T(8,128)(2,1)S(1)}, u32[]{:S(2)}) copy-start(bf16[64,8,128]{2,1,0:T(8,128)(2,1)S(1)} %all-to-all-done.2) | copy-start | bytes 393220
  120.5 68.2 %all-to-all-start.5 = ((bf16[64,8,768]{2,1,0:T(8,128)(2,1)}), bf16[64,8,768]{2,1,0:T(8,128)(2,1)}, u32[]{:S(2)}, u32[]{:S(2)}) async-start(bf16[64,8,768]{2,1,0:T(8,128)(2,1)} %bitcast.91), calls=%async_computation.5 | async-start | bytes 1572864 | tf_op jit(solution)/shard_map/all_to_all | solution.py:113
  126.4 219.0 %reduce-scatter.2.cloned.1.call-start = ((), (), s32[]{:S(2)}) async-start(), calls=%async_computation.7 | async-start | bytes 1966080 | tf_op jit(solution)/shard_map/reduce_scatter | solution.py:196
  304.0 3.1 copy-start.1
  307.1 10.8 %copy-start.8 = (f32[768]{0:T(1024)S(1)}, f32[768]{0:T(1024)}, u32[]{:S(2)}) copy-start(f32[768]{0:T(1024)} %param.20) | copy-start | bytes 9220
Sparse Core Ops, SparseCore 0:
  101.3 90.1 all-gather.3
  322.2 23.1 reduce-scatter.1
where the time goes:
time: 355 us; the launch traced here: 352 us
  other arithmetic  114 us (32%)
  blocking collectives  62.8 us (18%)
  waiting for transfers between devices  59.5 us (17%)
  local copies, waits for them, and re-layouts  41.6 us (12%)
  starting transfers between devices  39.8 us (11%)
  matrix products  18.6 us (5%)
  between operations  14.9 us (4%)
    select_n x64, other arithmetic, hop(): return jax.tree.map(lambda a, b: jnp.where(reached, a, b), new, before)  67.2 us
    all_gather x1, blocking collectives, prefix(): lax.all_gather(part.astype(kind), axis)  54.1 us
    convert_element_type x64, other arithmetic, hop(): part[k].astype(own.dtype)  33.3 us
    reduce_scatter x1, waiting for transfers between devices, body(): lax.psum_scatter(jnp.dot(normed, out_weight, preferred_element_type=jnp.f...  23.3 us
    scatter x5, local copies, waits for them, and re-layouts, pack_rows(): blank.at[slot_index].set(values)  16 us
    scatter x6, local copies, waits for them, and re-layouts, unpack_rows(): return blank.at[arrived].set(flattened, mode='drop')  15.8 us
    all_to_all x1, starting transfers between devices, body(): lax.all_to_all(slot_place, 'seq', split_axis=0, concat_axis=0, tiled=True)  13 us
    all_to_all x1, waiting for transfers between devices, body(): lax.all_to_all(pack_rows(features_in), 'seq', split_axis=0, concat_axis=0...  11.4 us
  transfers between devices with their start and end apart: 8, of which 6 were waited for; matrix products, arithmetic and copies ran while one was open for 13% of the time, Pallas kernels for 0%

commit v1 on v0

--- a/solution.py
+++ b/solution.py
@@ -12,23 +12,31 @@
 norm_eps = 1e-05
 
 
-def prefix(x, axis, combine, identity):
+def combine(earlier, later):
+    return (earlier[0] * later[0], later[0][:, None, None] * earlier[1] + later[1])
+
+
+def exclusive_prefix(kept, state, axis):
     length, here = (lax.axis_size(axis), lax.axis_index(axis))
-    everything = jax.tree.map(
-        lambda part, kind: lax.all_gather(part.astype(kind), axis), x, (jnp.bfloat16, jnp.bfloat16)
-    )
-    start = jax.tree.map(
-        lambda part, zero: jnp.broadcast_to(jnp.asarray(zero, part.dtype), part.shape), x, identity
-    )
-
-    def hop(k, before):
-        reached = k < here
-        new = combine(
-            before, jax.tree.map(lambda part, own: part[k].astype(own.dtype), everything, x)
-        )
-        return jax.tree.map(lambda a, b: jnp.where(reached, a, b), new, before)
-
-    return lax.fori_loop(0, length, hop, start)
+    heads = kept.shape[0]
+    span = (kept, state)
+    before = (jnp.ones_like(kept), jnp.zeros_like(state))
+    distance = 1
+    while distance < length:
+        packed = jnp.concatenate(
+            [span[1], jnp.broadcast_to(span[0][:, None, None], (heads, 1, state.shape[2]))], axis=1
+        ).astype(jnp.bfloat16)
+        pairs = [(j, j + distance) for j in range(length - distance)]
+        got = lax.ppermute(packed, axis, pairs).astype(jnp.float32)
+        got = (got[:, -1, 0], got[:, :-1, :])
+        reached = here >= distance
+        new_before = combine(got, before)
+        before = jax.tree.map(lambda a, b: jnp.where(reached, a, b), new_before, before)
+        if distance * 2 < length:
+            new_span = combine(got, span)
+            span = jax.tree.map(lambda a, b: jnp.where(reached, a, b), new_span, span)
+        distance *= 2
+    return before
 
 
 def doc_index(places, starts):
@@ -67,10 +75,6 @@
         "tn,hpn->thp", query_block.astype(jnp.float32), carry_state, precision=lax.Precision.HIGHEST
     )
     return carried * entry_weight[:, :, None]
-
-
-def combine(earlier, later):
-    return (earlier[0] * later[0], later[0][:, None, None] * earlier[1] + later[1])
 
 
 def body(
@@ -87,7 +91,9 @@
 ):
     tok_dev = features_in.shape[0]
     heads_here = log_decay.shape[1]
-    width = features_in.shape[1] // heads_here
+    feats = features_in.shape[1]
+    width = feats // heads_here
+    n_state = b_input.shape[1]
     shards = lax.axis_size("seq")
     capacity = tok_dev // shards
     owner = row_target // tok_dev
@@ -97,37 +103,33 @@
     )
     slot_rank = jnp.sum((jnp.cumsum(owner_hits, axis=0) - owner_hits) * owner_hits, axis=1)
     slot_index = owner * capacity + slot_rank
-
-    def pack_rows(values):
-        blank = jnp.zeros((shards * capacity,) + values.shape[1:], values.dtype)
-        return blank.at[slot_index].set(values).reshape((shards, capacity) + values.shape[1:])
-
-    slot_place = (
-        jnp.full((shards * capacity,), tok_dev, jnp.int32)
-        .at[slot_index]
-        .set(local_place)
-        .reshape(shards, capacity)
-    )
-    moved_inputs, gate_early, moved_keys, moved_queries, moved_decay, moved_place = (
-        lax.all_to_all(pack_rows(features_in), "seq", split_axis=0, concat_axis=0, tiled=True),
-        lax.all_to_all(pack_rows(gate_in), "seq", split_axis=0, concat_axis=0, tiled=True),
-        lax.all_to_all(pack_rows(b_input), "seq", split_axis=0, concat_axis=0, tiled=True),
-        lax.all_to_all(pack_rows(c_input), "seq", split_axis=0, concat_axis=0, tiled=True),
-        lax.all_to_all(pack_rows(log_decay), "seq", split_axis=0, concat_axis=0, tiled=True),
-        lax.all_to_all(slot_place, "seq", split_axis=0, concat_axis=0, tiled=True),
-    )
-    arrived = moved_place.reshape(shards * capacity)
-
-    def unpack_rows(values):
-        flattened = values.reshape((shards * capacity,) + values.shape[2:])
-        blank = jnp.zeros((tok_dev,) + values.shape[2:], values.dtype)
-        return blank.at[arrived].set(flattened, mode="drop")
-
-    features = unpack_rows(moved_inputs)
-    key_rows = unpack_rows(moved_keys)
-    query_rows = unpack_rows(moved_queries)
-    decays = unpack_rows(moved_decay)
-    key_full, query_full = (key_rows, query_rows)
+    place_hi = (local_place // 32).astype(jnp.bfloat16)
+    place_lo = (local_place % 32).astype(jnp.bfloat16)
+    rows_out = jnp.concatenate(
+        [features_in, gate_in, b_input, c_input, log_decay, place_hi[:, None], place_lo[:, None]],
+        axis=1,
+    )
+    to_slot = (
+        lax.broadcasted_iota(jnp.int32, (tok_dev, tok_dev), 0) == slot_index[None, :]
+    ).astype(jnp.bfloat16)
+    packed = jnp.dot(to_slot, rows_out, preferred_element_type=jnp.float32).astype(jnp.bfloat16)
+    moved = lax.all_to_all(
+        packed.reshape(shards, capacity, packed.shape[1]), "seq", split_axis=0, concat_axis=0, tiled=True
+    ).reshape(tok_dev, packed.shape[1])
+    columns = packed.shape[1]
+    arrived = (
+        moved[:, columns - 2].astype(jnp.int32) * 32 + moved[:, columns - 1].astype(jnp.int32)
+    )
+    to_place = (
+        lax.broadcasted_iota(jnp.int32, (tok_dev, tok_dev), 0) == arrived[None, :]
+    ).astype(jnp.bfloat16)
+    rows = jnp.dot(to_place, moved, preferred_element_type=jnp.float32).astype(jnp.bfloat16)
+    features = rows[:, :feats]
+    gate_rows = rows[:, feats : 2 * feats]
+    key_full = rows[:, 2 * feats : 2 * feats + n_state]
+    query_full = rows[:, 2 * feats + n_state : 2 * feats + 2 * n_state]
+    decays = rows[:, 2 * feats + 2 * n_state : 2 * feats + 2 * n_state + heads_here]
+
     doc_starts = jnp.cumsum(doc_lengths) - doc_lengths
     first_place = lax.axis_index("seq") * tok_dev
     blocks = tok_dev // BLOCK
@@ -137,8 +139,8 @@
         first_place + lax.broadcasted_iota(jnp.int32, (blocks,), 0) * BLOCK - 1, doc_starts
     )
     inputs_blocks = features.reshape(blocks, BLOCK, heads_here, width)
-    key_blocks = key_full.reshape(blocks, BLOCK, key_full.shape[1])
-    query_blocks = query_full.reshape(blocks, BLOCK, query_full.shape[1])
+    key_blocks = key_full.reshape(blocks, BLOCK, n_state)
+    query_blocks = query_full.reshape(blocks, BLOCK, n_state)
     decay_blocks = decays.reshape(blocks, BLOCK, heads_here)
 
     def state_pass(carry, pieces):
@@ -150,7 +152,7 @@
         new_carry = (through[:, None, None] * carry_state + block_state, through * kept_share)
         return (new_carry, (block_state, through, running))
 
-    zero_state = jnp.zeros((heads_here, width, key_full.shape[1]), jnp.float32)
+    zero_state = jnp.zeros((heads_here, width, n_state), jnp.float32)
     ones_here = jnp.ones((heads_here,), jnp.float32)
     local_carry, block_outputs = lax.scan(
         state_pass,
@@ -159,9 +161,7 @@
     )
     local_state, local_kept = local_carry
     block_states, throughs, runnings = (block_outputs[0], block_outputs[1], block_outputs[2])
-    entry_kept, entry_state = prefix(
-        (local_kept, local_state), "seq", combine, (ones_here, zero_state)
-    )
+    entry_kept, entry_state = exclusive_prefix(local_kept, local_state, "seq")
 
     def mix_pass(carry_state, pieces):
         by_head, key_block, query_block, running, doc_block, before, block_state, through = pieces
@@ -188,7 +188,6 @@
         ),
     )
     mixed = mixed.reshape(tok_dev, heads_here * width)
-    gate_rows = unpack_rows(gate_early)
     gated = mixed * jax.nn.silu(gate_rows.astype(jnp.float32))
     squares = lax.psum(jnp.sum(gated * gated, axis=1), "head")
     row_scale = lax.rsqrt(squares / (ATTENTION_LANES * HEAD_DIM) + norm_eps)

time: 355 us -> 212 us (0.60)
  other arithmetic: 114 us -> 15.3 us
  blocking collectives: 62.8 us -> 8.69 us
  local copies, waits for them, and re-layouts: 41.6 us -> 13.7 us
  waiting for transfers between devices: 59.5 us -> 82.5 us
  starting transfers between devices: 39.8 us -> 53.4 us
  matrix products: 18.6 us -> 22.3 us
    select_n x66 -> x6, other arithmetic: 67.2 us -> 2.27 us  [the longest x5 2.27 us: exclusive_prefix(): jnp.where(reached, a, b)]
    all_gather x1 -> x0, blocking collectives: 54.1 us -> none  [prefix(): lax.all_gather(part.astype(kind), axis)]
    ppermute x0 -> x6, starting transfers between devices: none -> 40.1 us  [exclusive_prefix(): got = lax.ppermute(packed, axis, pairs).astype(jnp.float32)]
    scatter x12 -> x0, local copies, waits for them, and re-layouts: 34.3 us -> none  [the longest x5 16 us: pack_rows(): blank.at[slot_index].set(values)]
    convert_element_type x66 -> x7, other arithmetic: 35.3 us -> 1.49 us  [the longest x1 0.7 us: body(): place_lo = (local_place % 32).astype(jnp.bfloat16)]
    all_to_all x6 -> x1, starting transfers between devices: 39.6 us -> 13.3 us  [body(): lax.all_to_all(packed.reshape(shards, capacity, packed.shape[1]), 'seq',...]
    ppermute x0 -> x6, waiting for transfers between devices: none -> 11.1 us  [exclusive_prefix(): got = lax.ppermute(packed, axis, pairs).astype(jnp.float32)]
    all_to_all x6 -> x1, waiting for transfers between devices: 36.1 us -> 44.7 us  [body(): lax.all_to_all(packed.reshape(shards, capacity, packed.shape[1]), 'seq',...]
  transfers between devices with their start and end apart: 8 -> 8, of which waited for: 6 -> 7; matrix products, arithmetic and copies ran while one was open for 13% -> 5% of each run, Pallas kernels for 0% -> 0%
where the time goes in v1:
time: 212 us; the launch traced here: 211 us
  waiting for transfers between devices  82.5 us (39%)
  starting transfers between devices  53.4 us (25%)
  matrix products  22.3 us (11%)
  other arithmetic  15.3 us (7%)
  between operations  15.2 us (7%)
  local copies, waits for them, and re-layouts  13.7 us (6%)
  blocking collectives  8.69 us (4%)
    all_to_all x1, waiting for transfers between devices, body(): lax.all_to_all(packed.reshape(shards, capacity, packed.shape[1]), 'seq',...  44.7 us
    ppermute x6, starting transfers between devices, exclusive_prefix(): got = lax.ppermute(packed, axis, pairs).astype(jnp.float32)  40.1 us
    reduce_scatter x1, waiting for transfers between devices, body(): lax.psum_scatter(jnp.dot(normed, out_weight, preferred_element_type=jnp.f...  26.7 us
    all_to_all x1, starting transfers between devices, body(): lax.all_to_all(packed.reshape(shards, capacity, packed.shape[1]), 'seq',...  13.3 us
    ppermute x6, waiting for transfers between devices, exclusive_prefix(): got = lax.ppermute(packed, axis, pairs).astype(jnp.float32)  11.1 us
    psum x1, blocking collectives, body(): squares = lax.psum(jnp.sum(gated * gated, axis=1), 'head')  8.69 us
    dot_general x1, matrix products, inner_terms(): jnp.einsum('hts,shp->thp', affinity_logits, by_head, preferred_element_ty...  4.96 us
    another operation x18, other arithmetic  4.67 us
  transfers between devices with their start and end apart: 8, of which 7 were waited for; matrix products, arithmetic and copies ran while one was open for 5% of the time, Pallas kernels for 0%

profile of v1, /device:TPU:1, one launch (start us, length us, event | category | flops | bytes accessed | tf_op | source)
XLA Modules:
  0.0 211.0 jit_solution(8935762640745943866)
XLA Ops:
  6.5 1.0 copy.44
  7.6 0.7 fusion.59
  8.3 1.2 reduce-window.24
  9.5 0.2 slice_reduce_fusion
  9.8 0.1 fusion.44
  9.9 0.7 multiply_add_fusion
  10.6 0.1 broadcast_in_dim.90
  10.7 0.1 broadcast_in_dim.91
  10.9 3.8 %concatenate.27 = bf16[512,1806]{1,0:T(8,128)(2,1)} concatenate(bf16[512,768]{1,0:T(8,128)(2,1)} %param.10, bf16[512,768]{1,0:T(8,128)(2,1)} %param.11, bf16[512,128]{1,0:T(8,128)(2,1)} %param.12, bf16[512,128]{1,0:T(8,128)(2,1)} %param.13, bf16[512,12]{1,0:T(8,128)(2,1)S(1)} %copy.44, bf16[512,1]{1,0:T(8,128)(2,1)S(1)} %broadcast_in_dim.90, bf16[512,1]{1,0:T(8,128)(2,1)S(1)} %broadcast_in_dim.91), dimensions={1} | concatenate | bytes 3698688 | tf_op jit(solution)/shard_map/concatenate | solution.py:108
  14.7 4.0 %convolution_convert_fusion.2 = bf16[512,1806]{0,1:T(8,128)(2,1)} fusion(bf16[512,1806]{1,0:T(8,128)(2,1)} %concatenate.27, s32[512]{0:T(512)S(1)} %get-tuple-element.109), kind=kOutput, calls=%fused_computation.6 | convolution fusion | flops 948050944 | bytes 3700736 | tf_op jit(solution)/shard_map/dot_general | solution.py:115
  18.7 4.0 %copy.47 = bf16[512,1806]{1,0:T(8,128)(2,1)} copy(bf16[512,1806]{0,1:T(8,128)(2,1)} %convolution_convert_fusion.2) | data formatting | bytes 3698688 | tf_op jit(solution)/shard_map/convert_element_type | solution.py:115
  22.6 13.3 %all-to-all-start = ((bf16[64,8,1806]{2,1,0:T(8,128)(2,1)}), bf16[64,8,1806]{2,1,0:T(8,128)(2,1)}, u32[]{:S(2)}, u32[]{:S(2)}) async-start(bf16[64,8,1806]{2,1,0:T(8,128)(2,1)} %bitcast.52), calls=%async_computation | async-start | bytes 3932160 | tf_op jit(solution)/shard_map/all_to_all | solution.py:116
  36.0 0.2 reduce-window.31
  36.2 0.6 fusion.62
  36.8 0.1 convert_reduce_fusion
  36.9 0.6 slice.90
  38.8 0.6 compare_convert_fusion.1
  39.4 44.7 %all-to-all-done = bf16[64,8,1806]{2,1,0:T(8,128)(2,1)} async-done(((bf16[64,8,1806]{2,1,0:T(8,128)(2,1)}), bf16[64,8,1806]{2,1,0:T(8,128)(2,1)}, u32[]{:S(2)}, u32[]{:S(2)}) %all-to-all-start) | async-done | bytes 1849376 | tf_op jit(solution)/shard_map/all_to_all | solution.py:116
  84.1 1.2 add_reduce_fusion
  85.3 2.8 %convolution_convert_fusion.1 = bf16[512,1806]{0,1:T(8,128)(2,1)S(1)} fusion(s32[512]{0:T(512)S(1)} %add_reduce_fusion, bf16[64,8,1806]{2,1,0:T(8,128)(2,1)} %all-to-all-done), kind=kOutput, calls=%fused_computation.5 | convolution fusion | flops 948050944 | bytes 3700736 | tf_op jit(solution)/shard_map/dot_general | solution.py:126
  88.2 1.2 copy-done.6
  89.4 1.2 reduce-window.32
  90.5 0.2 slice_reduce_fusion.1
  90.9 0.2 multiply_reduce_fusion.1
  91.1 0.6 broadcast_multiply_fusion
  91.7 0.6 convert.49
  92.2 0.8 copy.50
  93.1 0.1 exponential_multiply_fusion.1
  93.2 2.0 fusion.73
  95.4 2.3 %collective-permute-start = (bf16[12,65,128]{2,1,0:T(8,128)(2,1)S(1)}, bf16[12,65,128]{2,1,0:T(8,128)(2,1)S(1)}, u32[]{:S(2)}, u32[]{:S(2)}) collective-permute-start(bf16[12,65,128]{2,1,0:T(8,128)(2,1)S(1)} %pad_maximum_fusion), channel_id=1, source_target_pairs={{0,4},{4,8},{8,12},{12,16},{16,20},{20,24},{24,28},{28,32},{32,36}... | collective-permute-start | bytes 599048 | tf_op jit(solution)/shard_map/ppermute | solution.py:30
  97.7 2.8 %collective-permute-done = bf16[12,65,128]{2,1,0:T(8,128)(2,1)S(1)} collective-permute-done((bf16[12,65,128]{2,1,0:T(8,128)(2,1)S(1)}, bf16[12,65,128]{2,1,0:T(8,128)(2,1)S(1)}, u32[]{:S(2)}, u32[]{:S(2)}) %collective-permute-start) | collective-permute-done | bytes 199712 | tf_op jit(solution)/shard_map/ppermute | solution.py:30
  100.6 0.8 fusion.56
  101.3 0.1 fusion.51
  101.6 3.3 %collective-permute-start.1 = (bf16[12,65,128]{2,1,0:T(8,128)(2,1)S(1)}, bf16[12,65,128]{2,1,0:T(8,128)(2,1)S(1)}, u32[]{:S(2)}, u32[]{:S(2)}) collective-permute-start(bf16[12,65,128]{2,1,0:T(8,128)(2,1)S(1)} %pad_maximum_fusion.1), channel_id=1, source_target_pairs={{0,8},{4,12},{8,16},{12,20},{16,24},{20,28},{24,32},{28,36},{32,40... | collective-permute-start | bytes 599048 | tf_op jit(solution)/shard_map/ppermute | solution.py:30
  104.9 0.2 fusion.11
  105.1 3.2 %collective-permute-done.1 = bf16[12,65,128]{2,1,0:T(8,128)(2,1)S(1)} collective-permute-done((bf16[12,65,128]{2,1,0:T(8,128)(2,1)S(1)}, bf16[12,65,128]{2,1,0:T(8,128)(2,1)S(1)}, u32[]{:S(2)}, u32[]{:S(2)}) %collective-permute-start.1) | collective-permute-done | bytes 199712 | tf_op jit(solution)/shard_map/ppermute | solution.py:30
  108.4 0.3 convert_reduce_fusion.2
  108.6 0.2 fusion.72
  108.9 4.9 %collective-permute-start.2 = (bf16[12,65,128]{2,1,0:T(8,128)(2,1)S(1)}, bf16[12,65,128]{2,1,0:T(8,128)(2,1)S(1)}, u32[]{:S(2)}, u32[]{:S(2)}) collective-permute-start(bf16[12,65,128]{2,1,0:T(8,128)(2,1)S(1)} %pad_maximum_fusion.2), channel_id=1, source_target_pairs={{0,16},{4,20},{8,24},{12,28},{16,32},{20,36},{24,40},{28,44},{32,4... | collective-permute-start | bytes 599048 | tf_op jit(solution)/shard_map/ppermute | solution.py:30
  113.9 1.3 fusion.47
  115.2 0.2 slice_reduce_fusion.5
  115.3 1.4 collective-permute-done.2
  116.8 0.2 slice_reduce_fusion.4
  117.0 0.1 fusion.52
  117.2 9.1 %collective-permute-start.3 = (bf16[12,65,128]{2,1,0:T(8,128)(2,1)S(1)}, bf16[12,65,128]{2,1,0:T(8,128)(2,1)S(1)}, u32[]{:S(2)}, u32[]{:S(2)}) collective-permute-start(bf16[12,65,128]{2,1,0:T(8,128)(2,1)S(1)} %pad_maximum_fusion.3), channel_id=1, source_target_pairs={{0,32},{4,36},{8,40},{12,44},{16,48},{20,52},{24,56},{28,60},{32,6... | collective-permute-start | bytes 599048 | tf_op jit(solution)/shard_map/ppermute | solution.py:30
  126.3 5.0 %fusion = f32[12,64,512]{2,1,0:T(8,128)} fusion(bf16[512,12,64]{0,2,1:T(8,128)(2,1)S(1)} %bitcast.55, f32[12,512]{1,0:T(8,128)S(1)} %bitcast.58, f32[512,512]{1,0:T(8,128)S(1)} %fusion.47, pred[512,512]{1,0:T(8,128)(4,1)S(1)} %fusion.11), kind=kOutput, calls=%fused_computation.1 | convolution fusion | flops 415236096 | bytes 3694592 | tf_op jit(solution)/shard_map/while/body/eval_jaxpr/hts,shp->thp/dot_general | solution.py:69
  131.3 0.2 broadcast_select_fusion
  131.5 0.2 convert_reduce_fusion.1
  131.7 0.2 fusion.70
  132.0 9.6 %collective-permute-start.4 = (bf16[12,65,128]{2,1,0:T(8,128)(2,1)S(1)}, bf16[12,65,128]{2,1,0:T(8,128)(2,1)S(1)}, u32[]{:S(2)}, u32[]{:S(2)}) collective-permute-start(bf16[12,65,128]{2,1,0:T(8,128)(2,1)S(1)} %pad_maximum_fusion.4), channel_id=1, source_target_pairs={{0,64},{4,68},{8,72},{12,76},{16,80},{20,84},{24,88},{28,92},{32,9... | collective-permute-start | bytes 599048 | tf_op jit(solution)/shard_map/ppermute | solution.py:30
  141.6 2.8 %collective-permute-done.4 = bf16[12,65,128]{2,1,0:T(8,128)(2,1)S(1)} collective-permute-done((bf16[12,65,128]{2,1,0:T(8,128)(2,1)S(1)}, bf16[12,65,128]{2,1,0:T(8,128)(2,1)S(1)}, u32[]{:S(2)}, u32[]{:S(2)}) %collective-permute-start.4) | collective-permute-done | bytes 199712 | tf_op jit(solution)/shard_map/ppermute | solution.py:30
  144.5 0.2 fusion.54
  144.6 0.6 copy-done.2
  145.2 0.1 fusion.16
  145.5 10.9 %collective-permute-start.5 = (bf16[12,65,128]{2,1,0:T(8,128)(2,1)S(1)}, bf16[12,65,128]{2,1,0:T(8,128)(2,1)}, u32[]{:S(2)}, u32[]{:S(2)}) collective-permute-start(bf16[12,65,128]{2,1,0:T(8,128)(2,1)S(1)} %pad_maximum_fusion.5), channel_id=1, source_target_pairs={{0,128},{4,132},{8,136},{12,140},{16,144},{20,148},{24,152},{28,15... | collective-permute-start | bytes 599048 | tf_op jit(solution)/shard_map/ppermute | solution.py:30
  156.4 0.2 reduce.19
  156.6 0.2 reduce.18
  156.8 1.0 fusion.55
  157.8 0.8 collective-permute-done.5
  158.6 3.2 %fusion.7 = f32[512,12,64]{0,2,1:T(8,128)S(1)} fusion(f32[12,64,512]{2,1,0:T(8,128)} %fusion, bf16[512,12,64]{0,2,1:T(8,128)(2,1)} %bitcast.54, f32[12]{0:T(128)S(1)} %copy-done.10, f32[512,12]{0,1:T(8,128)S(1)} %exponential_multiply_fusion, f32[12,65,128]{2,1,0:T(8,128)} %copy-done.2, f32[12,65,128]{2,1,0:T(8,128)} %copy-done.3, ...), kind=kOutput, calls=%fused_computation.15 | convolution fusion | flops 607617024 | bytes 6261766 | tf_op jit(solution)/shard_map/while/body/eval_jaxpr/tn,hpn->thp/dot_general | solution.py:74
  161.8 2.8 %multiply_reduce_fusion = (f32[512]{0:T(512)S(1)}, f32[512,768]{0,1:T(8,128)}) fusion(bf16[512,1806]{0,1:T(8,128)(2,1)} %copy-done.6, f32[512,12,64]{0,2,1:T(8,128)S(1)} %fusion.7), kind=kLoop, calls=%fused_computation.17 | loop fusion | flops 3145216 | bytes 3934208 | tf_op jit(solution)/shard_map/reduce_sum | solution.py:192
  164.6 8.7 %psum.7 = f32[512]{0:T(512)S(1)} all-reduce(f32[512]{0:T(512)S(1)} %get-tuple-element.55), channel_id=1, replica_groups=mesh['seq'=64,'head'=4] {'head'}, use_global_device_ids=true, to_apply=%region_9.10 | all-reduce | flops 512 | bytes 4096 | tf_op jit(solution)/shard_map/psum | solution.py:192
  173.3 4.1 %convolution_convert_fusion = bf16[512,1536]{1,0:T(8,128)(2,1)} fusion(bf16[768,1536]{1,0:T(8,128)(2,1)S(1)} %copy-done, f32[512,768]{0,1:T(8,128)} %get-tuple-element.68, f32[768]{0:T(1024)S(1)} %copy-done.13, f32[512]{0:T(512)S(1)} %add_rsqrt_fusion), kind=kOutput, calls=%fused_computation.4 | convolution fusion | flops 1209925632 | bytes 5510144 | tf_op jit(solution)/shard_map/dot_general | solution.py:196
  177.4 26.7 %reduce-scatter.2.cloned.1.call-done = bf16[128,1536]{1,0:T(8,128)(2,1)} async-done(((bf16[512,1536]{1,0:T(8,128)(2,1)}), bf16[128,1536]{1,0:T(8,128)(2,1)}) %reduce-scatter.2.cloned.1.call-update) | async-done | bytes 393232 | tf_op jit(solution)/shard_map/reduce_scatter | solution.py:195
  (67 shorter events, 1.2 us)
Async XLA Ops:
  6.5 166.7 %copy-start = (bf16[768,1536]{1,0:T(8,128)(2,1)S(1)}, bf16[768,1536]{1,0:T(8,128)(2,1)}, u32[]{:S(2)}) copy-start(bf16[768,1536]{1,0:T(8,128)(2,1)} %param.19) | copy-start | bytes 7077892
  22.6 13.3 %copy-start.11 = (s32[4]{0:T(128)S(1)}, s32[4]{0:T(128)}, u32[]{:S(2)}) copy-start(s32[4]{0:T(128)} %param.16) | copy-start | bytes 52
  22.6 61.5 %all-to-all-start = ((bf16[64,8,1806]{2,1,0:T(8,128)(2,1)}), bf16[64,8,1806]{2,1,0:T(8,128)(2,1)}, u32[]{:S(2)}, u32[]{:S(2)}) async-start(bf16[64,8,1806]{2,1,0:T(8,128)(2,1)} %bitcast.52), calls=%async_computation | async-start | bytes 3932160 | tf_op jit(solution)/shard_map/all_to_all | solution.py:116
  35.9 168.2 %reduce-scatter.2.cloned.1.call-start = ((), (), s32[]{:S(2)}) async-start(), calls=%async_computation.2 | async-start | bytes 1966080 | tf_op jit(solution)/shard_map/reduce_scatter | solution.py:195
  88.1 1.3 copy-start.6
  88.1 7.1 %copy-start.4 = (bf16[512,768]{0,1:T(8,128)(2,1)}, bf16[512,768]{0,1:T(8,128)(2,1)S(1)}, u32[]{:S(2)}) copy-start(bf16[512,768]{0,1:T(8,128)(2,1)S(1)} %slice.107) | copy-start | bytes 2359300
  90.9 2.3 %copy-start.7 = (f32[2,8,4,128]{3,1,2,0:T(8,128)}, f32[2,8,4,128]{3,1,2,0:T(8,128)S(1)}, u32[]{:S(2)}) copy-start(f32[2,8,4,128]{3,1,2,0:T(8,128)S(1)} %copy.57) | copy-start | bytes 98308
  93.1 2.2 %copy-start.12 = (bf16[12]{0:T(256)(128)(2,1)S(1)}, bf16[12]{0:T(256)(128)(2,1)}, u32[]{:S(2)}) copy-start(bf16[12]{0:T(256)(128)(2,1)} %convert.49) | copy-start | bytes 76
  95.4 5.2 %collective-permute-start = (bf16[12,65,128]{2,1,0:T(8,128)(2,1)S(1)}, bf16[12,65,128]{2,1,0:T(8,128)(2,1)S(1)}, u32[]{:S(2)}, u32[]{:S(2)}) collective-permute-start(bf16[12,65,128]{2,1,0:T(8,128)(2,1)S(1)} %pad_maximum_fusion), channel_id=1, source_target_pairs={{0,4},{4,8},{8,12},{12,16},{16,20},{20,24},{24,28},{28,32},{32,36}... | collective-permute-start | bytes 599048 | tf_op jit(solution)/shard_map/ppermute | solution.py:30
  101.6 6.7 %collective-permute-start.1 = (bf16[12,65,128]{2,1,0:T(8,128)(2,1)S(1)}, bf16[12,65,128]{2,1,0:T(8,128)(2,1)S(1)}, u32[]{:S(2)}, u32[]{:S(2)}) collective-permute-start(bf16[12,65,128]{2,1,0:T(8,128)(2,1)S(1)} %pad_maximum_fusion.1), channel_id=1, source_target_pairs={{0,8},{4,12},{8,16},{12,20},{16,24},{20,28},{24,32},{28,36},{32,40... | collective-permute-start | bytes 599048 | tf_op jit(solution)/shard_map/ppermute | solution.py:30
  108.3 23.0 %copy-start.1 = (f32[12,65,128]{2,1,0:T(8,128)}, f32[12,65,128]{2,1,0:T(8,128)S(1)}, u32[]{:S(2)}) copy-start(f32[12,65,128]{2,1,0:T(8,128)S(1)} %convert_element_type.131) | copy-start | bytes 1198084
  108.9 17.4 %copy-start.5 = (bf16[512,768]{0,1:T(8,128)(2,1)S(1)}, bf16[512,768]{0,1:T(8,128)(2,1)}, u32[]{:S(2)}) copy-start(bf16[512,768]{0,1:T(8,128)(2,1)} %copy-done.4) | copy-start | bytes 2359300
  108.9 17.4 %copy-start.8 = (f32[2,8,4,128]{3,1,2,0:T(8,128)S(1)}, f32[2,8,4,128]{3,1,2,0:T(8,128)}, u32[]{:S(2)}) copy-start(f32[2,8,4,128]{3,1,2,0:T(8,128)} %copy-done.7) | copy-start | bytes 98308
  108.9 7.8 %collective-permute-start.2 = (bf16[12,65,128]{2,1,0:T(8,128)(2,1)S(1)}, bf16[12,65,128]{2,1,0:T(8,128)(2,1)S(1)}, u32[]{:S(2)}, u32[]{:S(2)}) collective-permute-start(bf16[12,65,128]{2,1,0:T(8,128)(2,1)S(1)} %pad_maximum_fusion.2), channel_id=1, source_target_pairs={{0,16},{4,20},{8,24},{12,28},{16,32},{20,36},{24,40},{28,44},{32,4... | collective-permute-start | bytes 599048 | tf_op jit(solution)/shard_map/ppermute | solution.py:30
  117.2 14.1 %collective-permute-start.3 = (bf16[12,65,128]{2,1,0:T(8,128)(2,1)S(1)}, bf16[12,65,128]{2,1,0:T(8,128)(2,1)S(1)}, u32[]{:S(2)}, u32[]{:S(2)}) collective-permute-start(bf16[12,65,128]{2,1,0:T(8,128)(2,1)S(1)} %pad_maximum_fusion.3), channel_id=1, source_target_pairs={{0,32},{4,36},{8,40},{12,44},{16,48},{20,52},{24,56},{28,60},{32,6... | collective-permute-start | bytes 599048 | tf_op jit(solution)/shard_map/ppermute | solution.py:30
  131.3 14.1 %copy-start.3 = (f32[12,65,128]{2,1,0:T(8,128)}, f32[12,65,128]{2,1,0:T(8,128)S(1)}, u32[]{:S(2)}) copy-start(f32[12,65,128]{2,1,0:T(8,128)S(1)} %convert_element_type.133) | copy-start | bytes 1198084
  131.7 26.9 %copy-start.9 = (f32[12]{0:T(128)S(1)}, f32[12]{0:T(128)}, u32[]{:S(2)}) copy-start(f32[12]{0:T(128)} %get-tuple-element.48) | copy-start | bytes 148
  131.7 26.9 %copy-start.10 = (f32[12]{0:T(128)S(1)}, f32[12]{0:T(128)}, u32[]{:S(2)}) copy-start(f32[12]{0:T(128)} %param.17) | copy-start | bytes 148
  132.0 12.4 %collective-permute-start.4 = (bf16[12,65,128]{2,1,0:T(8,128)(2,1)S(1)}, bf16[12,65,128]{2,1,0:T(8,128)(2,1)S(1)}, u32[]{:S(2)}, u32[]{:S(2)}) collective-permute-start(bf16[12,65,128]{2,1,0:T(8,128)(2,1)S(1)} %pad_maximum_fusion.4), channel_id=1, source_target_pairs={{0,64},{4,68},{8,72},{12,76},{16,80},{20,84},{24,88},{28,92},{32,9... | collective-permute-start | bytes 599048 | tf_op jit(solution)/shard_map/ppermute | solution.py:30
  144.5 0.8 copy-start.2
  145.5 13.1 %collective-permute-start.5 = (bf16[12,65,128]{2,1,0:T(8,128)(2,1)S(1)}, bf16[12,65,128]{2,1,0:T(8,128)(2,1)}, u32[]{:S(2)}, u32[]{:S(2)}) collective-permute-start(bf16[12,65,128]{2,1,0:T(8,128)(2,1)S(1)} %pad_maximum_fusion.5), channel_id=1, source_target_pairs={{0,128},{4,132},{8,136},{12,140},{16,144},{20,148},{24,152},{28,15... | collective-permute-start | bytes 599048 | tf_op jit(solution)/shard_map/ppermute | solution.py:30
  161.8 11.5 %copy-start.13 = (f32[768]{0:T(1024)S(1)}, f32[768]{0:T(1024)}, u32[]{:S(2)}) copy-start(f32[768]{0:T(1024)} %param.18) | copy-start | bytes 9220
Sparse Core Ops, SparseCore 0:
  177.5 26.5 reduce-scatter.1

commit v2 on v1

--- a/solution.py
+++ b/solution.py
@@ -16,7 +16,7 @@
     return (earlier[0] * later[0], later[0][:, None, None] * earlier[1] + later[1])
 
 
-def exclusive_prefix(kept, state, axis):
+def exclusive_prefix(kept, state, axis, radix=4):
     length, here = (lax.axis_size(axis), lax.axis_index(axis))
     heads = kept.shape[0]
     span = (kept, state)
@@ -26,16 +26,23 @@
         packed = jnp.concatenate(
             [span[1], jnp.broadcast_to(span[0][:, None, None], (heads, 1, state.shape[2]))], axis=1
         ).astype(jnp.bfloat16)
-        pairs = [(j, j + distance) for j in range(length - distance)]
-        got = lax.ppermute(packed, axis, pairs).astype(jnp.float32)
-        got = (got[:, -1, 0], got[:, :-1, :])
-        reached = here >= distance
-        new_before = combine(got, before)
-        before = jax.tree.map(lambda a, b: jnp.where(reached, a, b), new_before, before)
-        if distance * 2 < length:
-            new_span = combine(got, span)
-            span = jax.tree.map(lambda a, b: jnp.where(reached, a, b), new_span, span)
-        distance *= 2
+        gots = []
+        for step in range(1, radix):
+            shift = step * distance
+            if shift < length:
+                pairs = [(j, j + shift) for j in range(length - shift)]
+                gots.append((shift, lax.ppermute(packed, axis, pairs)))
+        last = distance * radix >= length
+        for shift, got in gots:
+            got = got.astype(jnp.float32)
+            got = (got[:, -1, 0], got[:, :-1, :])
+            reached = here >= shift
+            new_before = combine(got, before)
+            before = jax.tree.map(lambda a, b: jnp.where(reached, a, b), new_before, before)
+            if not last:
+                new_span = combine(got, span)
+                span = jax.tree.map(lambda a, b: jnp.where(reached, a, b), new_span, span)
+        distance *= radix
     return before
 
 

time: 212 us -> 216 us (1.019)
  other arithmetic: 15.3 us -> 19.1 us
    ppermute x6 -> x9, waiting for transfers between devices: 11.1 us -> 16.5 us  [exclusive_prefix(): gots.append((shift, lax.ppermute(packed, axis, pairs)))]
    reduce_scatter x1, waiting for transfers between devices: 26.7 us -> 24.3 us  [body(): lax.psum_scatter(jnp.dot(normed, out_weight, preferred_element_type=jnp.f...]
    ppermute x6 -> x9, starting transfers between devices: 40.1 us -> 39 us  [exclusive_prefix(): gots.append((shift, lax.ppermute(packed, axis, pairs)))]
    another operation x18 -> x12, other arithmetic: 4.67 us -> 5.53 us
  transfers between devices with their start and end apart: 8 -> 11, of which waited for: 7 -> 8; matrix products, arithmetic and copies ran while one was open for 5% -> 5% of each run, Pallas kernels for 0% -> 0%
where the time goes in v2:
time: 216 us; the launch traced here: 215 us
  waiting for transfers between devices  84.5 us (39%)
  starting transfers between devices  52.3 us (24%)
  matrix products  23.1 us (11%)
  other arithmetic  19.1 us (9%)
  between operations  15.1 us (7%)
  local copies, waits for them, and re-layouts  12.1 us (6%)
  blocking collectives  8.62 us (4%)
    all_to_all x1, waiting for transfers between devices, body(): lax.all_to_all(packed.reshape(shards, capacity, packed.shape[1]), 'seq',...  43.7 us
    ppermute x9, starting transfers between devices, exclusive_prefix(): gots.append((shift, lax.ppermute(packed, axis, pairs)))  39 us
    reduce_scatter x1, waiting for transfers between devices, body(): lax.psum_scatter(jnp.dot(normed, out_weight, preferred_element_type=jnp.f...  24.3 us
    ppermute x9, waiting for transfers between devices, exclusive_prefix(): gots.append((shift, lax.ppermute(packed, axis, pairs)))  16.5 us
    all_to_all x1, starting transfers between devices, body(): lax.all_to_all(packed.reshape(shards, capacity, packed.shape[1]), 'seq',...  13.3 us
    psum x1, blocking collectives, body(): squares = lax.psum(jnp.sum(gated * gated, axis=1), 'head')  8.62 us
    another operation x12, other arithmetic  5.53 us
    dot_general x1, matrix products, inner_terms(): jnp.einsum('hts,shp->thp', affinity_logits, by_head, preferred_element_ty...  4.93 us
  transfers between devices with their start and end apart: 11, of which 8 were waited for; matrix products, arithmetic and copies ran while one was open for 5% of the time, Pallas kernels for 0%

profile of v2, /device:TPU:1, one launch (start us, length us, event | category | flops | bytes accessed | tf_op | source)
XLA Modules:
  0.0 214.9 jit_solution(6165856639712629981)
XLA Ops:
  6.5 1.0 copy.44
  7.6 0.7 fusion.65
  8.3 1.2 reduce-window.24
  9.5 0.2 slice_reduce_fusion
  9.9 0.7 multiply_add_fusion
  10.6 0.1 broadcast_in_dim.67
  10.9 3.8 %concatenate.15 = bf16[512,1806]{1,0:T(8,128)(2,1)} concatenate(bf16[512,768]{1,0:T(8,128)(2,1)} %param.10, bf16[512,768]{1,0:T(8,128)(2,1)} %param.11, bf16[512,128]{1,0:T(8,128)(2,1)} %param.12, bf16[512,128]{1,0:T(8,128)(2,1)} %param.13, bf16[512,12]{1,0:T(8,128)(2,1)S(1)} %copy.44, bf16[512,1]{1,0:T(8,128)(2,1)S(1)} %broadcast_in_dim.67, bf16[512,1]{1,0:T(8,128)(2,1)S(1)} %broadcast_in_dim.68), dimensions={1} | concatenate | bytes 3698688 | tf_op jit(solution)/shard_map/concatenate | solution.py:115
  14.7 4.0 %convolution_convert_fusion.2 = bf16[512,1806]{0,1:T(8,128)(2,1)} fusion(bf16[512,1806]{1,0:T(8,128)(2,1)} %concatenate.15, s32[512]{0:T(512)S(1)} %get-tuple-element.109), kind=kOutput, calls=%fused_computation.6 | convolution fusion | flops 948050944 | bytes 3700736 | tf_op jit(solution)/shard_map/dot_general | solution.py:122
  18.7 4.0 %copy.47 = bf16[512,1806]{1,0:T(8,128)(2,1)} copy(bf16[512,1806]{0,1:T(8,128)(2,1)} %convolution_convert_fusion.2) | data formatting | bytes 3698688 | tf_op jit(solution)/shard_map/convert_element_type | solution.py:122
  22.6 13.3 %all-to-all-start = ((bf16[64,8,1806]{2,1,0:T(8,128)(2,1)}), bf16[64,8,1806]{2,1,0:T(8,128)(2,1)}, u32[]{:S(2)}, u32[]{:S(2)}) async-start(bf16[64,8,1806]{2,1,0:T(8,128)(2,1)} %bitcast.52), calls=%async_computation | async-start | bytes 3932160 | tf_op jit(solution)/shard_map/all_to_all | solution.py:123
  36.0 0.2 reduce-window.31
  36.2 0.6 fusion.68
  36.9 0.6 slice.108
  38.8 0.6 compare_convert_fusion.1
  39.5 0.9 fusion.11
  40.4 43.7 %all-to-all-done = bf16[64,8,1806]{2,1,0:T(8,128)(2,1)} async-done(((bf16[64,8,1806]{2,1,0:T(8,128)(2,1)}), bf16[64,8,1806]{2,1,0:T(8,128)(2,1)}, u32[]{:S(2)}, u32[]{:S(2)}) %all-to-all-start) | async-done | bytes 1849376 | tf_op jit(solution)/shard_map/all_to_all | solution.py:123
  84.1 1.2 add_reduce_fusion
  85.3 2.8 %convolution_convert_fusion.1 = bf16[512,1806]{0,1:T(8,128)(2,1)S(1)} fusion(s32[512]{0:T(512)S(1)} %add_reduce_fusion, bf16[64,8,1806]{2,1,0:T(8,128)(2,1)} %all-to-all-done), kind=kOutput, calls=%fused_computation.5 | convolution fusion | flops 948050944 | bytes 3700736 | tf_op jit(solution)/shard_map/dot_general | solution.py:133
  88.2 1.6 fusion.55
  89.8 1.2 reduce-window.32
  90.9 0.2 slice_reduce_fusion.1
  91.3 0.2 multiply_reduce_fusion.1
  91.5 0.9 copy.50
  92.5 2.1 fusion.77
  94.7 2.3 %collective-permute-start.1 = (bf16[12,65,128]{2,1,0:T(8,128)(2,1)S(1)}, bf16[12,65,128]{2,1,0:T(8,128)(2,1)S(1)}, u32[]{:S(2)}, u32[]{:S(2)}) collective-permute-start(bf16[12,65,128]{2,1,0:T(8,128)(2,1)S(1)} %pad_maximum_fusion), channel_id=1, source_target_pairs={{0,4},{4,8},{8,12},{12,16},{16,20},{20,24},{24,28},{28,32},{32,36}... | collective-permute-start | bytes 599048 | tf_op jit(solution)/shard_map/ppermute | solution.py:34
  97.0 3.3 %collective-permute-start = (bf16[12,65,128]{2,1,0:T(8,128)(2,1)S(1)}, bf16[12,65,128]{2,1,0:T(8,128)(2,1)S(1)}, u32[]{:S(2)}, u32[]{:S(2)}) collective-permute-start(bf16[12,65,128]{2,1,0:T(8,128)(2,1)S(1)} %pad_maximum_fusion), channel_id=1, source_target_pairs={{0,8},{4,12},{8,16},{12,20},{16,24},{20,28},{24,32},{28,36},{32,40... | collective-permute-start | bytes 599048 | tf_op jit(solution)/shard_map/ppermute | solution.py:34
  100.3 2.2 %collective-permute-start.2 = (bf16[12,65,128]{2,1,0:T(8,128)(2,1)S(1)}, bf16[12,65,128]{2,1,0:T(8,128)(2,1)S(1)}, u32[]{:S(2)}, u32[]{:S(2)}) collective-permute-start(bf16[12,65,128]{2,1,0:T(8,128)(2,1)S(1)} %pad_maximum_fusion), channel_id=1, source_target_pairs={{0,12},{4,16},{8,20},{12,24},{16,28},{20,32},{24,36},{28,40},{32,4... | collective-permute-start | bytes 599048 | tf_op jit(solution)/shard_map/ppermute | solution.py:34
  102.6 4.9 %fusion = f32[12,64,512]{2,1,0:T(8,128)} fusion(bf16[512,12,64]{0,2,1:T(8,128)(2,1)S(1)} %bitcast.54, f32[12,512]{1,0:T(8,128)S(1)} %bitcast.58, f32[512,512]{1,0:T(8,128)S(1)} %copy-done.8, pred[512,512]{1,0:T(8,128)(4,1)S(1)} %copy-done.9), kind=kOutput, calls=%fused_computation.1 | convolution fusion | flops 415236096 | bytes 3694592 | tf_op jit(solution)/shard_map/while/body/eval_jaxpr/hts,shp->thp/dot_general | solution.py:76
  107.6 0.3 fusion.62
  107.9 3.2 %collective-permute-done.2 = bf16[12,65,128]{2,1,0:T(8,128)(2,1)S(1)} collective-permute-done((bf16[12,65,128]{2,1,0:T(8,128)(2,1)S(1)}, bf16[12,65,128]{2,1,0:T(8,128)(2,1)S(1)}, u32[]{:S(2)}, u32[]{:S(2)}) %collective-permute-start.2) | collective-permute-done | bytes 199712 | tf_op jit(solution)/shard_map/ppermute | solution.py:34
  111.1 0.2 convert_reduce_fusion.1
  111.3 1.0 fusion.75
  112.4 0.7 pad_maximum_fusion.1
  113.1 8.1 %collective-permute-start.3 = (bf16[12,65,128]{2,1,0:T(8,128)(2,1)}, bf16[12,65,128]{2,1,0:T(8,128)(2,1)S(1)}, u32[]{:S(2)}, u32[]{:S(2)}) collective-permute-start(bf16[12,65,128]{2,1,0:T(8,128)(2,1)} %pad_maximum_fusion.1), channel_id=1, source_target_pairs={{0,32},{4,36},{8,40},{12,44},{16,48},{20,52},{24,56},{28,60},{32,6... | collective-permute-start | bytes 599048 | tf_op jit(solution)/shard_map/ppermute | solution.py:34
  121.2 2.5 %collective-permute-start.4 = (bf16[12,65,128]{2,1,0:T(8,128)(2,1)}, bf16[12,65,128]{2,1,0:T(8,128)(2,1)S(1)}, u32[]{:S(2)}, u32[]{:S(2)}) collective-permute-start(bf16[12,65,128]{2,1,0:T(8,128)(2,1)} %pad_maximum_fusion.1), channel_id=1, source_target_pairs={{0,16},{4,20},{8,24},{12,28},{16,32},{20,36},{24,40},{28,44},{32,4... | collective-permute-start | bytes 599048 | tf_op jit(solution)/shard_map/ppermute | solution.py:34
  123.7 5.5 %collective-permute-start.5 = (bf16[12,65,128]{2,1,0:T(8,128)(2,1)}, bf16[12,65,128]{2,1,0:T(8,128)(2,1)}, u32[]{:S(2)}, u32[]{:S(2)}) collective-permute-start(bf16[12,65,128]{2,1,0:T(8,128)(2,1)} %pad_maximum_fusion.1), channel_id=1, source_target_pairs={{0,48},{4,52},{8,56},{12,60},{16,64},{20,68},{24,72},{28,76},{32,8... | collective-permute-start | bytes 599048 | tf_op jit(solution)/shard_map/ppermute | solution.py:34
  129.2 0.2 slice_reduce_fusion.3
  129.4 1.7 collective-permute-done.3
  131.1 4.7 %collective-permute-done.4 = bf16[12,65,128]{2,1,0:T(8,128)(2,1)S(1)} collective-permute-done((bf16[12,65,128]{2,1,0:T(8,128)(2,1)}, bf16[12,65,128]{2,1,0:T(8,128)(2,1)S(1)}, u32[]{:S(2)}, u32[]{:S(2)}) %collective-permute-start.4) | collective-permute-done | bytes 199712 | tf_op jit(solution)/shard_map/ppermute | solution.py:34
  135.8 0.2 fusion.74
  136.0 0.6 copy-done.3
  136.6 0.2 reduce.11
  136.8 2.4 %collective-permute-done.5 = bf16[12,65,128]{2,1,0:T(8,128)(2,1)} collective-permute-done((bf16[12,65,128]{2,1,0:T(8,128)(2,1)}, bf16[12,65,128]{2,1,0:T(8,128)(2,1)}, u32[]{:S(2)}, u32[]{:S(2)}) %collective-permute-start.5) | collective-permute-done | bytes 199712 | tf_op jit(solution)/shard_map/ppermute | solution.py:34
  139.2 1.0 convert_element_type.141
  140.2 0.2 fusion.60
  140.4 1.5 fusion.16
  141.9 0.7 pad_maximum_fusion.2
  142.6 7.3 %collective-permute-start.7 = (bf16[12,65,128]{2,1,0:T(8,128)(2,1)}, bf16[12,65,128]{2,1,0:T(8,128)(2,1)S(1)}, u32[]{:S(2)}, u32[]{:S(2)}) collective-permute-start(bf16[12,65,128]{2,1,0:T(8,128)(2,1)} %pad_maximum_fusion.2), channel_id=1, source_target_pairs={{0,64},{4,68},{8,72},{12,76},{16,80},{20,84},{24,88},{28,92},{32,9... | collective-permute-start | bytes 599048 | tf_op jit(solution)/shard_map/ppermute | solution.py:34
  149.9 5.9 %collective-permute-start.6 = (bf16[12,65,128]{2,1,0:T(8,128)(2,1)}, bf16[12,65,128]{2,1,0:T(8,128)(2,1)S(1)}, u32[]{:S(2)}, u32[]{:S(2)}) collective-permute-start(bf16[12,65,128]{2,1,0:T(8,128)(2,1)} %pad_maximum_fusion.2), channel_id=1, source_target_pairs={{0,128},{4,132},{8,136},{12,140},{16,144},{20,148},{24,152},{28,15... | collective-permute-start | bytes 599048 | tf_op jit(solution)/shard_map/ppermute | solution.py:34
  155.8 2.0 collective-permute-start.8
  157.9 1.1 broadcast_select_fusion
  158.9 0.2 reduce.22
  159.1 0.2 reduce.21
  159.3 0.2 reduce.20
  159.5 0.2 reduce.19
  159.6 0.2 reduce.18
  159.8 0.6 collective-permute-done.6
  160.4 0.2 fusion.61
  160.6 3.9 %collective-permute-done.8 = bf16[12,65,128]{2,1,0:T(8,128)(2,1)} collective-permute-done((bf16[12,65,128]{2,1,0:T(8,128)(2,1)}, bf16[12,65,128]{2,1,0:T(8,128)(2,1)}, u32[]{:S(2)}, u32[]{:S(2)}) %collective-permute-start.8) | collective-permute-done | bytes 199712 | tf_op jit(solution)/shard_map/ppermute | solution.py:34
  164.5 3.6 %fusion.7 = f32[512,12,64]{0,2,1:T(8,128)S(1)} fusion(f32[12,64,512]{2,1,0:T(8,128)} %fusion, bf16[512,12,64]{0,2,1:T(8,128)(2,1)} %bitcast.55, f32[12]{0:T(128)} %param.17, f32[512,12]{0,1:T(8,128)S(1)} %exponential_multiply_fusion, f32[12,65,128]{2,1,0:T(8,128)} %copy-done.7, f32[12,65,128]{2,1,0:T(8,128)S(1)} %convert_element_type.142, ...), kind=kOutput, calls=%fused_computation.15 | convolution fusion | flops 608501760 | bytes 7442953 | tf_op jit(solution)/shard_map/while/body/eval_jaxpr/tn,hpn->thp/dot_general | solution.py:81
  168.2 2.8 %multiply_reduce_fusion = (f32[512]{0:T(512)S(1)}, f32[512,768]{0,1:T(8,128)}) fusion(bf16[512,1806]{0,1:T(8,128)(2,1)} %copy-done.6, f32[512,12,64]{0,2,1:T(8,128)S(1)} %fusion.7), kind=kLoop, calls=%fused_computation.17 | loop fusion | flops 3145216 | bytes 3934208 | tf_op jit(solution)/shard_map/reduce_sum | solution.py:199
  171.0 8.6 %psum.7 = f32[512]{0:T(512)S(1)} all-reduce(f32[512]{0:T(512)S(1)} %get-tuple-element.55), channel_id=1, replica_groups=mesh['seq'=64,'head'=4] {'head'}, use_global_device_ids=true, to_apply=%region_9.10 | all-reduce | flops 512 | bytes 4096 | tf_op jit(solution)/shard_map/psum | solution.py:199
  179.6 4.1 %convolution_convert_fusion = bf16[512,1536]{1,0:T(8,128)(2,1)} fusion(bf16[768,1536]{1,0:T(8,128)(2,1)S(1)} %copy-done, f32[512,768]{0,1:T(8,128)} %get-tuple-element.68, f32[768]{0:T(1024)S(1)} %copy-done.11, f32[512]{0:T(512)S(1)} %add_rsqrt_fusion), kind=kOutput, calls=%fused_computation.4 | convolution fusion | flops 1209925632 | bytes 5510144 | tf_op jit(solution)/shard_map/dot_general | solution.py:203
  183.7 24.3 %reduce-scatter.2.cloned.1.call-done = bf16[128,1536]{1,0:T(8,128)(2,1)} async-done(((bf16[512,1536]{1,0:T(8,128)(2,1)}), bf16[128,1536]{1,0:T(8,128)(2,1)}) %reduce-scatter.2.cloned.1.call-update) | async-done | bytes 393232 | tf_op jit(solution)/shard_map/reduce_scatter | solution.py:202
  (64 shorter events, 1.4 us)
Async XLA Ops:
  6.5 173.1 %copy-start = (bf16[768,1536]{1,0:T(8,128)(2,1)S(1)}, bf16[768,1536]{1,0:T(8,128)(2,1)}, u32[]{:S(2)}) copy-start(bf16[768,1536]{1,0:T(8,128)(2,1)} %param.19) | copy-start | bytes 7077892
  22.6 13.3 %copy-start.10 = (s32[4]{0:T(128)S(1)}, s32[4]{0:T(128)}, u32[]{:S(2)}) copy-start(s32[4]{0:T(128)} %param.16) | copy-start | bytes 52
  22.6 61.4 %all-to-all-start = ((bf16[64,8,1806]{2,1,0:T(8,128)(2,1)}), bf16[64,8,1806]{2,1,0:T(8,128)(2,1)}, u32[]{:S(2)}, u32[]{:S(2)}) async-start(bf16[64,8,1806]{2,1,0:T(8,128)(2,1)} %bitcast.52), calls=%async_computation | async-start | bytes 3932160 | tf_op jit(solution)/shard_map/all_to_all | solution.py:123
  35.9 172.1 %reduce-scatter.2.cloned.1.call-start = ((), (), s32[]{:S(2)}) async-start(), calls=%async_computation.2 | async-start | bytes 1966080 | tf_op jit(solution)/shard_map/reduce_scatter | solution.py:202
  88.1 1.7 copy-start.6
  88.1 14.4 %copy-start.5 = (bf16[512,768]{0,1:T(8,128)(2,1)}, bf16[512,768]{0,1:T(8,128)(2,1)S(1)}, u32[]{:S(2)}) copy-start(bf16[512,768]{0,1:T(8,128)(2,1)S(1)} %slice.131) | copy-start | bytes 2359300
  92.4 10.2 %copy-start.8 = (f32[512,512]{1,0:T(8,128)S(1)}, f32[512,512]{1,0:T(8,128)}, u32[]{:S(2)}) copy-start(f32[512,512]{1,0:T(8,128)} %fusion.55) | copy-start | bytes 3145732
  92.4 10.2 %copy-start.9 = (pred[512,512]{1,0:T(8,128)(4,1)S(1)}, pred[512,512]{1,0:T(8,128)(4,1)}, u32[]{:S(2)}) copy-start(pred[512,512]{1,0:T(8,128)(4,1)} %fusion.11) | copy-start | bytes 786436
  94.7 12.8 %collective-permute-start.1 = (bf16[12,65,128]{2,1,0:T(8,128)(2,1)S(1)}, bf16[12,65,128]{2,1,0:T(8,128)(2,1)S(1)}, u32[]{:S(2)}, u32[]{:S(2)}) collective-permute-start(bf16[12,65,128]{2,1,0:T(8,128)(2,1)S(1)} %pad_maximum_fusion), channel_id=1, source_target_pairs={{0,4},{4,8},{8,12},{12,16},{16,20},{20,24},{24,28},{28,32},{32,36}... | collective-permute-start | bytes 599048 | tf_op jit(solution)/shard_map/ppermute | solution.py:34
  97.0 10.5 %collective-permute-start = (bf16[12,65,128]{2,1,0:T(8,128)(2,1)S(1)}, bf16[12,65,128]{2,1,0:T(8,128)(2,1)S(1)}, u32[]{:S(2)}, u32[]{:S(2)}) collective-permute-start(bf16[12,65,128]{2,1,0:T(8,128)(2,1)S(1)} %pad_maximum_fusion), channel_id=1, source_target_pairs={{0,8},{4,12},{8,16},{12,20},{16,24},{20,28},{24,32},{28,36},{32,40... | collective-permute-start | bytes 599048 | tf_op jit(solution)/shard_map/ppermute | solution.py:34
  100.3 10.8 %collective-permute-start.2 = (bf16[12,65,128]{2,1,0:T(8,128)(2,1)S(1)}, bf16[12,65,128]{2,1,0:T(8,128)(2,1)S(1)}, u32[]{:S(2)}, u32[]{:S(2)}) collective-permute-start(bf16[12,65,128]{2,1,0:T(8,128)(2,1)S(1)} %pad_maximum_fusion), channel_id=1, source_target_pairs={{0,12},{4,16},{8,20},{12,24},{16,28},{20,32},{24,36},{28,40},{32,4... | collective-permute-start | bytes 599048 | tf_op jit(solution)/shard_map/ppermute | solution.py:34
  107.6 23.5 %copy-start.1 = (f32[12,65,128]{2,1,0:T(8,128)}, f32[12,65,128]{2,1,0:T(8,128)S(1)}, u32[]{:S(2)}) copy-start(f32[12,65,128]{2,1,0:T(8,128)S(1)} %convert_element_type.136) | copy-start | bytes 1198084
  113.1 17.9 %collective-permute-start.3 = (bf16[12,65,128]{2,1,0:T(8,128)(2,1)}, bf16[12,65,128]{2,1,0:T(8,128)(2,1)S(1)}, u32[]{:S(2)}, u32[]{:S(2)}) collective-permute-start(bf16[12,65,128]{2,1,0:T(8,128)(2,1)} %pad_maximum_fusion.1), channel_id=1, source_target_pairs={{0,32},{4,36},{8,40},{12,44},{16,48},{20,52},{24,56},{28,60},{32,6... | collective-permute-start | bytes 599048 | tf_op jit(solution)/shard_map/ppermute | solution.py:34
  121.2 14.6 %collective-permute-start.4 = (bf16[12,65,128]{2,1,0:T(8,128)(2,1)}, bf16[12,65,128]{2,1,0:T(8,128)(2,1)S(1)}, u32[]{:S(2)}, u32[]{:S(2)}) collective-permute-start(bf16[12,65,128]{2,1,0:T(8,128)(2,1)} %pad_maximum_fusion.1), channel_id=1, source_target_pairs={{0,16},{4,20},{8,24},{12,28},{16,32},{20,36},{24,40},{28,44},{32,4... | collective-permute-start | bytes 599048 | tf_op jit(solution)/shard_map/ppermute | solution.py:34
  123.7 15.5 %collective-permute-start.5 = (bf16[12,65,128]{2,1,0:T(8,128)(2,1)}, bf16[12,65,128]{2,1,0:T(8,128)(2,1)}, u32[]{:S(2)}, u32[]{:S(2)}) collective-permute-start(bf16[12,65,128]{2,1,0:T(8,128)(2,1)} %pad_maximum_fusion.1), channel_id=1, source_target_pairs={{0,48},{4,52},{8,56},{12,60},{16,64},{20,68},{24,72},{28,76},{32,8... | collective-permute-start | bytes 599048 | tf_op jit(solution)/shard_map/ppermute | solution.py:34
  131.1 4.7 %copy-start.2 = (f32[12,65,128]{2,1,0:T(8,128)}, f32[12,65,128]{2,1,0:T(8,128)S(1)}, u32[]{:S(2)}) copy-start(f32[12,65,128]{2,1,0:T(8,128)S(1)} %convert_element_type.139) | copy-start | bytes 1198084
  135.8 0.8 copy-start.3
  140.2 17.7 %copy-start.4 = (f32[12,65,128]{2,1,0:T(8,128)}, f32[12,65,128]{2,1,0:T(8,128)S(1)}, u32[]{:S(2)}) copy-start(f32[12,65,128]{2,1,0:T(8,128)S(1)} %convert_element_type.141) | copy-start | bytes 1198084
  142.6 15.2 %collective-permute-start.7 = (bf16[12,65,128]{2,1,0:T(8,128)(2,1)}, bf16[12,65,128]{2,1,0:T(8,128)(2,1)S(1)}, u32[]{:S(2)}, u32[]{:S(2)}) collective-permute-start(bf16[12,65,128]{2,1,0:T(8,128)(2,1)} %pad_maximum_fusion.2), channel_id=1, source_target_pairs={{0,64},{4,68},{8,72},{12,76},{16,80},{20,84},{24,88},{28,92},{32,9... | collective-permute-start | bytes 599048 | tf_op jit(solution)/shard_map/ppermute | solution.py:34
  149.9 10.4 %collective-permute-start.6 = (bf16[12,65,128]{2,1,0:T(8,128)(2,1)}, bf16[12,65,128]{2,1,0:T(8,128)(2,1)S(1)}, u32[]{:S(2)}, u32[]{:S(2)}) collective-permute-start(bf16[12,65,128]{2,1,0:T(8,128)(2,1)} %pad_maximum_fusion.2), channel_id=1, source_target_pairs={{0,128},{4,132},{8,136},{12,140},{16,144},{20,148},{24,152},{28,15... | collective-permute-start | bytes 599048 | tf_op jit(solution)/shard_map/ppermute | solution.py:34
  155.8 8.7 %collective-permute-start.8 = (bf16[12,65,128]{2,1,0:T(8,128)(2,1)}, bf16[12,65,128]{2,1,0:T(8,128)(2,1)}, u32[]{:S(2)}, u32[]{:S(2)}) collective-permute-start(bf16[12,65,128]{2,1,0:T(8,128)(2,1)} %pad_maximum_fusion.2), channel_id=1, source_target_pairs={{0,192},{4,196},{8,200},{12,204},{16,208},{20,212},{24,216},{28,22... | collective-permute-start | bytes 599048 | tf_op jit(solution)/shard_map/ppermute | solution.py:34
  157.9 1.1 copy-start.7
  168.2 11.5 %copy-start.11 = (f32[768]{0:T(1024)S(1)}, f32[768]{0:T(1024)}, u32[]{:S(2)}) copy-start(f32[768]{0:T(1024)} %param.18) | copy-start | bytes 9220
Sparse Core Ops, SparseCore 0:
  183.8 24.1 reduce-scatter.1

commit v3 on v1

--- a/solution.py
+++ b/solution.py
@@ -16,27 +16,38 @@
     return (earlier[0] * later[0], later[0][:, None, None] * earlier[1] + later[1])
 
 
-def exclusive_prefix(kept, state, axis):
-    length, here = (lax.axis_size(axis), lax.axis_index(axis))
-    heads = kept.shape[0]
-    span = (kept, state)
-    before = (jnp.ones_like(kept), jnp.zeros_like(state))
-    distance = 1
-    while distance < length:
-        packed = jnp.concatenate(
-            [span[1], jnp.broadcast_to(span[0][:, None, None], (heads, 1, state.shape[2]))], axis=1
-        ).astype(jnp.bfloat16)
-        pairs = [(j, j + distance) for j in range(length - distance)]
-        got = lax.ppermute(packed, axis, pairs).astype(jnp.float32)
-        got = (got[:, -1, 0], got[:, :-1, :])
-        reached = here >= distance
-        new_before = combine(got, before)
-        before = jax.tree.map(lambda a, b: jnp.where(reached, a, b), new_before, before)
-        if distance * 2 < length:
-            new_span = combine(got, span)
-            span = jax.tree.map(lambda a, b: jnp.where(reached, a, b), new_span, span)
-        distance *= 2
-    return before
+def group_weights(kept, here):
+    count = kept.shape[0]
+    j = lax.broadcasted_iota(jnp.int32, (count, count), 0)
+    k = lax.broadcasted_iota(jnp.int32, (count, count), 1)
+    between = (j < k) & (k < here)
+    after = j < k
+    into_here = jnp.prod(jnp.where(between[:, :, None], kept[None, :, :], 1.0), axis=1)
+    into_here = into_here * (lax.broadcasted_iota(jnp.int32, (count, 1), 0) < here)
+    into_end = jnp.prod(jnp.where(after[:, :, None], kept[None, :, :], 1.0), axis=1)
+    ahead = lax.broadcasted_iota(jnp.int32, (count, 1), 0) < here
+    kept_before = jnp.prod(jnp.where(ahead, kept, 1.0), axis=0)
+    return into_here, into_end, kept_before, jnp.prod(kept, axis=0)
+
+
+def pack_state(kept, state):
+    flat = jnp.broadcast_to(kept[:, None, None], (kept.shape[0], 1, state.shape[2]))
+    return jnp.concatenate([state, flat], axis=1).astype(jnp.bfloat16)
+
+
+def exclusive_prefix(kept, state, outer, inner):
+    gathered = lax.all_gather(pack_state(kept, state), inner)
+    g_kept = gathered[:, :, -1, 0].astype(jnp.float32)
+    g_state = gathered[:, :, :-1, :].astype(jnp.float32)
+    into_here, into_end, kept_before, kept_all = group_weights(g_kept, lax.axis_index(inner))
+    local_before = jnp.einsum("jh,jhpn->hpn", into_here, g_state)
+    group_total = jnp.einsum("jh,jhpn->hpn", into_end, g_state)
+    totals = lax.all_gather(pack_state(kept_all, group_total), outer)
+    t_kept = totals[:, :, -1, 0].astype(jnp.float32)
+    t_state = totals[:, :, :-1, :].astype(jnp.float32)
+    group_into, _, _, _ = group_weights(t_kept, lax.axis_index(outer))
+    group_before = jnp.einsum("jh,jhpn->hpn", group_into, t_state)
+    return kept_before[:, None, None] * group_before + local_before
 
 
 def doc_index(places, starts):
@@ -94,7 +105,7 @@
     feats = features_in.shape[1]
     width = feats // heads_here
     n_state = b_input.shape[1]
-    shards = lax.axis_size("seq")
+    shards = lax.axis_size(("sx", "sz"))
     capacity = tok_dev // shards
     owner = row_target // tok_dev
     local_place = row_target - owner * tok_dev
@@ -114,7 +125,7 @@
     ).astype(jnp.bfloat16)
     packed = jnp.dot(to_slot, rows_out, preferred_element_type=jnp.float32).astype(jnp.bfloat16)
     moved = lax.all_to_all(
-        packed.reshape(shards, capacity, packed.shape[1]), "seq", split_axis=0, concat_axis=0, tiled=True
+        packed.reshape(shards, capacity, packed.shape[1]), ("sx", "sz"), split_axis=0, concat_axis=0, tiled=True
     ).reshape(tok_dev, packed.shape[1])
     columns = packed.shape[1]
     arrived = (
@@ -131,7 +142,7 @@
     decays = rows[:, 2 * feats + 2 * n_state : 2 * feats + 2 * n_state + heads_here]
 
     doc_starts = jnp.cumsum(doc_lengths) - doc_lengths
-    first_place = lax.axis_index("seq") * tok_dev
+    first_place = lax.axis_index(("sx", "sz")) * tok_dev
     blocks = tok_dev // BLOCK
     places = first_place + lax.broadcasted_iota(jnp.int32, (tok_dev,), 0)
     doc_ids = doc_index(places, doc_starts).reshape(blocks, BLOCK)
@@ -161,7 +172,7 @@
     )
     local_state, local_kept = local_carry
     block_states, throughs, runnings = (block_outputs[0], block_outputs[1], block_outputs[2])
-    entry_kept, entry_state = exclusive_prefix(local_kept, local_state, "seq")
+    entry_state = exclusive_prefix(local_kept, local_state, "sx", "sz")
 
     def mix_pass(carry_state, pieces):
         by_head, key_block, query_block, running, doc_block, before, block_state, through = pieces
@@ -201,17 +212,24 @@
 
 
 def solution(mesh):
+    seq = mesh.shape["seq"]
+    inner = 16 if seq % 16 == 0 else seq
+    devices = mesh.devices.reshape(seq // inner, inner, mesh.shape["head"])
+    split_mesh = jax.sharding.Mesh(devices, ("sx", "sz", "head"))
+    rows = ("sx", "sz")
     in_specs = (
-        P("seq", "head"),
-        P("seq", "head"),
-        P("seq", None),
-        P("seq", None),
-        P("seq", "head"),
-        P("seq"),
+        P(rows, "head"),
+        P(rows, "head"),
+        P(rows, None),
+        P(rows, None),
+        P(rows, "head"),
+        P(rows),
         P(),
         P("head"),
         P("head"),
         P("head", None),
     )
-    out_specs = P(("seq", "head"), None)
-    return jax.shard_map(body, mesh=mesh, in_specs=in_specs, out_specs=out_specs, check_vma=False)
+    out_specs = P(("sx", "sz", "head"), None)
+    return jax.shard_map(
+        body, mesh=split_mesh, in_specs=in_specs, out_specs=out_specs, check_vma=False
+    )

time: 212 us -> 213 us (level)
  starting transfers between devices: 53.4 us -> 13.4 us
  waiting for transfers between devices: 82.5 us -> 105 us
  blocking collectives: 8.69 us -> 20.9 us
  matrix products: 22.3 us -> 27.8 us
  local copies, waits for them, and re-layouts: 13.7 us -> 16.7 us
    ppermute x6 -> x0, starting transfers between devices: 40.1 us -> none  [exclusive_prefix(): got = lax.ppermute(packed, axis, pairs).astype(jnp.float32)]
    all_gather x0 -> x1, waiting for transfers between devices: none -> 32.4 us  [exclusive_prefix(): gathered = lax.all_gather(pack_state(kept, state), inner)]
    all_gather x0 -> x1, blocking collectives: none -> 12.5 us  [exclusive_prefix(): totals = lax.all_gather(pack_state(kept_all, group_total), outer)]
    ppermute x6 -> x0, waiting for transfers between devices: 11.1 us -> none  [exclusive_prefix(): got = lax.ppermute(packed, axis, pairs).astype(jnp.float32)]
    dot_general x0 -> x3, matrix products: none -> 6.56 us  [the longest x1 3.95 us: exclusive_prefix(): local_before = jnp.einsum('jh,jhpn->hpn', into_here, g_state)]
    slice x2 -> x3, local copies, waits for them, and re-layouts: 0.35 us -> 4.02 us  [the longest x1 2.83 us: exclusive_prefix(): g_state = gathered[:, :, :-1, :].astype(jnp.float32)]
    select_n x6 -> x0, other arithmetic: 2.27 us -> none  [the longest x5 2.27 us: exclusive_prefix(): jnp.where(reached, a, b)]
    another operation x18 -> x7, other arithmetic: 4.67 us -> 2.68 us
  transfers between devices with their start and end apart: 8 -> 3, of which waited for: 7 -> 3; matrix products, arithmetic and copies ran while one was open for 5% -> 4% of each run, Pallas kernels for 0% -> 0%
where the time goes in v3:
time: 213 us; the launch traced here: 212 us
  waiting for transfers between devices  105 us (49%)
  matrix products  27.8 us (13%)
  blocking collectives  20.9 us (10%)
  local copies, waits for them, and re-layouts  16.7 us (8%)
  between operations  15 us (7%)
  starting transfers between devices  13.4 us (6%)
  other arithmetic  13.2 us (6%)
    all_to_all x1, waiting for transfers between devices, body(): lax.all_to_all(packed.reshape(shards, capacity, packed.shape[1]), ('sx',...  44.7 us
    all_gather x1, waiting for transfers between devices, exclusive_prefix(): gathered = lax.all_gather(pack_state(kept, state), inner)  32.4 us
    reduce_scatter x1, waiting for transfers between devices, body(): lax.psum_scatter(jnp.dot(normed, out_weight, preferred_element_type=jnp.f...  27.6 us
    all_to_all x1, starting transfers between devices, body(): lax.all_to_all(packed.reshape(shards, capacity, packed.shape[1]), ('sx',...  13.3 us
    all_gather x1, blocking collectives, exclusive_prefix(): totals = lax.all_gather(pack_state(kept_all, group_total), outer)  12.5 us
    psum x1, blocking collectives, body(): squares = lax.psum(jnp.sum(gated * gated, axis=1), 'head')  8.42 us
    dot_general x1, matrix products, inner_terms(): jnp.einsum('hts,shp->thp', affinity_logits, by_head, preferred_element_ty...  4.93 us
  transfers between devices with their start and end apart: 3, of which 3 were waited for; matrix products, arithmetic and copies ran while one was open for 4% of the time, Pallas kernels for 0%

profile of v3, /device:TPU:1, one launch (start us, length us, event | category | flops | bytes accessed | tf_op | source)
XLA Modules:
  0.0 211.7 jit_solution(7958366222959184901)
XLA Ops:
  6.5 0.0 copy-start
  6.5 0.8 fusion.41
  7.4 1.2 reduce-window.24
  8.6 0.2 slice_reduce_fusion
  8.9 0.1 fusion.29
  9.0 0.7 multiply_add_fusion
  9.7 0.1 broadcast_in_dim.172
  9.8 0.1 broadcast_in_dim.173
  10.0 0.9 copy.48
  10.9 3.8 %concatenate.29 = bf16[512,1806]{1,0:T(8,128)(2,1)} concatenate(bf16[512,768]{1,0:T(8,128)(2,1)} %param.10, bf16[512,768]{1,0:T(8,128)(2,1)} %param.11, bf16[512,128]{1,0:T(8,128)(2,1)} %param.12, bf16[512,128]{1,0:T(8,128)(2,1)} %param.13, bf16[512,12]{1,0:T(8,128)(2,1)S(1)} %copy.48, bf16[512,1]{1,0:T(8,128)(2,1)S(1)} %broadcast_in_dim.172, bf16[512,1]{1,0:T(8,128)(2,1)S(1)} %broadcast_in_dim.173), dimensions={1} | concatenate | bytes 3698688 | tf_op jit(solution)/shard_map/concatenate | solution.py:119
  14.7 4.0 %convolution_convert_fusion.2 = bf16[512,1806]{0,1:T(8,128)(2,1)} fusion(bf16[512,1806]{1,0:T(8,128)(2,1)} %concatenate.29, s32[512]{0:T(512)S(1)} %get-tuple-element.72), kind=kOutput, calls=%fused_computation.6 | convolution fusion | flops 948050944 | bytes 3700736 | tf_op jit(solution)/shard_map/dot_general | solution.py:126
  18.7 4.0 %copy.51 = bf16[512,1806]{1,0:T(8,128)(2,1)} copy(bf16[512,1806]{0,1:T(8,128)(2,1)} %convolution_convert_fusion.2) | data formatting | bytes 3698688 | tf_op jit(solution)/shard_map/convert_element_type | solution.py:126
  22.6 13.3 %all-to-all-start = ((bf16[64,8,1806]{2,1,0:T(8,128)(2,1)}), bf16[64,8,1806]{2,1,0:T(8,128)(2,1)}, u32[]{:S(2)}, u32[]{:S(2)}) async-start(bf16[64,8,1806]{2,1,0:T(8,128)(2,1)} %bitcast.73), calls=%async_computation | async-start | bytes 3932160 | tf_op jit(solution)/shard_map/all_to_all | solution.py:127
  35.9 0.0 all-gather.2.cloned.1.call-start
  36.0 0.0 copy-done.5
  36.0 0.2 reduce-window.31
  36.2 0.6 fusion.45
  36.8 0.1 convert_reduce_fusion
  36.9 0.6 slice.66
  38.8 0.6 compare_convert_fusion.1
  39.4 44.7 %all-to-all-done = bf16[64,8,1806]{2,1,0:T(8,128)(2,1)} async-done(((bf16[64,8,1806]{2,1,0:T(8,128)(2,1)}), bf16[64,8,1806]{2,1,0:T(8,128)(2,1)}, u32[]{:S(2)}, u32[]{:S(2)}) %all-to-all-start) | async-done | bytes 1849376 | tf_op jit(solution)/shard_map/all_to_all | solution.py:127
  84.1 1.2 add_reduce_fusion
  85.3 2.8 %convolution_convert_fusion.1 = bf16[512,1806]{0,1:T(8,128)(2,1)S(1)} fusion(s32[512]{0:T(512)S(1)} %add_reduce_fusion, bf16[64,8,1806]{2,1,0:T(8,128)(2,1)} %all-to-all-done), kind=kOutput, calls=%fused_computation.5 | convolution fusion | flops 948050944 | bytes 3700736 | tf_op jit(solution)/shard_map/dot_general | solution.py:137
  88.1 0.1 slice.75
  88.1 1.2 copy-done.2
  89.4 1.2 reduce-window.32
  90.5 0.2 slice_reduce_fusion.1
  90.7 0.1 broadcast_add_fusion
  90.9 0.2 slice_reduce_fusion.2
  91.1 0.8 copy.54
  91.9 0.1 exponential_multiply_fusion.1
  92.0 2.3 %fusion.16 = bf16[1,12,64,128]{3,2,1,0:T(8,128)(2,1)S(1)} fusion(bf16[512,12,64]{0,2,1:T(8,128)(2,1)S(1)} %bitcast.74, f32[12,512]{1,0:T(8,128)S(1)} %exponential_multiply_fusion.1, f32[512,128]{1,0:T(8,128)} %copy.54, f32[12]{0:T(128)S(1)} %get-tuple-element.74), kind=kOutput, calls=%fused_computation.26 | convolution fusion | flops 102432768 | bytes 1269808 | tf_op jit(solution)/shard_map/while/body/eval_jaxpr/hsn,shp->hpn/dot_general | solution.py:64
  94.3 0.1 broadcast_in_dim.162
  94.4 0.7 pad_maximum_fusion
  95.1 0.0 all-gather.2.cloned.1.call-update
  95.1 0.0 reduce-scatter.2.cloned.1.call-start
  95.2 0.2 fusion.17
  95.5 1.3 fusion.32
  96.8 4.9 %fusion = f32[12,64,512]{2,1,0:T(8,128)} fusion(bf16[512,12,64]{0,2,1:T(8,128)(2,1)S(1)} %bitcast.75, f32[12,512]{1,0:T(8,128)S(1)} %bitcast.83, f32[512,512]{1,0:T(8,128)S(1)} %fusion.32, pred[512,512]{1,0:T(8,128)(4,1)S(1)} %fusion.17), kind=kOutput, calls=%fused_computation.1 | convolution fusion | flops 415236096 | bytes 3694592 | tf_op jit(solution)/shard_map/while/body/eval_jaxpr/hts,shp->thp/dot_general | solution.py:80
  101.7 32.4 %all-gather.2.cloned.1.call-done = bf16[16,12,65,128]{3,2,1,0:T(8,128)(2,1)} async-done(((bf16[1,12,65,128]{3,2,1,0:T(8,128)(2,1)}), bf16[16,12,65,128]{3,2,1,0:T(8,128)(2,1)}) %all-gather.2.cloned.1.call-update) | async-done | bytes 3194896 | tf_op jit(solution)/shard_map/all_gather | solution.py:39
  134.1 1.3 slice_reduce_fusion.3
  135.4 0.2 copy.68
  135.6 0.1 copy.56
  135.7 0.5 select_reduce_fusion.1
  136.2 2.8 %slice.82 = bf16[16,12,64,128]{3,2,1,0:T(8,128)(2,1)S(1)} slice(bf16[16,12,65,128]{3,2,1,0:T(8,128)(2,1)} %all-gather.2.cloned.1.call-done), slice={[0:16], [0:12], [0:64], [0:128]} | slice | bytes 6291456 | tf_op jit(solution)/shard_map/slice | solution.py:41
  139.1 1.9 fusion.4
  141.0 0.1 broadcast_in_dim.168
  141.1 12.5 %all_gather.9 = bf16[4,12,65,128]{3,2,1,0:T(8,128)(2,1)S(1)} all-gather(bf16[1,12,65,128]{3,2,1,0:T(8,128)(2,1)S(1)} %pad_maximum_fusion.1), channel_id=1, replica_groups=mesh['sx'=4,'sz'=16,'head'=4] {'sx'}, dimensions={0}, use_global_device_ids=true | all-gather | bytes 998400 | tf_op jit(solution)/shard_map/all_gather | solution.py:45
  153.7 1.0 slice.84
  154.7 0.2 fusion.36
  154.8 0.1 select_reduce_fusion.3
  154.9 0.1 select_reduce_fusion.2
  155.0 0.1 multiply_bitcast_fusion.1
  155.1 0.1 copy.61
  155.2 0.0 copy-start.6
  155.2 3.9 %fusion.2 = f32[12,1,64,128]{3,1,2,0:T(1,128)S(1)} fusion(bf16[16,12,64,128]{3,2,1,0:T(8,128)(2,1)} %copy-done.1, bf16[16,12,1,1]{0,1,2,3:T(8,128)(2,1)S(1)} %multiply_bitcast_fusion), kind=kOutput, calls=%fused_computation.7 | convolution fusion | flops 3145728 | bytes 3539328 | tf_op jit(solution)/shard_map/jh,jhpn->hpn/dot_general | solution.py:43
  159.2 0.7 fusion.20
  159.9 2.0 fusion.11
  161.9 0.0 copy-start.7
  161.9 2.8 %multiply_reduce_fusion = (f32[512]{0:T(512)S(1)}, f32[512,768]{0,1:T(8,128)}) fusion(bf16[512,1806]{0,1:T(8,128)(2,1)} %copy-done.2, f32[512,12,64]{0,2,1:T(8,128)S(1)} %fusion.11), kind=kLoop, calls=%fused_computation.21 | loop fusion | flops 3145216 | bytes 3934208 | tf_op jit(solution)/shard_map/reduce_sum | solution.py:203
  164.7 8.4 %psum.7 = f32[512]{0:T(512)S(1)} all-reduce(f32[512]{0:T(512)S(1)} %get-tuple-element.50), channel_id=1, replica_groups=mesh['sx'=4,'sz'=16,'head'=4] {'head'}, use_global_device_ids=true, to_apply=%region_14.15 | all-reduce | flops 512 | bytes 4096 | tf_op jit(solution)/shard_map/psum | solution.py:203
  173.1 4.1 %convolution_convert_fusion = bf16[512,1536]{1,0:T(8,128)(2,1)} fusion(bf16[768,1536]{1,0:T(8,128)(2,1)S(1)} %copy-done, f32[512,768]{0,1:T(8,128)} %get-tuple-element.51, f32[768]{0:T(1024)S(1)} %copy-done.7, f32[512]{0:T(512)S(1)} %add_rsqrt_fusion), kind=kOutput, calls=%fused_computation.4 | convolution fusion | flops 1209925632 | bytes 5510144 | tf_op jit(solution)/shard_map/dot_general | solution.py:207
  177.2 0.0 reduce-scatter.2.cloned.1.call-update
  177.2 27.6 %reduce-scatter.2.cloned.1.call-done = bf16[128,1536]{1,0:T(8,128)(2,1)} async-done(((bf16[512,1536]{1,0:T(8,128)(2,1)}), bf16[128,1536]{1,0:T(8,128)(2,1)}) %reduce-scatter.2.cloned.1.call-update) | async-done | bytes 393232 | tf_op jit(solution)/shard_map/reduce_scatter | solution.py:206
  (37 shorter events, 0.3 us)
Async XLA Ops:
  6.5 166.6 %copy-start = (bf16[768,1536]{1,0:T(8,128)(2,1)S(1)}, bf16[768,1536]{1,0:T(8,128)(2,1)}, u32[]{:S(2)}) copy-start(bf16[768,1536]{1,0:T(8,128)(2,1)} %param.19) | copy-start | bytes 7077892
  22.6 13.4 %copy-start.5 = (s32[4]{0:T(128)S(1)}, s32[4]{0:T(128)}, u32[]{:S(2)}) copy-start(s32[4]{0:T(128)} %param.16) | copy-start | bytes 52
  22.6 61.5 %all-to-all-start = ((bf16[64,8,1806]{2,1,0:T(8,128)(2,1)}), bf16[64,8,1806]{2,1,0:T(8,128)(2,1)}, u32[]{:S(2)}, u32[]{:S(2)}) async-start(bf16[64,8,1806]{2,1,0:T(8,128)(2,1)} %bitcast.73), calls=%async_computation | async-start | bytes 3932160 | tf_op jit(solution)/shard_map/all_to_all | solution.py:127
  35.9 98.2 %all-gather.2.cloned.1.call-start = ((), (), s32[]{:S(2)}) async-start(), calls=%async_computation.2 | async-start | bytes 3760128 | tf_op jit(solution)/shard_map/all_gather | solution.py:39
  88.1 1.3 copy-start.2
  95.1 109.7 %reduce-scatter.2.cloned.1.call-start = ((), (), s32[]{:S(2)}) async-start(), calls=%async_computation.3 | async-start | bytes 1966080 | tf_op jit(solution)/shard_map/reduce_scatter | solution.py:206
  139.1 2.0 copy-start.1
  155.2 4.0 %copy-start.4 = (bf16[4,12,64,128]{3,2,1,0:T(8,128)(2,1)S(1)}, bf16[4,12,64,128]{3,2,1,0:T(8,128)(2,1)}, u32[]{:S(2)}) copy-start(bf16[4,12,64,128]{3,2,1,0:T(8,128)(2,1)} %slice.84) | copy-start | bytes 2359300
  155.2 4.7 %copy-start.3 = (f32[12,64,512]{2,1,0:T(8,128)S(1)}, f32[12,64,512]{2,1,0:T(8,128)}, u32[]{:S(2)}) copy-start(f32[12,64,512]{2,1,0:T(8,128)} %fusion) | copy-start | bytes 4718596
  155.2 4.7 %copy-start.6 = (f32[12]{0:T(128)S(1)}, f32[12]{0:T(128)}, u32[]{:S(2)}) copy-start(f32[12]{0:T(128)} %param.17) | copy-start | bytes 148
  161.9 11.3 %copy-start.7 = (f32[768]{0:T(1024)S(1)}, f32[768]{0:T(1024)}, u32[]{:S(2)}) copy-start(f32[768]{0:T(1024)} %param.18) | copy-start | bytes 9220
Sparse Core Ops, SparseCore 0:
  95.2 38.7 all-gather.1
  177.4 27.4 reduce-scatter.1

commit v4 on v1

--- a/solution.py
+++ b/solution.py
@@ -16,18 +16,19 @@
     return (earlier[0] * later[0], later[0][:, None, None] * earlier[1] + later[1])
 
 
+def pack_state(kept, state):
+    flat = jnp.broadcast_to(kept[:, None, None], (kept.shape[0], 1, state.shape[2]))
+    return jnp.concatenate([state, flat], axis=1).astype(jnp.bfloat16)
+
+
 def exclusive_prefix(kept, state, axis):
     length, here = (lax.axis_size(axis), lax.axis_index(axis))
-    heads = kept.shape[0]
     span = (kept, state)
     before = (jnp.ones_like(kept), jnp.zeros_like(state))
     distance = 1
     while distance < length:
-        packed = jnp.concatenate(
-            [span[1], jnp.broadcast_to(span[0][:, None, None], (heads, 1, state.shape[2]))], axis=1
-        ).astype(jnp.bfloat16)
         pairs = [(j, j + distance) for j in range(length - distance)]
-        got = lax.ppermute(packed, axis, pairs).astype(jnp.float32)
+        got = lax.ppermute(pack_state(*span), axis, pairs).astype(jnp.float32)
         got = (got[:, -1, 0], got[:, :-1, :])
         reached = here >= distance
         new_before = combine(got, before)
@@ -36,7 +37,7 @@
             new_span = combine(got, span)
             span = jax.tree.map(lambda a, b: jnp.where(reached, a, b), new_span, span)
         distance *= 2
-    return before
+    return before[1]
 
 
 def doc_index(places, starts):
@@ -94,7 +95,7 @@
     feats = features_in.shape[1]
     width = feats // heads_here
     n_state = b_input.shape[1]
-    shards = lax.axis_size("seq")
+    shards = lax.axis_size(("sx", "sz"))
     capacity = tok_dev // shards
     owner = row_target // tok_dev
     local_place = row_target - owner * tok_dev
@@ -106,32 +107,43 @@
     place_hi = (local_place // 32).astype(jnp.bfloat16)
     place_lo = (local_place % 32).astype(jnp.bfloat16)
     rows_out = jnp.concatenate(
-        [features_in, gate_in, b_input, c_input, log_decay, place_hi[:, None], place_lo[:, None]],
-        axis=1,
+        [features_in, b_input, c_input, log_decay, place_hi[:, None], place_lo[:, None]], axis=1
     )
     to_slot = (
         lax.broadcasted_iota(jnp.int32, (tok_dev, tok_dev), 0) == slot_index[None, :]
     ).astype(jnp.bfloat16)
-    packed = jnp.dot(to_slot, rows_out, preferred_element_type=jnp.float32).astype(jnp.bfloat16)
-    moved = lax.all_to_all(
-        packed.reshape(shards, capacity, packed.shape[1]), "seq", split_axis=0, concat_axis=0, tiled=True
-    ).reshape(tok_dev, packed.shape[1])
-    columns = packed.shape[1]
+
+    def send(values):
+        packed = jnp.dot(to_slot, values, preferred_element_type=jnp.float32).astype(jnp.bfloat16)
+        return lax.all_to_all(
+            packed.reshape(shards, capacity, packed.shape[1]),
+            ("sx", "sz"),
+            split_axis=0,
+            concat_axis=0,
+            tiled=True,
+        ).reshape(tok_dev, packed.shape[1])
+
+    moved = send(rows_out)
+    columns = rows_out.shape[1]
     arrived = (
         moved[:, columns - 2].astype(jnp.int32) * 32 + moved[:, columns - 1].astype(jnp.int32)
     )
     to_place = (
         lax.broadcasted_iota(jnp.int32, (tok_dev, tok_dev), 0) == arrived[None, :]
     ).astype(jnp.bfloat16)
-    rows = jnp.dot(to_place, moved, preferred_element_type=jnp.float32).astype(jnp.bfloat16)
+
+    def place(values):
+        return jnp.dot(to_place, values, preferred_element_type=jnp.float32).astype(jnp.bfloat16)
+
+    rows = place(moved)
     features = rows[:, :feats]
-    gate_rows = rows[:, feats : 2 * feats]
-    key_full = rows[:, 2 * feats : 2 * feats + n_state]
-    query_full = rows[:, 2 * feats + n_state : 2 * feats + 2 * n_state]
-    decays = rows[:, 2 * feats + 2 * n_state : 2 * feats + 2 * n_state + heads_here]
+    key_full = rows[:, feats : feats + n_state]
+    query_full = rows[:, feats + n_state : feats + 2 * n_state]
+    decays = rows[:, feats + 2 * n_state : feats + 2 * n_state + heads_here]
+    gate_moved = send(gate_in)
 
     doc_starts = jnp.cumsum(doc_lengths) - doc_lengths
-    first_place = lax.axis_index("seq") * tok_dev
+    first_place = lax.axis_index(("sx", "sz")) * tok_dev
     blocks = tok_dev // BLOCK
     places = first_place + lax.broadcasted_iota(jnp.int32, (tok_dev,), 0)
     doc_ids = doc_index(places, doc_starts).reshape(blocks, BLOCK)
@@ -161,7 +173,7 @@
     )
     local_state, local_kept = local_carry
     block_states, throughs, runnings = (block_outputs[0], block_outputs[1], block_outputs[2])
-    entry_kept, entry_state = exclusive_prefix(local_kept, local_state, "seq")
+    entry_state = exclusive_prefix(local_kept, local_state, ("sx", "sz"))
 
     def mix_pass(carry_state, pieces):
         by_head, key_block, query_block, running, doc_block, before, block_state, through = pieces
@@ -188,30 +200,50 @@
         ),
     )
     mixed = mixed.reshape(tok_dev, heads_here * width)
+    gate_rows = place(gate_moved)
     gated = mixed * jax.nn.silu(gate_rows.astype(jnp.float32))
-    squares = lax.psum(jnp.sum(gated * gated, axis=1), "head")
-    row_scale = lax.rsqrt(squares / (ATTENTION_LANES * HEAD_DIM) + norm_eps)
-    normed = (gated * row_scale[:, None] * norm_gain[None, :]).astype(jnp.bfloat16)
-    return lax.psum_scatter(
-        jnp.dot(normed, out_weight, preferred_element_type=jnp.float32).astype(jnp.bfloat16),
-        "head",
-        scatter_dimension=0,
-        tiled=True,
-    )
+    squares = jnp.sum(gated * gated, axis=1)
+    square_hi = squares.astype(jnp.bfloat16)
+    square_lo = (squares - square_hi.astype(jnp.float32)).astype(jnp.bfloat16)
+    unscaled = (gated * norm_gain[None, :]).astype(jnp.bfloat16)
+    partial = jnp.dot(unscaled, out_weight, preferred_element_type=jnp.float32).astype(jnp.bfloat16)
+    groups = lax.axis_size("head")
+    chunk = tok_dev // groups
+    d_model = partial.shape[1]
+    extra = jnp.concatenate(
+        [square_hi.reshape(groups, 1, chunk), square_lo.reshape(groups, 1, chunk)], axis=1
+    )
+    extra = jnp.pad(extra, ((0, 0), (0, 6), (0, d_model - chunk)))
+    sent = jnp.concatenate([partial.reshape(groups, chunk, d_model), extra], axis=1)
+    summed = lax.psum_scatter(
+        sent.reshape(groups * (chunk + 8), d_model), "head", scatter_dimension=0, tiled=True
+    )
+    total_squares = summed[chunk, :chunk].astype(jnp.float32) + summed[
+        chunk + 1, :chunk
+    ].astype(jnp.float32)
+    row_scale = lax.rsqrt(total_squares / (ATTENTION_LANES * HEAD_DIM) + norm_eps)
+    return (summed[:chunk].astype(jnp.float32) * row_scale[:, None]).astype(jnp.bfloat16)
 
 
 def solution(mesh):
+    seq = mesh.shape["seq"]
+    inner = 16 if seq % 16 == 0 else seq
+    devices = mesh.devices.reshape(seq // inner, inner, mesh.shape["head"])
+    split_mesh = jax.sharding.Mesh(devices, ("sx", "sz", "head"))
+    rows = ("sx", "sz")
     in_specs = (
-        P("seq", "head"),
-        P("seq", "head"),
-        P("seq", None),
-        P("seq", None),
-        P("seq", "head"),
-        P("seq"),
+        P(rows, "head"),
+        P(rows, "head"),
+        P(rows, None),
+        P(rows, None),
+        P(rows, "head"),
+        P(rows),
         P(),
         P("head"),
         P("head"),
         P("head", None),
     )
-    out_specs = P(("seq", "head"), None)
-    return jax.shard_map(body, mesh=mesh, in_specs=in_specs, out_specs=out_specs, check_vma=False)
+    out_specs = P(("sx", "sz", "head"), None)
+    return jax.shard_map(
+        body, mesh=split_mesh, in_specs=in_specs, out_specs=out_specs, check_vma=False
+    )

time: 212 us -> 212 us (level)
  blocking collectives: 8.69 us -> 0 us
  waiting for transfers between devices: 82.5 us -> 89.2 us
    ppermute x6, waiting for transfers between devices: 11.1 us -> 28 us  [exclusive_prefix(): got = lax.ppermute(pack_state(*span), axis, pairs).astype(jnp.float32)]
    all_to_all x1 -> x2, waiting for transfers between devices: 44.7 us -> 27.7 us  [send(): lax.all_to_all(packed.reshape(shards, capacity, packed.shape[1]), ('sx',...]
    psum x1 -> x0, blocking collectives: 8.69 us -> none  [body(): squares = lax.psum(jnp.sum(gated * gated, axis=1), 'head')]
    reduce_scatter x1, waiting for transfers between devices: 26.7 us -> 33.5 us  [body(): lax.psum_scatter(sent.reshape(groups * (chunk + 8), d_model), 'head', sca...]
    all_to_all x1 -> x2, starting transfers between devices: 13.3 us -> 18.9 us  [send(): lax.all_to_all(packed.reshape(shards, capacity, packed.shape[1]), ('sx',...]
    ppermute x6, starting transfers between devices: 40.1 us -> 36.5 us  [exclusive_prefix(): got = lax.ppermute(pack_state(*span), axis, pairs).astype(jnp.float32)]
    reshape x0 -> x1, local copies, waits for them, and re-layouts: none -> 3.07 us  [body(): mixed = mixed.reshape(tok_dev, heads_here * width)]
    dot_general x3 -> x5, matrix products: 10.8 us -> 7.97 us  [the longest x2 3.33 us: place(): jnp.dot(to_place, values, preferred_element_type=jnp.float32)]
  transfers between devices with their start and end apart: 8 -> 9, of which waited for: 7 -> 7; matrix products, arithmetic and copies ran while one was open for 5% -> 10% of each run, Pallas kernels for 0% -> 0%
where the time goes in v4:
time: 212 us
  waiting for transfers between devices  89.2 us (42%)
  starting transfers between devices  55.5 us (26%)
  matrix products  20.6 us (10%)
  other arithmetic  15.5 us (7%)
  local copies, waits for them, and re-layouts  15.4 us (7%)
  between operations  15.3 us (7%)
    ppermute x6, starting transfers between devices, exclusive_prefix(): got = lax.ppermute(pack_state(*span), axis, pairs).astype(jnp.float32)  36.5 us
    reduce_scatter x1, waiting for transfers between devices, body(): lax.psum_scatter(sent.reshape(groups * (chunk + 8), d_model), 'head', sca...  33.5 us
    ppermute x6, waiting for transfers between devices, exclusive_prefix(): got = lax.ppermute(pack_state(*span), axis, pairs).astype(jnp.float32)  28 us
    all_to_all x2, waiting for transfers between devices, send(): lax.all_to_all(packed.reshape(shards, capacity, packed.shape[1]), ('sx',...  27.7 us
    all_to_all x2, starting transfers between devices, send(): lax.all_to_all(packed.reshape(shards, capacity, packed.shape[1]), ('sx',...  18.9 us
    dot_general x1, matrix products, inner_terms(): jnp.einsum('hts,shp->thp', affinity_logits, by_head, preferred_element_ty...  4.95 us
    another operation x18, other arithmetic  4.58 us
    dot_general x1, matrix products, entry_terms(): jnp.einsum('tn,hpn->thp', query_block.astype(jnp.float32), carry_state, p...  4.33 us
  transfers between devices with their start and end apart: 9, of which 7 were waited for; matrix products, arithmetic and copies ran while one was open for 10% of the time, Pallas kernels for 0%

profile of v4, /device:TPU:1, one launch (start us, length us, event | category | flops | bytes accessed | tf_op | source)
XLA Modules:
  0.0 211.5 jit_solution(1106349536173803706)
XLA Ops:
  6.5 1.7 copy.47
  8.2 0.7 fusion.68
  8.9 1.2 reduce-window.24
  10.1 0.2 slice_reduce_fusion
  10.5 0.7 multiply_add_fusion
  11.2 0.8 broadcast_in_dim.90
  12.0 0.8 broadcast_in_dim.91
  12.8 2.4 %concatenate.33 = bf16[512,1038]{1,0:T(8,128)(2,1)S(1)} concatenate(bf16[512,768]{1,0:T(8,128)(2,1)} %param.10, bf16[512,128]{1,0:T(8,128)(2,1)} %param.12, bf16[512,128]{1,0:T(8,128)(2,1)} %param.13, bf16[512,12]{1,0:T(8,128)(2,1)} %copy.47, bf16[512,1]{1,0:T(8,128)(2,1)} %broadcast_in_dim.90, bf16[512,1]{1,0:T(8,128)(2,1)} %broadcast_in_dim.91), dimensions={1} | concatenate | bytes 2125824 | tf_op jit(solution)/shard_map/concatenate | solution.py:109
  15.2 1.8 convolution_convert_fusion.2
  17.0 2.4 %copy.50 = bf16[512,1038]{1,0:T(8,128)(2,1)} copy(bf16[512,1038]{0,1:T(8,128)(2,1)} %convolution_convert_fusion.2) | data formatting | bytes 2125824 | tf_op jit(solution)/shard_map/convert_element_type | solution.py:117
  19.4 13.1 %all-to-all-start = ((bf16[64,8,1038]{2,1,0:T(8,128)(2,1)}), bf16[64,8,1038]{2,1,0:T(8,128)(2,1)S(1)}, u32[]{:S(2)}, u32[]{:S(2)}) async-start(bf16[64,8,1038]{2,1,0:T(8,128)(2,1)} %bitcast.2), calls=%async_computation | async-start | bytes 2359296 | tf_op jit(solution)/shard_map/all_to_all | solution.py:118
  32.5 0.2 reduce-window.31
  32.7 0.6 fusion.71
  33.4 0.7 slice.96
  35.4 0.7 compare_convert_fusion.1
  36.1 27.7 %all-to-all-done = bf16[64,8,1038]{2,1,0:T(8,128)(2,1)S(1)} async-done(((bf16[64,8,1038]{2,1,0:T(8,128)(2,1)}), bf16[64,8,1038]{2,1,0:T(8,128)(2,1)S(1)}, u32[]{:S(2)}, u32[]{:S(2)}) %all-to-all-start) | async-done | bytes 1062944 | tf_op jit(solution)/shard_map/all_to_all | solution.py:118
  63.9 0.2 add_reduce_fusion
  64.1 0.8 convolution_convert_fusion.1
  65.0 0.9 copy-done.6
  66.0 1.2 reduce-window.32
  67.1 0.2 slice_reduce_fusion.1
  67.5 0.7 multiply_reduce_fusion.1
  68.2 0.6 broadcast_multiply_fusion
  68.7 0.5 convert.49
  69.2 0.8 copy.53
  70.2 2.1 fusion.83
  72.4 2.9 %collective-permute-start = (bf16[12,65,128]{2,1,0:T(8,128)(2,1)S(1)}, bf16[12,65,128]{2,1,0:T(8,128)(2,1)S(1)}, u32[]{:S(2)}, u32[]{:S(2)}) collective-permute-start(bf16[12,65,128]{2,1,0:T(8,128)(2,1)S(1)} %pad_maximum_fusion.1), channel_id=1, source_target_pairs={{0,4},{4,8},{8,12},{12,16},{16,20},{20,24},{24,28},{28,32},{32,36}... | collective-permute-start | bytes 599048 | tf_op jit(solution)/shard_map/ppermute | solution.py:31
  75.3 1.5 fusion.10
  76.8 5.8 %all-to-all-start.1 = ((bf16[64,8,768]{2,1,0:T(8,128)(2,1)}), bf16[64,8,768]{2,1,0:T(8,128)(2,1)}, u32[]{:S(2)}, u32[]{:S(2)}) async-start(bf16[64,8,768]{2,1,0:T(8,128)(2,1)} %fusion.10), calls=%async_computation.1 | async-start | bytes 1572864 | tf_op jit(solution)/shard_map/all_to_all | solution.py:118
  82.7 0.3 fusion.65
  83.2 3.3 %collective-permute-start.1 = (bf16[12,65,128]{2,1,0:T(8,128)(2,1)S(1)}, bf16[12,65,128]{2,1,0:T(8,128)(2,1)S(1)}, u32[]{:S(2)}, u32[]{:S(2)}) collective-permute-start(bf16[12,65,128]{2,1,0:T(8,128)(2,1)S(1)} %pad_maximum_fusion.2), channel_id=1, source_target_pairs={{0,8},{4,12},{8,16},{12,20},{16,24},{20,28},{24,32},{28,36},{32,40... | collective-permute-start | bytes 599048 | tf_op jit(solution)/shard_map/ppermute | solution.py:31
  86.5 0.2 fusion.12
  86.8 17.2 %collective-permute-done.1 = bf16[12,65,128]{2,1,0:T(8,128)(2,1)S(1)} collective-permute-done((bf16[12,65,128]{2,1,0:T(8,128)(2,1)S(1)}, bf16[12,65,128]{2,1,0:T(8,128)(2,1)S(1)}, u32[]{:S(2)}, u32[]{:S(2)}) %collective-permute-start.1) | collective-permute-done | bytes 199712 | tf_op jit(solution)/shard_map/ppermute | solution.py:31
  104.0 0.3 convert_reduce_fusion.2
  104.2 0.2 fusion.82
  104.6 5.5 %collective-permute-start.2 = (bf16[12,65,128]{2,1,0:T(8,128)(2,1)S(1)}, bf16[12,65,128]{2,1,0:T(8,128)(2,1)S(1)}, u32[]{:S(2)}, u32[]{:S(2)}) collective-permute-start(bf16[12,65,128]{2,1,0:T(8,128)(2,1)S(1)} %pad_maximum_fusion.3), channel_id=1, source_target_pairs={{0,16},{4,20},{8,24},{12,28},{16,32},{20,36},{24,40},{28,44},{32,4... | collective-permute-start | bytes 599048 | tf_op jit(solution)/shard_map/ppermute | solution.py:31
  110.0 1.3 fusion.55
  111.3 0.2 slice_reduce_fusion.5
  111.5 5.1 %collective-permute-done.2 = bf16[12,65,128]{2,1,0:T(8,128)(2,1)S(1)} collective-permute-done((bf16[12,65,128]{2,1,0:T(8,128)(2,1)S(1)}, bf16[12,65,128]{2,1,0:T(8,128)(2,1)S(1)}, u32[]{:S(2)}, u32[]{:S(2)}) %collective-permute-start.2) | collective-permute-done | bytes 199712 | tf_op jit(solution)/shard_map/ppermute | solution.py:31
  116.6 0.2 slice_reduce_fusion.4
  116.8 0.1 fusion.61
  117.0 9.0 %collective-permute-start.3 = (bf16[12,65,128]{2,1,0:T(8,128)(2,1)S(1)}, bf16[12,65,128]{2,1,0:T(8,128)(2,1)S(1)}, u32[]{:S(2)}, u32[]{:S(2)}) collective-permute-start(bf16[12,65,128]{2,1,0:T(8,128)(2,1)S(1)} %pad_maximum_fusion.4), channel_id=1, source_target_pairs={{0,32},{4,36},{8,40},{12,44},{16,48},{20,52},{24,56},{28,60},{32,6... | collective-permute-start | bytes 599048 | tf_op jit(solution)/shard_map/ppermute | solution.py:31
  126.1 5.0 %fusion = f32[12,64,512]{2,1,0:T(8,128)} fusion(bf16[512,12,64]{0,2,1:T(8,128)(2,1)S(1)} %bitcast.67, f32[12,512]{1,0:T(8,128)S(1)} %bitcast.72, f32[512,512]{1,0:T(8,128)S(1)} %fusion.55, pred[512,512]{1,0:T(8,128)(4,1)S(1)} %fusion.12), kind=kOutput, calls=%fused_computation.1 | convolution fusion | flops 415236096 | bytes 3694592 | tf_op jit(solution)/shard_map/while/body/eval_jaxpr/hts,shp->thp/dot_general | solution.py:70
  131.1 1.0 collective-permute-done.3
  132.1 0.2 broadcast_select_fusion
  132.3 0.2 fusion.80
  132.5 0.2 convert_reduce_fusion.1
  132.8 10.3 %collective-permute-start.4 = (bf16[12,65,128]{2,1,0:T(8,128)(2,1)S(1)}, bf16[12,65,128]{2,1,0:T(8,128)(2,1)S(1)}, u32[]{:S(2)}, u32[]{:S(2)}) collective-permute-start(bf16[12,65,128]{2,1,0:T(8,128)(2,1)S(1)} %pad_maximum_fusion.5), channel_id=1, source_target_pairs={{0,64},{4,68},{8,72},{12,76},{16,80},{20,84},{24,88},{28,92},{32,9... | collective-permute-start | bytes 599048 | tf_op jit(solution)/shard_map/ppermute | solution.py:31
  143.1 4.0 %collective-permute-done.4 = bf16[12,65,128]{2,1,0:T(8,128)(2,1)S(1)} collective-permute-done((bf16[12,65,128]{2,1,0:T(8,128)(2,1)S(1)}, bf16[12,65,128]{2,1,0:T(8,128)(2,1)S(1)}, u32[]{:S(2)}, u32[]{:S(2)}) %collective-permute-start.4) | collective-permute-done | bytes 199712 | tf_op jit(solution)/shard_map/ppermute | solution.py:31
  147.1 0.2 fusion.63
  147.3 0.6 copy-done.2
  148.1 5.5 %collective-permute-start.5 = (bf16[12,65,128]{2,1,0:T(8,128)(2,1)S(1)}, bf16[12,65,128]{2,1,0:T(8,128)(2,1)}, u32[]{:S(2)}, u32[]{:S(2)}) collective-permute-start(bf16[12,65,128]{2,1,0:T(8,128)(2,1)S(1)} %pad_maximum_fusion.6), channel_id=1, source_target_pairs={{0,128},{4,132},{8,136},{12,140},{16,144},{20,148},{24,152},{28,15... | collective-permute-start | bytes 599048 | tf_op jit(solution)/shard_map/ppermute | solution.py:31
  153.7 0.2 reduce.19
  153.9 0.2 reduce.18
  154.0 1.0 fusion.64
  155.0 0.8 collective-permute-done.5
  155.8 4.3 %fusion.7 = f32[512,12,64]{0,2,1:T(8,128)} fusion(f32[12,64,512]{2,1,0:T(8,128)} %fusion, bf16[512,12,64]{0,2,1:T(8,128)(2,1)} %bitcast.66, f32[12]{0:T(128)S(1)} %copy-done.14, f32[512,12]{0,1:T(8,128)S(1)} %exponential_multiply_fusion, f32[12,65,128]{2,1,0:T(8,128)} %copy-done.2, f32[12,65,128]{2,1,0:T(8,128)} %copy-done.3, ...), kind=kOutput, calls=%fused_computation.16 | convolution fusion | flops 607617024 | bytes 6261766 | tf_op jit(solution)/shard_map/while/body/eval_jaxpr/tn,hpn->thp/dot_general | solution.py:75
  160.2 3.1 %copy.57 = f32[512,768]{1,0:T(8,128)} copy(f32[512,768]{0,1:T(8,128)} %bitcast.64) | data formatting | bytes 3145728 | tf_op jit(solution)/shard_map/reshape | solution.py:202
  163.3 2.5 %multiply_reduce_fusion = (f32[512]{0:T(512)S(1)}, f32[512,768]{1,0:T(8,128)S(1)}) fusion(f32[512,768]{1,0:T(8,128)} %copy.57, bf16[64,8,768]{2,1,0:T(8,128)(2,1)} %all-to-all-done.1, s32[512]{0:T(512)S(1)} %copy-done.11), kind=kOutput, calls=%fused_computation.17 | convolution fusion | flops 406453760 | bytes 3936256 | tf_op jit(solution)/shard_map/dot_general | solution.py:136
  165.9 1.4 convolution_convert_fusion
  167.2 1.3 pad_maximum_fusion
  168.6 33.5 %reduce-scatter.2.cloned.1.call-done = bf16[136,1536]{1,0:T(8,128)(2,1)} async-done(((bf16[544,1536]{1,0:T(8,128)(2,1)}), bf16[136,1536]{1,0:T(8,128)(2,1)}) %reduce-scatter.2.cloned.1.call-update) | async-done | bytes 417808 | tf_op jit(solution)/shard_map/reduce_scatter | solution.py:218
  202.1 0.8 rsqrt_bitcast_fusion
  202.8 1.9 multiply_convert_fusion.8
  (85 shorter events, 1.8 us)
Async XLA Ops:
  6.5 159.3 %copy-start = (bf16[768,1536]{1,0:T(8,128)(2,1)S(1)}, bf16[768,1536]{1,0:T(8,128)(2,1)}, u32[]{:S(2)}) copy-start(bf16[768,1536]{1,0:T(8,128)(2,1)} %param.19) | copy-start | bytes 7077892
  11.2 5.8 %copy-start.12 = (s32[512]{0:T(512)}, s32[512]{0:T(512)S(1)}, u32[]{:S(2)}) copy-start(s32[512]{0:T(512)S(1)} %get-tuple-element.107) | copy-start | bytes 6148
  19.4 13.1 %copy-start.15 = (s32[4]{0:T(128)S(1)}, s32[4]{0:T(128)}, u32[]{:S(2)}) copy-start(s32[4]{0:T(128)} %param.16) | copy-start | bytes 52
  19.4 44.5 %all-to-all-start = ((bf16[64,8,1038]{2,1,0:T(8,128)(2,1)}), bf16[64,8,1038]{2,1,0:T(8,128)(2,1)S(1)}, u32[]{:S(2)}, u32[]{:S(2)}) async-start(bf16[64,8,1038]{2,1,0:T(8,128)(2,1)} %bitcast.2), calls=%async_computation | async-start | bytes 2359296 | tf_op jit(solution)/shard_map/all_to_all | solution.py:118
  64.1 0.9 copy-start.10
  64.9 1.0 copy-start.6
  65.0 7.3 %copy-start.4 = (bf16[512,768]{0,1:T(8,128)(2,1)}, bf16[512,768]{0,1:T(8,128)(2,1)S(1)}, u32[]{:S(2)}) copy-start(bf16[512,768]{0,1:T(8,128)(2,1)S(1)} %slice.115) | copy-start | bytes 2359300
  67.4 2.7 %copy-start.7 = (f32[2,8,4,128]{3,1,2,0:T(8,128)}, f32[2,8,4,128]{3,1,2,0:T(8,128)S(1)}, u32[]{:S(2)}) copy-start(f32[2,8,4,128]{3,1,2,0:T(8,128)S(1)} %copy.61) | copy-start | bytes 98308
  70.1 2.2 %copy-start.16 = (bf16[12]{0:T(256)(128)(2,1)S(1)}, bf16[12]{0:T(256)(128)(2,1)}, u32[]{:S(2)}) copy-start(bf16[12]{0:T(256)(128)(2,1)} %convert.49) | copy-start | bytes 76
  70.1 5.2 %copy-start.13 = (s32[512]{0:T(512)S(1)}, s32[512]{0:T(512)}, u32[]{:S(2)}) copy-start(s32[512]{0:T(512)} %copy-done.12) | copy-start | bytes 6148
  70.1 5.2 %copy-start.17 = (bf16[512,768]{1,0:T(8,128)(2,1)S(1)}, bf16[512,768]{1,0:T(8,128)(2,1)}, u32[]{:S(2)}) copy-start(bf16[512,768]{1,0:T(8,128)(2,1)} %param.11) | copy-start | bytes 2359300
  72.4 10.3 %collective-permute-start = (bf16[12,65,128]{2,1,0:T(8,128)(2,1)S(1)}, bf16[12,65,128]{2,1,0:T(8,128)(2,1)S(1)}, u32[]{:S(2)}, u32[]{:S(2)}) collective-permute-start(bf16[12,65,128]{2,1,0:T(8,128)(2,1)S(1)} %pad_maximum_fusion.1), channel_id=1, source_target_pairs={{0,4},{4,8},{8,12},{12,16},{16,20},{20,24},{24,28},{28,32},{32,36}... | collective-permute-start | bytes 599048 | tf_op jit(solution)/shard_map/ppermute | solution.py:31
  76.8 5.9 %copy-start.9 = (f32[12]{0:T(128)S(1)}, f32[12]{0:T(128)}, u32[]{:S(2)}) copy-start(f32[12]{0:T(128)} %get-tuple-element.51) | copy-start | bytes 148
  76.8 86.5 %all-to-all-start.1 = ((bf16[64,8,768]{2,1,0:T(8,128)(2,1)}), bf16[64,8,768]{2,1,0:T(8,128)(2,1)}, u32[]{:S(2)}, u32[]{:S(2)}) async-start(bf16[64,8,768]{2,1,0:T(8,128)(2,1)} %fusion.10), calls=%async_computation.1 | async-start | bytes 1572864 | tf_op jit(solution)/shard_map/all_to_all | solution.py:118
  82.6 119.5 %reduce-scatter.2.cloned.1.call-start = ((), (), s32[]{:S(2)}) async-start(), calls=%async_computation.3 | async-start | bytes 2088960 | tf_op jit(solution)/shard_map/reduce_scatter | solution.py:218
  83.2 20.7 %collective-permute-start.1 = (bf16[12,65,128]{2,1,0:T(8,128)(2,1)S(1)}, bf16[12,65,128]{2,1,0:T(8,128)(2,1)S(1)}, u32[]{:S(2)}, u32[]{:S(2)}) collective-permute-start(bf16[12,65,128]{2,1,0:T(8,128)(2,1)S(1)} %pad_maximum_fusion.2), channel_id=1, source_target_pairs={{0,8},{4,12},{8,16},{12,20},{16,24},{20,28},{24,32},{28,36},{32,40... | collective-permute-start | bytes 599048 | tf_op jit(solution)/shard_map/ppermute | solution.py:31
  104.0 28.1 %copy-start.1 = (f32[12,65,128]{2,1,0:T(8,128)}, f32[12,65,128]{2,1,0:T(8,128)S(1)}, u32[]{:S(2)}) copy-start(f32[12,65,128]{2,1,0:T(8,128)S(1)} %convert_element_type.195) | copy-start | bytes 1198084
  104.6 21.5 %copy-start.5 = (bf16[512,768]{0,1:T(8,128)(2,1)S(1)}, bf16[512,768]{0,1:T(8,128)(2,1)}, u32[]{:S(2)}) copy-start(bf16[512,768]{0,1:T(8,128)(2,1)} %copy-done.4) | copy-start | bytes 2359300
  104.6 21.5 %copy-start.8 = (f32[2,8,4,128]{3,1,2,0:T(8,128)S(1)}, f32[2,8,4,128]{3,1,2,0:T(8,128)}, u32[]{:S(2)}) copy-start(f32[2,8,4,128]{3,1,2,0:T(8,128)} %copy-done.7) | copy-start | bytes 98308
  104.6 12.0 %collective-permute-start.2 = (bf16[12,65,128]{2,1,0:T(8,128)(2,1)S(1)}, bf16[12,65,128]{2,1,0:T(8,128)(2,1)S(1)}, u32[]{:S(2)}, u32[]{:S(2)}) collective-permute-start(bf16[12,65,128]{2,1,0:T(8,128)(2,1)S(1)} %pad_maximum_fusion.3), channel_id=1, source_target_pairs={{0,16},{4,20},{8,24},{12,28},{16,32},{20,36},{24,40},{28,44},{32,4... | collective-permute-start | bytes 599048 | tf_op jit(solution)/shard_map/ppermute | solution.py:31
  117.0 15.0 %collective-permute-start.3 = (bf16[12,65,128]{2,1,0:T(8,128)(2,1)S(1)}, bf16[12,65,128]{2,1,0:T(8,128)(2,1)S(1)}, u32[]{:S(2)}, u32[]{:S(2)}) collective-permute-start(bf16[12,65,128]{2,1,0:T(8,128)(2,1)S(1)} %pad_maximum_fusion.4), channel_id=1, source_target_pairs={{0,32},{4,36},{8,40},{12,44},{16,48},{20,52},{24,56},{28,60},{32,6... | collective-permute-start | bytes 599048 | tf_op jit(solution)/shard_map/ppermute | solution.py:31
  132.1 15.9 %copy-start.3 = (f32[12,65,128]{2,1,0:T(8,128)}, f32[12,65,128]{2,1,0:T(8,128)S(1)}, u32[]{:S(2)}) copy-start(f32[12,65,128]{2,1,0:T(8,128)S(1)} %convert_element_type.197) | copy-start | bytes 1198084
  132.5 23.4 %copy-start.14 = (f32[12]{0:T(128)S(1)}, f32[12]{0:T(128)}, u32[]{:S(2)}) copy-start(f32[12]{0:T(128)} %param.17) | copy-start | bytes 148
  132.8 14.3 %collective-permute-start.4 = (bf16[12,65,128]{2,1,0:T(8,128)(2,1)S(1)}, bf16[12,65,128]{2,1,0:T(8,128)(2,1)S(1)}, u32[]{:S(2)}, u32[]{:S(2)}) collective-permute-start(bf16[12,65,128]{2,1,0:T(8,128)(2,1)S(1)} %pad_maximum_fusion.5), channel_id=1, source_target_pairs={{0,64},{4,68},{8,72},{12,76},{16,80},{20,84},{24,88},{28,92},{32,9... | collective-permute-start | bytes 599048 | tf_op jit(solution)/shard_map/ppermute | solution.py:31
  147.1 0.8 copy-start.2
  148.1 7.7 %collective-permute-start.5 = (bf16[12,65,128]{2,1,0:T(8,128)(2,1)S(1)}, bf16[12,65,128]{2,1,0:T(8,128)(2,1)}, u32[]{:S(2)}, u32[]{:S(2)}) collective-permute-start(bf16[12,65,128]{2,1,0:T(8,128)(2,1)S(1)} %pad_maximum_fusion.6), channel_id=1, source_target_pairs={{0,128},{4,132},{8,136},{12,140},{16,144},{20,148},{24,152},{28,15... | collective-permute-start | bytes 599048 | tf_op jit(solution)/shard_map/ppermute | solution.py:31
  160.2 3.1 %copy-start.11 = (s32[512]{0:T(512)S(1)}, s32[512]{0:T(512)}, u32[]{:S(2)}) copy-start(s32[512]{0:T(512)} %copy-done.10) | copy-start | bytes 6148
  163.2 2.6 %copy-start.18 = (f32[768]{0:T(1024)S(1)}, f32[768]{0:T(1024)}, u32[]{:S(2)}) copy-start(f32[768]{0:T(1024)} %param.18) | copy-start | bytes 9220
Sparse Core Ops, SparseCore 0:
  168.7 33.2 reduce-scatter.1

commit v5 on v4

--- a/solution.py
+++ b/solution.py
@@ -4,6 +4,7 @@
 from jax.sharding import PartitionSpec as P
 
 ATTENTION_LANES = 48
+ROWS = ("sx", "sz", "sc")
 HEAD_DIM = 64
 BLOCK = 512
 
@@ -21,23 +22,33 @@
     return jnp.concatenate([state, flat], axis=1).astype(jnp.bfloat16)
 
 
-def exclusive_prefix(kept, state, axis):
-    length, here = (lax.axis_size(axis), lax.axis_index(axis))
-    span = (kept, state)
-    before = (jnp.ones_like(kept), jnp.zeros_like(state))
-    distance = 1
-    while distance < length:
-        pairs = [(j, j + distance) for j in range(length - distance)]
-        got = lax.ppermute(pack_state(*span), axis, pairs).astype(jnp.float32)
-        got = (got[:, -1, 0], got[:, :-1, :])
-        reached = here >= distance
-        new_before = combine(got, before)
-        before = jax.tree.map(lambda a, b: jnp.where(reached, a, b), new_before, before)
-        if distance * 2 < length:
-            new_span = combine(got, span)
-            span = jax.tree.map(lambda a, b: jnp.where(reached, a, b), new_span, span)
-        distance *= 2
-    return before[1]
+def group_weights(kept, here):
+    count = kept.shape[0]
+    j = lax.broadcasted_iota(jnp.int32, (count, count), 0)
+    k = lax.broadcasted_iota(jnp.int32, (count, count), 1)
+    ahead = lax.broadcasted_iota(jnp.int32, (count, 1), 0) < here
+    between = (j < k) & (k < here)
+    into_here = jnp.prod(jnp.where(between[:, :, None], kept[None, :, :], 1.0), axis=1) * ahead
+    into_end = jnp.prod(jnp.where((j < k)[:, :, None], kept[None, :, :], 1.0), axis=1)
+    kept_before = jnp.prod(jnp.where(ahead, kept, 1.0), axis=0)
+    return into_here, into_end, kept_before, jnp.prod(kept, axis=0)
+
+
+def exclusive_prefix(kept, state, axes):
+    levels = []
+    for level, axis in enumerate(axes):
+        gathered = lax.all_gather(pack_state(kept, state), axis)
+        g_kept = gathered[:, :, -1, 0].astype(jnp.float32)
+        g_state = gathered[:, :, :-1, :].astype(jnp.float32)
+        into_here, into_end, kept_before, kept_all = group_weights(g_kept, lax.axis_index(axis))
+        levels.append((kept_before, jnp.einsum("jh,jhpn->hpn", into_here, g_state)))
+        if level + 1 < len(axes):
+            state = jnp.einsum("jh,jhpn->hpn", into_end, g_state)
+            kept = kept_all
+    result = levels[-1][1]
+    for kept_before, local_before in reversed(levels[:-1]):
+        result = kept_before[:, None, None] * result + local_before
+    return result
 
 
 def doc_index(places, starts):
@@ -95,7 +106,7 @@
     feats = features_in.shape[1]
     width = feats // heads_here
     n_state = b_input.shape[1]
-    shards = lax.axis_size(("sx", "sz"))
+    shards = lax.axis_size(ROWS)
     capacity = tok_dev // shards
     owner = row_target // tok_dev
     local_place = row_target - owner * tok_dev
@@ -107,7 +118,8 @@
     place_hi = (local_place // 32).astype(jnp.bfloat16)
     place_lo = (local_place % 32).astype(jnp.bfloat16)
     rows_out = jnp.concatenate(
-        [features_in, b_input, c_input, log_decay, place_hi[:, None], place_lo[:, None]], axis=1
+        [features_in, gate_in, b_input, c_input, log_decay, place_hi[:, None], place_lo[:, None]],
+        axis=1,
     )
     to_slot = (
         lax.broadcasted_iota(jnp.int32, (tok_dev, tok_dev), 0) == slot_index[None, :]
@@ -117,7 +129,7 @@
         packed = jnp.dot(to_slot, values, preferred_element_type=jnp.float32).astype(jnp.bfloat16)
         return lax.all_to_all(
             packed.reshape(shards, capacity, packed.shape[1]),
-            ("sx", "sz"),
+            ROWS,
             split_axis=0,
             concat_axis=0,
             tiled=True,
@@ -137,13 +149,13 @@
 
     rows = place(moved)
     features = rows[:, :feats]
-    key_full = rows[:, feats : feats + n_state]
-    query_full = rows[:, feats + n_state : feats + 2 * n_state]
-    decays = rows[:, feats + 2 * n_state : feats + 2 * n_state + heads_here]
-    gate_moved = send(gate_in)
+    gate_rows = rows[:, feats : 2 * feats]
+    key_full = rows[:, 2 * feats : 2 * feats + n_state]
+    query_full = rows[:, 2 * feats + n_state : 2 * feats + 2 * n_state]
+    decays = rows[:, 2 * feats + 2 * n_state : 2 * feats + 2 * n_state + heads_here]
 
     doc_starts = jnp.cumsum(doc_lengths) - doc_lengths
-    first_place = lax.axis_index(("sx", "sz")) * tok_dev
+    first_place = lax.axis_index(ROWS) * tok_dev
     blocks = tok_dev // BLOCK
     places = first_place + lax.broadcasted_iota(jnp.int32, (tok_dev,), 0)
     doc_ids = doc_index(places, doc_starts).reshape(blocks, BLOCK)
@@ -173,7 +185,7 @@
     )
     local_state, local_kept = local_carry
     block_states, throughs, runnings = (block_outputs[0], block_outputs[1], block_outputs[2])
-    entry_state = exclusive_prefix(local_kept, local_state, ("sx", "sz"))
+    entry_state = exclusive_prefix(local_kept, local_state, ("sc", "sz", "sx"))
 
     def mix_pass(carry_state, pieces):
         by_head, key_block, query_block, running, doc_block, before, block_state, through = pieces
@@ -200,7 +212,6 @@
         ),
     )
     mixed = mixed.reshape(tok_dev, heads_here * width)
-    gate_rows = place(gate_moved)
     gated = mixed * jax.nn.silu(gate_rows.astype(jnp.float32))
     squares = jnp.sum(gated * gated, axis=1)
     square_hi = squares.astype(jnp.bfloat16)
@@ -227,23 +238,21 @@
 
 def solution(mesh):
     seq = mesh.shape["seq"]
-    inner = 16 if seq % 16 == 0 else seq
-    devices = mesh.devices.reshape(seq // inner, inner, mesh.shape["head"])
-    split_mesh = jax.sharding.Mesh(devices, ("sx", "sz", "head"))
-    rows = ("sx", "sz")
+    devices = mesh.devices.reshape(seq // 16, 8, 2, mesh.shape["head"])
+    split_mesh = jax.sharding.Mesh(devices, ROWS + ("head",))
     in_specs = (
-        P(rows, "head"),
-        P(rows, "head"),
-        P(rows, None),
-        P(rows, None),
-        P(rows, "head"),
-        P(rows),
+        P(ROWS, "head"),
+        P(ROWS, "head"),
+        P(ROWS, None),
+        P(ROWS, None),
+        P(ROWS, "head"),
+        P(ROWS),
         P(),
         P("head"),
         P("head"),
         P("head", None),
     )
-    out_specs = P(("sx", "sz", "head"), None)
+    out_specs = P(ROWS + ("head",), None)
     return jax.shard_map(
         body, mesh=split_mesh, in_specs=in_specs, out_specs=out_specs, check_vma=False
     )

time: 212 us -> 214 us (level)
  starting transfers between devices: 55.5 us -> 13.4 us
  blocking collectives: 0 us -> 14.2 us
  other arithmetic: 15.5 us -> 27.1 us
  waiting for transfers between devices: 89.2 us -> 96.6 us
  matrix products: 20.6 us -> 27.1 us
  local copies, waits for them, and re-layouts: 15.4 us -> 19.8 us
    ppermute x6 -> x0, starting transfers between devices: 36.5 us -> none  [exclusive_prefix(): got = lax.ppermute(pack_state(*span), axis, pairs).astype(jnp.float32)]
    ppermute x6 -> x0, waiting for transfers between devices: 28 us -> none  [exclusive_prefix(): got = lax.ppermute(pack_state(*span), axis, pairs).astype(jnp.float32)]
    all_gather x0 -> x1, waiting for transfers between devices: none -> 19.2 us  [exclusive_prefix(): gathered = lax.all_gather(pack_state(kept, state), axis)]
    all_to_all x2 -> x1, waiting for transfers between devices: 27.7 us -> 44.1 us  [send(): lax.all_to_all(packed.reshape(shards, capacity, packed.shape[1]), ROWS, s...]
    all_gather x0 -> x2, blocking collectives: none -> 14.2 us  [exclusive_prefix(): gathered = lax.all_gather(pack_state(kept, state), axis)]
    dot_general x0 -> x5, matrix products: none -> 8.32 us  [the longest x3 6 us: exclusive_prefix(): levels.append((kept_before, jnp.einsum('jh,jhpn->hpn', into_here, g_state)))]
    reduce_prod x0 -> x7, other arithmetic: none -> 7.26 us  [the longest x2 3.29 us: group_weights(): return (into_here, into_end, kept_before, jnp.prod(kept, axis=0))]
    all_to_all x2 -> x1, starting transfers between devices: 18.9 us -> 13.3 us  [send(): lax.all_to_all(packed.reshape(shards, capacity, packed.shape[1]), ROWS, s...]
  transfers between devices with their start and end apart: 9 -> 3, of which waited for: 7 -> 3; matrix products, arithmetic and copies ran while one was open for 10% -> 8% of each run, Pallas kernels for 0% -> 0%
where the time goes in v5:
time: 214 us; the launch traced here: 213 us
  waiting for transfers between devices  96.6 us (45%)
  other arithmetic  27.1 us (13%)
  matrix products  27.1 us (13%)
  local copies, waits for them, and re-layouts  19.8 us (9%)
  between operations  15.2 us (7%)
  blocking collectives  14.2 us (7%)
  starting transfers between devices  13.4 us (6%)
    all_to_all x1, waiting for transfers between devices, send(): lax.all_to_all(packed.reshape(shards, capacity, packed.shape[1]), ROWS, s...  44.1 us
    reduce_scatter x1, waiting for transfers between devices, body(): lax.psum_scatter(sent.reshape(groups * (chunk + 8), d_model), 'head', sca...  33.3 us
    all_gather x1, waiting for transfers between devices, exclusive_prefix(): gathered = lax.all_gather(pack_state(kept, state), axis)  19.2 us
    all_gather x2, blocking collectives, exclusive_prefix(): gathered = lax.all_gather(pack_state(kept, state), axis)  14.2 us
    all_to_all x1, starting transfers between devices, send(): lax.all_to_all(packed.reshape(shards, capacity, packed.shape[1]), ROWS, s...  13.3 us
    dot_general x3, matrix products, exclusive_prefix(): levels.append((kept_before, jnp.einsum('jh,jhpn->hpn', into_here, g_state)))  6 us
    dot_general x1, matrix products, inner_terms(): jnp.einsum('hts,shp->thp', affinity_logits, by_head, preferred_element_ty...  4.93 us
  transfers between devices with their start and end apart: 3, of which 3 were waited for; matrix products, arithmetic and copies ran while one was open for 8% of the time, Pallas kernels for 0%

profile of v5, /device:TPU:1, one launch (start us, length us, event | category | flops | bytes accessed | tf_op | source)
XLA Modules:
  0.0 213.4 jit_solution(8347698712288535015)
XLA Ops:
  6.5 0.8 fusion.51
  7.4 1.2 reduce-window.24
  8.6 0.2 slice_reduce_fusion
  9.0 0.7 multiply_add_fusion
  9.7 0.1 broadcast_in_dim.231
  10.0 0.9 copy.48
  10.9 3.8 %concatenate.48 = bf16[512,1806]{1,0:T(8,128)(2,1)} concatenate(bf16[512,768]{1,0:T(8,128)(2,1)} %param.10, bf16[512,768]{1,0:T(8,128)(2,1)} %param.11, bf16[512,128]{1,0:T(8,128)(2,1)} %param.12, bf16[512,128]{1,0:T(8,128)(2,1)} %param.13, bf16[512,12]{1,0:T(8,128)(2,1)S(1)} %copy.48, bf16[512,1]{1,0:T(8,128)(2,1)S(1)} %broadcast_in_dim.231, bf16[512,1]{1,0:T(8,128)(2,1)S(1)} %broadcast_in_dim.232), dimensions={1} | concatenate | bytes 3698688 | tf_op jit(solution)/shard_map/concatenate | solution.py:120
  14.7 4.0 %convolution_convert_fusion.2 = bf16[512,1806]{0,1:T(8,128)(2,1)} fusion(bf16[512,1806]{1,0:T(8,128)(2,1)} %concatenate.48, s32[512]{0:T(512)S(1)} %get-tuple-element.74), kind=kOutput, calls=%fused_computation.6 | convolution fusion | flops 948050944 | bytes 3700736 | tf_op jit(solution)/shard_map/dot_general | solution.py:129
  18.7 4.0 %copy.51 = bf16[512,1806]{1,0:T(8,128)(2,1)} copy(bf16[512,1806]{0,1:T(8,128)(2,1)} %convolution_convert_fusion.2) | data formatting | bytes 3698688 | tf_op jit(solution)/shard_map/convert_element_type | solution.py:129
  22.6 13.3 %all-to-all-start = ((bf16[64,8,1806]{2,1,0:T(8,128)(2,1)}), bf16[64,8,1806]{2,1,0:T(8,128)(2,1)}, u32[]{:S(2)}, u32[]{:S(2)}) async-start(bf16[64,8,1806]{2,1,0:T(8,128)(2,1)} %bitcast.91), calls=%async_computation | async-start | bytes 3932160 | tf_op jit(solution)/shard_map/all_to_all | solution.py:130
  36.0 0.2 reduce-window.31
  36.2 0.6 fusion.55
  36.9 0.6 slice.81
  38.8 0.6 iota_compare_fusion.11
  39.4 0.6 compare_convert_fusion.1
  40.0 44.1 %all-to-all-done = bf16[64,8,1806]{2,1,0:T(8,128)(2,1)} async-done(((bf16[64,8,1806]{2,1,0:T(8,128)(2,1)}), bf16[64,8,1806]{2,1,0:T(8,128)(2,1)}, u32[]{:S(2)}, u32[]{:S(2)}) %all-to-all-start) | async-done | bytes 1849376 | tf_op jit(solution)/shard_map/all_to_all | solution.py:130
  84.1 1.2 add_reduce_fusion
  85.3 2.8 %convolution_convert_fusion.1 = bf16[512,1806]{0,1:T(8,128)(2,1)S(1)} fusion(s32[512]{0:T(512)S(1)} %add_reduce_fusion, bf16[64,8,1806]{2,1,0:T(8,128)(2,1)} %all-to-all-done), kind=kOutput, calls=%fused_computation.5 | convolution fusion | flops 948050944 | bytes 3700736 | tf_op jit(solution)/shard_map/dot_general | solution.py:148
  88.2 1.2 copy-done.2
  89.4 1.2 reduce-window.32
  90.6 0.2 slice_reduce_fusion.1
  90.9 0.2 slice_reduce_fusion.2
  91.1 0.8 copy.54
  92.0 2.3 %fusion.16 = bf16[1,12,64,128]{3,2,1,0:T(8,128)(2,1)S(1)} fusion(bf16[512,12,64]{0,2,1:T(8,128)(2,1)S(1)} %bitcast.93, f32[12,512]{1,0:T(8,128)S(1)} %exponential_multiply_fusion.1, f32[512,128]{1,0:T(8,128)} %copy.54, f32[12]{0:T(128)S(1)} %get-tuple-element.76), kind=kOutput, calls=%fused_computation.27 | convolution fusion | flops 102432768 | bytes 1269808 | tf_op jit(solution)/shard_map/while/body/eval_jaxpr/hsn,shp->hpn/dot_general | solution.py:65
  94.5 2.2 %all_gather.12 = bf16[2,12,65,128]{3,2,1,0:T(8,128)(2,1)S(1)} all-gather(bf16[1,12,65,128]{3,2,1,0:T(8,128)(2,1)S(1)} %pad_maximum_fusion.1), channel_id=1, replica_groups=mesh['sx'=4,'sz'=8,'sc'=2,'head'=4] {'sc'}, dimensions={0}, use_global_device_ids=true | all-gather | bytes 599040 | tf_op jit(solution)/shard_map/all_gather | solution.py:40
  96.7 0.2 convert_reduce_fusion
  96.9 0.9 slice_reduce_fusion.3
  97.8 0.7 select_reduce_fusion.5
  98.5 1.4 copy.57
  99.8 1.2 fusion.29
  101.2 0.7 pad_maximum_fusion.2
  102.0 0.5 fusion.62
  102.6 0.5 iota_compare_fusion.12
  103.1 0.6 fusion.54
  103.7 0.6 iota_compare_fusion.9
  104.3 0.9 fusion.17
  105.3 0.7 copy.68
  106.0 1.3 select_reduce_fusion.6
  107.3 1.4 exponential_multiply_fusion
  108.6 1.6 fusion.27
  110.2 1.3 fusion.43
  111.5 4.9 %fusion = f32[12,64,512]{2,1,0:T(8,128)} fusion(bf16[512,12,64]{0,2,1:T(8,128)(2,1)S(1)} %bitcast.94, f32[12,512]{1,0:T(8,128)S(1)} %bitcast.105, f32[512,512]{1,0:T(8,128)S(1)} %fusion.43, pred[512,512]{1,0:T(8,128)(4,1)S(1)} %copy-done.7), kind=kOutput, calls=%fused_computation.1 | convolution fusion | flops 415236096 | bytes 3694592 | tf_op jit(solution)/shard_map/while/body/eval_jaxpr/hts,shp->thp/dot_general | solution.py:81
  116.5 19.2 %all-gather.2.cloned.1.call-done = bf16[8,12,65,128]{3,2,1,0:T(8,128)(2,1)} async-done(((bf16[1,12,65,128]{3,2,1,0:T(8,128)(2,1)}), bf16[8,12,65,128]{3,2,1,0:T(8,128)(2,1)}) %all-gather.2.cloned.1.call-update) | async-done | bytes 1597456 | tf_op jit(solution)/shard_map/all_gather | solution.py:40
  135.7 2.4 %slice_reduce_fusion.4 = (bf16[12]{0:T(256)(128)(2,1)}, bf16[8,12,1,1]{3,2,1,0:T(2,128)(2,1)}) fusion(bf16[8,12,65,128]{3,2,1,0:T(8,128)(2,1)} %all-gather.2.cloned.1.call-done), kind=kLoop, calls=%fused_computation.148 | loop fusion | flops 84 | bytes 408 | tf_op jit(solution)/shard_map/reduce_prod | solution.py:34
  138.1 0.9 copy.72
  139.0 1.3 select_reduce_fusion.1
  140.4 0.8 copy.60
  141.1 1.6 slice.104
  142.8 1.1 fusion.12
  144.0 12.0 %all_gather.14 = bf16[4,12,65,128]{3,2,1,0:T(8,128)(2,1)S(1)} all-gather(bf16[1,12,65,128]{3,2,1,0:T(8,128)(2,1)S(1)} %pad_maximum_fusion.3), channel_id=1, replica_groups=mesh['sx'=4,'sz'=8,'sc'=2,'head'=4] {'sx'}, dimensions={0}, use_global_device_ids=true | all-gather | bytes 998400 | tf_op jit(solution)/shard_map/all_gather | solution.py:40
  156.0 1.0 slice.106
  157.1 0.2 fusion.48
  157.2 0.6 select_reduce_fusion.3
  158.0 0.7 copy.63
  158.7 0.7 multiply_bitcast_fusion
  159.5 2.6 %fusion.10 = f32[12,1,64,128]{3,1,2,0:T(1,128)S(1)} fusion(bf16[8,12,1,1]{0,2,3,1:T(2,128)(2,1)S(1)} %copy.66, bf16[8,12,64,128]{3,2,1,0:T(8,128)(2,1)} %copy-done.1), kind=kOutput, calls=%fused_computation.21 | convolution fusion | flops 1572864 | bytes 1966272 | tf_op jit(solution)/shard_map/jh,jhpn->hpn/dot_general | solution.py:44
  162.1 1.8 fusion.19
  164.0 2.0 fusion.7
  166.0 1.7 multiply_reduce_fusion
  167.8 1.5 convolution_convert_fusion
  169.3 1.3 pad_maximum_fusion
  170.6 33.3 %reduce-scatter.2.cloned.1.call-done = bf16[136,1536]{1,0:T(8,128)(2,1)} async-done(((bf16[544,1536]{1,0:T(8,128)(2,1)}), bf16[136,1536]{1,0:T(8,128)(2,1)}) %reduce-scatter.2.cloned.1.call-update) | async-done | bytes 417808 | tf_op jit(solution)/shard_map/reduce_scatter | solution.py:229
  203.9 0.8 rsqrt_bitcast_fusion
  204.7 1.9 multiply_convert_fusion.12
  (89 shorter events, 1.7 us)
Async XLA Ops:
  6.5 161.2 %copy-start = (bf16[768,1536]{1,0:T(8,128)(2,1)S(1)}, bf16[768,1536]{1,0:T(8,128)(2,1)}, u32[]{:S(2)}) copy-start(bf16[768,1536]{1,0:T(8,128)(2,1)} %param.19) | copy-start | bytes 7077892
  22.6 13.4 %copy-start.16 = (s32[4]{0:T(128)S(1)}, s32[4]{0:T(128)}, u32[]{:S(2)}) copy-start(s32[4]{0:T(128)} %param.16) | copy-start | bytes 52
  22.6 61.5 %all-to-all-start = ((bf16[64,8,1806]{2,1,0:T(8,128)(2,1)}), bf16[64,8,1806]{2,1,0:T(8,128)(2,1)}, u32[]{:S(2)}, u32[]{:S(2)}) async-start(bf16[64,8,1806]{2,1,0:T(8,128)(2,1)} %bitcast.91), calls=%async_computation | async-start | bytes 3932160 | tf_op jit(solution)/shard_map/all_to_all | solution.py:130
  35.9 99.8 %all-gather.2.cloned.1.call-start = ((), (), s32[]{:S(2)}) async-start(), calls=%async_computation.2 | async-start | bytes 1990656 | tf_op jit(solution)/shard_map/all_gather | solution.py:40
  38.8 49.3 %copy-start.21 = (pred[2]{0:T(512)(128)(4,1)}, pred[2]{0:T(512)(128)(4,1)S(1)}, u32[]{:S(2)}) copy-start(pred[2]{0:T(512)(128)(4,1)S(1)} %iota_compare_fusion.14) | copy-start | bytes 10
  88.1 1.3 copy-start.2
  90.9 3.6 %copy-start.5 = (f32[2,8,4,128]{3,1,2,0:T(8,128)}, f32[2,8,4,128]{3,1,2,0:T(8,128)S(1)}, u32[]{:S(2)}) copy-start(f32[2,8,4,128]{3,1,2,0:T(8,128)S(1)} %copy.75) | copy-start | bytes 98308
  92.0 5.8 %copy-start.18 = (pred[2,2]{1,0:T(4,128)(4,1)S(1)}, pred[2,2]{1,0:T(4,128)(4,1)}, u32[]{:S(2)}) copy-start(pred[2,2]{1,0:T(4,128)(4,1)} %get-tuple-element.92) | copy-start | bytes 16
  92.0 5.7 %copy-start.19 = (pred[2,2]{1,0:T(4,128)(4,1)S(1)}, pred[2,2]{1,0:T(4,128)(4,1)}, u32[]{:S(2)}) copy-start(pred[2,2]{1,0:T(4,128)(4,1)} %get-tuple-element.94) | copy-start | bytes 16
  96.7 10.6 %copy-start.4 = (bf16[2,12,64,128]{3,2,1,0:T(8,128)(2,1)}, bf16[2,12,64,128]{3,2,1,0:T(8,128)(2,1)S(1)}, u32[]{:S(2)}) copy-start(bf16[2,12,64,128]{3,2,1,0:T(8,128)(2,1)S(1)} %slice.102) | copy-start | bytes 1179652
  99.8 1.3 copy-start.15
  101.9 102.0 %reduce-scatter.2.cloned.1.call-start = ((), (), s32[]{:S(2)}) async-start(), calls=%async_computation.3 | async-start | bytes 2088960 | tf_op jit(solution)/shard_map/reduce_scatter | solution.py:229
  102.0 1.7 copy-start.13
  106.0 5.5 %copy-start.6 = (f32[2,8,4,128]{3,1,2,0:T(8,128)S(1)}, f32[2,8,4,128]{3,1,2,0:T(8,128)}, u32[]{:S(2)}) copy-start(f32[2,8,4,128]{3,1,2,0:T(8,128)} %copy-done.5) | copy-start | bytes 98308
  106.0 5.5 %copy-start.7 = (pred[512,512]{1,0:T(8,128)(4,1)S(1)}, pred[512,512]{1,0:T(8,128)(4,1)}, u32[]{:S(2)}) copy-start(pred[512,512]{1,0:T(8,128)(4,1)} %fusion.17) | copy-start | bytes 786436
  111.5 27.5 %copy-start.10 = (pred[8,8]{1,0:T(8,128)(4,1)S(1)}, pred[8,8]{1,0:T(8,128)(4,1)}, u32[]{:S(2)}) copy-start(pred[8,8]{1,0:T(8,128)(4,1)} %get-tuple-element.96) | copy-start | bytes 196
  142.7 13.3 %copy-start.1 = (bf16[8,12,64,128]{3,2,1,0:T(8,128)(2,1)}, bf16[8,12,64,128]{3,2,1,0:T(8,128)(2,1)S(1)}, u32[]{:S(2)}) copy-start(bf16[8,12,64,128]{3,2,1,0:T(8,128)(2,1)S(1)} %slice.104) | copy-start | bytes 4718596
  142.7 1.2 copy-start.12
  143.8 13.4 %copy-start.14 = (pred[8]{0:T(512)(128)(4,1)S(1)}, pred[8]{0:T(512)(128)(4,1)}, u32[]{:S(2)}) copy-start(pred[8]{0:T(512)(128)(4,1)} %copy-done.13) | copy-start | bytes 28
  143.8 14.0 %copy-start.20 = (pred[4,4]{1,0:T(4,128)(4,1)S(1)}, pred[4,4]{1,0:T(4,128)(4,1)}, u32[]{:S(2)}) copy-start(pred[4,4]{1,0:T(4,128)(4,1)} %fusion.54) | copy-start | bytes 52
  143.9 14.1 %copy-start.17 = (f32[4]{0:T(128)S(1)}, f32[4]{0:T(128)}, u32[]{:S(2)}) copy-start(f32[4]{0:T(128)} %get-tuple-element.79) | copy-start | bytes 52
  159.4 4.6 %copy-start.11 = (f32[12]{0:T(128)S(1)}, f32[12]{0:T(128)}, u32[]{:S(2)}) copy-start(f32[12]{0:T(128)} %select_reduce_fusion.3) | copy-start | bytes 148
  159.5 2.6 %copy-start.9 = (bf16[4,12,1,1]{0,2,3,1:T(2,128)(2,1)S(1)}, bf16[4,12,1,1]{0,2,3,1:T(2,128)(2,1)}, u32[]{:S(2)}) copy-start(bf16[4,12,1,1]{0,2,3,1:T(2,128)(2,1)} %copy.63) | copy-start | bytes 292
  159.5 4.5 %copy-start.3 = (f32[12,64,512]{2,1,0:T(8,128)S(1)}, f32[12,64,512]{2,1,0:T(8,128)}, u32[]{:S(2)}) copy-start(f32[12,64,512]{2,1,0:T(8,128)} %fusion) | copy-start | bytes 4718596
  159.5 4.5 %copy-start.8 = (f32[512,12]{0,1:T(8,128)S(1)}, f32[512,12]{0,1:T(8,128)}, u32[]{:S(2)}) copy-start(f32[512,12]{0,1:T(8,128)} %exponential_multiply_fusion) | copy-start | bytes 73732
  166.0 1.7 copy-start.22
Sparse Core Ops, SparseCore 0:
  102.1 33.5 all-gather.1
  170.8 33.0 reduce-scatter.1

commit v6 on v5

--- a/solution.py
+++ b/solution.py
@@ -34,21 +34,29 @@
     return into_here, into_end, kept_before, jnp.prod(kept, axis=0)
 
 
-def exclusive_prefix(kept, state, axes):
-    levels = []
-    for level, axis in enumerate(axes):
-        gathered = lax.all_gather(pack_state(kept, state), axis)
-        g_kept = gathered[:, :, -1, 0].astype(jnp.float32)
-        g_state = gathered[:, :, :-1, :].astype(jnp.float32)
-        into_here, into_end, kept_before, kept_all = group_weights(g_kept, lax.axis_index(axis))
-        levels.append((kept_before, jnp.einsum("jh,jhpn->hpn", into_here, g_state)))
-        if level + 1 < len(axes):
-            state = jnp.einsum("jh,jhpn->hpn", into_end, g_state)
-            kept = kept_all
-    result = levels[-1][1]
-    for kept_before, local_before in reversed(levels[:-1]):
-        result = kept_before[:, None, None] * result + local_before
-    return result
+def gathered_level(kept, state, axis):
+    gathered = lax.all_gather(pack_state(kept, state), axis)
+    g_kept = gathered[:, :, -1, 0].astype(jnp.float32)
+    into_here, into_end, kept_before, kept_all = group_weights(g_kept, lax.axis_index(axis))
+    rows = state.shape[1]
+    before = jnp.einsum("jh,jhpn->hpn", into_here, gathered.astype(jnp.float32))[:, :rows]
+    total = jnp.einsum("jh,jhpn->hpn", into_end, gathered.astype(jnp.float32))[:, :rows]
+    return before, kept_before, total, kept_all
+
+
+def exclusive_prefix(kept, state, pair, line, lines):
+    pair_before, pair_kept_before, pair_total, pair_kept = gathered_level(kept, state, pair)
+    half = kept.shape[0] // 2
+    mine = lax.axis_index(pair) * half
+    part_total = lax.dynamic_slice_in_dim(pair_total, mine, half, 0)
+    part_kept = lax.dynamic_slice_in_dim(pair_kept, mine, half, 0)
+    line_before, line_kept_before, line_total, line_kept = gathered_level(
+        part_kept, part_total, line
+    )
+    outer_before, _, _, _ = gathered_level(line_kept, line_total, lines)
+    start_state = line_kept_before[:, None, None] * outer_before + line_before
+    whole = lax.all_gather(start_state, pair, tiled=True)
+    return pair_kept_before[:, None, None] * whole + pair_before
 
 
 def doc_index(places, starts):
@@ -185,7 +193,7 @@
     )
     local_state, local_kept = local_carry
     block_states, throughs, runnings = (block_outputs[0], block_outputs[1], block_outputs[2])
-    entry_state = exclusive_prefix(local_kept, local_state, ("sc", "sz", "sx"))
+    entry_state = exclusive_prefix(local_kept, local_state, "sc", "sz", "sx")
 
     def mix_pass(carry_state, pieces):
         by_head, key_block, query_block, running, doc_block, before, block_state, through = pieces

time: 214 us -> 193 us (0.902)
  waiting for transfers between devices: 96.6 us -> 67 us
  blocking collectives: 14.2 us -> 43.7 us
  other arithmetic: 27.1 us -> 17.5 us
  local copies, waits for them, and re-layouts: 19.8 us -> 13.8 us
  matrix products: 27.1 us -> 22.3 us
    all_gather x2 -> x4, blocking collectives: 14.2 us -> 43.7 us  [the longest x3 33.6 us: gathered_level(): gathered = lax.all_gather(pack_state(kept, state), axis)]
    all_gather x1 -> x0, waiting for transfers between devices: 19.2 us -> none  [exclusive_prefix(): gathered = lax.all_gather(pack_state(kept, state), axis)]
    reduce_scatter x1, waiting for transfers between devices: 33.3 us -> 25.6 us  [body(): lax.psum_scatter(sent.reshape(groups * (chunk + 8), d_model), 'head', sca...]
    dot_general x5, matrix products: 8.32 us -> 4.32 us  [the longest x3 3.4 us: gathered_level(): jnp.einsum('jh,jhpn->hpn', into_here, gathered.astype(jnp.float32))]
    reduce_prod x2, other arithmetic: 3.29 us -> 0.59 us  [group_weights(): return (into_here, into_end, kept_before, jnp.prod(kept, axis=0))]
    all_to_all x1, waiting for transfers between devices: 44.1 us -> 41.4 us  [send(): lax.all_to_all(packed.reshape(shards, capacity, packed.shape[1]), ROWS, s...]
    slice x3 -> x1, local copies, waits for them, and re-layouts: 2.63 us -> 0.01 us  [gathered_level(): jnp.einsum('jh,jhpn->hpn', into_end, gathered.astype(jnp.float32))[:, :rows]]
  transfers between devices with their start and end apart: 3 -> 2, of which waited for: 3 -> 2; matrix products, arithmetic and copies ran while one was open for 8% -> 3% of each run, Pallas kernels for 0% -> 0%
where the time goes in v6:
time: 193 us
  waiting for transfers between devices  67 us (35%)
  blocking collectives  43.7 us (23%)
  matrix products  22.3 us (12%)
  other arithmetic  17.5 us (9%)
  between operations  15.1 us (8%)
  local copies, waits for them, and re-layouts  13.8 us (7%)
  starting transfers between devices  13.3 us (7%)
    all_to_all x1, waiting for transfers between devices, send(): lax.all_to_all(packed.reshape(shards, capacity, packed.shape[1]), ROWS, s...  41.4 us
    all_gather x3, blocking collectives, gathered_level(): gathered = lax.all_gather(pack_state(kept, state), axis)  33.6 us
    reduce_scatter x1, waiting for transfers between devices, body(): lax.psum_scatter(sent.reshape(groups * (chunk + 8), d_model), 'head', sca...  25.6 us
    all_to_all x1, starting transfers between devices, send(): lax.all_to_all(packed.reshape(shards, capacity, packed.shape[1]), ROWS, s...  13.3 us
    all_gather x1, blocking collectives, exclusive_prefix(): whole = lax.all_gather(start_state, pair, tiled=True)  10.1 us
    dot_general x1, matrix products, send(): jnp.dot(to_slot, values, preferred_element_type=jnp.float32)  3.98 us
    convert_element_type x1, local copies, waits for them, and re-layouts, send(): jnp.dot(to_slot, values, preferred_element_type=jnp.float32)  3.95 us
  transfers between devices with their start and end apart: 2, of which 2 were waited for; matrix products, arithmetic and copies ran while one was open for 3% of the time, Pallas kernels for 0%

profile of v6, /device:TPU:1, one launch (start us, length us, event | category | flops | bytes accessed | tf_op | source)
XLA Modules:
  0.0 192.8 jit_solution(16908941050465766524)
XLA Ops:
  6.5 1.0 copy.48
  7.6 0.7 fusion.53
  8.3 1.2 reduce-window.24
  9.5 0.2 slice_reduce_fusion
  9.8 0.1 fusion.36
  9.9 0.7 multiply_add_fusion
  10.6 0.1 broadcast_in_dim.231
  10.7 0.1 broadcast_in_dim.232
  10.9 3.8 %concatenate.48 = bf16[512,1806]{1,0:T(8,128)(2,1)} concatenate(bf16[512,768]{1,0:T(8,128)(2,1)} %param.10, bf16[512,768]{1,0:T(8,128)(2,1)} %param.11, bf16[512,128]{1,0:T(8,128)(2,1)} %param.12, bf16[512,128]{1,0:T(8,128)(2,1)} %param.13, bf16[512,12]{1,0:T(8,128)(2,1)S(1)} %copy.48, bf16[512,1]{1,0:T(8,128)(2,1)S(1)} %broadcast_in_dim.231, bf16[512,1]{1,0:T(8,128)(2,1)S(1)} %broadcast_in_dim.232), dimensions={1} | concatenate | bytes 3698688 | tf_op jit(solution)/shard_map/concatenate | solution.py:128
  14.7 4.0 %convolution_convert_fusion.2 = bf16[512,1806]{0,1:T(8,128)(2,1)} fusion(bf16[512,1806]{1,0:T(8,128)(2,1)} %concatenate.48, s32[512]{0:T(512)S(1)} %get-tuple-element.76), kind=kOutput, calls=%fused_computation.6 | convolution fusion | flops 948050944 | bytes 3700736 | tf_op jit(solution)/shard_map/dot_general | solution.py:137
  18.7 4.0 %copy.51 = bf16[512,1806]{1,0:T(8,128)(2,1)} copy(bf16[512,1806]{0,1:T(8,128)(2,1)} %convolution_convert_fusion.2) | data formatting | bytes 3698688 | tf_op jit(solution)/shard_map/convert_element_type | solution.py:137
  22.6 13.3 %all-to-all-start = ((bf16[64,8,1806]{2,1,0:T(8,128)(2,1)}), bf16[64,8,1806]{2,1,0:T(8,128)(2,1)}, u32[]{:S(2)}, u32[]{:S(2)}) async-start(bf16[64,8,1806]{2,1,0:T(8,128)(2,1)} %bitcast.94), calls=%async_computation | async-start | bytes 3932160 | tf_op jit(solution)/shard_map/all_to_all | solution.py:138
  36.0 0.2 reduce-window.31
  36.2 0.6 fusion.57
  36.8 0.1 convert_reduce_fusion
  36.9 0.6 slice.88
  38.8 0.6 fusion.63
  39.4 0.6 iota_compare_fusion.13
  40.0 0.6 iota_compare_fusion.12
  40.6 0.5 fusion.56
  41.1 0.6 compare_convert_fusion.1
  41.7 0.9 fusion.13
  42.7 41.4 %all-to-all-done = bf16[64,8,1806]{2,1,0:T(8,128)(2,1)} async-done(((bf16[64,8,1806]{2,1,0:T(8,128)(2,1)}), bf16[64,8,1806]{2,1,0:T(8,128)(2,1)}, u32[]{:S(2)}, u32[]{:S(2)}) %all-to-all-start) | async-done | bytes 1849376 | tf_op jit(solution)/shard_map/all_to_all | solution.py:138
  84.1 1.2 add_reduce_fusion
  85.3 2.8 %convolution_convert_fusion.1 = bf16[512,1806]{0,1:T(8,128)(2,1)S(1)} fusion(s32[512]{0:T(512)S(1)} %add_reduce_fusion, bf16[64,8,1806]{2,1,0:T(8,128)(2,1)} %all-to-all-done), kind=kOutput, calls=%fused_computation.5 | convolution fusion | flops 948050944 | bytes 3700736 | tf_op jit(solution)/shard_map/dot_general | solution.py:156
  88.2 1.6 fusion.39
  89.8 1.2 reduce-window.32
  91.0 0.2 slice_reduce_fusion.1
  91.3 0.2 slice_reduce_fusion.2
  91.5 0.8 copy.54
  92.3 0.1 exponential_multiply_fusion.1
  92.4 2.3 %fusion.12 = bf16[1,12,64,128]{3,2,1,0:T(8,128)(2,1)S(1)} fusion(bf16[512,12,64]{0,2,1:T(8,128)(2,1)S(1)} %bitcast.96, f32[12,512]{1,0:T(8,128)S(1)} %exponential_multiply_fusion.1, f32[512,128]{1,0:T(8,128)} %copy.54, f32[12]{0:T(128)S(1)} %get-tuple-element.78), kind=kOutput, calls=%fused_computation.23 | convolution fusion | flops 102432768 | bytes 1269808 | tf_op jit(solution)/shard_map/while/body/eval_jaxpr/hsn,shp->hpn/dot_general | solution.py:73
  94.8 2.2 %all_gather.15 = bf16[2,12,65,128]{3,2,1,0:T(8,128)(2,1)S(1)} all-gather(bf16[1,12,65,128]{3,2,1,0:T(8,128)(2,1)S(1)} %pad_maximum_fusion.1), channel_id=1, replica_groups=mesh['sx'=4,'sz'=8,'sc'=2,'head'=4] {'sc'}, dimensions={0}, use_global_device_ids=true | all-gather | bytes 599040 | tf_op jit(solution)/shard_map/all_gather | solution.py:38
  97.0 0.4 fusion.47
  97.4 0.1 select_reduce_fusion.5
  97.5 0.1 copy.58
  97.6 0.6 fusion.30
  98.4 20.9 %all_gather.16 = bf16[8,6,65,128]{3,2,1,0:T(8,128)(2,1)S(1)} all-gather(bf16[1,6,65,128]{3,2,1,0:T(8,128)(2,1)S(1)} %pad_maximum_fusion.2), channel_id=1, replica_groups=mesh['sx'=4,'sz'=8,'sc'=2,'head'=4] {'sz'}, dimensions={0}, use_global_device_ids=true | all-gather | bytes 898560 | tf_op jit(solution)/shard_map/all_gather | solution.py:38
  119.3 0.2 slice_reduce_fusion.3
  119.5 0.1 copy.73
  119.7 0.1 select_reduce_fusion.3
  119.8 0.1 select_reduce_fusion.6
  119.9 0.1 copy.69
  120.1 1.6 fusion.28
  121.6 0.8 copy.97
  122.5 0.3 select_reduce_fusion.1
  122.8 0.4 fusion.15
  123.2 0.4 fusion.17
  123.7 10.5 %all_gather.17 = bf16[4,6,65,128]{3,2,1,0:T(8,128)(2,1)S(1)} all-gather(bf16[1,6,65,128]{3,2,1,0:T(8,128)(2,1)S(1)} %pad_maximum_fusion.3), channel_id=1, replica_groups=mesh['sx'=4,'sz'=8,'sc'=2,'head'=4] {'sx'}, dimensions={0}, use_global_device_ids=true | all-gather | bytes 499200 | tf_op jit(solution)/shard_map/all_gather | solution.py:38
  134.3 0.8 copy-done.7
  135.0 0.1 fusion.46
  135.2 0.1 select_reduce_fusion.2
  135.3 0.1 copy.64
  135.5 1.5 fusion.21
  137.0 0.1 slice_add_fusion.2
  137.1 10.1 %all_gather.18 = f32[12,64,128]{2,1,0:T(8,128)S(1)} all-gather(f32[6,64,128]{2,1,0:T(8,128)S(1)} %slice_add_fusion.2), channel_id=1, replica_groups=mesh['sx'=4,'sz'=8,'sc'=2,'head'=4] {'sc'}, dimensions={0}, use_global_device_ids=true | all-gather | bytes 589824 | tf_op jit(solution)/shard_map/all_gather | solution.py:58
  147.2 3.8 %fusion = f32[12,64,512]{2,1,0:T(8,128)S(1)} fusion(bf16[512,12,64]{0,2,1:T(8,128)(2,1)S(1)} %bitcast.97, f32[12,512]{1,0:T(8,128)S(1)} %bitcast.108, f32[512,512]{1,0:T(8,128)S(1)} %copy-done.5, pred[512,512]{1,0:T(8,128)(4,1)S(1)} %copy-done.8), kind=kOutput, calls=%fused_computation.1 | convolution fusion | flops 415236096 | bytes 3694592 | tf_op jit(solution)/shard_map/while/body/eval_jaxpr/hts,shp->thp/dot_general | solution.py:89
  151.1 2.0 %fusion.7 = f32[512,12,64]{0,2,1:T(8,128)S(1)} fusion(f32[12,64,512]{2,1,0:T(8,128)S(1)} %fusion, bf16[512,12,64]{0,2,1:T(8,128)(2,1)S(1)} %bitcast.98, f32[12]{0:T(128)S(1)} %copy-done.14, f32[512,12]{0,1:T(8,128)S(1)} %exponential_multiply_fusion, f32[12,65,128]{2,1,0:T(8,128)S(1)} %bitcast.99, f32[12,64,128]{2,1,0:T(8,128)S(1)} %all_gather.18, ...), kind=kOutput, calls=%fused_computation.16 | convolution fusion | flops 606142464 | bytes 4883456 | tf_op jit(solution)/shard_map/while/body/eval_jaxpr/tn,hpn->thp/dot_general | solution.py:94
  153.1 1.7 multiply_reduce_fusion
  154.8 1.5 convolution_convert_fusion
  156.3 1.3 pad_maximum_fusion
  157.7 25.6 %reduce-scatter.2.cloned.1.call-done = bf16[136,1536]{1,0:T(8,128)(2,1)} async-done(((bf16[544,1536]{1,0:T(8,128)(2,1)}), bf16[136,1536]{1,0:T(8,128)(2,1)}) %reduce-scatter.2.cloned.1.call-update) | async-done | bytes 417808 | tf_op jit(solution)/shard_map/reduce_scatter | solution.py:237
  183.3 0.8 rsqrt_bitcast_fusion
  184.0 1.9 multiply_convert_fusion.12
  (77 shorter events, 1.2 us)
Async XLA Ops:
  6.5 148.2 %copy-start = (bf16[768,1536]{1,0:T(8,128)(2,1)S(1)}, bf16[768,1536]{1,0:T(8,128)(2,1)}, u32[]{:S(2)}) copy-start(bf16[768,1536]{1,0:T(8,128)(2,1)} %param.19) | copy-start | bytes 7077892
  22.6 13.3 %copy-start.9 = (s32[4]{0:T(128)S(1)}, s32[4]{0:T(128)}, u32[]{:S(2)}) copy-start(s32[4]{0:T(128)} %param.16) | copy-start | bytes 52
  22.6 61.4 %all-to-all-start = ((bf16[64,8,1806]{2,1,0:T(8,128)(2,1)}), bf16[64,8,1806]{2,1,0:T(8,128)(2,1)}, u32[]{:S(2)}, u32[]{:S(2)}) async-start(bf16[64,8,1806]{2,1,0:T(8,128)(2,1)} %bitcast.94), calls=%async_computation | async-start | bytes 3932160 | tf_op jit(solution)/shard_map/all_to_all | solution.py:138
  35.9 147.3 %reduce-scatter.2.cloned.1.call-start = ((), (), s32[]{:S(2)}) async-start(), calls=%async_computation.2 | async-start | bytes 2088960 | tf_op jit(solution)/shard_map/reduce_scatter | solution.py:237
  88.1 1.7 copy-start.3
  88.1 6.6 %copy-start.1 = (bf16[512,768]{0,1:T(8,128)(2,1)}, bf16[512,768]{0,1:T(8,128)(2,1)S(1)}, u32[]{:S(2)}) copy-start(bf16[512,768]{0,1:T(8,128)(2,1)S(1)} %slice.104) | copy-start | bytes 2359300
  97.0 1.4 copy-start.6
  97.6 22.3 %copy-start.12 = (f32[2]{0:T(128)S(1)}, f32[2]{0:T(128)}, u32[]{:S(2)}) copy-start(f32[2]{0:T(128)} %fusion.63) | copy-start | bytes 28
  98.4 24.4 %copy-start.13 = (f32[8]{0:T(128)S(1)}, f32[8]{0:T(128)}, u32[]{:S(2)}) copy-start(f32[8]{0:T(128)} %get-tuple-element.94) | copy-start | bytes 100
  122.8 12.4 %copy-start.11 = (pred[4,4]{1,0:T(4,128)(4,1)S(1)}, pred[4,4]{1,0:T(4,128)(4,1)}, u32[]{:S(2)}) copy-start(pred[4,4]{1,0:T(4,128)(4,1)} %fusion.56) | copy-start | bytes 52
  122.8 12.4 %copy-start.10 = (f32[4]{0:T(128)S(1)}, f32[4]{0:T(128)}, u32[]{:S(2)}) copy-start(f32[4]{0:T(128)} %get-tuple-element.97) | copy-start | bytes 52
  123.6 23.6 %copy-start.2 = (bf16[512,768]{0,1:T(8,128)(2,1)S(1)}, bf16[512,768]{0,1:T(8,128)(2,1)}, u32[]{:S(2)}) copy-start(bf16[512,768]{0,1:T(8,128)(2,1)} %copy-done.1) | copy-start | bytes 2359300
  134.3 0.8 copy-start.7
  135.5 11.7 %copy-start.5 = (f32[512,512]{1,0:T(8,128)S(1)}, f32[512,512]{1,0:T(8,128)}, u32[]{:S(2)}) copy-start(f32[512,512]{1,0:T(8,128)} %fusion.39) | copy-start | bytes 3145732
  135.5 11.7 %copy-start.8 = (pred[512,512]{1,0:T(8,128)(4,1)S(1)}, pred[512,512]{1,0:T(8,128)(4,1)}, u32[]{:S(2)}) copy-start(pred[512,512]{1,0:T(8,128)(4,1)} %fusion.13) | copy-start | bytes 786436
  147.2 3.8 %copy-start.4 = (f32[12,1,65,128]{3,2,0,1:T(8,128)S(1)}, f32[12,1,65,128]{3,2,0,1:T(8,128)}, u32[]{:S(2)}) copy-start(f32[12,1,65,128]{3,2,0,1:T(8,128)} %copy.97) | copy-start | bytes 1198084
  147.2 3.8 %copy-start.14 = (f32[12]{0:T(128)S(1)}, f32[12]{0:T(128)}, u32[]{:S(2)}) copy-start(f32[12]{0:T(128)} %param.17) | copy-start | bytes 148
  153.1 1.7 copy-start.15
Sparse Core Ops, SparseCore 0:
  157.8 25.4 reduce-scatter.1

commit v7 on v6

--- a/solution.py
+++ b/solution.py
@@ -44,17 +44,13 @@
     return before, kept_before, total, kept_all
 
 
-def exclusive_prefix(kept, state, pair, line, lines):
+def exclusive_prefix(kept, state, pair, lines):
     pair_before, pair_kept_before, pair_total, pair_kept = gathered_level(kept, state, pair)
     half = kept.shape[0] // 2
     mine = lax.axis_index(pair) * half
     part_total = lax.dynamic_slice_in_dim(pair_total, mine, half, 0)
     part_kept = lax.dynamic_slice_in_dim(pair_kept, mine, half, 0)
-    line_before, line_kept_before, line_total, line_kept = gathered_level(
-        part_kept, part_total, line
-    )
-    outer_before, _, _, _ = gathered_level(line_kept, line_total, lines)
-    start_state = line_kept_before[:, None, None] * outer_before + line_before
+    start_state, _, _, _ = gathered_level(part_kept, part_total, lines)
     whole = lax.all_gather(start_state, pair, tiled=True)
     return pair_kept_before[:, None, None] * whole + pair_before
 
@@ -193,7 +189,7 @@
     )
     local_state, local_kept = local_carry
     block_states, throughs, runnings = (block_outputs[0], block_outputs[1], block_outputs[2])
-    entry_state = exclusive_prefix(local_kept, local_state, "sc", "sz", "sx")
+    entry_state = exclusive_prefix(local_kept, local_state, "sc", ("sx", "sz"))
 
     def mix_pass(carry_state, pieces):
         by_head, key_block, query_block, running, doc_block, before, block_state, through = pieces

time: 193 us -> 227 us (1.18)
  waiting for transfers between devices: 67 us -> 135 us
  blocking collectives: 43.7 us -> 8.15 us
  other arithmetic: 17.5 us -> 14.5 us
  matrix products: 22.3 us -> 24.6 us
    all_gather x0 -> x1, waiting for transfers between devices: none -> 65 us  [gathered_level(): gathered = lax.all_gather(pack_state(kept, state), axis)]
    all_gather x3 -> x1, blocking collectives: 33.6 us -> 2.17 us  [gathered_level(): gathered = lax.all_gather(pack_state(kept, state), axis)]
    all_gather x1, blocking collectives: 10.1 us -> 5.98 us  [exclusive_prefix(): whole = lax.all_gather(start_state, pair, tiled=True)]
    all_to_all x1, waiting for transfers between devices: 41.4 us -> 44.6 us  [send(): lax.all_to_all(packed.reshape(shards, capacity, packed.shape[1]), ROWS, s...]
  transfers between devices with their start and end apart: 2 -> 3, of which waited for: 2 -> 3; matrix products, arithmetic and copies ran while one was open for 3% -> 5% of each run, Pallas kernels for 0% -> 0%
where the time goes in v7:
time: 227 us; the launch traced here: 226 us
  waiting for transfers between devices  135 us (59%)
  matrix products  24.6 us (11%)
  local copies, waits for them, and re-layouts  15.6 us (7%)
  between operations  15.1 us (7%)
  other arithmetic  14.5 us (6%)
  starting transfers between devices  13.4 us (6%)
  blocking collectives  8.15 us (4%)
    all_gather x1, waiting for transfers between devices, gathered_level(): gathered = lax.all_gather(pack_state(kept, state), axis)  65 us
    all_to_all x1, waiting for transfers between devices, send(): lax.all_to_all(packed.reshape(shards, capacity, packed.shape[1]), ROWS, s...  44.6 us
    reduce_scatter x1, waiting for transfers between devices, body(): lax.psum_scatter(sent.reshape(groups * (chunk + 8), d_model), 'head', sca...  25.3 us
    all_to_all x1, starting transfers between devices, send(): lax.all_to_all(packed.reshape(shards, capacity, packed.shape[1]), ROWS, s...  13.3 us
    all_gather x1, blocking collectives, exclusive_prefix(): whole = lax.all_gather(start_state, pair, tiled=True)  5.98 us
    dot_general x1, matrix products, inner_terms(): jnp.einsum('hts,shp->thp', affinity_logits, by_head, preferred_element_ty...  4.92 us
  transfers between devices with their start and end apart: 3, of which 3 were waited for; matrix products, arithmetic and copies ran while one was open for 5% of the time, Pallas kernels for 0%

profile of v7, /device:TPU:1, one launch (start us, length us, event | category | flops | bytes accessed | tf_op | source)
XLA Modules:
  0.0 226.2 jit_solution(6297851505301490064)
XLA Ops:
  6.5 0.8 fusion.47
  7.4 1.2 reduce-window.24
  8.6 0.2 slice_reduce_fusion
  8.9 0.1 fusion.32
  9.0 0.7 multiply_add_fusion
  9.7 0.1 broadcast_in_dim.172
  9.8 0.1 broadcast_in_dim.173
  10.0 0.9 copy.51
  10.9 3.8 %concatenate.35 = bf16[512,1806]{1,0:T(8,128)(2,1)} concatenate(bf16[512,768]{1,0:T(8,128)(2,1)} %param.10, bf16[512,768]{1,0:T(8,128)(2,1)} %param.11, bf16[512,128]{1,0:T(8,128)(2,1)} %param.12, bf16[512,128]{1,0:T(8,128)(2,1)} %param.13, bf16[512,12]{1,0:T(8,128)(2,1)S(1)} %copy.51, bf16[512,1]{1,0:T(8,128)(2,1)S(1)} %broadcast_in_dim.172, bf16[512,1]{1,0:T(8,128)(2,1)S(1)} %broadcast_in_dim.173), dimensions={1} | concatenate | bytes 3698688 | tf_op jit(solution)/shard_map/concatenate | solution.py:124
  14.7 4.0 %convolution_convert_fusion.2 = bf16[512,1806]{0,1:T(8,128)(2,1)} fusion(bf16[512,1806]{1,0:T(8,128)(2,1)} %concatenate.35, s32[512]{0:T(512)S(1)} %get-tuple-element.72), kind=kOutput, calls=%fused_computation.8 | convolution fusion | flops 948050944 | bytes 3700736 | tf_op jit(solution)/shard_map/dot_general | solution.py:133
  18.7 4.0 %copy.54 = bf16[512,1806]{1,0:T(8,128)(2,1)} copy(bf16[512,1806]{0,1:T(8,128)(2,1)} %convolution_convert_fusion.2) | data formatting | bytes 3698688 | tf_op jit(solution)/shard_map/convert_element_type | solution.py:133
  22.6 13.3 %all-to-all-start = ((bf16[64,8,1806]{2,1,0:T(8,128)(2,1)}), bf16[64,8,1806]{2,1,0:T(8,128)(2,1)}, u32[]{:S(2)}, u32[]{:S(2)}) async-start(bf16[64,8,1806]{2,1,0:T(8,128)(2,1)} %bitcast.80), calls=%async_computation | async-start | bytes 3932160 | tf_op jit(solution)/shard_map/all_to_all | solution.py:134
  35.9 0.0 all-gather.2.cloned.1.call-start
  36.0 0.2 reduce-window.31
  36.2 0.6 fusion.50
  36.8 0.1 convert_reduce_fusion
  36.9 0.6 slice.78
  38.8 0.6 compare_convert_fusion.1
  39.5 44.6 %all-to-all-done = bf16[64,8,1806]{2,1,0:T(8,128)(2,1)} async-done(((bf16[64,8,1806]{2,1,0:T(8,128)(2,1)}), bf16[64,8,1806]{2,1,0:T(8,128)(2,1)}, u32[]{:S(2)}, u32[]{:S(2)}) %all-to-all-start) | async-done | bytes 1849376 | tf_op jit(solution)/shard_map/all_to_all | solution.py:134
  84.1 1.2 add_reduce_fusion
  85.3 2.8 %convolution_convert_fusion.1 = bf16[512,1806]{0,1:T(8,128)(2,1)S(1)} fusion(s32[512]{0:T(512)S(1)} %add_reduce_fusion, bf16[64,8,1806]{2,1,0:T(8,128)(2,1)} %all-to-all-done), kind=kOutput, calls=%fused_computation.7 | convolution fusion | flops 948050944 | bytes 3700736 | tf_op jit(solution)/shard_map/dot_general | solution.py:152
  88.1 0.1 slice.91
  88.1 1.2 copy-done.1
  89.4 1.2 reduce-window.32
  90.5 0.2 slice_reduce_fusion.1
  90.7 0.1 broadcast_add_fusion
  90.9 0.2 slice_reduce_fusion.2
  91.0 0.8 copy.57
  91.9 0.1 exponential_multiply_fusion.1
  92.0 2.3 %fusion.14 = bf16[1,12,64,128]{3,2,1,0:T(8,128)(2,1)S(1)} fusion(bf16[512,12,64]{0,2,1:T(8,128)(2,1)S(1)} %bitcast.82, f32[12,512]{1,0:T(8,128)S(1)} %exponential_multiply_fusion.1, f32[512,128]{1,0:T(8,128)} %copy.57, f32[12]{0:T(128)S(1)} %get-tuple-element.74), kind=kOutput, calls=%fused_computation.25 | convolution fusion | flops 102432768 | bytes 1269808 | tf_op jit(solution)/shard_map/while/body/eval_jaxpr/hsn,shp->hpn/dot_general | solution.py:69
  94.3 0.1 broadcast_in_dim.162
  94.4 2.2 all_gather.11
  96.6 0.8 copy-done.4
  97.4 0.4 fusion.42
  97.7 0.1 select_reduce_fusion.2
  97.8 0.1 copy.60
  98.0 1.6 fusion.26
  99.6 0.1 dynamic_slice.46
  99.7 0.1 broadcast_in_dim.168
  99.8 0.7 pad_maximum_fusion.2
  100.4 0.0 all-gather.2.cloned.1.call-update
  100.5 0.0 reduce-scatter.2.cloned.1.call-start
  100.6 0.2 fusion.15
  100.8 0.1 multiply_bitcast_fusion.1
  100.9 0.1 copy.66
  101.0 1.6 fusion.24
  102.6 0.8 copy.85
  103.4 0.1 select_reduce_fusion.3
  103.5 1.3 fusion.35
  104.8 4.9 %fusion = f32[12,64,512]{2,1,0:T(8,128)} fusion(bf16[512,12,64]{0,2,1:T(8,128)(2,1)S(1)} %bitcast.83, f32[12,512]{1,0:T(8,128)S(1)} %bitcast.92, f32[512,512]{1,0:T(8,128)S(1)} %fusion.35, pred[512,512]{1,0:T(8,128)(4,1)S(1)} %fusion.15), kind=kOutput, calls=%fused_computation.1 | convolution fusion | flops 415236096 | bytes 3694592 | tf_op jit(solution)/shard_map/while/body/eval_jaxpr/hts,shp->thp/dot_general | solution.py:85
  109.7 65.0 %all-gather.2.cloned.1.call-done = bf16[32,6,65,128]{3,2,1,0:T(8,128)(2,1)} async-done(((bf16[1,6,65,128]{3,2,1,0:T(8,128)(2,1)}), bf16[32,6,65,128]{3,2,1,0:T(8,128)(2,1)}) %all-gather.2.cloned.1.call-update) | async-done | bytes 3194896 | tf_op jit(solution)/shard_map/all_gather | solution.py:38
  174.6 1.0 slice.99
  175.7 0.1 copy.70
  175.8 0.2 select_reduce_fusion
  176.1 2.8 %fusion.2 = f32[6,1,65,128]{3,1,2,0:T(1,128)S(1)} fusion(bf16[32,6,65,128]{3,2,1,0:T(8,128)(2,1)} %all-gather.2.cloned.1.call-done, bf16[32,6,1,1]{0,1,2,3:T(8,128)(2,1)S(1)} %multiply_bitcast_fusion), kind=kOutput, calls=%fused_computation.3 | convolution fusion | flops 3194880 | bytes 3394944 | tf_op jit(solution)/shard_map/jh,jhpn->hpn/dot_general | solution.py:42
  178.9 6.0 %all_gather.13 = f32[12,64,128]{2,1,0:T(8,128)S(1)} all-gather(f32[6,64,128]{2,1,0:T(8,128)S(1)} %slice.100), channel_id=1, replica_groups=mesh['sx'=4,'sz'=8,'sc'=2,'head'=4] {'sc'}, dimensions={0}, use_global_device_ids=true | all-gather | bytes 589824 | tf_op jit(solution)/shard_map/all_gather | solution.py:54
  184.9 2.0 fusion.9
  186.8 1.7 multiply_reduce_fusion
  188.6 1.5 convolution_convert_fusion
  190.1 1.3 pad_maximum_fusion
  191.4 0.0 reduce-scatter.2.cloned.1.call-update
  191.5 25.3 %reduce-scatter.2.cloned.1.call-done = bf16[136,1536]{1,0:T(8,128)(2,1)} async-done(((bf16[544,1536]{1,0:T(8,128)(2,1)}), bf16[136,1536]{1,0:T(8,128)(2,1)}) %reduce-scatter.2.cloned.1.call-update) | async-done | bytes 417808 | tf_op jit(solution)/shard_map/reduce_scatter | solution.py:233
  216.8 0.8 rsqrt_bitcast_fusion
  217.5 1.9 multiply_convert_fusion.12
  (46 shorter events, 0.4 us)
Async XLA Ops:
  6.5 182.0 %copy-start = (bf16[768,1536]{1,0:T(8,128)(2,1)S(1)}, bf16[768,1536]{1,0:T(8,128)(2,1)}, u32[]{:S(2)}) copy-start(bf16[768,1536]{1,0:T(8,128)(2,1)} %param.19) | copy-start | bytes 7077892
  22.6 13.4 %copy-start.5 = (s32[4]{0:T(128)S(1)}, s32[4]{0:T(128)}, u32[]{:S(2)}) copy-start(s32[4]{0:T(128)} %param.16) | copy-start | bytes 52
  22.6 61.5 %all-to-all-start = ((bf16[64,8,1806]{2,1,0:T(8,128)(2,1)}), bf16[64,8,1806]{2,1,0:T(8,128)(2,1)}, u32[]{:S(2)}, u32[]{:S(2)}) async-start(bf16[64,8,1806]{2,1,0:T(8,128)(2,1)} %bitcast.80), calls=%async_computation | async-start | bytes 3932160 | tf_op jit(solution)/shard_map/all_to_all | solution.py:134
  35.9 138.7 %all-gather.2.cloned.1.call-start = ((), (), s32[]{:S(2)}) async-start(), calls=%async_computation.2 | async-start | bytes 3649536 | tf_op jit(solution)/shard_map/all_gather | solution.py:38
  88.1 1.2 copy-start.1
  96.6 0.8 copy-start.4
  100.5 116.3 %reduce-scatter.2.cloned.1.call-start = ((), (), s32[]{:S(2)}) async-start(), calls=%async_computation.3 | async-start | bytes 2088960 | tf_op jit(solution)/shard_map/reduce_scatter | solution.py:233
  176.0 8.8 %copy-start.2 = (f32[12,1,65,128]{3,2,0,1:T(8,128)S(1)}, f32[12,1,65,128]{3,2,0,1:T(8,128)}, u32[]{:S(2)}) copy-start(f32[12,1,65,128]{3,2,0,1:T(8,128)} %copy.85) | copy-start | bytes 1198084
  176.0 8.8 %copy-start.3 = (f32[12,64,512]{2,1,0:T(8,128)S(1)}, f32[12,64,512]{2,1,0:T(8,128)}, u32[]{:S(2)}) copy-start(f32[12,64,512]{2,1,0:T(8,128)} %fusion) | copy-start | bytes 4718596
  176.0 8.8 %copy-start.6 = (f32[12]{0:T(128)S(1)}, f32[12]{0:T(128)}, u32[]{:S(2)}) copy-start(f32[12]{0:T(128)} %param.17) | copy-start | bytes 148
  186.8 1.7 copy-start.7
Sparse Core Ops, SparseCore 0:
  100.6 74.0 all-gather.1
  191.6 25.1 reduce-scatter.1

commit v8 on v7

--- a/solution.py
+++ b/solution.py
@@ -4,7 +4,8 @@
 from jax.sharding import PartitionSpec as P
 
 ATTENTION_LANES = 48
-ROWS = ("sx", "sz", "sc")
+ROWS = ("xh", "xl", "zh", "zm", "zl", "sc")
+LEVELS = ("zl", "zm", "zh", "xl", "xh")
 HEAD_DIM = 64
 BLOCK = 512
 
@@ -44,13 +45,19 @@
     return before, kept_before, total, kept_all
 
 
-def exclusive_prefix(kept, state, pair, lines):
+def exclusive_prefix(kept, state, pair, levels):
     pair_before, pair_kept_before, pair_total, pair_kept = gathered_level(kept, state, pair)
     half = kept.shape[0] // 2
     mine = lax.axis_index(pair) * half
     part_total = lax.dynamic_slice_in_dim(pair_total, mine, half, 0)
     part_kept = lax.dynamic_slice_in_dim(pair_kept, mine, half, 0)
-    start_state, _, _, _ = gathered_level(part_kept, part_total, lines)
+    found = []
+    for level, axis in enumerate(levels):
+        before, kept_before, part_total, part_kept = gathered_level(part_kept, part_total, axis)
+        found.append((before, kept_before))
+    start_state = found[-1][0]
+    for before, kept_before in reversed(found[:-1]):
+        start_state = kept_before[:, None, None] * start_state + before
     whole = lax.all_gather(start_state, pair, tiled=True)
     return pair_kept_before[:, None, None] * whole + pair_before
 
@@ -189,7 +196,7 @@
     )
     local_state, local_kept = local_carry
     block_states, throughs, runnings = (block_outputs[0], block_outputs[1], block_outputs[2])
-    entry_state = exclusive_prefix(local_kept, local_state, "sc", ("sx", "sz"))
+    entry_state = exclusive_prefix(local_kept, local_state, "sc", LEVELS)
 
     def mix_pass(carry_state, pieces):
         by_head, key_block, query_block, running, doc_block, before, block_state, through = pieces
@@ -242,7 +249,7 @@
 
 def solution(mesh):
     seq = mesh.shape["seq"]
-    devices = mesh.devices.reshape(seq // 16, 8, 2, mesh.shape["head"])
+    devices = mesh.devices.reshape(seq // 32, 2, 2, 2, 2, 2, mesh.shape["head"])
     split_mesh = jax.sharding.Mesh(devices, ROWS + ("head",))
     in_specs = (
         P(ROWS, "head"),

time: 227 us -> 209 us (0.921)
  waiting for transfers between devices: 135 us -> 68.4 us
  blocking collectives: 8.15 us -> 41.5 us
  matrix products: 24.6 us -> 30.8 us
  other arithmetic: 14.5 us -> 19.3 us
  local copies, waits for them, and re-layouts: 15.6 us -> 19.7 us
    all_gather x1 -> x0, waiting for transfers between devices: 65 us -> none  [gathered_level(): gathered = lax.all_gather(pack_state(kept, state), axis)]
    all_gather x1 -> x6, blocking collectives: 2.17 us -> 36.1 us  [gathered_level(): gathered = lax.all_gather(pack_state(kept, state), axis)]
    dot_general x1 -> x5, matrix products: 1.58 us -> 5.8 us  [gathered_level(): jnp.einsum('jh,jhpn->hpn', into_end, gathered.astype(jnp.float32))[:, :rows]]
    dot_general x2 -> x6, matrix products: 4.34 us -> 7.18 us  [gathered_level(): jnp.einsum('jh,jhpn->hpn', into_here, gathered.astype(jnp.float32))]
    all_to_all x1, waiting for transfers between devices: 44.6 us -> 41.9 us  [send(): lax.all_to_all(packed.reshape(shards, capacity, packed.shape[1]), ROWS, s...]
    unnamed x20 -> x49, local copies, waits for them, and re-layouts: 3 us -> 4.66 us
  transfers between devices with their start and end apart: 3 -> 2, of which waited for: 3 -> 2; matrix products, arithmetic and copies ran while one was open for 5% -> 2% of each run, Pallas kernels for 0% -> 0%
where the time goes in v8:
time: 209 us; the launch traced here: 208 us
  waiting for transfers between devices  68.4 us (33%)
  blocking collectives  41.5 us (20%)
  matrix products  30.8 us (15%)
  local copies, waits for them, and re-layouts  19.7 us (9%)
  other arithmetic  19.3 us (9%)
  between operations  15.4 us (7%)
  starting transfers between devices  13.3 us (6%)
    all_to_all x1, waiting for transfers between devices, send(): lax.all_to_all(packed.reshape(shards, capacity, packed.shape[1]), ROWS, s...  41.9 us
    all_gather x6, blocking collectives, gathered_level(): gathered = lax.all_gather(pack_state(kept, state), axis)  36.1 us
    reduce_scatter x1, waiting for transfers between devices, body(): lax.psum_scatter(sent.reshape(groups * (chunk + 8), d_model), 'head', sca...  26.5 us
    all_to_all x1, starting transfers between devices, send(): lax.all_to_all(packed.reshape(shards, capacity, packed.shape[1]), ROWS, s...  13.3 us
    dot_general x6, matrix products, gathered_level(): jnp.einsum('jh,jhpn->hpn', into_here, gathered.astype(jnp.float32))  7.18 us
    dot_general x5, matrix products, gathered_level(): jnp.einsum('jh,jhpn->hpn', into_end, gathered.astype(jnp.float32))[:, :rows]  5.8 us
    all_gather x1, blocking collectives, exclusive_prefix(): whole = lax.all_gather(start_state, pair, tiled=True)  5.43 us
    unnamed x49, local copies, waits for them, and re-layouts  4.66 us
  transfers between devices with their start and end apart: 2, of which 2 were waited for; matrix products, arithmetic and copies ran while one was open for 2% of the time, Pallas kernels for 0%

profile of v8, /device:TPU:1, one launch (start us, length us, event | category | flops | bytes accessed | tf_op | source)
XLA Modules:
  0.0 208.5 jit_solution(11147807348719435011)
XLA Ops:
  6.5 1.0 copy.47
  7.6 0.7 fusion.69
  8.3 1.2 reduce-window.24
  9.5 0.2 slice_reduce_fusion
  9.9 0.7 multiply_add_fusion
  10.9 3.8 %concatenate.87 = bf16[512,1806]{1,0:T(8,128)(2,1)} concatenate(bf16[512,768]{1,0:T(8,128)(2,1)} %param.10, bf16[512,768]{1,0:T(8,128)(2,1)} %param.11, bf16[512,128]{1,0:T(8,128)(2,1)} %param.12, bf16[512,128]{1,0:T(8,128)(2,1)} %param.13, bf16[512,12]{1,0:T(8,128)(2,1)S(1)} %copy.47, bf16[512,1]{1,0:T(8,128)(2,1)S(1)} %broadcast_in_dim.344, bf16[512,1]{1,0:T(8,128)(2,1)S(1)} %broadcast_in_dim.345), dimensions={1} | concatenate | bytes 3698688 | tf_op jit(solution)/shard_map/concatenate | solution.py:131
  14.7 4.0 %convolution_convert_fusion.2 = bf16[512,1806]{0,1:T(8,128)(2,1)} fusion(bf16[512,1806]{1,0:T(8,128)(2,1)} %concatenate.87, s32[512]{0:T(512)S(1)} %get-tuple-element.92), kind=kOutput, calls=%fused_computation.6 | convolution fusion | flops 948050944 | bytes 3700736 | tf_op jit(solution)/shard_map/dot_general | solution.py:140
  18.7 4.0 %copy.50 = bf16[512,1806]{1,0:T(8,128)(2,1)} copy(bf16[512,1806]{0,1:T(8,128)(2,1)} %convolution_convert_fusion.2) | data formatting | bytes 3698688 | tf_op jit(solution)/shard_map/convert_element_type | solution.py:140
  22.6 13.3 %all-to-all-start = ((bf16[64,8,1806]{2,1,0:T(8,128)(2,1)}), bf16[64,8,1806]{2,1,0:T(8,128)(2,1)}, u32[]{:S(2)}, u32[]{:S(2)}) async-start(bf16[64,8,1806]{2,1,0:T(8,128)(2,1)} %bitcast.130), calls=%async_computation | async-start | bytes 3932160 | tf_op jit(solution)/shard_map/all_to_all | solution.py:141
  36.2 0.6 fusion.72
  36.9 0.6 slice.118
  38.9 0.6 fusion.78
  39.4 0.6 fusion.79
  40.2 0.5 copy-done.19
  40.7 0.6 compare_convert_fusion.1
  41.3 0.9 fusion.13
  42.2 41.9 %all-to-all-done = bf16[64,8,1806]{2,1,0:T(8,128)(2,1)} async-done(((bf16[64,8,1806]{2,1,0:T(8,128)(2,1)}), bf16[64,8,1806]{2,1,0:T(8,128)(2,1)}, u32[]{:S(2)}, u32[]{:S(2)}) %all-to-all-start) | async-done | bytes 1849376 | tf_op jit(solution)/shard_map/all_to_all | solution.py:141
  84.1 1.2 add_reduce_fusion
  85.3 2.8 %convolution_convert_fusion.1 = bf16[512,1806]{0,1:T(8,128)(2,1)S(1)} fusion(s32[512]{0:T(512)S(1)} %add_reduce_fusion, bf16[64,8,1806]{2,1,0:T(8,128)(2,1)} %all-to-all-done), kind=kOutput, calls=%fused_computation.5 | convolution fusion | flops 948050944 | bytes 3700736 | tf_op jit(solution)/shard_map/dot_general | solution.py:159
  88.1 1.5 fusion.38
  89.7 1.2 reduce-window.32
  91.4 0.9 copy.53
  92.3 2.3 %fusion.12 = bf16[1,12,64,128]{3,2,1,0:T(8,128)(2,1)S(1)} fusion(bf16[512,12,64]{0,2,1:T(8,128)(2,1)S(1)} %bitcast.132, f32[12,512]{1,0:T(8,128)S(1)} %exponential_multiply_fusion.1, f32[512,128]{1,0:T(8,128)} %copy.53, f32[12]{0:T(128)S(1)} %get-tuple-element.96), kind=kOutput, calls=%fused_computation.23 | convolution fusion | flops 102432768 | bytes 1269808 | tf_op jit(solution)/shard_map/while/body/eval_jaxpr/hsn,shp->hpn/dot_general | solution.py:76
  94.8 2.2 %all_gather.27 = bf16[2,12,65,128]{3,2,1,0:T(8,128)(2,1)S(1)} all-gather(bf16[1,12,65,128]{3,2,1,0:T(8,128)(2,1)S(1)} %pad_maximum_fusion.1), channel_id=1, replica_groups=mesh['xh'=2,'xl'=2,'zh'=2,'zm'=2,'zl'=2,'sc'=2,'head'=4] {'sc'}, dimensions={0}, use_global_device_ids=true | all-gather | bytes 599040 | tf_op jit(solution)/shard_map/all_gather | solution.py:39
  96.9 0.8 copy-done.4
  97.7 0.4 fusion.64
  98.3 1.6 fusion.29
  100.1 4.9 %all_gather.28 = bf16[2,6,65,128]{3,2,1,0:T(8,128)(2,1)S(1)} all-gather(bf16[1,6,65,128]{3,2,1,0:T(8,128)(2,1)S(1)} %pad_maximum_fusion.2), channel_id=1, replica_groups=mesh['xh'=2,'xl'=2,'zh'=2,'zm'=2,'zl'=2,'sc'=2,'head'=4] {'zl'}, dimensions={0}, use_global_device_ids=true | all-gather | bytes 299520 | tf_op jit(solution)/shard_map/all_gather | solution.py:39
  105.2 0.2 slice_reduce_fusion.6
  105.6 0.4 fusion.62
  106.1 8.5 %all_gather.29 = bf16[2,6,65,128]{3,2,1,0:T(8,128)(2,1)S(1)} all-gather(bf16[1,6,65,128]{3,2,1,0:T(8,128)(2,1)S(1)} %pad_maximum_fusion.3), channel_id=1, replica_groups=mesh['xh'=2,'xl'=2,'zh'=2,'zm'=2,'zl'=2,'sc'=2,'head'=4] {'zm'}, dimensions={0}, use_global_device_ids=true | all-gather | bytes 299520 | tf_op jit(solution)/shard_map/all_gather | solution.py:39
  114.7 0.5 copy-done.6
  115.3 0.2 slice_reduce_fusion.5
  115.7 1.3 fusion.58
  117.2 10.2 %all_gather.30 = bf16[2,6,65,128]{3,2,1,0:T(8,128)(2,1)S(1)} all-gather(bf16[1,6,65,128]{3,2,1,0:T(8,128)(2,1)S(1)} %pad_maximum_fusion.4), channel_id=1, replica_groups=mesh['xh'=2,'xl'=2,'zh'=2,'zm'=2,'zl'=2,'sc'=2,'head'=4] {'zh'}, dimensions={0}, use_global_device_ids=true | all-gather | bytes 299520 | tf_op jit(solution)/shard_map/all_gather | solution.py:39
  127.5 0.5 copy-done.8
  128.1 0.2 slice_reduce_fusion.4
  128.5 1.3 fusion.54
  129.9 4.5 %all_gather.31 = bf16[2,6,65,128]{3,2,1,0:T(8,128)(2,1)S(1)} all-gather(bf16[1,6,65,128]{3,2,1,0:T(8,128)(2,1)S(1)} %pad_maximum_fusion.5), channel_id=1, replica_groups=mesh['xh'=2,'xl'=2,'zh'=2,'zm'=2,'zl'=2,'sc'=2,'head'=4] {'xl'}, dimensions={0}, use_global_device_ids=true | all-gather | bytes 299520 | tf_op jit(solution)/shard_map/all_gather | solution.py:39
  134.5 0.6 copy-done.7
  135.1 0.2 slice_reduce_fusion.3
  135.8 1.6 fusion.27
  137.4 0.8 copy.121
  138.4 0.4 fusion.60
  139.0 1.3 fusion.56
  140.3 0.7 copy.124
  141.2 1.3 fusion.52
  142.5 0.7 copy.125
  143.5 1.3 fusion.48
  144.8 0.7 copy.126
  145.6 1.3 fusion.50
  147.0 5.8 %all_gather.32 = bf16[2,6,65,128]{3,2,1,0:T(8,128)(2,1)S(1)} all-gather(bf16[1,6,65,128]{3,2,1,0:T(8,128)(2,1)S(1)} %pad_maximum_fusion.6), channel_id=1, replica_groups=mesh['xh'=2,'xl'=2,'zh'=2,'zm'=2,'zl'=2,'sc'=2,'head'=4] {'xh'}, dimensions={0}, use_global_device_ids=true | all-gather | bytes 299520 | tf_op jit(solution)/shard_map/all_gather | solution.py:39
  152.8 0.7 copy-done.9
  153.9 1.4 fusion.18
  155.3 1.2 slice_add_fusion.2
  156.6 5.4 %all_gather.33 = f32[12,64,128]{2,1,0:T(8,128)S(1)} all-gather(f32[6,64,128]{2,1,0:T(8,128)S(1)} %slice_add_fusion.2), channel_id=1, replica_groups=mesh['xh'=2,'xl'=2,'zh'=2,'zm'=2,'zl'=2,'sc'=2,'head'=4] {'sc'}, dimensions={0}, use_global_device_ids=true | all-gather | bytes 589824 | tf_op jit(solution)/shard_map/all_gather | solution.py:61
  162.0 3.8 %fusion = f32[12,64,512]{2,1,0:T(8,128)S(1)} fusion(bf16[512,12,64]{0,2,1:T(8,128)(2,1)S(1)} %bitcast.133, f32[12,512]{1,0:T(8,128)S(1)} %bitcast.150, f32[512,512]{1,0:T(8,128)S(1)} %copy-done.3, pred[512,512]{1,0:T(8,128)(4,1)S(1)} %copy-done.5), kind=kOutput, calls=%fused_computation.1 | convolution fusion | flops 415236096 | bytes 3694592 | tf_op jit(solution)/shard_map/while/body/eval_jaxpr/hts,shp->thp/dot_general | solution.py:92
  165.8 2.0 fusion.7
  167.8 1.7 multiply_reduce_fusion
  169.6 1.5 convolution_convert_fusion
  171.1 1.3 pad_maximum_fusion
  172.5 26.5 %reduce-scatter.2.cloned.1.call-done = bf16[136,1536]{1,0:T(8,128)(2,1)} async-done(((bf16[544,1536]{1,0:T(8,128)(2,1)}), bf16[136,1536]{1,0:T(8,128)(2,1)}) %reduce-scatter.2.cloned.1.call-update) | async-done | bytes 417808 | tf_op jit(solution)/shard_map/reduce_scatter | solution.py:240
  199.0 0.8 rsqrt_bitcast_fusion
  199.8 1.9 multiply_convert_fusion.12
  (145 shorter events, 5.8 us)
Async XLA Ops:
  6.5 163.0 %copy-start = (bf16[768,1536]{1,0:T(8,128)(2,1)S(1)}, bf16[768,1536]{1,0:T(8,128)(2,1)}, u32[]{:S(2)}) copy-start(bf16[768,1536]{1,0:T(8,128)(2,1)} %param.19) | copy-start | bytes 7077892
  22.6 13.4 %copy-start.10 = (s32[4]{0:T(128)S(1)}, s32[4]{0:T(128)}, u32[]{:S(2)}) copy-start(s32[4]{0:T(128)} %param.16) | copy-start | bytes 52
  22.6 61.4 %all-to-all-start = ((bf16[64,8,1806]{2,1,0:T(8,128)(2,1)}), bf16[64,8,1806]{2,1,0:T(8,128)(2,1)}, u32[]{:S(2)}, u32[]{:S(2)}) async-start(bf16[64,8,1806]{2,1,0:T(8,128)(2,1)} %bitcast.130), calls=%async_computation | async-start | bytes 3932160 | tf_op jit(solution)/shard_map/all_to_all | solution.py:141
  35.9 163.1 %reduce-scatter.2.cloned.1.call-start = ((), (), s32[]{:S(2)}) async-start(), calls=%async_computation.2 | async-start | bytes 2088960 | tf_op jit(solution)/shard_map/reduce_scatter | solution.py:240
  38.8 1.8 copy-start.13
  39.4 1.2 copy-start.15
  40.0 0.6 copy-start.17
  40.0 0.6 copy-start.19
  88.1 1.6 copy-start.1
  96.9 0.8 copy-start.4
  114.6 0.7 copy-start.6
  115.7 19.6 %copy-start.20 = (pred[2]{0:T(512)(128)(4,1)S(1)}, pred[2]{0:T(512)(128)(4,1)}, u32[]{:S(2)}) copy-start(pred[2]{0:T(512)(128)(4,1)} %copy-done.19) | copy-start | bytes 10
  115.7 19.7 %copy-start.18 = (pred[2]{0:T(512)(128)(4,1)S(1)}, pred[2]{0:T(512)(128)(4,1)}, u32[]{:S(2)}) copy-start(pred[2]{0:T(512)(128)(4,1)} %copy-done.17) | copy-start | bytes 10
  115.7 19.7 %copy-start.16 = (pred[2]{0:T(512)(128)(4,1)S(1)}, pred[2]{0:T(512)(128)(4,1)}, u32[]{:S(2)}) copy-start(pred[2]{0:T(512)(128)(4,1)} %copy-done.15) | copy-start | bytes 10
  115.7 19.8 %copy-start.14 = (pred[2]{0:T(512)(128)(4,1)S(1)}, pred[2]{0:T(512)(128)(4,1)}, u32[]{:S(2)}) copy-start(pred[2]{0:T(512)(128)(4,1)} %copy-done.13) | copy-start | bytes 10
  115.7 19.9 %copy-start.12 = (f32[2]{0:T(128)S(1)}, f32[2]{0:T(128)}, u32[]{:S(2)}) copy-start(f32[2]{0:T(128)} %fusion.78) | copy-start | bytes 28
  127.4 0.7 copy-start.8
  129.8 8.5 %copy-start.11 = (f32[2]{0:T(128)S(1)}, f32[2]{0:T(128)}, u32[]{:S(2)}) copy-start(f32[2]{0:T(128)} %fusion.79) | copy-start | bytes 28
  134.4 0.7 copy-start.7
  152.8 0.7 copy-start.9
  153.9 8.1 %copy-start.3 = (f32[512,512]{1,0:T(8,128)S(1)}, f32[512,512]{1,0:T(8,128)}, u32[]{:S(2)}) copy-start(f32[512,512]{1,0:T(8,128)} %fusion.38) | copy-start | bytes 3145732
  153.9 8.1 %copy-start.5 = (pred[512,512]{1,0:T(8,128)(4,1)S(1)}, pred[512,512]{1,0:T(8,128)(4,1)}, u32[]{:S(2)}) copy-start(pred[512,512]{1,0:T(8,128)(4,1)} %fusion.13) | copy-start | bytes 786436
  162.0 3.8 %copy-start.2 = (f32[12,1,65,128]{3,2,0,1:T(8,128)S(1)}, f32[12,1,65,128]{3,2,0,1:T(8,128)}, u32[]{:S(2)}) copy-start(f32[12,1,65,128]{3,2,0,1:T(8,128)} %copy.121) | copy-start | bytes 1198084
  162.0 3.8 %copy-start.21 = (f32[12]{0:T(128)S(1)}, f32[12]{0:T(128)}, u32[]{:S(2)}) copy-start(f32[12]{0:T(128)} %param.17) | copy-start | bytes 148
  167.8 1.7 copy-start.22
Sparse Core Ops, SparseCore 0:
  172.6 26.3 reduce-scatter.1

commit v9 on v6

--- a/solution.py
+++ b/solution.py
@@ -234,14 +234,11 @@
     )
     extra = jnp.pad(extra, ((0, 0), (0, 6), (0, d_model - chunk)))
     sent = jnp.concatenate([partial.reshape(groups, chunk, d_model), extra], axis=1)
-    summed = lax.psum_scatter(
-        sent.reshape(groups * (chunk + 8), d_model), "head", scatter_dimension=0, tiled=True
-    )
-    total_squares = summed[chunk, :chunk].astype(jnp.float32) + summed[
-        chunk + 1, :chunk
-    ].astype(jnp.float32)
+    arrived_parts = lax.all_to_all(sent, "head", split_axis=0, concat_axis=0, tiled=True)
+    summed = jnp.sum(arrived_parts.astype(jnp.float32), axis=0)
+    total_squares = summed[chunk, :chunk] + summed[chunk + 1, :chunk]
     row_scale = lax.rsqrt(total_squares / (ATTENTION_LANES * HEAD_DIM) + norm_eps)
-    return (summed[:chunk].astype(jnp.float32) * row_scale[:, None]).astype(jnp.bfloat16)
+    return (summed[:chunk] * row_scale[:, None]).astype(jnp.bfloat16)
 
 
 def solution(mesh):

time: 193 us -> 177 us (0.917)
  waiting for transfers between devices: 67 us -> 41.5 us
  blocking collectives: 43.7 us -> 68.7 us
  between operations: 15.1 us -> 1.76 us
  other arithmetic: 17.5 us -> 14.7 us
    reduce_scatter x1 -> x0, waiting for transfers between devices: 25.6 us -> none  [body(): lax.psum_scatter(sent.reshape(groups * (chunk + 8), d_model), 'head', sca...]
    all_to_all x0 -> x1, blocking collectives: none -> 25 us  [body(): lax.all_to_all(sent, 'head', split_axis=0, concat_axis=0, tiled=True)]
  transfers between devices with their start and end apart: 2 -> 1, of which waited for: 2 -> 1; matrix products, arithmetic and copies ran while one was open for 3% -> 3% of each run, Pallas kernels for 0% -> 0%
where the time goes in v9:
time: 177 us; the launch traced here: 176 us
  blocking collectives  68.7 us (39%)
  waiting for transfers between devices  41.5 us (23%)
  matrix products  22.3 us (13%)
  other arithmetic  14.7 us (8%)
  local copies, waits for them, and re-layouts  13.8 us (8%)
  starting transfers between devices  13.3 us (8%)
    all_to_all x1, waiting for transfers between devices, send(): lax.all_to_all(packed.reshape(shards, capacity, packed.shape[1]), ROWS, s...  41.5 us
    all_gather x3, blocking collectives, gathered_level(): gathered = lax.all_gather(pack_state(kept, state), axis)  33.6 us
    all_to_all x1, blocking collectives, body(): lax.all_to_all(sent, 'head', split_axis=0, concat_axis=0, tiled=True)  25 us
    all_to_all x1, starting transfers between devices, send(): lax.all_to_all(packed.reshape(shards, capacity, packed.shape[1]), ROWS, s...  13.3 us
    all_gather x1, blocking collectives, exclusive_prefix(): whole = lax.all_gather(start_state, pair, tiled=True)  10.1 us
    dot_general x1, matrix products, send(): jnp.dot(to_slot, values, preferred_element_type=jnp.float32)  3.98 us
    convert_element_type x1, local copies, waits for them, and re-layouts, send(): jnp.dot(to_slot, values, preferred_element_type=jnp.float32)  3.95 us
    concatenate x1, local copies, waits for them, and re-layouts, body(): jnp.concatenate([features_in, gate_in, b_input, c_input, log_decay, place...  3.85 us
  transfers between devices with their start and end apart: 1, of which 1 were waited for; matrix products, arithmetic and copies ran while one was open for 3% of the time, Pallas kernels for 0%

profile of v9, /device:TPU:1, one launch (start us, length us, event | category | flops | bytes accessed | tf_op | source)
XLA Modules:
  0.0 176.0 jit_solution(2774853400894599403)
XLA Ops:
  0.0 1.0 copy.48
  1.0 0.7 fusion.54
  1.7 1.2 reduce-window.24
  2.9 0.2 slice_reduce_fusion
  3.2 0.1 fusion.37
  3.3 0.7 multiply_add_fusion
  4.0 0.1 broadcast_in_dim.231
  4.2 0.1 broadcast_in_dim.232
  4.3 3.8 %concatenate.48 = bf16[512,1806]{1,0:T(8,128)(2,1)} concatenate(bf16[512,768]{1,0:T(8,128)(2,1)} %param.10, bf16[512,768]{1,0:T(8,128)(2,1)} %param.11, bf16[512,128]{1,0:T(8,128)(2,1)} %param.12, bf16[512,128]{1,0:T(8,128)(2,1)} %param.13, bf16[512,12]{1,0:T(8,128)(2,1)S(1)} %copy.48, bf16[512,1]{1,0:T(8,128)(2,1)S(1)} %broadcast_in_dim.231, bf16[512,1]{1,0:T(8,128)(2,1)S(1)} %broadcast_in_dim.232), dimensions={1} | concatenate | bytes 3698688 | tf_op jit(solution)/shard_map/concatenate | solution.py:128
  8.2 4.0 %convolution_convert_fusion.2 = bf16[512,1806]{0,1:T(8,128)(2,1)} fusion(bf16[512,1806]{1,0:T(8,128)(2,1)} %concatenate.48, s32[512]{0:T(512)S(1)} %get-tuple-element.76), kind=kOutput, calls=%fused_computation.7 | convolution fusion | flops 948050944 | bytes 3700736 | tf_op jit(solution)/shard_map/dot_general | solution.py:137
  12.1 4.0 %copy.51 = bf16[512,1806]{1,0:T(8,128)(2,1)} copy(bf16[512,1806]{0,1:T(8,128)(2,1)} %convolution_convert_fusion.2) | data formatting | bytes 3698688 | tf_op jit(solution)/shard_map/convert_element_type | solution.py:137
  16.1 13.3 %all-to-all-start = ((bf16[64,8,1806]{2,1,0:T(8,128)(2,1)}), bf16[64,8,1806]{2,1,0:T(8,128)(2,1)}, u32[]{:S(2)}, u32[]{:S(2)}) async-start(bf16[64,8,1806]{2,1,0:T(8,128)(2,1)} %bitcast.93), calls=%async_computation | async-start | bytes 3932160 | tf_op jit(solution)/shard_map/all_to_all | solution.py:138
  29.4 0.2 reduce-window.31
  29.6 0.6 fusion.58
  30.2 0.1 convert_reduce_fusion.1
  30.3 0.6 slice.88
  32.2 0.6 fusion.63
  32.8 0.6 iota_compare_fusion.13
  33.4 0.6 iota_compare_fusion.12
  34.0 0.5 fusion.57
  34.5 0.6 compare_convert_fusion.1
  35.2 0.9 fusion.13
  36.1 41.5 %all-to-all-done = bf16[64,8,1806]{2,1,0:T(8,128)(2,1)} async-done(((bf16[64,8,1806]{2,1,0:T(8,128)(2,1)}), bf16[64,8,1806]{2,1,0:T(8,128)(2,1)}, u32[]{:S(2)}, u32[]{:S(2)}) %all-to-all-start) | async-done | bytes 1849376 | tf_op jit(solution)/shard_map/all_to_all | solution.py:138
  77.6 1.2 add_reduce_fusion
  78.8 2.8 %convolution_convert_fusion.1 = bf16[512,1806]{0,1:T(8,128)(2,1)S(1)} fusion(s32[512]{0:T(512)S(1)} %add_reduce_fusion, bf16[64,8,1806]{2,1,0:T(8,128)(2,1)} %all-to-all-done), kind=kOutput, calls=%fused_computation.6 | convolution fusion | flops 948050944 | bytes 3700736 | tf_op jit(solution)/shard_map/dot_general | solution.py:156
  81.6 1.6 fusion.40
  83.3 1.2 reduce-window.32
  84.4 0.2 slice_reduce_fusion.1
  84.8 0.2 slice_reduce_fusion.2
  84.9 0.8 copy.54
  85.8 0.1 exponential_multiply_fusion.1
  85.9 2.3 %fusion.12 = bf16[1,12,64,128]{3,2,1,0:T(8,128)(2,1)S(1)} fusion(bf16[512,12,64]{0,2,1:T(8,128)(2,1)S(1)} %bitcast.94, f32[12,512]{1,0:T(8,128)S(1)} %exponential_multiply_fusion.1, f32[512,128]{1,0:T(8,128)} %copy.54, f32[12]{0:T(128)S(1)} %get-tuple-element.78), kind=kOutput, calls=%fused_computation.24 | convolution fusion | flops 102432768 | bytes 1269808 | tf_op jit(solution)/shard_map/while/body/eval_jaxpr/hsn,shp->hpn/dot_general | solution.py:73
  88.3 2.2 %all_gather.15 = bf16[2,12,65,128]{3,2,1,0:T(8,128)(2,1)S(1)} all-gather(bf16[1,12,65,128]{3,2,1,0:T(8,128)(2,1)S(1)} %pad_maximum_fusion.1), channel_id=1, replica_groups=mesh['sx'=4,'sz'=8,'sc'=2,'head'=4] {'sc'}, dimensions={0}, use_global_device_ids=true | all-gather | bytes 599040 | tf_op jit(solution)/shard_map/all_gather | solution.py:38
  90.5 0.4 fusion.48
  90.9 0.1 select_reduce_fusion.5
  91.0 0.1 copy.58
  91.1 0.6 fusion.31
  91.9 20.9 %all_gather.16 = bf16[8,6,65,128]{3,2,1,0:T(8,128)(2,1)S(1)} all-gather(bf16[1,6,65,128]{3,2,1,0:T(8,128)(2,1)S(1)} %pad_maximum_fusion.2), channel_id=1, replica_groups=mesh['sx'=4,'sz'=8,'sc'=2,'head'=4] {'sz'}, dimensions={0}, use_global_device_ids=true | all-gather | bytes 898560 | tf_op jit(solution)/shard_map/all_gather | solution.py:38
  112.8 0.2 slice_reduce_fusion.3
  113.0 0.1 copy.73
  113.1 0.1 select_reduce_fusion.3
  113.2 0.1 select_reduce_fusion.6
  113.4 0.1 copy.69
  113.5 1.6 fusion.29
  115.1 0.8 copy.97
  116.0 0.3 select_reduce_fusion.1
  116.3 0.4 fusion.16
  116.7 0.4 fusion.18
  117.2 10.5 %all_gather.17 = bf16[4,6,65,128]{3,2,1,0:T(8,128)(2,1)S(1)} all-gather(bf16[1,6,65,128]{3,2,1,0:T(8,128)(2,1)S(1)} %pad_maximum_fusion.3), channel_id=1, replica_groups=mesh['sx'=4,'sz'=8,'sc'=2,'head'=4] {'sx'}, dimensions={0}, use_global_device_ids=true | all-gather | bytes 499200 | tf_op jit(solution)/shard_map/all_gather | solution.py:38
  127.7 0.8 copy-done.7
  128.5 0.1 fusion.47
  128.6 0.1 select_reduce_fusion.2
  128.8 0.1 copy.64
  128.9 1.5 fusion.22
  130.4 0.1 slice_add_fusion.2
  130.5 10.1 %all_gather.18 = f32[12,64,128]{2,1,0:T(8,128)S(1)} all-gather(f32[6,64,128]{2,1,0:T(8,128)S(1)} %slice_add_fusion.2), channel_id=1, replica_groups=mesh['sx'=4,'sz'=8,'sc'=2,'head'=4] {'sc'}, dimensions={0}, use_global_device_ids=true | all-gather | bytes 589824 | tf_op jit(solution)/shard_map/all_gather | solution.py:58
  140.7 3.8 %fusion = f32[12,64,512]{2,1,0:T(8,128)S(1)} fusion(bf16[512,12,64]{0,2,1:T(8,128)(2,1)S(1)} %bitcast.95, f32[12,512]{1,0:T(8,128)S(1)} %bitcast.106, f32[512,512]{1,0:T(8,128)S(1)} %copy-done.5, pred[512,512]{1,0:T(8,128)(4,1)S(1)} %copy-done.8), kind=kOutput, calls=%fused_computation.1 | convolution fusion | flops 415236096 | bytes 3694592 | tf_op jit(solution)/shard_map/while/body/eval_jaxpr/hts,shp->thp/dot_general | solution.py:89
  144.5 2.0 %fusion.7 = f32[512,12,64]{0,2,1:T(8,128)S(1)} fusion(f32[12,64,512]{2,1,0:T(8,128)S(1)} %fusion, bf16[512,12,64]{0,2,1:T(8,128)(2,1)S(1)} %bitcast.96, f32[12]{0:T(128)S(1)} %copy-done.14, f32[512,12]{0,1:T(8,128)S(1)} %exponential_multiply_fusion, f32[12,65,128]{2,1,0:T(8,128)S(1)} %bitcast.97, f32[12,64,128]{2,1,0:T(8,128)S(1)} %all_gather.18, ...), kind=kOutput, calls=%fused_computation.17 | convolution fusion | flops 606142464 | bytes 4883456 | tf_op jit(solution)/shard_map/while/body/eval_jaxpr/tn,hpn->thp/dot_general | solution.py:94
  146.5 1.7 multiply_reduce_fusion
  148.3 1.5 convolution_convert_fusion
  149.8 0.1 pad_maximum_fusion
  149.9 25.0 %all_to_all.10 = bf16[4,136,1536]{2,1,0:T(8,128)(2,1)S(1)} all-to-all(bf16[4,136,1536]{2,1,0:T(8,128)(2,1)S(1)} %pad_maximum_fusion), channel_id=1, replica_groups=mesh['sx'=4,'sz'=8,'sc'=2,'head'=4] {'head'}, dimensions={0} | all-to-all | bytes 3342336 | tf_op jit(solution)/shard_map/all_to_all | solution.py:237
  174.9 0.2 convert_reduce_fusion
  175.2 0.9 fusion.14
  (76 shorter events, 1.2 us)
Async XLA Ops:
  0.0 148.2 %copy-start = (bf16[768,1536]{1,0:T(8,128)(2,1)S(1)}, bf16[768,1536]{1,0:T(8,128)(2,1)}, u32[]{:S(2)}) copy-start(bf16[768,1536]{1,0:T(8,128)(2,1)} %param.19) | copy-start | bytes 7077892
  16.1 13.3 %copy-start.9 = (s32[4]{0:T(128)S(1)}, s32[4]{0:T(128)}, u32[]{:S(2)}) copy-start(s32[4]{0:T(128)} %param.16) | copy-start | bytes 52
  16.1 61.4 %all-to-all-start = ((bf16[64,8,1806]{2,1,0:T(8,128)(2,1)}), bf16[64,8,1806]{2,1,0:T(8,128)(2,1)}, u32[]{:S(2)}, u32[]{:S(2)}) async-start(bf16[64,8,1806]{2,1,0:T(8,128)(2,1)} %bitcast.93), calls=%async_computation | async-start | bytes 3932160 | tf_op jit(solution)/shard_map/all_to_all | solution.py:138
  81.5 1.7 copy-start.3
  81.6 6.6 %copy-start.1 = (bf16[512,768]{0,1:T(8,128)(2,1)}, bf16[512,768]{0,1:T(8,128)(2,1)S(1)}, u32[]{:S(2)}) copy-start(bf16[512,768]{0,1:T(8,128)(2,1)S(1)} %slice.104) | copy-start | bytes 2359300
  90.5 1.4 copy-start.6
  91.1 22.3 %copy-start.12 = (f32[2]{0:T(128)S(1)}, f32[2]{0:T(128)}, u32[]{:S(2)}) copy-start(f32[2]{0:T(128)} %fusion.63) | copy-start | bytes 28
  91.9 24.4 %copy-start.13 = (f32[8]{0:T(128)S(1)}, f32[8]{0:T(128)}, u32[]{:S(2)}) copy-start(f32[8]{0:T(128)} %get-tuple-element.94) | copy-start | bytes 100
  116.3 12.4 %copy-start.11 = (pred[4,4]{1,0:T(4,128)(4,1)S(1)}, pred[4,4]{1,0:T(4,128)(4,1)}, u32[]{:S(2)}) copy-start(pred[4,4]{1,0:T(4,128)(4,1)} %fusion.57) | copy-start | bytes 52
  116.3 12.4 %copy-start.10 = (f32[4]{0:T(128)S(1)}, f32[4]{0:T(128)}, u32[]{:S(2)}) copy-start(f32[4]{0:T(128)} %get-tuple-element.97) | copy-start | bytes 52
  117.1 23.6 %copy-start.2 = (bf16[512,768]{0,1:T(8,128)(2,1)S(1)}, bf16[512,768]{0,1:T(8,128)(2,1)}, u32[]{:S(2)}) copy-start(bf16[512,768]{0,1:T(8,128)(2,1)} %copy-done.1) | copy-start | bytes 2359300
  127.7 0.8 copy-start.7
  128.9 11.7 %copy-start.5 = (f32[512,512]{1,0:T(8,128)S(1)}, f32[512,512]{1,0:T(8,128)}, u32[]{:S(2)}) copy-start(f32[512,512]{1,0:T(8,128)} %fusion.40) | copy-start | bytes 3145732
  128.9 11.7 %copy-start.8 = (pred[512,512]{1,0:T(8,128)(4,1)S(1)}, pred[512,512]{1,0:T(8,128)(4,1)}, u32[]{:S(2)}) copy-start(pred[512,512]{1,0:T(8,128)(4,1)} %fusion.13) | copy-start | bytes 786436
  140.7 3.8 %copy-start.4 = (f32[12,1,65,128]{3,2,0,1:T(8,128)S(1)}, f32[12,1,65,128]{3,2,0,1:T(8,128)}, u32[]{:S(2)}) copy-start(f32[12,1,65,128]{3,2,0,1:T(8,128)} %copy.97) | copy-start | bytes 1198084
  140.7 3.8 %copy-start.14 = (f32[12]{0:T(128)S(1)}, f32[12]{0:T(128)}, u32[]{:S(2)}) copy-start(f32[12]{0:T(128)} %param.17) | copy-start | bytes 148
  146.5 1.7 copy-start.15

commit v10 on v9

--- a/solution.py
+++ b/solution.py
@@ -129,12 +129,12 @@
         [features_in, gate_in, b_input, c_input, log_decay, place_hi[:, None], place_lo[:, None]],
         axis=1,
     )
-    to_slot = (
-        lax.broadcasted_iota(jnp.int32, (tok_dev, tok_dev), 0) == slot_index[None, :]
-    ).astype(jnp.bfloat16)
+    from_slot = (
+        jnp.zeros((tok_dev,), jnp.int32).at[slot_index].set(lax.iota(jnp.int32, tok_dev))
+    )
 
     def send(values):
-        packed = jnp.dot(to_slot, values, preferred_element_type=jnp.float32).astype(jnp.bfloat16)
+        packed = jnp.take(values, from_slot, axis=0, mode="clip")
         return lax.all_to_all(
             packed.reshape(shards, capacity, packed.shape[1]),
             ROWS,
@@ -148,12 +148,10 @@
     arrived = (
         moved[:, columns - 2].astype(jnp.int32) * 32 + moved[:, columns - 1].astype(jnp.int32)
     )
-    to_place = (
-        lax.broadcasted_iota(jnp.int32, (tok_dev, tok_dev), 0) == arrived[None, :]
-    ).astype(jnp.bfloat16)
+    from_place = jnp.zeros((tok_dev,), jnp.int32).at[arrived].set(lax.iota(jnp.int32, tok_dev))
 
     def place(values):
-        return jnp.dot(to_place, values, preferred_element_type=jnp.float32).astype(jnp.bfloat16)
+        return jnp.take(values, from_place, axis=0, mode="clip")
 
     rows = place(moved)
     features = rows[:, :feats]

time: 177 us -> 193 us (1.090)
  local copies, waits for them, and re-layouts: 13.8 us -> 31.9 us
  matrix products: 22.3 us -> 17.8 us
  waiting for transfers between devices: 41.5 us -> 43.7 us
    gather x0 -> x2, local copies, waits for them, and re-layouts: none -> 13.8 us  [the longest x1 6.88 us: place(): return jnp.take(values, from_place, axis=0, mode='clip')]
    dot_general x2 -> x0, matrix products: 6.73 us -> none  [the longest x1 3.98 us: send(): jnp.dot(to_slot, values, preferred_element_type=jnp.float32)]
    scatter x0 -> x2, local copies, waits for them, and re-layouts: none -> 4.87 us  [the longest x1 2.44 us: body(): jnp.zeros((tok_dev,), jnp.int32).at[slot_index]]
    convert_element_type x2 -> x0, local copies, waits for them, and re-layouts: 4.78 us -> none  [the longest x1 3.95 us: send(): jnp.dot(to_slot, values, preferred_element_type=jnp.float32)]
    reshape x0 -> x1, local copies, waits for them, and re-layouts: none -> 3.01 us  [body(): mixed = mixed.reshape(tok_dev, heads_here * width)]
    all_to_all x1, waiting for transfers between devices: 41.5 us -> 43.7 us  [send(): lax.all_to_all(packed.reshape(shards, capacity, packed.shape[1]), ROWS, s...]
    select_n x0 -> x2, other arithmetic: none -> 1.94 us  [the longest x1 1.24 us: body(): jnp.zeros((tok_dev,), jnp.int32).at[arrived]]
  transfers between devices with their start and end apart: 1 -> 1, of which waited for: 1 -> 1; matrix products, arithmetic and copies ran while one was open for 3% -> 2% of each run, Pallas kernels for 0% -> 0%
where the time goes in v10:
time: 193 us; the launch traced here: 192 us
  blocking collectives  68.7 us (36%)
  waiting for transfers between devices  43.7 us (23%)
  local copies, waits for them, and re-layouts  31.9 us (17%)
  matrix products  17.8 us (9%)
  other arithmetic  14.9 us (8%)
  starting transfers between devices  13.3 us (7%)
    all_to_all x1, waiting for transfers between devices, send(): lax.all_to_all(packed.reshape(shards, capacity, packed.shape[1]), ROWS, s...  43.7 us
    all_gather x3, blocking collectives, gathered_level(): gathered = lax.all_gather(pack_state(kept, state), axis)  33.8 us
    all_to_all x1, blocking collectives, body(): lax.all_to_all(sent, 'head', split_axis=0, concat_axis=0, tiled=True)  25 us
    all_to_all x1, starting transfers between devices, send(): lax.all_to_all(packed.reshape(shards, capacity, packed.shape[1]), ROWS, s...  13.3 us
    all_gather x1, blocking collectives, exclusive_prefix(): whole = lax.all_gather(start_state, pair, tiled=True)  9.93 us
    gather x1, local copies, waits for them, and re-layouts, place(): return jnp.take(values, from_place, axis=0, mode='clip')  6.88 us
    gather x1, local copies, waits for them, and re-layouts, send(): packed = jnp.take(values, from_slot, axis=0, mode='clip')  6.88 us
    concatenate x1, local copies, waits for them, and re-layouts, body(): jnp.concatenate([features_in, gate_in, b_input, c_input, log_decay, place...  3.9 us
  transfers between devices with their start and end apart: 1, of which 1 were waited for; matrix products, arithmetic and copies ran while one was open for 2% of the time, Pallas kernels for 0%

profile of v10, /device:TPU:1, one launch (start us, length us, event | category | flops | bytes accessed | tf_op | source)
XLA Modules:
  0.0 192.0 jit_solution(8873253752948776447)
XLA Ops:
  0.0 1.0 copy.44
  1.0 0.7 fusion.53
  1.7 1.2 reduce-window.24
  2.9 0.2 slice_reduce_fusion
  3.2 0.1 fusion.36
  3.3 0.7 compare_select_fusion.1
  4.0 0.1 broadcast_in_dim.243
  4.2 0.1 broadcast_in_dim.244
  4.3 2.4 %scatter_custom_fusion = s32[512]{0:T(512)S(1)} fusion(s32[512]{0:T(512)S(1)} %get-tuple-element.74, s32[512]{0:T(512)S(1)} %iota.131, s32[]{:T(128)} %constant.119.clone.1), kind=kCustom, calls=%fused_computation.140 | custom fusion | bytes 2052 | tf_op jit(solution)/shard_map/scatter | solution.py:133
  6.8 3.9 %concatenate.48 = bf16[512,1806]{1,0:T(8,128)(2,1)} concatenate(bf16[512,768]{1,0:T(8,128)(2,1)} %param.10, bf16[512,768]{1,0:T(8,128)(2,1)} %param.11, bf16[512,128]{1,0:T(8,128)(2,1)} %param.12, bf16[512,128]{1,0:T(8,128)(2,1)} %param.13, bf16[512,12]{1,0:T(8,128)(2,1)S(1)} %copy.44, bf16[512,1]{1,0:T(8,128)(2,1)S(1)} %broadcast_in_dim.243, bf16[512,1]{1,0:T(8,128)(2,1)S(1)} %broadcast_in_dim.244), dimensions={1} | concatenate | bytes 3698688 | tf_op jit(solution)/shard_map/concatenate | solution.py:128
  10.7 6.9 %gather_fusion = bf16[512,1806]{1,0:T(8,128)(2,1)} fusion(bf16[512,1806]{1,0:T(8,128)(2,1)} %concatenate.48, s32[1024]{0:T(1024)S(1)} %pad_clamp_fusion.1), kind=kCustom, calls=%fused_computation | custom fusion | bytes 3700736 | tf_op jit(solution)/shard_map/jit(_take)/gather | solution.py:137
  17.6 13.3 %all-to-all-start = ((bf16[64,8,1806]{2,1,0:T(8,128)(2,1)}), bf16[64,8,1806]{2,1,0:T(8,128)(2,1)}, u32[]{:S(2)}, u32[]{:S(2)}) async-start(bf16[64,8,1806]{2,1,0:T(8,128)(2,1)} %bitcast.89), calls=%async_computation | async-start | bytes 3932160 | tf_op jit(solution)/shard_map/all_to_all | solution.py:138
  30.9 0.2 reduce-window.31
  31.1 0.6 fusion.61
  31.7 0.1 convert_reduce_fusion.1
  31.8 0.6 slice.88
  33.8 0.6 compare_convert_fusion.1
  34.4 0.9 fusion.13
  35.3 43.7 %all-to-all-done = bf16[64,8,1806]{2,1,0:T(8,128)(2,1)} async-done(((bf16[64,8,1806]{2,1,0:T(8,128)(2,1)}), bf16[64,8,1806]{2,1,0:T(8,128)(2,1)}, u32[]{:S(2)}, u32[]{:S(2)}) %all-to-all-start) | async-done | bytes 1849376 | tf_op jit(solution)/shard_map/all_to_all | solution.py:138
  79.0 1.2 fusion.23
  80.3 2.4 %scatter_custom_fusion.1 = s32[512]{0:T(512)S(1)} fusion(s32[512]{0:T(512)S(1)} %fusion.23, s32[512]{0:T(512)S(1)} %iota.132, s32[]{:T(128)} %constant.119.clone.1), kind=kCustom, calls=%fused_computation.143 | custom fusion | bytes 2052 | tf_op jit(solution)/shard_map/scatter | solution.py:151
  82.7 6.9 %gather_fusion.1 = bf16[512,1806]{1,0:T(8,128)(2,1)} fusion(bf16[512,1806]{1,0:T(8,128)(2,1)} %bitcast.3, s32[1024]{0:T(1024)S(1)} %pad_clamp_fusion), kind=kCustom, calls=%fused_computation.1 | custom fusion | bytes 3700736 | tf_op jit(solution)/shard_map/jit(_take)/gather | solution.py:154
  89.6 1.1 slice_convert_fusion.1
  90.7 2.2 %fusion.39 = f32[512,512]{1,0:T(8,128)} fusion(bf16[512,1806]{1,0:T(8,128)(2,1)} %gather_fusion.1), kind=kOutput, calls=%fused_computation.76 | convolution fusion | flops 67108864 | bytes 1310720 | tf_op jit(solution)/shard_map/while/body/eval_jaxpr/tn,sn->ts/dot_general | solution.py:87
  92.9 0.7 slice_convert_fusion.2
  93.6 1.2 copy.48
  94.8 0.1 copy.49
  94.9 1.1 reduce-window.32
  96.1 0.2 slice_reduce_fusion.1
  96.4 0.2 slice_reduce_fusion.2
  96.7 2.3 %fusion.12 = bf16[1,12,64,128]{3,2,1,0:T(8,128)(2,1)S(1)} fusion(bf16[512,12,64]{0,2,1:T(8,128)(2,1)} %bitcast.91, f32[12,512]{1,0:T(8,128)S(1)} %exponential_multiply_fusion.1, f32[512,128]{1,0:T(8,128)} %slice_convert_fusion.2, f32[12]{0:T(128)S(1)} %get-tuple-element.76), kind=kOutput, calls=%fused_computation.26 | convolution fusion | flops 102432768 | bytes 1269808 | tf_op jit(solution)/shard_map/while/body/eval_jaxpr/hsn,shp->hpn/dot_general | solution.py:73
  99.1 2.2 %all_gather.15 = bf16[2,12,65,128]{3,2,1,0:T(8,128)(2,1)S(1)} all-gather(bf16[1,12,65,128]{3,2,1,0:T(8,128)(2,1)S(1)} %pad_maximum_fusion.1), channel_id=1, replica_groups=mesh['sx'=4,'sz'=8,'sc'=2,'head'=4] {'sc'}, dimensions={0}, use_global_device_ids=true | all-gather | bytes 599040 | tf_op jit(solution)/shard_map/all_gather | solution.py:38
  101.3 0.4 fusion.47
  101.7 0.1 select_reduce_fusion.5
  101.8 0.1 copy.54
  101.9 0.6 fusion.30
  102.7 21.2 %all_gather.16 = bf16[8,6,65,128]{3,2,1,0:T(8,128)(2,1)S(1)} all-gather(bf16[1,6,65,128]{3,2,1,0:T(8,128)(2,1)S(1)} %pad_maximum_fusion.2), channel_id=1, replica_groups=mesh['sx'=4,'sz'=8,'sc'=2,'head'=4] {'sz'}, dimensions={0}, use_global_device_ids=true | all-gather | bytes 898560 | tf_op jit(solution)/shard_map/all_gather | solution.py:38
  123.9 0.2 slice_reduce_fusion.3
  124.1 0.1 copy.67
  124.2 0.1 select_reduce_fusion.3
  124.3 0.1 select_reduce_fusion.6
  124.5 0.1 copy.65
  124.6 1.6 fusion.28
  126.2 0.8 copy.91
  127.1 0.3 select_reduce_fusion.1
  127.4 0.4 fusion.16
  127.8 0.4 fusion.18
  128.3 10.4 %all_gather.17 = bf16[4,6,65,128]{3,2,1,0:T(8,128)(2,1)S(1)} all-gather(bf16[1,6,65,128]{3,2,1,0:T(8,128)(2,1)S(1)} %pad_maximum_fusion.3), channel_id=1, replica_groups=mesh['sx'=4,'sz'=8,'sc'=2,'head'=4] {'sx'}, dimensions={0}, use_global_device_ids=true | all-gather | bytes 499200 | tf_op jit(solution)/shard_map/all_gather | solution.py:38
  138.7 0.8 copy-done.8
  139.4 0.1 fusion.46
  139.6 0.1 select_reduce_fusion.2
  139.7 0.1 copy.60
  139.9 1.5 fusion.20
  141.4 0.1 slice_add_fusion.2
  141.5 9.9 %all_gather.18 = f32[12,64,128]{2,1,0:T(8,128)S(1)} all-gather(f32[6,64,128]{2,1,0:T(8,128)S(1)} %slice_add_fusion.2), channel_id=1, replica_groups=mesh['sx'=4,'sz'=8,'sc'=2,'head'=4] {'sc'}, dimensions={0}, use_global_device_ids=true | all-gather | bytes 589824 | tf_op jit(solution)/shard_map/all_gather | solution.py:58
  151.4 3.8 %fusion = f32[12,64,512]{2,1,0:T(8,128)S(1)} fusion(bf16[512,12,64]{0,2,1:T(8,128)(2,1)S(1)} %bitcast.92, f32[12,512]{1,0:T(8,128)S(1)} %bitcast.104, f32[512,512]{1,0:T(8,128)S(1)} %copy-done.6, pred[512,512]{1,0:T(8,128)(4,1)S(1)} %copy-done.9), kind=kOutput, calls=%fused_computation.5 | convolution fusion | flops 415236096 | bytes 3694592 | tf_op jit(solution)/shard_map/while/body/eval_jaxpr/hts,shp->thp/dot_general | solution.py:89
  155.3 2.2 %fusion.7 = f32[512,12,64]{0,2,1:T(8,128)} fusion(f32[12,64,512]{2,1,0:T(8,128)S(1)} %fusion, bf16[512,12,64]{0,2,1:T(8,128)(2,1)S(1)} %bitcast.93, f32[12]{0:T(128)S(1)} %copy-done.11, f32[512,12]{0,1:T(8,128)S(1)} %exponential_multiply_fusion, f32[12,65,128]{2,1,0:T(8,128)S(1)} %bitcast.94, f32[12,64,128]{2,1,0:T(8,128)S(1)} %all_gather.18, ...), kind=kOutput, calls=%fused_computation.19 | convolution fusion | flops 606142464 | bytes 4883456 | tf_op jit(solution)/shard_map/while/body/eval_jaxpr/tn,hpn->thp/dot_general | solution.py:94
  157.5 3.0 %copy.53 = f32[512,768]{1,0:T(8,128)} copy(f32[512,768]{0,1:T(8,128)} %bitcast.90) | data formatting | bytes 3145728 | tf_op jit(solution)/shard_map/reshape | solution.py:220
  160.5 2.3 %multiply_reduce_fusion = f32[512]{0:T(512)S(1)} fusion(f32[512,768]{1,0:T(8,128)} %copy.53, bf16[512,1806]{1,0:T(8,128)(2,1)} %gather_fusion.1), kind=kLoop, calls=%fused_computation.20 | loop fusion | flops 3145216 | bytes 2361344 | tf_op jit(solution)/shard_map/reduce_sum | solution.py:222
  162.9 2.9 %convolution_convert_fusion = bf16[512,1536]{1,0:T(8,128)(2,1)S(1)} fusion(bf16[768,1536]{1,0:T(8,128)(2,1)S(1)} %copy-done, f32[768]{0:T(1024)S(1)} %copy-done.12, f32[512,768]{1,0:T(8,128)} %copy.53, bf16[512,1806]{1,0:T(8,128)(2,1)S(1)} %copy-done.3), kind=kOutput, calls=%fused_computation.9 | convolution fusion | flops 1211891712 | bytes 6295552 | tf_op jit(solution)/shard_map/dot_general | solution.py:226
  165.8 0.1 pad_maximum_fusion
  166.0 25.0 %all_to_all.10 = bf16[4,136,1536]{2,1,0:T(8,128)(2,1)S(1)} all-to-all(bf16[4,136,1536]{2,1,0:T(8,128)(2,1)S(1)} %pad_maximum_fusion), channel_id=1, replica_groups=mesh['sx'=4,'sz'=8,'sc'=2,'head'=4] {'head'}, dimensions={0} | all-to-all | bytes 3342336 | tf_op jit(solution)/shard_map/all_to_all | solution.py:235
  190.9 0.2 convert_reduce_fusion
  191.2 0.9 fusion.14
  (76 shorter events, 1.2 us)
Async XLA Ops:
  0.0 162.9 %copy-start = (bf16[768,1536]{1,0:T(8,128)(2,1)S(1)}, bf16[768,1536]{1,0:T(8,128)(2,1)}, u32[]{:S(2)}) copy-start(bf16[768,1536]{1,0:T(8,128)(2,1)} %param.19) | copy-start | bytes 7077892
  17.6 13.3 %copy-start.10 = (s32[4]{0:T(128)S(1)}, s32[4]{0:T(128)}, u32[]{:S(2)}) copy-start(s32[4]{0:T(128)} %param.16) | copy-start | bytes 52
  17.6 61.4 %all-to-all-start = ((bf16[64,8,1806]{2,1,0:T(8,128)(2,1)}), bf16[64,8,1806]{2,1,0:T(8,128)(2,1)}, u32[]{:S(2)}, u32[]{:S(2)}) async-start(bf16[64,8,1806]{2,1,0:T(8,128)(2,1)} %bitcast.89), calls=%async_computation | async-start | bytes 3932160 | tf_op jit(solution)/shard_map/all_to_all | solution.py:138
  89.6 3.3 %copy-start.1 = (bf16[512,1806]{1,0:T(8,128)(2,1)S(1)}, bf16[512,1806]{1,0:T(8,128)(2,1)}, u32[]{:S(2)}) copy-start(bf16[512,1806]{1,0:T(8,128)(2,1)} %gather_fusion.1) | copy-start | bytes 5548036
  89.6 4.0 %slice-start = ((bf16[512,1806]{1,0:T(8,128)(2,1)}), bf16[512,768]{1,0:T(8,128)(2,1)S(1)}, s32[]{:S(2)}) async-start(bf16[512,1806]{1,0:T(8,128)(2,1)} %gather_fusion.1), calls=%async_computation.2 | async-start | bytes 1572864 | tf_op jit(solution)/shard_map/slice | solution.py:157
  101.3 1.4 copy-start.7
  128.1 23.3 %copy-start.4 = (bf16[512,768]{0,1:T(8,128)(2,1)S(1)}, bf16[512,768]{0,1:T(8,128)(2,1)}, u32[]{:S(2)}) copy-start(bf16[512,768]{0,1:T(8,128)(2,1)} %copy.48) | copy-start | bytes 2359300
  138.7 0.8 copy-start.8
  139.9 11.5 %copy-start.6 = (f32[512,512]{1,0:T(8,128)S(1)}, f32[512,512]{1,0:T(8,128)}, u32[]{:S(2)}) copy-start(f32[512,512]{1,0:T(8,128)} %fusion.39) | copy-start | bytes 3145732
  139.9 11.5 %copy-start.9 = (pred[512,512]{1,0:T(8,128)(4,1)S(1)}, pred[512,512]{1,0:T(8,128)(4,1)}, u32[]{:S(2)}) copy-start(pred[512,512]{1,0:T(8,128)(4,1)} %fusion.13) | copy-start | bytes 786436
  151.4 3.8 %copy-start.2 = (bf16[512,1806]{1,0:T(8,128)(2,1)S(1)}, bf16[512,1806]{1,0:T(8,128)(2,1)}, u32[]{:S(2)}) copy-start(bf16[512,1806]{1,0:T(8,128)(2,1)} %gather_fusion.1) | copy-start | bytes 5548036
  151.4 3.8 %copy-start.5 = (f32[12,1,65,128]{3,2,0,1:T(8,128)S(1)}, f32[12,1,65,128]{3,2,0,1:T(8,128)}, u32[]{:S(2)}) copy-start(f32[12,1,65,128]{3,2,0,1:T(8,128)} %copy.91) | copy-start | bytes 1198084
  151.4 3.8 %copy-start.11 = (f32[12]{0:T(128)S(1)}, f32[12]{0:T(128)}, u32[]{:S(2)}) copy-start(f32[12]{0:T(128)} %param.17) | copy-start | bytes 148
  160.5 2.4 %copy-start.3 = (bf16[512,1806]{1,0:T(8,128)(2,1)S(1)}, bf16[512,1806]{1,0:T(8,128)(2,1)}, u32[]{:S(2)}) copy-start(bf16[512,1806]{1,0:T(8,128)(2,1)} %gather_fusion.1) | copy-start | bytes 5548036
  160.5 2.4 %copy-start.12 = (f32[768]{0:T(1024)S(1)}, f32[768]{0:T(1024)}, u32[]{:S(2)}) copy-start(f32[768]{0:T(1024)} %param.18) | copy-start | bytes 9220

commit v11 on v8

--- a/solution.py
+++ b/solution.py
@@ -4,8 +4,8 @@
 from jax.sharding import PartitionSpec as P
 
 ATTENTION_LANES = 48
-ROWS = ("xh", "xl", "zh", "zm", "zl", "sc")
-LEVELS = ("zl", "zm", "zh", "xl", "xh")
+ROWS = ("sx", "zh", "zl", "sc")
+LEVELS = ("zl", "zh", "sx")
 HEAD_DIM = 64
 BLOCK = 512
 
@@ -52,7 +52,7 @@
     part_total = lax.dynamic_slice_in_dim(pair_total, mine, half, 0)
     part_kept = lax.dynamic_slice_in_dim(pair_kept, mine, half, 0)
     found = []
-    for level, axis in enumerate(levels):
+    for axis in levels:
         before, kept_before, part_total, part_kept = gathered_level(part_kept, part_total, axis)
         found.append((before, kept_before))
     start_state = found[-1][0]
@@ -237,19 +237,16 @@
     )
     extra = jnp.pad(extra, ((0, 0), (0, 6), (0, d_model - chunk)))
     sent = jnp.concatenate([partial.reshape(groups, chunk, d_model), extra], axis=1)
-    summed = lax.psum_scatter(
-        sent.reshape(groups * (chunk + 8), d_model), "head", scatter_dimension=0, tiled=True
-    )
-    total_squares = summed[chunk, :chunk].astype(jnp.float32) + summed[
-        chunk + 1, :chunk
-    ].astype(jnp.float32)
+    arrived_parts = lax.all_to_all(sent, "head", split_axis=0, concat_axis=0, tiled=True)
+    summed = jnp.sum(arrived_parts.astype(jnp.float32), axis=0)
+    total_squares = summed[chunk, :chunk] + summed[chunk + 1, :chunk]
     row_scale = lax.rsqrt(total_squares / (ATTENTION_LANES * HEAD_DIM) + norm_eps)
-    return (summed[:chunk].astype(jnp.float32) * row_scale[:, None]).astype(jnp.bfloat16)
+    return (summed[:chunk] * row_scale[:, None]).astype(jnp.bfloat16)
 
 
 def solution(mesh):
     seq = mesh.shape["seq"]
-    devices = mesh.devices.reshape(seq // 32, 2, 2, 2, 2, 2, mesh.shape["head"])
+    devices = mesh.devices.reshape(seq // 16, 4, 2, 2, mesh.shape["head"])
     split_mesh = jax.sharding.Mesh(devices, ROWS + ("head",))
     in_specs = (
         P(ROWS, "head"),

time: 209 us -> 181 us (0.87)
  waiting for transfers between devices: 68.4 us -> 43.2 us
  blocking collectives: 41.5 us -> 64.8 us
  between operations: 15.4 us -> 1.78 us
  other arithmetic: 19.3 us -> 14 us
  matrix products: 30.8 us -> 25.9 us
  local copies, waits for them, and re-layouts: 19.7 us -> 16.7 us
    reduce_scatter x1 -> x0, waiting for transfers between devices: 26.5 us -> none  [body(): lax.psum_scatter(sent.reshape(groups * (chunk + 8), d_model), 'head', sca...]
    all_to_all x0 -> x1, blocking collectives: none -> 25 us  [body(): lax.all_to_all(sent, 'head', split_axis=0, concat_axis=0, tiled=True)]
    all_gather x6 -> x4, blocking collectives: 36.1 us -> 30.9 us  [gathered_level(): gathered = lax.all_gather(pack_state(kept, state), axis)]
    all_gather x1, blocking collectives: 5.43 us -> 8.86 us  [exclusive_prefix(): whole = lax.all_gather(start_state, pair, tiled=True)]
    dot_general x5 -> x3, matrix products: 5.8 us -> 3.29 us  [gathered_level(): jnp.einsum('jh,jhpn->hpn', into_end, gathered.astype(jnp.float32))[:, :rows]]
    dot_general x6 -> x4, matrix products: 7.18 us -> 4.77 us  [gathered_level(): jnp.einsum('jh,jhpn->hpn', into_here, gathered.astype(jnp.float32))]
    unnamed x49 -> x29, local copies, waits for them, and re-layouts: 4.66 us -> 3.7 us
  transfers between devices with their start and end apart: 2 -> 1, of which waited for: 2 -> 1; matrix products, arithmetic and copies ran while one was open for 2% -> 2% of each run, Pallas kernels for 0% -> 0%
where the time goes in v11:
time: 181 us; the launch traced here: 180 us
  blocking collectives  64.8 us (36%)
  waiting for transfers between devices  43.2 us (24%)
  matrix products  25.9 us (14%)
  local copies, waits for them, and re-layouts  16.7 us (9%)
  other arithmetic  14 us (8%)
  starting transfers between devices  13.3 us (7%)
    all_to_all x1, waiting for transfers between devices, send(): lax.all_to_all(packed.reshape(shards, capacity, packed.shape[1]), ROWS, s...  43.2 us
    all_gather x4, blocking collectives, gathered_level(): gathered = lax.all_gather(pack_state(kept, state), axis)  30.9 us
    all_to_all x1, blocking collectives, body(): lax.all_to_all(sent, 'head', split_axis=0, concat_axis=0, tiled=True)  25 us
    all_to_all x1, starting transfers between devices, send(): lax.all_to_all(packed.reshape(shards, capacity, packed.shape[1]), ROWS, s...  13.3 us
    all_gather x1, blocking collectives, exclusive_prefix(): whole = lax.all_gather(start_state, pair, tiled=True)  8.86 us
    dot_general x4, matrix products, gathered_level(): jnp.einsum('jh,jhpn->hpn', into_here, gathered.astype(jnp.float32))  4.77 us
    dot_general x1, matrix products, send(): jnp.dot(to_slot, values, preferred_element_type=jnp.float32)  3.98 us
    convert_element_type x1, local copies, waits for them, and re-layouts, send(): jnp.dot(to_slot, values, preferred_element_type=jnp.float32)  3.95 us
  transfers between devices with their start and end apart: 1, of which 1 were waited for; matrix products, arithmetic and copies ran while one was open for 2% of the time, Pallas kernels for 0%

profile of v11, /device:TPU:1, one launch (start us, length us, event | category | flops | bytes accessed | tf_op | source)
XLA Modules:
  0.0 179.7 jit_solution(6281079808307696363)
XLA Ops:
  0.0 1.0 copy.47
  1.0 0.7 fusion.58
  1.7 1.2 reduce-window.24
  2.9 0.2 slice_reduce_fusion
  3.2 0.1 fusion.38
  3.3 0.7 multiply_add_fusion
  4.0 0.1 broadcast_in_dim.280
  4.2 0.1 broadcast_in_dim.281
  4.3 3.8 %concatenate.61 = bf16[512,1806]{1,0:T(8,128)(2,1)} concatenate(bf16[512,768]{1,0:T(8,128)(2,1)} %param.10, bf16[512,768]{1,0:T(8,128)(2,1)} %param.11, bf16[512,128]{1,0:T(8,128)(2,1)} %param.12, bf16[512,128]{1,0:T(8,128)(2,1)} %param.13, bf16[512,12]{1,0:T(8,128)(2,1)S(1)} %copy.47, bf16[512,1]{1,0:T(8,128)(2,1)S(1)} %broadcast_in_dim.280, bf16[512,1]{1,0:T(8,128)(2,1)S(1)} %broadcast_in_dim.281), dimensions={1} | concatenate | bytes 3698688 | tf_op jit(solution)/shard_map/concatenate | solution.py:131
  8.2 4.0 %convolution_convert_fusion.2 = bf16[512,1806]{0,1:T(8,128)(2,1)} fusion(bf16[512,1806]{1,0:T(8,128)(2,1)} %concatenate.61, s32[512]{0:T(512)S(1)} %get-tuple-element.76), kind=kOutput, calls=%fused_computation.7 | convolution fusion | flops 948050944 | bytes 3700736 | tf_op jit(solution)/shard_map/dot_general | solution.py:140
  12.1 4.0 %copy.50 = bf16[512,1806]{1,0:T(8,128)(2,1)} copy(bf16[512,1806]{0,1:T(8,128)(2,1)} %convolution_convert_fusion.2) | data formatting | bytes 3698688 | tf_op jit(solution)/shard_map/convert_element_type | solution.py:140
  16.1 13.3 %all-to-all-start = ((bf16[64,8,1806]{2,1,0:T(8,128)(2,1)}), bf16[64,8,1806]{2,1,0:T(8,128)(2,1)}, u32[]{:S(2)}, u32[]{:S(2)}) async-start(bf16[64,8,1806]{2,1,0:T(8,128)(2,1)} %bitcast.103), calls=%async_computation | async-start | bytes 3932160 | tf_op jit(solution)/shard_map/all_to_all | solution.py:141
  29.4 0.2 reduce-window.31
  29.6 0.6 fusion.61
  30.3 0.6 slice.98
  32.3 0.5 copy-done.9
  32.8 0.6 compare_convert_fusion.1
  33.4 0.9 fusion.13
  34.3 43.2 %all-to-all-done = bf16[64,8,1806]{2,1,0:T(8,128)(2,1)} async-done(((bf16[64,8,1806]{2,1,0:T(8,128)(2,1)}), bf16[64,8,1806]{2,1,0:T(8,128)(2,1)}, u32[]{:S(2)}, u32[]{:S(2)}) %all-to-all-start) | async-done | bytes 1849376 | tf_op jit(solution)/shard_map/all_to_all | solution.py:141
  77.6 1.2 add_reduce_fusion
  78.8 2.8 %convolution_convert_fusion.1 = bf16[512,1806]{0,1:T(8,128)(2,1)S(1)} fusion(s32[512]{0:T(512)S(1)} %add_reduce_fusion, bf16[64,8,1806]{2,1,0:T(8,128)(2,1)} %all-to-all-done), kind=kOutput, calls=%fused_computation.6 | convolution fusion | flops 948050944 | bytes 3700736 | tf_op jit(solution)/shard_map/dot_general | solution.py:159
  81.6 1.5 fusion.41
  83.2 1.2 reduce-window.32
  84.3 0.2 slice_reduce_fusion.1
  84.7 0.2 slice_reduce_fusion.2
  84.8 0.9 copy.53
  85.8 2.3 %fusion.12 = bf16[1,12,64,128]{3,2,1,0:T(8,128)(2,1)S(1)} fusion(bf16[512,12,64]{0,2,1:T(8,128)(2,1)S(1)} %bitcast.104, f32[12,512]{1,0:T(8,128)S(1)} %exponential_multiply_fusion.1, f32[512,128]{1,0:T(8,128)} %copy.53, f32[12]{0:T(128)S(1)} %get-tuple-element.78), kind=kOutput, calls=%fused_computation.24 | convolution fusion | flops 102432768 | bytes 1269808 | tf_op jit(solution)/shard_map/while/body/eval_jaxpr/hsn,shp->hpn/dot_general | solution.py:76
  88.2 2.2 %all_gather.19 = bf16[2,12,65,128]{3,2,1,0:T(8,128)(2,1)S(1)} all-gather(bf16[1,12,65,128]{3,2,1,0:T(8,128)(2,1)S(1)} %pad_maximum_fusion.1), channel_id=1, replica_groups=mesh['sx'=4,'zh'=4,'zl'=2,'sc'=2,'head'=4] {'sc'}, dimensions={0}, use_global_device_ids=true | all-gather | bytes 599040 | tf_op jit(solution)/shard_map/all_gather | solution.py:39
  90.4 0.8 copy-done.5
  91.2 0.4 fusion.54
  91.6 0.1 copy.55
  91.8 1.6 fusion.32
  93.6 4.9 %all_gather.20 = bf16[2,6,65,128]{3,2,1,0:T(8,128)(2,1)S(1)} all-gather(bf16[1,6,65,128]{3,2,1,0:T(8,128)(2,1)S(1)} %pad_maximum_fusion.2), channel_id=1, replica_groups=mesh['sx'=4,'zh'=4,'zl'=2,'sc'=2,'head'=4] {'zl'}, dimensions={0}, use_global_device_ids=true | all-gather | bytes 299520 | tf_op jit(solution)/shard_map/all_gather | solution.py:39
  98.5 0.1 convert_reduce_fusion.3
  98.7 0.2 slice_reduce_fusion.4
  99.1 0.4 fusion.51
  99.6 13.8 %all_gather.21 = bf16[4,6,65,128]{3,2,1,0:T(8,128)(2,1)S(1)} all-gather(bf16[1,6,65,128]{3,2,1,0:T(8,128)(2,1)S(1)} %pad_maximum_fusion.3), channel_id=1, replica_groups=mesh['sx'=4,'zh'=4,'zl'=2,'sc'=2,'head'=4] {'zh'}, dimensions={0}, use_global_device_ids=true | all-gather | bytes 499200 | tf_op jit(solution)/shard_map/all_gather | solution.py:39
  113.4 0.1 convert_reduce_fusion.1
  113.6 0.6 copy-done.4
  114.2 0.2 slice_reduce_fusion.3
  114.7 0.1 copy.71
  114.8 1.6 fusion.30
  116.4 0.8 copy.99
  117.2 0.1 copy.69
  117.4 0.4 fusion.49
  118.0 0.1 copy.67
  118.1 1.4 fusion.21
  119.5 0.7 copy.102
  120.3 1.4 fusion.23
  121.8 10.0 %all_gather.22 = bf16[4,6,65,128]{3,2,1,0:T(8,128)(2,1)S(1)} all-gather(bf16[1,6,65,128]{3,2,1,0:T(8,128)(2,1)S(1)} %pad_maximum_fusion.4), channel_id=1, replica_groups=mesh['sx'=4,'zh'=4,'zl'=2,'sc'=2,'head'=4] {'sx'}, dimensions={0}, use_global_device_ids=true | all-gather | bytes 499200 | tf_op jit(solution)/shard_map/all_gather | solution.py:39
  131.8 0.8 copy-done.6
  132.6 0.1 fusion.53
  132.9 0.1 copy.64
  133.0 1.5 fusion.18
  134.5 1.0 slice_add_fusion.2
  135.5 8.9 %all_gather.23 = f32[12,64,128]{2,1,0:T(8,128)S(1)} all-gather(f32[6,64,128]{2,1,0:T(8,128)S(1)} %slice_add_fusion.2), channel_id=1, replica_groups=mesh['sx'=4,'zh'=4,'zl'=2,'sc'=2,'head'=4] {'sc'}, dimensions={0}, use_global_device_ids=true | all-gather | bytes 589824 | tf_op jit(solution)/shard_map/all_gather | solution.py:61
  144.4 3.8 %fusion = f32[12,64,512]{2,1,0:T(8,128)S(1)} fusion(bf16[512,12,64]{0,2,1:T(8,128)(2,1)S(1)} %bitcast.105, f32[12,512]{1,0:T(8,128)S(1)} %bitcast.118, f32[512,512]{1,0:T(8,128)S(1)} %copy-done.3, pred[512,512]{1,0:T(8,128)(4,1)S(1)} %copy-done.7), kind=kOutput, calls=%fused_computation.1 | convolution fusion | flops 415236096 | bytes 3694592 | tf_op jit(solution)/shard_map/while/body/eval_jaxpr/hts,shp->thp/dot_general | solution.py:92
  148.2 2.0 %fusion.7 = f32[512,12,64]{0,2,1:T(8,128)S(1)} fusion(f32[12,64,512]{2,1,0:T(8,128)S(1)} %fusion, bf16[512,12,64]{0,2,1:T(8,128)(2,1)S(1)} %bitcast.106, f32[12]{0:T(128)S(1)} %copy-done.11, f32[512,12]{0,1:T(8,128)S(1)} %exponential_multiply_fusion, f32[12,65,128]{2,1,0:T(8,128)S(1)} %bitcast.107, f32[12,64,128]{2,1,0:T(8,128)S(1)} %all_gather.23, ...), kind=kOutput, calls=%fused_computation.17 | convolution fusion | flops 606142464 | bytes 4883456 | tf_op jit(solution)/shard_map/while/body/eval_jaxpr/tn,hpn->thp/dot_general | solution.py:97
  150.2 1.7 multiply_reduce_fusion
  151.9 1.5 convolution_convert_fusion
  153.4 0.1 pad_maximum_fusion
  153.6 25.0 %all_to_all.10 = bf16[4,136,1536]{2,1,0:T(8,128)(2,1)S(1)} all-to-all(bf16[4,136,1536]{2,1,0:T(8,128)(2,1)S(1)} %pad_maximum_fusion), channel_id=1, replica_groups=mesh['sx'=4,'zh'=4,'zl'=2,'sc'=2,'head'=4] {'head'}, dimensions={0} | all-to-all | bytes 3342336 | tf_op jit(solution)/shard_map/all_to_all | solution.py:240
  178.6 0.2 convert_reduce_fusion
  178.9 0.9 fusion.14
  (88 shorter events, 2.4 us)
Async XLA Ops:
  0.0 151.9 %copy-start = (bf16[768,1536]{1,0:T(8,128)(2,1)S(1)}, bf16[768,1536]{1,0:T(8,128)(2,1)}, u32[]{:S(2)}) copy-start(bf16[768,1536]{1,0:T(8,128)(2,1)} %param.19) | copy-start | bytes 7077892
  16.1 13.3 %copy-start.8 = (s32[4]{0:T(128)S(1)}, s32[4]{0:T(128)}, u32[]{:S(2)}) copy-start(s32[4]{0:T(128)} %param.16) | copy-start | bytes 52
  16.1 61.4 %all-to-all-start = ((bf16[64,8,1806]{2,1,0:T(8,128)(2,1)}), bf16[64,8,1806]{2,1,0:T(8,128)(2,1)}, u32[]{:S(2)}, u32[]{:S(2)}) async-start(bf16[64,8,1806]{2,1,0:T(8,128)(2,1)} %bitcast.103), calls=%async_computation | async-start | bytes 3932160 | tf_op jit(solution)/shard_map/all_to_all | solution.py:141
  32.2 0.5 copy-start.9
  81.5 1.6 copy-start.1
  90.4 0.8 copy-start.5
  93.4 21.0 %copy-start.10 = (pred[2]{0:T(512)(128)(4,1)S(1)}, pred[2]{0:T(512)(128)(4,1)}, u32[]{:S(2)}) copy-start(pred[2]{0:T(512)(128)(4,1)} %copy-done.9) | copy-start | bytes 10
  113.4 0.8 copy-start.4
  131.8 0.8 copy-start.6
  133.0 11.4 %copy-start.3 = (f32[512,512]{1,0:T(8,128)S(1)}, f32[512,512]{1,0:T(8,128)}, u32[]{:S(2)}) copy-start(f32[512,512]{1,0:T(8,128)} %fusion.41) | copy-start | bytes 3145732
  133.0 11.4 %copy-start.7 = (pred[512,512]{1,0:T(8,128)(4,1)S(1)}, pred[512,512]{1,0:T(8,128)(4,1)}, u32[]{:S(2)}) copy-start(pred[512,512]{1,0:T(8,128)(4,1)} %fusion.13) | copy-start | bytes 786436
  144.4 3.8 %copy-start.2 = (f32[12,1,65,128]{3,2,0,1:T(8,128)S(1)}, f32[12,1,65,128]{3,2,0,1:T(8,128)}, u32[]{:S(2)}) copy-start(f32[12,1,65,128]{3,2,0,1:T(8,128)} %copy.99) | copy-start | bytes 1198084
  144.4 3.8 %copy-start.11 = (f32[12]{0:T(128)S(1)}, f32[12]{0:T(128)}, u32[]{:S(2)}) copy-start(f32[12]{0:T(128)} %param.17) | copy-start | bytes 148
  150.2 1.7 copy-start.12

commit v12 on v9

--- a/solution.py
+++ b/solution.py
@@ -125,16 +125,19 @@
     slot_index = owner * capacity + slot_rank
     place_hi = (local_place // 32).astype(jnp.bfloat16)
     place_lo = (local_place % 32).astype(jnp.bfloat16)
-    rows_out = jnp.concatenate(
-        [features_in, gate_in, b_input, c_input, log_decay, place_hi[:, None], place_lo[:, None]],
-        axis=1,
-    )
+    pieces = [features_in, gate_in, b_input, c_input, log_decay, place_hi[:, None], place_lo[:, None]]
     to_slot = (
         lax.broadcasted_iota(jnp.int32, (tok_dev, tok_dev), 0) == slot_index[None, :]
     ).astype(jnp.bfloat16)
 
     def send(values):
-        packed = jnp.dot(to_slot, values, preferred_element_type=jnp.float32).astype(jnp.bfloat16)
+        packed = jnp.concatenate(
+            [
+                jnp.dot(to_slot, v, preferred_element_type=jnp.float32).astype(jnp.bfloat16)
+                for v in values
+            ],
+            axis=1,
+        )
         return lax.all_to_all(
             packed.reshape(shards, capacity, packed.shape[1]),
             ROWS,
@@ -143,8 +146,10 @@
             tiled=True,
         ).reshape(tok_dev, packed.shape[1])
 
-    moved = send(rows_out)
-    columns = rows_out.shape[1]
+    rows_out = jnp.concatenate(pieces[4:], axis=1)
+    pieces = pieces[:4] + [rows_out]
+    moved = send(pieces)
+    columns = moved.shape[1]
     arrived = (
         moved[:, columns - 2].astype(jnp.int32) * 32 + moved[:, columns - 1].astype(jnp.int32)
     )

time: 177 us -> 171 us (0.966)
  local copies, waits for them, and re-layouts: 13.8 us -> 5.62 us
  matrix products: 22.3 us -> 24.7 us
    convert_element_type x1, local copies, waits for them, and re-layouts: 3.95 us -> 0.15 us  [send(): jnp.dot(to_slot, v, preferred_element_type=jnp.float32).astype(jnp.bfloat16)]
    concatenate x1, local copies, waits for them, and re-layouts: 3.85 us -> 0.69 us  [send(): jnp.concatenate([jnp.dot(to_slot, v, preferred_element_type=jnp.float32)....]
    dot_general x1 -> x5, matrix products: 3.98 us -> 6.44 us  [send(): jnp.dot(to_slot, v, preferred_element_type=jnp.float32).astype(jnp.bfloat16)]
where the time goes in v12:
time: 171 us; the launch traced here: 170 us
  blocking collectives  68.7 us (40%)
  waiting for transfers between devices  41.5 us (24%)
  matrix products  24.7 us (14%)
  other arithmetic  14.9 us (9%)
  starting transfers between devices  13.3 us (8%)
  local copies, waits for them, and re-layouts  5.62 us (3%)
  between operations  1.78 us (1%)
    all_to_all x1, waiting for transfers between devices, send(): lax.all_to_all(packed.reshape(shards, capacity, packed.shape[1]), ROWS, s...  41.5 us
    all_gather x3, blocking collectives, gathered_level(): gathered = lax.all_gather(pack_state(kept, state), axis)  33.6 us
    all_to_all x1, blocking collectives, body(): lax.all_to_all(sent, 'head', split_axis=0, concat_axis=0, tiled=True)  25 us
    all_to_all x1, starting transfers between devices, send(): lax.all_to_all(packed.reshape(shards, capacity, packed.shape[1]), ROWS, s...  13.3 us
    all_gather x1, blocking collectives, exclusive_prefix(): whole = lax.all_gather(start_state, pair, tiled=True)  10.1 us
    dot_general x5, matrix products, send(): jnp.dot(to_slot, v, preferred_element_type=jnp.float32).astype(jnp.bfloat16)  6.44 us
    dot_general x1, matrix products, inner_terms(): jnp.einsum('hts,shp->thp', affinity_logits, by_head, preferred_element_ty...  3.78 us
  transfers between devices with their start and end apart: 1, of which 1 were waited for; matrix products, arithmetic and copies ran while one was open for 3% of the time, Pallas kernels for 0%

profile of v12, /device:TPU:1, one launch (start us, length us, event | category | flops | bytes accessed | tf_op | source)
XLA Modules:
  0.0 170.4 jit_solution(11054895643215754931)
XLA Ops:
  0.0 0.8 fusion.66
  0.9 1.2 reduce-window.24
  2.1 0.2 slice_reduce_fusion
  2.4 0.1 fusion.45
  2.5 0.7 fusion.67
  3.2 2.6 %fusion.11 = bf16[512,1806]{1,0:T(8,128)(2,1)} fusion(bf16[512,768]{1,0:T(8,128)(2,1)} %param.10, s32[512]{0:T(512)S(1)} %get-tuple-element.77), kind=kOutput, calls=%fused_computation.24 | convolution fusion | flops 403308544 | bytes 1574912 | tf_op jit(solution)/shard_map/dot_general | solution.py:136
  5.8 0.3 convolution_convert_fusion.6
  6.1 0.2 copy.60
  6.3 1.5 fusion.10
  7.8 1.0 fusion.15
  8.8 1.0 fusion.14
  9.8 0.7 constant_dynamic-update-slice_fusion
  10.5 13.3 %all-to-all-start = ((bf16[64,8,1806]{2,1,0:T(8,128)(2,1)}), bf16[64,8,1806]{2,1,0:T(8,128)(2,1)}, u32[]{:S(2)}, u32[]{:S(2)}) async-start(bf16[64,8,1806]{2,1,0:T(8,128)(2,1)} %bitcast.99), calls=%async_computation | async-start | bytes 3932160 | tf_op jit(solution)/shard_map/all_to_all | solution.py:141
  23.8 0.2 reduce-window.31
  24.0 0.6 fusion.71
  24.6 0.1 convert_reduce_fusion.1
  24.7 0.6 slice.88
  26.6 0.6 fusion.77
  27.2 0.6 iota_compare_fusion.17
  27.8 0.6 iota_compare_fusion.16
  28.4 0.5 fusion.70
  28.9 0.6 compare_convert_fusion.1
  29.6 0.9 fusion.17
  30.5 41.5 %all-to-all-done = bf16[64,8,1806]{2,1,0:T(8,128)(2,1)} async-done(((bf16[64,8,1806]{2,1,0:T(8,128)(2,1)}), bf16[64,8,1806]{2,1,0:T(8,128)(2,1)}, u32[]{:S(2)}, u32[]{:S(2)}) %all-to-all-start) | async-done | bytes 1849376 | tf_op jit(solution)/shard_map/all_to_all | solution.py:141
  72.0 1.2 add_reduce_fusion
  73.2 2.8 %convolution_convert_fusion.1 = bf16[512,1806]{0,1:T(8,128)(2,1)S(1)} fusion(s32[512]{0:T(512)S(1)} %add_reduce_fusion, bf16[64,8,1806]{2,1,0:T(8,128)(2,1)} %all-to-all-done), kind=kOutput, calls=%fused_computation.6 | convolution fusion | flops 948050944 | bytes 3700736 | tf_op jit(solution)/shard_map/dot_general | solution.py:161
  76.0 1.6 fusion.48
  77.7 1.2 reduce-window.32
  78.9 0.2 slice_reduce_fusion.1
  79.2 0.2 slice_reduce_fusion.2
  79.4 0.8 copy.63
  80.3 2.3 %fusion.16 = bf16[1,12,64,128]{3,2,1,0:T(8,128)(2,1)S(1)} fusion(bf16[512,12,64]{0,2,1:T(8,128)(2,1)S(1)} %bitcast.96, f32[12,512]{1,0:T(8,128)S(1)} %exponential_multiply_fusion.1, f32[512,128]{1,0:T(8,128)} %copy.63, f32[12]{0:T(128)S(1)} %get-tuple-element.78), kind=kOutput, calls=%fused_computation.31 | convolution fusion | flops 102432768 | bytes 1269808 | tf_op jit(solution)/shard_map/while/body/eval_jaxpr/hsn,shp->hpn/dot_general | solution.py:73
  82.7 2.2 %all_gather.15 = bf16[2,12,65,128]{3,2,1,0:T(8,128)(2,1)S(1)} all-gather(bf16[1,12,65,128]{3,2,1,0:T(8,128)(2,1)S(1)} %pad_maximum_fusion.1), channel_id=1, replica_groups=mesh['sx'=4,'sz'=8,'sc'=2,'head'=4] {'sc'}, dimensions={0}, use_global_device_ids=true | all-gather | bytes 599040 | tf_op jit(solution)/shard_map/all_gather | solution.py:38
  84.9 0.4 fusion.61
  85.3 0.1 select_reduce_fusion.5
  85.4 0.1 copy.69
  85.5 0.6 fusion.39
  86.3 20.9 %all_gather.16 = bf16[8,6,65,128]{3,2,1,0:T(8,128)(2,1)S(1)} all-gather(bf16[1,6,65,128]{3,2,1,0:T(8,128)(2,1)S(1)} %pad_maximum_fusion.2), channel_id=1, replica_groups=mesh['sx'=4,'sz'=8,'sc'=2,'head'=4] {'sz'}, dimensions={0}, use_global_device_ids=true | all-gather | bytes 898560 | tf_op jit(solution)/shard_map/all_gather | solution.py:38
  107.2 0.2 slice_reduce_fusion.3
  107.4 0.1 copy.84
  107.6 0.1 select_reduce_fusion.3
  107.7 0.1 select_reduce_fusion.6
  107.9 0.1 copy.80
  108.0 1.6 fusion.37
  109.6 0.8 copy.108
  110.5 0.3 select_reduce_fusion.1
  110.8 0.4 fusion.20
  111.2 0.4 fusion.22
  111.7 10.5 %all_gather.17 = bf16[4,6,65,128]{3,2,1,0:T(8,128)(2,1)S(1)} all-gather(bf16[1,6,65,128]{3,2,1,0:T(8,128)(2,1)S(1)} %pad_maximum_fusion.3), channel_id=1, replica_groups=mesh['sx'=4,'sz'=8,'sc'=2,'head'=4] {'sx'}, dimensions={0}, use_global_device_ids=true | all-gather | bytes 499200 | tf_op jit(solution)/shard_map/all_gather | solution.py:38
  122.2 0.8 copy-done.7
  123.0 0.1 fusion.60
  123.1 0.1 select_reduce_fusion.2
  123.3 0.1 copy.75
  123.4 1.5 fusion.30
  124.9 0.1 slice_add_fusion.2
  125.0 10.1 %all_gather.18 = f32[12,64,128]{2,1,0:T(8,128)S(1)} all-gather(f32[6,64,128]{2,1,0:T(8,128)S(1)} %slice_add_fusion.2), channel_id=1, replica_groups=mesh['sx'=4,'sz'=8,'sc'=2,'head'=4] {'sc'}, dimensions={0}, use_global_device_ids=true | all-gather | bytes 589824 | tf_op jit(solution)/shard_map/all_gather | solution.py:58
  135.1 3.8 %fusion = f32[12,64,512]{2,1,0:T(8,128)S(1)} fusion(bf16[512,12,64]{0,2,1:T(8,128)(2,1)S(1)} %bitcast.97, f32[12,512]{1,0:T(8,128)S(1)} %bitcast.109, f32[512,512]{1,0:T(8,128)S(1)} %copy-done.5, pred[512,512]{1,0:T(8,128)(4,1)S(1)} %copy-done.8), kind=kOutput, calls=%fused_computation.1 | convolution fusion | flops 415236096 | bytes 3694592 | tf_op jit(solution)/shard_map/while/body/eval_jaxpr/hts,shp->thp/dot_general | solution.py:89
  138.9 2.0 %fusion.7 = f32[512,12,64]{0,2,1:T(8,128)S(1)} fusion(f32[12,64,512]{2,1,0:T(8,128)S(1)} %fusion, bf16[512,12,64]{0,2,1:T(8,128)(2,1)S(1)} %bitcast.98, f32[12]{0:T(128)S(1)} %copy-done.14, f32[512,12]{0,1:T(8,128)S(1)} %exponential_multiply_fusion, f32[12,65,128]{2,1,0:T(8,128)S(1)} %bitcast.100, f32[12,64,128]{2,1,0:T(8,128)S(1)} %all_gather.18, ...), kind=kOutput, calls=%fused_computation.16 | convolution fusion | flops 606142464 | bytes 4883456 | tf_op jit(solution)/shard_map/while/body/eval_jaxpr/tn,hpn->thp/dot_general | solution.py:94
  140.9 1.7 multiply_reduce_fusion
  142.6 1.5 convolution_convert_fusion
  144.2 0.1 pad_maximum_fusion
  144.3 25.0 %all_to_all.10 = bf16[4,136,1536]{2,1,0:T(8,128)(2,1)S(1)} all-to-all(bf16[4,136,1536]{2,1,0:T(8,128)(2,1)S(1)} %pad_maximum_fusion), channel_id=1, replica_groups=mesh['sx'=4,'sz'=8,'sc'=2,'head'=4] {'head'}, dimensions={0} | all-to-all | bytes 3342336 | tf_op jit(solution)/shard_map/all_to_all | solution.py:242
  169.3 0.2 convert_reduce_fusion
  169.6 0.9 fusion.18
  (87 shorter events, 1.3 us)
Async XLA Ops:
  0.0 142.6 %copy-start = (bf16[768,1536]{1,0:T(8,128)(2,1)S(1)}, bf16[768,1536]{1,0:T(8,128)(2,1)}, u32[]{:S(2)}) copy-start(bf16[768,1536]{1,0:T(8,128)(2,1)} %param.19) | copy-start | bytes 7077892
  0.9 5.4 %copy-start.15 = (bf16[512,768]{1,0:T(8,128)(2,1)S(1)}, bf16[512,768]{1,0:T(8,128)(2,1)}, u32[]{:S(2)}) copy-start(bf16[512,768]{1,0:T(8,128)(2,1)} %param.11) | copy-start | bytes 2359300
  2.1 3.8 %copy-start.18 = (bf16[512,12]{0,1:T(8,128)(2,1)S(1)}, bf16[512,12]{0,1:T(8,128)(2,1)}, u32[]{:S(2)}) copy-start(bf16[512,12]{0,1:T(8,128)(2,1)} %param.14) | copy-start | bytes 36868
  5.8 2.0 %copy-start.16 = (bf16[512,128]{1,0:T(8,128)(2,1)S(1)}, bf16[512,128]{1,0:T(8,128)(2,1)}, u32[]{:S(2)}) copy-start(bf16[512,128]{1,0:T(8,128)(2,1)} %param.12) | copy-start | bytes 393220
  6.3 2.5 %copy-start.17 = (bf16[512,128]{1,0:T(8,128)(2,1)S(1)}, bf16[512,128]{1,0:T(8,128)(2,1)}, u32[]{:S(2)}) copy-start(bf16[512,128]{1,0:T(8,128)(2,1)} %param.13) | copy-start | bytes 393220
  10.5 13.3 %copy-start.9 = (s32[4]{0:T(128)S(1)}, s32[4]{0:T(128)}, u32[]{:S(2)}) copy-start(s32[4]{0:T(128)} %param.16) | copy-start | bytes 52
  10.5 61.4 %all-to-all-start = ((bf16[64,8,1806]{2,1,0:T(8,128)(2,1)}), bf16[64,8,1806]{2,1,0:T(8,128)(2,1)}, u32[]{:S(2)}, u32[]{:S(2)}) async-start(bf16[64,8,1806]{2,1,0:T(8,128)(2,1)} %bitcast.99), calls=%async_computation | async-start | bytes 3932160 | tf_op jit(solution)/shard_map/all_to_all | solution.py:141
  76.0 1.7 copy-start.3
  76.0 6.6 %copy-start.1 = (bf16[512,768]{0,1:T(8,128)(2,1)}, bf16[512,768]{0,1:T(8,128)(2,1)S(1)}, u32[]{:S(2)}) copy-start(bf16[512,768]{0,1:T(8,128)(2,1)S(1)} %slice.104) | copy-start | bytes 2359300
  84.9 1.4 copy-start.6
  85.5 22.3 %copy-start.12 = (f32[2]{0:T(128)S(1)}, f32[2]{0:T(128)}, u32[]{:S(2)}) copy-start(f32[2]{0:T(128)} %fusion.77) | copy-start | bytes 28
  86.3 24.4 %copy-start.13 = (f32[8]{0:T(128)S(1)}, f32[8]{0:T(128)}, u32[]{:S(2)}) copy-start(f32[8]{0:T(128)} %get-tuple-element.94) | copy-start | bytes 100
  110.8 12.4 %copy-start.11 = (pred[4,4]{1,0:T(4,128)(4,1)S(1)}, pred[4,4]{1,0:T(4,128)(4,1)}, u32[]{:S(2)}) copy-start(pred[4,4]{1,0:T(4,128)(4,1)} %fusion.70) | copy-start | bytes 52
  110.8 12.4 %copy-start.10 = (f32[4]{0:T(128)S(1)}, f32[4]{0:T(128)}, u32[]{:S(2)}) copy-start(f32[4]{0:T(128)} %get-tuple-element.97) | copy-start | bytes 52
  111.5 23.6 %copy-start.2 = (bf16[512,768]{0,1:T(8,128)(2,1)S(1)}, bf16[512,768]{0,1:T(8,128)(2,1)}, u32[]{:S(2)}) copy-start(bf16[512,768]{0,1:T(8,128)(2,1)} %copy-done.1) | copy-start | bytes 2359300
  122.2 0.8 copy-start.7
  123.4 11.7 %copy-start.5 = (f32[512,512]{1,0:T(8,128)S(1)}, f32[512,512]{1,0:T(8,128)}, u32[]{:S(2)}) copy-start(f32[512,512]{1,0:T(8,128)} %fusion.48) | copy-start | bytes 3145732
  123.4 11.7 %copy-start.8 = (pred[512,512]{1,0:T(8,128)(4,1)S(1)}, pred[512,512]{1,0:T(8,128)(4,1)}, u32[]{:S(2)}) copy-start(pred[512,512]{1,0:T(8,128)(4,1)} %fusion.17) | copy-start | bytes 786436
  135.1 3.8 %copy-start.4 = (f32[12,1,65,128]{3,2,0,1:T(8,128)S(1)}, f32[12,1,65,128]{3,2,0,1:T(8,128)}, u32[]{:S(2)}) copy-start(f32[12,1,65,128]{3,2,0,1:T(8,128)} %copy.108) | copy-start | bytes 1198084
  135.1 3.8 %copy-start.14 = (f32[12]{0:T(128)S(1)}, f32[12]{0:T(128)}, u32[]{:S(2)}) copy-start(f32[12]{0:T(128)} %param.17) | copy-start | bytes 148
  140.9 1.7 %copy-start.19 = (f32[768]{0:T(1024)S(1)}, f32[768]{0:T(1024)}, u32[]{:S(2)}) copy-start(f32[768]{0:T(1024)} %param.18) | copy-start | bytes 9220

commit v13 on v12

--- a/solution.py
+++ b/solution.py
@@ -160,12 +160,11 @@
     def place(values):
         return jnp.dot(to_place, values, preferred_element_type=jnp.float32).astype(jnp.bfloat16)
 
-    rows = place(moved)
-    features = rows[:, :feats]
-    gate_rows = rows[:, feats : 2 * feats]
-    key_full = rows[:, 2 * feats : 2 * feats + n_state]
-    query_full = rows[:, 2 * feats + n_state : 2 * feats + 2 * n_state]
-    decays = rows[:, 2 * feats + 2 * n_state : 2 * feats + 2 * n_state + heads_here]
+    features = place(moved[:, :feats])
+    gate_rows = place(moved[:, feats : 2 * feats])
+    key_full = place(moved[:, 2 * feats : 2 * feats + n_state])
+    query_full = place(moved[:, 2 * feats + n_state : 2 * feats + 2 * n_state])
+    decays = place(moved[:, 2 * feats + 2 * n_state : 2 * feats + 2 * n_state + heads_here])
 
     doc_starts = jnp.cumsum(doc_lengths) - doc_lengths
     first_place = lax.axis_index(ROWS) * tok_dev
@@ -237,7 +236,7 @@
     extra = jnp.concatenate(
         [square_hi.reshape(groups, 1, chunk), square_lo.reshape(groups, 1, chunk)], axis=1
     )
-    extra = jnp.pad(extra, ((0, 0), (0, 6), (0, d_model - chunk)))
+    extra = jnp.pad(extra, ((0, 0), (0, 0), (0, d_model - chunk)))
     sent = jnp.concatenate([partial.reshape(groups, chunk, d_model), extra], axis=1)
     arrived_parts = lax.all_to_all(sent, "head", split_axis=0, concat_axis=0, tiled=True)
     summed = jnp.sum(arrived_parts.astype(jnp.float32), axis=0)

time: 171 us -> 182 us (1.064)
  matrix products: 24.7 us -> 32.8 us
  local copies, waits for them, and re-layouts: 5.62 us -> 9.9 us
  other arithmetic: 14.9 us -> 11 us
  waiting for transfers between devices: 41.5 us -> 43.7 us
    dot_general x1 -> x5, matrix products: 2.75 us -> 10.2 us  [place(): jnp.dot(to_place, values, preferred_element_type=jnp.float32)]
    reshape x0 -> x1, local copies, waits for them, and re-layouts: none -> 3.01 us  [body(): mixed = mixed.reshape(tok_dev, heads_here * width)]
    all_to_all x1, waiting for transfers between devices: 41.5 us -> 43.7 us  [send(): lax.all_to_all(packed.reshape(shards, capacity, packed.shape[1]), ROWS, s...]
  transfers between devices with their start and end apart: 1 -> 1, of which waited for: 1 -> 1; matrix products, arithmetic and copies ran while one was open for 3% -> 2% of each run, Pallas kernels for 0% -> 0%
where the time goes in v13:
time: 182 us; the launch traced here: 181 us
  blocking collectives  68.6 us (38%)
  waiting for transfers between devices  43.7 us (24%)
  matrix products  32.8 us (18%)
  starting transfers between devices  13.3 us (7%)
  other arithmetic  11 us (6%)
  local copies, waits for them, and re-layouts  9.9 us (5%)
    all_to_all x1, waiting for transfers between devices, send(): lax.all_to_all(packed.reshape(shards, capacity, packed.shape[1]), ROWS, s...  43.7 us
    all_gather x3, blocking collectives, gathered_level(): gathered = lax.all_gather(pack_state(kept, state), axis)  33.5 us
    all_to_all x1, blocking collectives, body(): lax.all_to_all(sent, 'head', split_axis=0, concat_axis=0, tiled=True)  25 us
    all_to_all x1, starting transfers between devices, send(): lax.all_to_all(packed.reshape(shards, capacity, packed.shape[1]), ROWS, s...  13.3 us
    dot_general x5, matrix products, place(): jnp.dot(to_place, values, preferred_element_type=jnp.float32)  10.2 us
    all_gather x1, blocking collectives, exclusive_prefix(): whole = lax.all_gather(start_state, pair, tiled=True)  10.1 us
    dot_general x5, matrix products, send(): jnp.dot(to_slot, v, preferred_element_type=jnp.float32).astype(jnp.bfloat16)  6.43 us
    dot_general x1, matrix products, inner_terms(): jnp.einsum('hts,shp->thp', affinity_logits, by_head, preferred_element_ty...  3.81 us
  transfers between devices with their start and end apart: 1, of which 1 were waited for; matrix products, arithmetic and copies ran while one was open for 2% of the time, Pallas kernels for 0%

profile of v13, /device:TPU:1, one launch (start us, length us, event | category | flops | bytes accessed | tf_op | source)
XLA Modules:
  0.0 181.0 jit_solution(18229670684418701614)
XLA Ops:
  0.0 0.9 fusion.69
  0.9 1.2 reduce-window.24
  2.1 0.2 slice_reduce_fusion
  2.4 0.1 fusion.47
  2.5 0.7 fusion.70
  3.2 2.6 %fusion.11 = bf16[512,1806]{1,0:T(8,128)(2,1)} fusion(bf16[512,768]{1,0:T(8,128)(2,1)} %param.10, s32[512]{0:T(512)S(1)} %get-tuple-element.75), kind=kOutput, calls=%fused_computation.25 | convolution fusion | flops 403308544 | bytes 1574912 | tf_op jit(solution)/shard_map/dot_general | solution.py:136
  5.8 0.3 convolution_convert_fusion.9
  6.1 0.2 copy.62
  6.3 1.5 fusion.10
  7.8 1.0 fusion.15
  8.8 1.0 fusion.14
  9.8 0.7 constant_dynamic-update-slice_fusion
  10.5 13.3 %all-to-all-start = ((bf16[64,8,1806]{2,1,0:T(8,128)(2,1)}), bf16[64,8,1806]{2,1,0:T(8,128)(2,1)}, u32[]{:S(2)}, u32[]{:S(2)}) async-start(bf16[64,8,1806]{2,1,0:T(8,128)(2,1)} %bitcast.96), calls=%async_computation | async-start | bytes 3932160 | tf_op jit(solution)/shard_map/all_to_all | solution.py:141
  23.8 0.2 reduce-window.31
  24.0 0.6 fusion.74
  24.7 0.6 slice.88
  26.7 0.6 compare_convert_fusion.1
  27.4 0.9 fusion.18
  28.3 43.7 %all-to-all-done = bf16[64,8,1806]{2,1,0:T(8,128)(2,1)} async-done(((bf16[64,8,1806]{2,1,0:T(8,128)(2,1)}), bf16[64,8,1806]{2,1,0:T(8,128)(2,1)}, u32[]{:S(2)}, u32[]{:S(2)}) %all-to-all-start) | async-done | bytes 1849376 | tf_op jit(solution)/shard_map/all_to_all | solution.py:141
  72.0 1.2 add_reduce_fusion
  73.2 2.6 %convolution_convert_fusion.2 = bf16[512,768]{1,0:T(8,128)(2,1)} fusion(bf16[512,1806]{1,0:T(8,128)(2,1)} %bitcast.3, s32[512]{0:T(512)S(1)} %add_reduce_fusion), kind=kOutput, calls=%fused_computation.21 | convolution fusion | flops 403308544 | bytes 1574912 | tf_op jit(solution)/shard_map/dot_general | solution.py:161
  75.8 1.2 fusion.17
  77.0 1.9 %convolution_convert_fusion.6 = bf16[512,128]{1,0:T(8,128)(2,1)} fusion(s32[512]{0:T(512)S(1)} %add_reduce_fusion, bf16[512,1806]{1,0:T(8,128)(2,1)} %bitcast.3), kind=kOutput, calls=%fused_computation.29 | convolution fusion | flops 67436544 | bytes 264192 | tf_op jit(solution)/shard_map/dot_general | solution.py:161
  78.9 2.0 %fusion.82 = (f32[512,128]{1,0:T(8,128)}, bf16[512,128]{1,0:T(8,128)(2,1)}) fusion(bf16[512,1806]{1,0:T(8,128)(2,1)} %bitcast.3, s32[512]{0:T(512)S(1)} %add_reduce_fusion), kind=kOutput, calls=%fused_computation.181 | convolution fusion | flops 67502080 | bytes 526336 | tf_op jit(solution)/shard_map/dot_general | solution.py:161
  80.8 1.4 copy.63
  82.3 1.2 reduce-window.32
  83.4 0.2 slice_reduce_fusion.1
  83.8 0.2 slice_reduce_fusion.2
  84.0 2.3 %fusion.16 = bf16[1,12,64,128]{3,2,1,0:T(8,128)(2,1)S(1)} fusion(bf16[512,12,64]{0,2,1:T(8,128)(2,1)S(1)} %bitcast.93, f32[12,512]{1,0:T(8,128)S(1)} %exponential_multiply_fusion.1, f32[512,128]{1,0:T(8,128)} %get-tuple-element.78, f32[12]{0:T(128)S(1)} %get-tuple-element.76), kind=kOutput, calls=%fused_computation.34 | convolution fusion | flops 102432768 | bytes 1269808 | tf_op jit(solution)/shard_map/while/body/eval_jaxpr/hsn,shp->hpn/dot_general | solution.py:73
  86.5 2.2 %all_gather.15 = bf16[2,12,65,128]{3,2,1,0:T(8,128)(2,1)S(1)} all-gather(bf16[1,12,65,128]{3,2,1,0:T(8,128)(2,1)S(1)} %pad_maximum_fusion.1), channel_id=1, replica_groups=mesh['sx'=4,'sz'=8,'sc'=2,'head'=4] {'sc'}, dimensions={0}, use_global_device_ids=true | all-gather | bytes 599040 | tf_op jit(solution)/shard_map/all_gather | solution.py:38
  88.6 0.8 copy-done.5
  89.4 0.4 fusion.64
  89.8 0.1 select_reduce_fusion.5
  89.9 0.1 copy.71
  90.0 1.6 fusion.43
  91.8 20.9 %all_gather.16 = bf16[8,6,65,128]{3,2,1,0:T(8,128)(2,1)S(1)} all-gather(bf16[1,6,65,128]{3,2,1,0:T(8,128)(2,1)S(1)} %pad_maximum_fusion.2), channel_id=1, replica_groups=mesh['sx'=4,'sz'=8,'sc'=2,'head'=4] {'sz'}, dimensions={0}, use_global_device_ids=true | all-gather | bytes 898560 | tf_op jit(solution)/shard_map/all_gather | solution.py:38
  112.8 0.2 slice_reduce_fusion.3
  113.0 0.1 copy.84
  113.1 0.1 select_reduce_fusion.3
  113.2 0.1 select_reduce_fusion.6
  113.4 0.1 copy.82
  113.5 1.6 fusion.41
  115.1 0.8 copy.108
  116.0 0.3 select_reduce_fusion.1
  116.3 0.4 fusion.23
  116.7 0.4 fusion.25
  117.2 10.4 %all_gather.17 = bf16[4,6,65,128]{3,2,1,0:T(8,128)(2,1)S(1)} all-gather(bf16[1,6,65,128]{3,2,1,0:T(8,128)(2,1)S(1)} %pad_maximum_fusion.3), channel_id=1, replica_groups=mesh['sx'=4,'sz'=8,'sc'=2,'head'=4] {'sx'}, dimensions={0}, use_global_device_ids=true | all-gather | bytes 499200 | tf_op jit(solution)/shard_map/all_gather | solution.py:38
  127.5 0.8 copy-done.6
  128.3 0.1 fusion.63
  128.4 0.1 select_reduce_fusion.2
  128.6 0.1 copy.77
  128.7 1.4 fusion.37
  130.2 0.1 slice_add_fusion.2
  130.2 10.1 %all_gather.18 = f32[12,64,128]{2,1,0:T(8,128)S(1)} all-gather(f32[6,64,128]{2,1,0:T(8,128)S(1)} %slice_add_fusion.2), channel_id=1, replica_groups=mesh['sx'=4,'sz'=8,'sc'=2,'head'=4] {'sc'}, dimensions={0}, use_global_device_ids=true | all-gather | bytes 589824 | tf_op jit(solution)/shard_map/all_gather | solution.py:58
  140.4 1.2 fusion.83
  141.6 3.8 %fusion = f32[12,64,512]{2,1,0:T(8,128)S(1)} fusion(bf16[512,12,64]{0,2,1:T(8,128)(2,1)S(1)} %bitcast.94, f32[12,512]{1,0:T(8,128)S(1)} %bitcast.106, f32[512,512]{1,0:T(8,128)S(1)} %fusion.83, pred[512,512]{1,0:T(8,128)(4,1)S(1)} %copy-done.7), kind=kOutput, calls=%fused_computation.1 | convolution fusion | flops 415236096 | bytes 3694592 | tf_op jit(solution)/shard_map/while/body/eval_jaxpr/hts,shp->thp/dot_general | solution.py:89
  145.5 2.2 %fusion.7 = f32[512,12,64]{0,2,1:T(8,128)} fusion(f32[12,64,512]{2,1,0:T(8,128)S(1)} %fusion, bf16[512,12,64]{0,2,1:T(8,128)(2,1)S(1)} %bitcast.95, f32[12]{0:T(128)S(1)} %copy-done.10, f32[512,12]{0,1:T(8,128)S(1)} %exponential_multiply_fusion, f32[12,65,128]{2,1,0:T(8,128)S(1)} %bitcast.97, f32[12,64,128]{2,1,0:T(8,128)S(1)} %all_gather.18, ...), kind=kOutput, calls=%fused_computation.15 | convolution fusion | flops 606142464 | bytes 4883456 | tf_op jit(solution)/shard_map/while/body/eval_jaxpr/tn,hpn->thp/dot_general | solution.py:94
  147.7 3.0 %copy.68 = f32[512,768]{1,0:T(8,128)} copy(f32[512,768]{0,1:T(8,128)} %bitcast.92) | data formatting | bytes 3145728 | tf_op jit(solution)/shard_map/reshape | solution.py:226
  150.7 2.5 %multiply_reduce_fusion = (f32[512]{0:T(512)S(1)}, f32[512,768]{1,0:T(8,128)S(1)}) fusion(f32[512,768]{1,0:T(8,128)} %copy.68, bf16[512,1806]{1,0:T(8,128)(2,1)} %bitcast.3, s32[512]{0:T(512)S(1)} %add_reduce_fusion), kind=kOutput, calls=%fused_computation.16 | convolution fusion | flops 406453760 | bytes 3936256 | tf_op jit(solution)/shard_map/dot_general | solution.py:161
  153.3 1.4 convolution_convert_fusion
  154.7 0.1 pad_maximum_fusion
  154.9 25.0 %all_to_all.10 = bf16[4,130,1536]{2,1,0:T(8,128)(2,1)S(1)} all-to-all(bf16[4,130,1536]{2,1,0:T(8,128)(2,1)S(1)} %pad_maximum_fusion), channel_id=1, replica_groups=mesh['sx'=4,'sz'=8,'sc'=2,'head'=4] {'head'}, dimensions={0} | all-to-all | bytes 3194880 | tf_op jit(solution)/shard_map/all_to_all | solution.py:241
  179.8 0.2 convert_reduce_fusion
  180.1 0.9 fusion.19
  (80 shorter events, 1.3 us)
Async XLA Ops:
  0.0 153.3 %copy-start = (bf16[768,1536]{1,0:T(8,128)(2,1)S(1)}, bf16[768,1536]{1,0:T(8,128)(2,1)}, u32[]{:S(2)}) copy-start(bf16[768,1536]{1,0:T(8,128)(2,1)} %param.19) | copy-start | bytes 7077892
  0.0 6.3 %copy-start.11 = (bf16[512,768]{1,0:T(8,128)(2,1)S(1)}, bf16[512,768]{1,0:T(8,128)(2,1)}, u32[]{:S(2)}) copy-start(bf16[512,768]{1,0:T(8,128)(2,1)} %param.11) | copy-start | bytes 2359300
  2.1 3.8 %copy-start.14 = (bf16[512,12]{0,1:T(8,128)(2,1)S(1)}, bf16[512,12]{0,1:T(8,128)(2,1)}, u32[]{:S(2)}) copy-start(bf16[512,12]{0,1:T(8,128)(2,1)} %param.14) | copy-start | bytes 36868
  5.8 2.0 %copy-start.12 = (bf16[512,128]{1,0:T(8,128)(2,1)S(1)}, bf16[512,128]{1,0:T(8,128)(2,1)}, u32[]{:S(2)}) copy-start(bf16[512,128]{1,0:T(8,128)(2,1)} %param.12) | copy-start | bytes 393220
  6.3 2.5 %copy-start.13 = (bf16[512,128]{1,0:T(8,128)(2,1)S(1)}, bf16[512,128]{1,0:T(8,128)(2,1)}, u32[]{:S(2)}) copy-start(bf16[512,128]{1,0:T(8,128)(2,1)} %param.13) | copy-start | bytes 393220
  10.5 13.3 %copy-start.9 = (s32[4]{0:T(128)S(1)}, s32[4]{0:T(128)}, u32[]{:S(2)}) copy-start(s32[4]{0:T(128)} %param.16) | copy-start | bytes 52
  10.5 61.5 %all-to-all-start = ((bf16[64,8,1806]{2,1,0:T(8,128)(2,1)}), bf16[64,8,1806]{2,1,0:T(8,128)(2,1)}, u32[]{:S(2)}, u32[]{:S(2)}) async-start(bf16[64,8,1806]{2,1,0:T(8,128)(2,1)} %bitcast.96), calls=%async_computation | async-start | bytes 3932160 | tf_op jit(solution)/shard_map/all_to_all | solution.py:141
  82.2 9.4 %copy-start.1 = (bf16[512,768]{0,1:T(8,128)(2,1)}, bf16[512,768]{0,1:T(8,128)(2,1)S(1)}, u32[]{:S(2)}) copy-start(bf16[512,768]{0,1:T(8,128)(2,1)S(1)} %copy.63) | copy-start | bytes 2359300
  88.6 0.8 copy-start.5
  127.5 0.8 copy-start.6
  128.3 13.3 %copy-start.2 = (bf16[512,768]{0,1:T(8,128)(2,1)S(1)}, bf16[512,768]{0,1:T(8,128)(2,1)}, u32[]{:S(2)}) copy-start(bf16[512,768]{0,1:T(8,128)(2,1)} %copy-done.1) | copy-start | bytes 2359300
  128.7 11.7 %copy-start.8 = (bf16[512,128]{1,0:T(8,128)(2,1)S(1)}, bf16[512,128]{1,0:T(8,128)(2,1)}, u32[]{:S(2)}) copy-start(bf16[512,128]{1,0:T(8,128)(2,1)} %get-tuple-element.79) | copy-start | bytes 393220
  128.7 12.9 %copy-start.7 = (pred[512,512]{1,0:T(8,128)(4,1)S(1)}, pred[512,512]{1,0:T(8,128)(4,1)}, u32[]{:S(2)}) copy-start(pred[512,512]{1,0:T(8,128)(4,1)} %fusion.18) | copy-start | bytes 786436
  141.6 3.8 %copy-start.3 = (f32[12,1,65,128]{3,2,0,1:T(8,128)S(1)}, f32[12,1,65,128]{3,2,0,1:T(8,128)}, u32[]{:S(2)}) copy-start(f32[12,1,65,128]{3,2,0,1:T(8,128)} %copy.108) | copy-start | bytes 1198084
  141.6 3.8 %copy-start.4 = (bf16[512,128]{1,0:T(8,128)(2,1)S(1)}, bf16[512,128]{1,0:T(8,128)(2,1)}, u32[]{:S(2)}) copy-start(bf16[512,128]{1,0:T(8,128)(2,1)} %convolution_convert_fusion.6) | copy-start | bytes 393220
  141.6 3.8 %copy-start.10 = (f32[12]{0:T(128)S(1)}, f32[12]{0:T(128)}, u32[]{:S(2)}) copy-start(f32[12]{0:T(128)} %param.17) | copy-start | bytes 148
  150.7 2.6 %copy-start.15 = (f32[768]{0:T(1024)S(1)}, f32[768]{0:T(1024)}, u32[]{:S(2)}) copy-start(f32[768]{0:T(1024)} %param.18) | copy-start | bytes 9220

commit v14 on v12

--- a/solution.py
+++ b/solution.py
@@ -147,7 +147,8 @@
         ).reshape(tok_dev, packed.shape[1])
 
     rows_out = jnp.concatenate(pieces[4:], axis=1)
-    pieces = pieces[:4] + [rows_out]
+    gate_piece = pieces[1]
+    pieces = [pieces[0]] + pieces[2:4] + [rows_out]
     moved = send(pieces)
     columns = moved.shape[1]
     arrived = (
@@ -162,10 +163,10 @@
 
     rows = place(moved)
     features = rows[:, :feats]
-    gate_rows = rows[:, feats : 2 * feats]
-    key_full = rows[:, 2 * feats : 2 * feats + n_state]
-    query_full = rows[:, 2 * feats + n_state : 2 * feats + 2 * n_state]
-    decays = rows[:, 2 * feats + 2 * n_state : 2 * feats + 2 * n_state + heads_here]
+    key_full = rows[:, feats : feats + n_state]
+    query_full = rows[:, feats + n_state : feats + 2 * n_state]
+    decays = rows[:, feats + 2 * n_state : feats + 2 * n_state + heads_here]
+    gate_moved = send([gate_piece])
 
     doc_starts = jnp.cumsum(doc_lengths) - doc_lengths
     first_place = lax.axis_index(ROWS) * tok_dev
@@ -225,6 +226,7 @@
         ),
     )
     mixed = mixed.reshape(tok_dev, heads_here * width)
+    gate_rows = place(gate_moved)
     gated = mixed * jax.nn.silu(gate_rows.astype(jnp.float32))
     squares = jnp.sum(gated * gated, axis=1)
     square_hi = squares.astype(jnp.bfloat16)

time: 171 us -> 163 us (0.953)
  waiting for transfers between devices: 41.5 us -> 20.2 us
  starting transfers between devices: 13.3 us -> 19.5 us
  blocking collectives: 68.7 us -> 73.1 us
  local copies, waits for them, and re-layouts: 5.62 us -> 8.16 us
    all_to_all x1 -> x2, waiting for transfers between devices: 41.5 us -> 20.2 us  [send(): lax.all_to_all(packed.reshape(shards, capacity, packed.shape[1]), ROWS, s...]
    all_to_all x1 -> x2, starting transfers between devices: 13.3 us -> 19.5 us  [send(): lax.all_to_all(packed.reshape(shards, capacity, packed.shape[1]), ROWS, s...]
    all_gather x3, blocking collectives: 33.6 us -> 37.8 us  [gathered_level(): gathered = lax.all_gather(pack_state(kept, state), axis)]
    reshape x0 -> x1, local copies, waits for them, and re-layouts: none -> 3.03 us  [body(): mixed = mixed.reshape(tok_dev, heads_here * width)]
  transfers between devices with their start and end apart: 1 -> 2, of which waited for: 1 -> 1; matrix products, arithmetic and copies ran while one was open for 3% -> 21% of each run, Pallas kernels for 0% -> 0%
where the time goes in v14:
time: 163 us; the launch traced here: 162 us
  blocking collectives  73.1 us (45%)
  matrix products  24.2 us (15%)
  waiting for transfers between devices  20.2 us (12%)
  starting transfers between devices  19.5 us (12%)
  other arithmetic  15 us (9%)
  local copies, waits for them, and re-layouts  8.16 us (5%)
  between operations  1.97 us (1%)
    all_gather x3, blocking collectives, gathered_level(): gathered = lax.all_gather(pack_state(kept, state), axis)  37.8 us
    all_to_all x1, blocking collectives, body(): lax.all_to_all(sent, 'head', split_axis=0, concat_axis=0, tiled=True)  25 us
    all_to_all x2, waiting for transfers between devices, send(): lax.all_to_all(packed.reshape(shards, capacity, packed.shape[1]), ROWS, s...  20.2 us
    all_to_all x2, starting transfers between devices, send(): lax.all_to_all(packed.reshape(shards, capacity, packed.shape[1]), ROWS, s...  19.5 us
    all_gather x1, blocking collectives, exclusive_prefix(): whole = lax.all_gather(start_state, pair, tiled=True)  10.3 us
    dot_general x5, matrix products, send(): jnp.dot(to_slot, v, preferred_element_type=jnp.float32).astype(jnp.bfloat16)  5.73 us
    dot_general x1, matrix products, inner_terms(): jnp.einsum('hts,shp->thp', affinity_logits, by_head, preferred_element_ty...  3.82 us
    dot_general x2, matrix products, place(): jnp.dot(to_place, values, preferred_element_type=jnp.float32)  3.34 us
  transfers between devices with their start and end apart: 2, of which 1 were waited for; matrix products, arithmetic and copies ran while one was open for 21% of the time, Pallas kernels for 0%

profile of v14, /device:TPU:1, one launch (start us, length us, event | category | flops | bytes accessed | tf_op | source)
XLA Modules:
  0.0 162.2 jit_solution(14255516051231671318)
XLA Ops:
  0.0 0.9 fusion.65
  0.9 1.2 reduce-window.24
  2.1 0.2 slice_reduce_fusion
  2.4 0.1 fusion.44
  2.5 0.7 fusion.66
  3.2 1.0 convolution_convert_fusion.7
  4.2 0.2 copy.65
  4.4 1.2 convolution_convert_fusion.5
  5.6 0.3 convolution_convert_fusion.6
  5.9 0.6 convolution_convert_fusion.4
  6.5 1.1 maximum_bitcast_fusion
  7.6 13.1 %all-to-all-start = ((bf16[64,8,1038]{2,1,0:T(8,128)(2,1)}), bf16[64,8,1038]{2,1,0:T(8,128)(2,1)S(1)}, u32[]{:S(2)}, u32[]{:S(2)}) async-start(bf16[64,8,1038]{2,1,0:T(8,128)(2,1)} %maximum_bitcast_fusion), calls=%async_computation | async-start | bytes 2359296 | tf_op jit(solution)/shard_map/all_to_all | solution.py:141
  20.8 0.2 reduce-window.31
  21.0 0.6 fusion.70
  21.7 0.7 slice.85
  23.7 0.5 fusion.76
  24.3 0.6 iota_compare_fusion.14
  24.8 0.5 iota_compare_fusion.18
  25.4 0.5 iota_compare_fusion.17
  25.9 2.6 %fusion.10 = bf16[64,8,768]{2,1,0:T(8,128)(2,1)} fusion(bf16[512,768]{1,0:T(8,128)(2,1)} %param.11, s32[512]{0:T(512)S(1)} %get-tuple-element.75), kind=kOutput, calls=%fused_computation.24 | convolution fusion | flops 403308544 | bytes 1574912 | tf_op jit(solution)/shard_map/dot_general | solution.py:136
  28.5 0.6 fusion.69
  29.1 0.6 iota_compare_fusion.16
  29.7 0.6 broadcast_and_fusion
  30.3 0.7 compare_convert_fusion.1
  31.0 0.9 fusion.14
  31.9 20.2 %all-to-all-done = bf16[64,8,1038]{2,1,0:T(8,128)(2,1)S(1)} async-done(((bf16[64,8,1038]{2,1,0:T(8,128)(2,1)}), bf16[64,8,1038]{2,1,0:T(8,128)(2,1)S(1)}, u32[]{:S(2)}, u32[]{:S(2)}) %all-to-all-start) | async-done | bytes 1062944 | tf_op jit(solution)/shard_map/all_to_all | solution.py:141
  52.1 6.4 %all-to-all-start.1 = ((bf16[64,8,768]{2,1,0:T(8,128)(2,1)}), bf16[64,8,768]{2,1,0:T(8,128)(2,1)}, u32[]{:S(2)}, u32[]{:S(2)}) async-start(bf16[64,8,768]{2,1,0:T(8,128)(2,1)} %fusion.10), calls=%async_computation.1 | async-start | bytes 1572864 | tf_op jit(solution)/shard_map/all_to_all | solution.py:141
  58.5 0.2 add_reduce_fusion
  58.7 0.8 convolution_convert_fusion.1
  59.6 0.9 copy-done.3
  60.6 1.2 reduce-window.32
  61.7 0.2 slice_reduce_fusion.1
  62.1 0.2 slice_reduce_fusion.2
  62.3 0.8 copy.68
  63.2 2.3 %fusion.13 = bf16[1,12,64,128]{3,2,1,0:T(8,128)(2,1)S(1)} fusion(bf16[512,12,64]{0,2,1:T(8,128)(2,1)S(1)} %bitcast.103, f32[12,512]{1,0:T(8,128)S(1)} %exponential_multiply_fusion.1, f32[512,128]{1,0:T(8,128)} %copy.68, f32[12]{0:T(128)S(1)} %get-tuple-element.76), kind=kOutput, calls=%fused_computation.30 | convolution fusion | flops 102432768 | bytes 1269808 | tf_op jit(solution)/shard_map/while/body/eval_jaxpr/hsn,shp->hpn/dot_general | solution.py:73
  65.7 2.3 %all_gather.15 = bf16[2,12,65,128]{3,2,1,0:T(8,128)(2,1)S(1)} all-gather(bf16[1,12,65,128]{3,2,1,0:T(8,128)(2,1)S(1)} %pad_maximum_fusion.1), channel_id=1, replica_groups=mesh['sx'=4,'sz'=8,'sc'=2,'head'=4] {'sc'}, dimensions={0}, use_global_device_ids=true | all-gather | bytes 599040 | tf_op jit(solution)/shard_map/all_gather | solution.py:38
  67.9 0.4 fusion.60
  68.3 0.1 select_reduce_fusion.5
  68.4 0.1 copy.75
  68.5 0.6 fusion.38
  69.4 25.6 %all_gather.16 = bf16[8,6,65,128]{3,2,1,0:T(8,128)(2,1)S(1)} all-gather(bf16[1,6,65,128]{3,2,1,0:T(8,128)(2,1)S(1)} %pad_maximum_fusion.2), channel_id=1, replica_groups=mesh['sx'=4,'sz'=8,'sc'=2,'head'=4] {'sz'}, dimensions={0}, use_global_device_ids=true | all-gather | bytes 898560 | tf_op jit(solution)/shard_map/all_gather | solution.py:38
  95.0 0.2 slice_reduce_fusion.3
  95.2 0.1 copy.90
  95.5 0.1 copy.86
  95.6 1.6 fusion.36
  97.2 0.8 copy.114
  98.1 0.3 select_reduce_fusion.1
  98.4 0.4 fusion.18
  98.8 0.4 fusion.20
  99.3 9.9 %all_gather.17 = bf16[4,6,65,128]{3,2,1,0:T(8,128)(2,1)S(1)} all-gather(bf16[1,6,65,128]{3,2,1,0:T(8,128)(2,1)S(1)} %pad_maximum_fusion.3), channel_id=1, replica_groups=mesh['sx'=4,'sz'=8,'sc'=2,'head'=4] {'sx'}, dimensions={0}, use_global_device_ids=true | all-gather | bytes 499200 | tf_op jit(solution)/shard_map/all_gather | solution.py:38
  109.2 0.1 fusion.59
  109.5 0.1 copy.81
  109.7 0.4 fusion.29
  110.2 10.3 %all_gather.18 = f32[12,64,128]{2,1,0:T(8,128)S(1)} all-gather(f32[6,64,128]{2,1,0:T(8,128)S(1)} %slice_add_fusion.2), channel_id=1, replica_groups=mesh['sx'=4,'sz'=8,'sc'=2,'head'=4] {'sc'}, dimensions={0}, use_global_device_ids=true | all-gather | bytes 589824 | tf_op jit(solution)/shard_map/all_gather | solution.py:58
  120.6 1.3 fusion.47
  121.9 3.8 %fusion = f32[12,64,512]{2,1,0:T(8,128)S(1)} fusion(bf16[512,12,64]{0,2,1:T(8,128)(2,1)S(1)} %bitcast.104, f32[12,512]{1,0:T(8,128)S(1)} %bitcast.116, f32[512,512]{1,0:T(8,128)S(1)} %fusion.47, pred[512,512]{1,0:T(8,128)(4,1)S(1)} %copy-done.6), kind=kOutput, calls=%fused_computation.1 | convolution fusion | flops 415236096 | bytes 3694592 | tf_op jit(solution)/shard_map/while/body/eval_jaxpr/hts,shp->thp/dot_general | solution.py:89
  125.8 3.1 %fusion.7 = f32[512,12,64]{0,2,1:T(8,128)} fusion(f32[12,64,512]{2,1,0:T(8,128)S(1)} %fusion, bf16[512,12,64]{0,2,1:T(8,128)(2,1)S(1)} %bitcast.105, f32[12]{0:T(128)S(1)} %copy-done.20, f32[512,12]{0,1:T(8,128)S(1)} %exponential_multiply_fusion, f32[12,65,128]{2,1,0:T(8,128)S(1)} %bitcast.107, f32[12,64,128]{2,1,0:T(8,128)S(1)} %all_gather.18, ...), kind=kOutput, calls=%fused_computation.16 | convolution fusion | flops 606142464 | bytes 4883456 | tf_op jit(solution)/shard_map/while/body/eval_jaxpr/tn,hpn->thp/dot_general | solution.py:94
  128.9 3.0 %copy.72 = f32[512,768]{1,0:T(8,128)} copy(f32[512,768]{0,1:T(8,128)} %bitcast.102) | data formatting | bytes 3145728 | tf_op jit(solution)/shard_map/reshape | solution.py:228
  131.9 2.5 %multiply_reduce_fusion = (f32[512]{0:T(512)S(1)}, f32[512,768]{1,0:T(8,128)S(1)}) fusion(f32[512,768]{1,0:T(8,128)} %copy.72, bf16[64,8,768]{2,1,0:T(8,128)(2,1)} %all-to-all-done.1, s32[512]{0:T(512)S(1)} %add_reduce_fusion), kind=kOutput, calls=%fused_computation.17 | convolution fusion | flops 406453760 | bytes 3936256 | tf_op jit(solution)/shard_map/dot_general | solution.py:162
  134.5 1.4 convolution_convert_fusion
  135.9 0.1 pad_maximum_fusion
  136.1 25.0 %all_to_all.15 = bf16[4,136,1536]{2,1,0:T(8,128)(2,1)S(1)} all-to-all(bf16[4,136,1536]{2,1,0:T(8,128)(2,1)S(1)} %pad_maximum_fusion), channel_id=1, replica_groups=mesh['sx'=4,'sz'=8,'sc'=2,'head'=4] {'head'}, dimensions={0} | all-to-all | bytes 3342336 | tf_op jit(solution)/shard_map/all_to_all | solution.py:244
  161.1 0.2 convert_reduce_fusion
  161.3 0.9 fusion.15
  (98 shorter events, 1.7 us)
Async XLA Ops:
  0.0 134.5 %copy-start = (bf16[768,1536]{1,0:T(8,128)(2,1)S(1)}, bf16[768,1536]{1,0:T(8,128)(2,1)}, u32[]{:S(2)}) copy-start(bf16[768,1536]{1,0:T(8,128)(2,1)} %param.19) | copy-start | bytes 7077892
  0.0 5.6 %copy-start.22 = (bf16[512,128]{1,0:T(8,128)(2,1)S(1)}, bf16[512,128]{1,0:T(8,128)(2,1)}, u32[]{:S(2)}) copy-start(bf16[512,128]{1,0:T(8,128)(2,1)} %param.12) | copy-start | bytes 393220
  0.0 5.9 %copy-start.21 = (bf16[512,768]{1,0:T(8,128)(2,1)S(1)}, bf16[512,768]{1,0:T(8,128)(2,1)}, u32[]{:S(2)}) copy-start(bf16[512,768]{1,0:T(8,128)(2,1)} %param.10) | copy-start | bytes 2359300
  7.6 13.2 %copy-start.9 = (s32[4]{0:T(128)S(1)}, s32[4]{0:T(128)}, u32[]{:S(2)}) copy-start(s32[4]{0:T(128)} %param.16) | copy-start | bytes 52
  7.6 44.5 %all-to-all-start = ((bf16[64,8,1038]{2,1,0:T(8,128)(2,1)}), bf16[64,8,1038]{2,1,0:T(8,128)(2,1)S(1)}, u32[]{:S(2)}, u32[]{:S(2)}) async-start(bf16[64,8,1038]{2,1,0:T(8,128)(2,1)} %maximum_bitcast_fusion), calls=%async_computation | async-start | bytes 2359296 | tf_op jit(solution)/shard_map/all_to_all | solution.py:141
  23.7 7.2 %copy-start.14 = (pred[2]{0:T(512)(128)(4,1)}, pred[2]{0:T(512)(128)(4,1)S(1)}, u32[]{:S(2)}) copy-start(pred[2]{0:T(512)(128)(4,1)S(1)} %iota_compare_fusion.19) | copy-start | bytes 10
  25.4 5.6 %copy-start.17 = (pred[8]{0:T(512)(128)(4,1)}, pred[8]{0:T(512)(128)(4,1)S(1)}, u32[]{:S(2)}) copy-start(pred[8]{0:T(512)(128)(4,1)S(1)} %get-tuple-element.92) | copy-start | bytes 28
  52.1 79.8 %all-to-all-start.1 = ((bf16[64,8,768]{2,1,0:T(8,128)(2,1)}), bf16[64,8,768]{2,1,0:T(8,128)(2,1)}, u32[]{:S(2)}, u32[]{:S(2)}) async-start(bf16[64,8,768]{2,1,0:T(8,128)(2,1)} %fusion.10), calls=%async_computation.1 | async-start | bytes 1572864 | tf_op jit(solution)/shard_map/all_to_all | solution.py:141
  59.5 1.0 copy-start.3
  59.6 5.9 %copy-start.1 = (bf16[512,768]{0,1:T(8,128)(2,1)}, bf16[512,768]{0,1:T(8,128)(2,1)S(1)}, u32[]{:S(2)}) copy-start(bf16[512,768]{0,1:T(8,128)(2,1)S(1)} %slice.100) | copy-start | bytes 2359300
  63.2 5.1 %copy-start.12 = (pred[2,2]{1,0:T(4,128)(4,1)S(1)}, pred[2,2]{1,0:T(4,128)(4,1)}, u32[]{:S(2)}) copy-start(pred[2,2]{1,0:T(4,128)(4,1)} %get-tuple-element.98) | copy-start | bytes 16
  63.2 5.1 %copy-start.13 = (pred[2,2]{1,0:T(4,128)(4,1)S(1)}, pred[2,2]{1,0:T(4,128)(4,1)}, u32[]{:S(2)}) copy-start(pred[2,2]{1,0:T(4,128)(4,1)} %get-tuple-element.99) | copy-start | bytes 16
  67.9 1.4 copy-start.5
  69.1 26.3 %copy-start.18 = (pred[8]{0:T(512)(128)(4,1)S(1)}, pred[8]{0:T(512)(128)(4,1)}, u32[]{:S(2)}) copy-start(pred[8]{0:T(512)(128)(4,1)} %copy-done.17) | copy-start | bytes 28
  69.1 26.3 %copy-start.16 = (f32[2]{0:T(128)S(1)}, f32[2]{0:T(128)}, u32[]{:S(2)}) copy-start(f32[2]{0:T(128)} %fusion.76) | copy-start | bytes 28
  69.4 28.7 %copy-start.7 = (pred[8,8]{1,0:T(8,128)(4,1)S(1)}, pred[8,8]{1,0:T(8,128)(4,1)}, u32[]{:S(2)}) copy-start(pred[8,8]{1,0:T(8,128)(4,1)} %iota_compare_fusion.14) | copy-start | bytes 196
  69.4 28.7 %copy-start.8 = (pred[8,8]{1,0:T(8,128)(4,1)S(1)}, pred[8,8]{1,0:T(8,128)(4,1)}, u32[]{:S(2)}) copy-start(pred[8,8]{1,0:T(8,128)(4,1)} %broadcast_and_fusion) | copy-start | bytes 196
  69.4 29.0 %copy-start.19 = (f32[8]{0:T(128)S(1)}, f32[8]{0:T(128)}, u32[]{:S(2)}) copy-start(f32[8]{0:T(128)} %get-tuple-element.94) | copy-start | bytes 100
  98.8 10.6 %copy-start.11 = (pred[4,4]{1,0:T(4,128)(4,1)S(1)}, pred[4,4]{1,0:T(4,128)(4,1)}, u32[]{:S(2)}) copy-start(pred[4,4]{1,0:T(4,128)(4,1)} %fusion.69) | copy-start | bytes 52
  98.8 10.7 %copy-start.10 = (f32[4]{0:T(128)S(1)}, f32[4]{0:T(128)}, u32[]{:S(2)}) copy-start(f32[4]{0:T(128)} %get-tuple-element.97) | copy-start | bytes 52
  99.3 21.2 %copy-start.15 = (pred[2]{0:T(512)(128)(4,1)S(1)}, pred[2]{0:T(512)(128)(4,1)}, u32[]{:S(2)}) copy-start(pred[2]{0:T(512)(128)(4,1)} %copy-done.14) | copy-start | bytes 10
  110.0 11.9 %copy-start.2 = (bf16[512,768]{0,1:T(8,128)(2,1)S(1)}, bf16[512,768]{0,1:T(8,128)(2,1)}, u32[]{:S(2)}) copy-start(bf16[512,768]{0,1:T(8,128)(2,1)} %copy-done.1) | copy-start | bytes 2359300
  110.0 11.9 %copy-start.6 = (pred[512,512]{1,0:T(8,128)(4,1)S(1)}, pred[512,512]{1,0:T(8,128)(4,1)}, u32[]{:S(2)}) copy-start(pred[512,512]{1,0:T(8,128)(4,1)} %fusion.14) | copy-start | bytes 786436
  121.9 3.8 %copy-start.4 = (f32[12,1,65,128]{3,2,0,1:T(8,128)S(1)}, f32[12,1,65,128]{3,2,0,1:T(8,128)}, u32[]{:S(2)}) copy-start(f32[12,1,65,128]{3,2,0,1:T(8,128)} %copy.114) | copy-start | bytes 1198084
  121.9 3.8 %copy-start.20 = (f32[12]{0:T(128)S(1)}, f32[12]{0:T(128)}, u32[]{:S(2)}) copy-start(f32[12]{0:T(128)} %param.17) | copy-start | bytes 148
  131.9 2.6 %copy-start.23 = (f32[768]{0:T(1024)S(1)}, f32[768]{0:T(1024)}, u32[]{:S(2)}) copy-start(f32[768]{0:T(1024)} %param.18) | copy-start | bytes 9220

commit v15 on v14

--- a/solution.py
+++ b/solution.py
@@ -147,8 +147,8 @@
         ).reshape(tok_dev, packed.shape[1])
 
     rows_out = jnp.concatenate(pieces[4:], axis=1)
-    gate_piece = pieces[1]
-    pieces = [pieces[0]] + pieces[2:4] + [rows_out]
+    late_pieces = [pieces[1], pieces[3]]
+    pieces = [pieces[0], pieces[2], rows_out]
     moved = send(pieces)
     columns = moved.shape[1]
     arrived = (
@@ -164,9 +164,10 @@
     rows = place(moved)
     features = rows[:, :feats]
     key_full = rows[:, feats : feats + n_state]
-    query_full = rows[:, feats + n_state : feats + 2 * n_state]
-    decays = rows[:, feats + 2 * n_state : feats + 2 * n_state + heads_here]
-    gate_moved = send([gate_piece])
+    decays = rows[:, feats + n_state : feats + n_state + heads_here]
+    late_rows = place(send(late_pieces))
+    gate_rows = late_rows[:, :feats]
+    query_full = late_rows[:, feats : feats + n_state]
 
     doc_starts = jnp.cumsum(doc_lengths) - doc_lengths
     first_place = lax.axis_index(ROWS) * tok_dev
@@ -226,7 +227,6 @@
         ),
     )
     mixed = mixed.reshape(tok_dev, heads_here * width)
-    gate_rows = place(gate_moved)
     gated = mixed * jax.nn.silu(gate_rows.astype(jnp.float32))
     squares = jnp.sum(gated * gated, axis=1)
     square_hi = squares.astype(jnp.bfloat16)

time: 163 us -> 168 us (1.031)
  blocking collectives: 73.1 us -> 76.1 us
    all_gather x3, blocking collectives: 37.8 us -> 40.5 us  [gathered_level(): gathered = lax.all_gather(pack_state(kept, state), axis)]
    reduce_sum x0 -> x1, other arithmetic: none -> 2.09 us  [body(): squares = jnp.sum(gated * gated, axis=1)]
  transfers between devices with their start and end apart: 2 -> 2, of which waited for: 1 -> 1; matrix products, arithmetic and copies ran while one was open for 21% -> 9% of each run, Pallas kernels for 0% -> 0%
where the time goes in v15:
time: 168 us; the launch traced here: 167 us
  blocking collectives  76.1 us (45%)
  matrix products  25.5 us (15%)
  waiting for transfers between devices  20.1 us (12%)
  starting transfers between devices  19.5 us (12%)
  other arithmetic  14.2 us (8%)
  local copies, waits for them, and re-layouts  9.81 us (6%)
  between operations  1.86 us (1%)
    all_gather x3, blocking collectives, gathered_level(): gathered = lax.all_gather(pack_state(kept, state), axis)  40.5 us
    all_to_all x1, blocking collectives, body(): lax.all_to_all(sent, 'head', split_axis=0, concat_axis=0, tiled=True)  25 us
    all_to_all x2, waiting for transfers between devices, send(): lax.all_to_all(packed.reshape(shards, capacity, packed.shape[1]), ROWS, s...  20.1 us
    all_to_all x2, starting transfers between devices, send(): lax.all_to_all(packed.reshape(shards, capacity, packed.shape[1]), ROWS, s...  19.5 us
    all_gather x1, blocking collectives, exclusive_prefix(): whole = lax.all_gather(start_state, pair, tiled=True)  10.5 us
    dot_general x5, matrix products, send(): jnp.dot(to_slot, v, preferred_element_type=jnp.float32).astype(jnp.bfloat16)  5.76 us
    dot_general x1, matrix products, inner_terms(): jnp.einsum('hts,shp->thp', affinity_logits, by_head, preferred_element_ty...  3.78 us
    dot_general x3, matrix products, gathered_level(): jnp.einsum('jh,jhpn->hpn', into_here, gathered.astype(jnp.float32))  3.39 us
  transfers between devices with their start and end apart: 2, of which 1 were waited for; matrix products, arithmetic and copies ran while one was open for 9% of the time, Pallas kernels for 0%

profile of v15, /device:TPU:1, one launch (start us, length us, event | category | flops | bytes accessed | tf_op | source)
XLA Modules:
  0.0 167.1 jit_solution(6275170289413834984)
XLA Ops:
  0.0 0.9 fusion.64
  0.9 1.2 reduce-window.24
  2.1 0.2 slice_reduce_fusion
  2.4 0.1 fusion.43
  2.5 0.7 fusion.65
  3.2 1.0 convolution_convert_fusion.7
  4.2 0.2 copy.59
  4.4 1.2 convolution_convert_fusion.6
  5.6 0.6 convolution_convert_fusion.4
  6.2 1.1 maximum_bitcast_fusion
  7.3 13.1 %all-to-all-start = ((bf16[64,8,910]{2,1,0:T(8,128)(2,1)}), bf16[64,8,910]{2,1,0:T(8,128)(2,1)S(1)}, u32[]{:S(2)}, u32[]{:S(2)}) async-start(bf16[64,8,910]{2,1,0:T(8,128)(2,1)} %maximum_bitcast_fusion), calls=%async_computation | async-start | bytes 2097152 | tf_op jit(solution)/shard_map/all_to_all | solution.py:141
  20.6 0.2 reduce-window.31
  20.7 0.6 fusion.69
  22.0 0.1 convert_reduce_fusion.1
  22.1 0.6 slice.88
  23.4 1.2 convolution_convert_fusion.5
  24.6 1.7 %convolution_convert_fusion.3 = bf16[512,768]{1,0:T(8,128)(2,1)S(1)} fusion(bf16[512,768]{1,0:T(8,128)(2,1)} %param.11, s32[512]{0:T(512)S(1)} %get-tuple-element.75), kind=kOutput, calls=%fused_computation.22 | convolution fusion | flops 403308544 | bytes 1574912 | tf_op jit(solution)/shard_map/dot_general | solution.py:136
  26.3 1.0 maximum_bitcast_fusion.1
  27.3 0.7 compare_convert_fusion.1
  28.0 0.9 fusion.13
  28.9 20.1 %all-to-all-done = bf16[64,8,910]{2,1,0:T(8,128)(2,1)S(1)} async-done(((bf16[64,8,910]{2,1,0:T(8,128)(2,1)}), bf16[64,8,910]{2,1,0:T(8,128)(2,1)S(1)}, u32[]{:S(2)}, u32[]{:S(2)}) %all-to-all-start) | async-done | bytes 931872 | tf_op jit(solution)/shard_map/all_to_all | solution.py:141
  49.0 6.4 %all-to-all-start.1 = ((bf16[64,8,896]{2,1,0:T(8,128)(2,1)}), bf16[64,8,896]{2,1,0:T(8,128)(2,1)}, u32[]{:S(2)}, u32[]{:S(2)}) async-start(bf16[64,8,896]{2,1,0:T(8,128)(2,1)} %maximum_bitcast_fusion.1), calls=%async_computation.1 | async-start | bytes 1835008 | tf_op jit(solution)/shard_map/all_to_all | solution.py:141
  55.4 0.2 add_reduce_fusion
  55.6 0.7 convolution_convert_fusion.1
  56.4 0.9 copy-done.5
  57.4 1.2 reduce-window.32
  58.5 0.2 slice_reduce_fusion.1
  58.9 0.2 slice_reduce_fusion.2
  59.1 0.8 copy.63
  60.0 2.3 %fusion.12 = bf16[1,12,64,128]{3,2,1,0:T(8,128)(2,1)S(1)} fusion(bf16[512,12,64]{0,2,1:T(8,128)(2,1)S(1)} %bitcast.101, f32[12,512]{1,0:T(8,128)S(1)} %exponential_multiply_fusion.1, f32[512,128]{1,0:T(8,128)} %copy.63, f32[12]{0:T(128)S(1)} %get-tuple-element.76), kind=kOutput, calls=%fused_computation.28 | convolution fusion | flops 102432768 | bytes 1269808 | tf_op jit(solution)/shard_map/while/body/eval_jaxpr/hsn,shp->hpn/dot_general | solution.py:73
  62.4 2.3 %all_gather.15 = bf16[2,12,65,128]{3,2,1,0:T(8,128)(2,1)S(1)} all-gather(bf16[1,12,65,128]{3,2,1,0:T(8,128)(2,1)S(1)} %pad_maximum_fusion.1), channel_id=1, replica_groups=mesh['sx'=4,'sz'=8,'sc'=2,'head'=4] {'sc'}, dimensions={0}, use_global_device_ids=true | all-gather | bytes 599040 | tf_op jit(solution)/shard_map/all_gather | solution.py:38
  64.7 0.4 fusion.59
  65.1 0.1 select_reduce_fusion.5
  65.2 0.1 copy.69
  65.3 0.6 fusion.37
  66.1 28.1 %all_gather.16 = bf16[8,6,65,128]{3,2,1,0:T(8,128)(2,1)S(1)} all-gather(bf16[1,6,65,128]{3,2,1,0:T(8,128)(2,1)S(1)} %pad_maximum_fusion.2), channel_id=1, replica_groups=mesh['sx'=4,'sz'=8,'sc'=2,'head'=4] {'sz'}, dimensions={0}, use_global_device_ids=true | all-gather | bytes 898560 | tf_op jit(solution)/shard_map/all_gather | solution.py:38
  94.2 0.2 slice_reduce_fusion.3
  94.4 0.1 copy.82
  94.8 1.9 %convolution_convert_fusion.2 = bf16[512,896]{1,0:T(8,128)(2,1)S(1)} fusion(bf16[64,8,896]{2,1,0:T(8,128)(2,1)} %all-to-all-done.1, s32[512]{0:T(512)S(1)} %add_reduce_fusion), kind=kOutput, calls=%fused_computation.21 | convolution fusion | flops 470482944 | bytes 1837056 | tf_op jit(solution)/shard_map/dot_general | solution.py:162
  96.7 0.9 copy-done.6
  97.6 2.2 %fusion.46 = f32[512,512]{1,0:T(8,128)} fusion(bf16[512,910]{0,1:T(8,128)(2,1)} %copy-done.5, bf16[512,896]{1,0:T(8,128)(2,1)S(1)} %convolution_convert_fusion.2), kind=kOutput, calls=%fused_computation.89 | convolution fusion | flops 67108864 | bytes 1310720 | tf_op jit(solution)/shard_map/while/body/eval_jaxpr/tn,sn->ts/dot_general | solution.py:87
  99.9 0.1 copy.80
  100.0 1.6 fusion.35
  101.6 0.8 copy.106
  102.4 0.3 select_reduce_fusion.1
  102.7 0.4 fusion.17
  103.1 0.3 fusion.19
  103.6 10.2 %all_gather.17 = bf16[4,6,65,128]{3,2,1,0:T(8,128)(2,1)S(1)} all-gather(bf16[1,6,65,128]{3,2,1,0:T(8,128)(2,1)S(1)} %pad_maximum_fusion.3), channel_id=1, replica_groups=mesh['sx'=4,'sz'=8,'sc'=2,'head'=4] {'sx'}, dimensions={0}, use_global_device_ids=true | all-gather | bytes 499200 | tf_op jit(solution)/shard_map/all_gather | solution.py:38
  113.8 0.8 copy-done.10
  114.5 0.1 fusion.58
  114.7 0.1 select_reduce_fusion.2
  114.8 0.1 copy.75
  114.9 1.5 fusion.28
  116.4 0.1 slice_add_fusion.2
  116.5 10.5 %all_gather.18 = f32[12,64,128]{2,1,0:T(8,128)S(1)} all-gather(f32[6,64,128]{2,1,0:T(8,128)S(1)} %slice_add_fusion.2), channel_id=1, replica_groups=mesh['sx'=4,'sz'=8,'sc'=2,'head'=4] {'sc'}, dimensions={0}, use_global_device_ids=true | all-gather | bytes 589824 | tf_op jit(solution)/shard_map/all_gather | solution.py:58
  127.1 3.8 %fusion = f32[12,64,512]{2,1,0:T(8,128)S(1)} fusion(bf16[512,12,64]{0,2,1:T(8,128)(2,1)S(1)} %bitcast.102, f32[12,512]{1,0:T(8,128)S(1)} %bitcast.114, f32[512,512]{1,0:T(8,128)S(1)} %copy-done.8, pred[512,512]{1,0:T(8,128)(4,1)S(1)} %copy-done.11), kind=kOutput, calls=%fused_computation.1 | convolution fusion | flops 415236096 | bytes 3694592 | tf_op jit(solution)/shard_map/while/body/eval_jaxpr/hts,shp->thp/dot_general | solution.py:89
  130.9 3.1 %fusion.7 = f32[512,12,64]{0,2,1:T(8,128)} fusion(f32[12,64,512]{2,1,0:T(8,128)S(1)} %fusion, bf16[512,12,64]{0,2,1:T(8,128)(2,1)S(1)} %bitcast.103, f32[12]{0:T(128)S(1)} %copy-done.13, f32[512,12]{0,1:T(8,128)S(1)} %exponential_multiply_fusion, f32[12,65,128]{2,1,0:T(8,128)S(1)} %bitcast.105, f32[12,64,128]{2,1,0:T(8,128)S(1)} %all_gather.18, ...), kind=kOutput, calls=%fused_computation.15 | convolution fusion | flops 606142464 | bytes 4883456 | tf_op jit(solution)/shard_map/while/body/eval_jaxpr/tn,hpn->thp/dot_general | solution.py:94
  134.0 3.1 %copy.66 = f32[512,768]{1,0:T(8,128)} copy(f32[512,768]{0,1:T(8,128)} %bitcast.100) | data formatting | bytes 3145728 | tf_op jit(solution)/shard_map/reshape | solution.py:229
  137.2 2.1 %multiply_reduce_fusion = f32[512]{0:T(512)S(1)} fusion(f32[512,768]{1,0:T(8,128)} %copy.66, bf16[512,896]{1,0:T(8,128)(2,1)S(1)} %copy-done.7), kind=kLoop, calls=%fused_computation.16 | loop fusion | flops 3145216 | bytes 2361344 | tf_op jit(solution)/shard_map/reduce_sum | solution.py:231
  139.3 1.5 convolution_convert_fusion
  140.8 0.1 pad_maximum_fusion
  141.0 25.0 %all_to_all.15 = bf16[4,136,1536]{2,1,0:T(8,128)(2,1)S(1)} all-to-all(bf16[4,136,1536]{2,1,0:T(8,128)(2,1)S(1)} %pad_maximum_fusion), channel_id=1, replica_groups=mesh['sx'=4,'sz'=8,'sc'=2,'head'=4] {'head'}, dimensions={0} | all-to-all | bytes 3342336 | tf_op jit(solution)/shard_map/all_to_all | solution.py:244
  165.9 0.2 convert_reduce_fusion
  166.2 0.9 fusion.15
  (84 shorter events, 1.4 us)
Async XLA Ops:
  0.0 139.3 %copy-start = (bf16[768,1536]{1,0:T(8,128)(2,1)S(1)}, bf16[768,1536]{1,0:T(8,128)(2,1)}, u32[]{:S(2)}) copy-start(bf16[768,1536]{1,0:T(8,128)(2,1)} %param.19) | copy-start | bytes 7077892
  0.0 5.6 %copy-start.14 = (bf16[512,768]{1,0:T(8,128)(2,1)S(1)}, bf16[512,768]{1,0:T(8,128)(2,1)}, u32[]{:S(2)}) copy-start(bf16[512,768]{1,0:T(8,128)(2,1)} %param.10) | copy-start | bytes 2359300
  7.3 13.2 %copy-start.12 = (s32[4]{0:T(128)S(1)}, s32[4]{0:T(128)}, u32[]{:S(2)}) copy-start(s32[4]{0:T(128)} %param.16) | copy-start | bytes 52
  7.3 41.7 %all-to-all-start = ((bf16[64,8,910]{2,1,0:T(8,128)(2,1)}), bf16[64,8,910]{2,1,0:T(8,128)(2,1)S(1)}, u32[]{:S(2)}, u32[]{:S(2)}) async-start(bf16[64,8,910]{2,1,0:T(8,128)(2,1)} %maximum_bitcast_fusion), calls=%async_computation | async-start | bytes 2097152 | tf_op jit(solution)/shard_map/all_to_all | solution.py:141
  49.0 45.8 %all-to-all-start.1 = ((bf16[64,8,896]{2,1,0:T(8,128)(2,1)}), bf16[64,8,896]{2,1,0:T(8,128)(2,1)}, u32[]{:S(2)}, u32[]{:S(2)}) async-start(bf16[64,8,896]{2,1,0:T(8,128)(2,1)} %maximum_bitcast_fusion.1), calls=%async_computation.1 | async-start | bytes 1835008 | tf_op jit(solution)/shard_map/all_to_all | solution.py:141
  56.4 0.9 copy-start.5
  57.3 5.0 %copy-start.2 = (bf16[512,768]{0,1:T(8,128)(2,1)}, bf16[512,768]{0,1:T(8,128)(2,1)S(1)}, u32[]{:S(2)}) copy-start(bf16[512,768]{0,1:T(8,128)(2,1)S(1)} %slice.104) | copy-start | bytes 2359300
  64.7 1.3 copy-start.9
  96.7 0.9 copy-start.6
  103.6 23.5 %copy-start.3 = (bf16[512,768]{0,1:T(8,128)(2,1)S(1)}, bf16[512,768]{0,1:T(8,128)(2,1)}, u32[]{:S(2)}) copy-start(bf16[512,768]{0,1:T(8,128)(2,1)} %copy-done.2) | copy-start | bytes 2359300
  113.8 0.8 copy-start.10
  114.9 12.1 %copy-start.8 = (f32[512,512]{1,0:T(8,128)S(1)}, f32[512,512]{1,0:T(8,128)}, u32[]{:S(2)}) copy-start(f32[512,512]{1,0:T(8,128)} %fusion.46) | copy-start | bytes 3145732
  114.9 12.1 %copy-start.11 = (pred[512,512]{1,0:T(8,128)(4,1)S(1)}, pred[512,512]{1,0:T(8,128)(4,1)}, u32[]{:S(2)}) copy-start(pred[512,512]{1,0:T(8,128)(4,1)} %fusion.13) | copy-start | bytes 786436
  127.1 3.8 %copy-start.4 = (f32[12,1,65,128]{3,2,0,1:T(8,128)S(1)}, f32[12,1,65,128]{3,2,0,1:T(8,128)}, u32[]{:S(2)}) copy-start(f32[12,1,65,128]{3,2,0,1:T(8,128)} %copy.106) | copy-start | bytes 1198084
  127.1 3.8 %copy-start.13 = (f32[12]{0:T(128)S(1)}, f32[12]{0:T(128)}, u32[]{:S(2)}) copy-start(f32[12]{0:T(128)} %param.17) | copy-start | bytes 148
  134.0 3.1 %copy-start.7 = (bf16[512,896]{1,0:T(8,128)(2,1)S(1)}, bf16[512,896]{1,0:T(8,128)(2,1)}, u32[]{:S(2)}) copy-start(bf16[512,896]{1,0:T(8,128)(2,1)} %copy-done.6) | copy-start | bytes 2752516
  137.1 2.1 %copy-start.1 = (f32[512,768]{1,0:T(8,128)S(1)}, f32[512,768]{1,0:T(8,128)}, u32[]{:S(2)}) copy-start(f32[512,768]{1,0:T(8,128)} %copy.66) | copy-start | bytes 4718596
  137.2 2.1 %copy-start.15 = (f32[768]{0:T(1024)S(1)}, f32[768]{0:T(1024)}, u32[]{:S(2)}) copy-start(f32[768]{0:T(1024)} %param.18) | copy-start | bytes 9220

commit v16 on v14

--- a/solution.py
+++ b/solution.py
@@ -239,7 +239,7 @@
     extra = jnp.concatenate(
         [square_hi.reshape(groups, 1, chunk), square_lo.reshape(groups, 1, chunk)], axis=1
     )
-    extra = jnp.pad(extra, ((0, 0), (0, 6), (0, d_model - chunk)))
+    extra = jnp.pad(extra, ((0, 0), (0, 0), (0, d_model - chunk)))
     sent = jnp.concatenate([partial.reshape(groups, chunk, d_model), extra], axis=1)
     arrived_parts = lax.all_to_all(sent, "head", split_axis=0, concat_axis=0, tiled=True)
     summed = jnp.sum(arrived_parts.astype(jnp.float32), axis=0)

time: 163 us -> 163 us (level)
  no operation moved by 1% of the time
where the time goes in v16:
time: 163 us; the launch traced here: 162 us
  blocking collectives  73.1 us (45%)
  matrix products  24.2 us (15%)
  waiting for transfers between devices  20.2 us (12%)
  starting transfers between devices  19.5 us (12%)
  other arithmetic  15 us (9%)
  local copies, waits for them, and re-layouts  8.16 us (5%)
  between operations  1.97 us (1%)
    all_gather x3, blocking collectives, gathered_level(): gathered = lax.all_gather(pack_state(kept, state), axis)  37.8 us
    all_to_all x1, blocking collectives, body(): lax.all_to_all(sent, 'head', split_axis=0, concat_axis=0, tiled=True)  25 us
    all_to_all x2, waiting for transfers between devices, send(): lax.all_to_all(packed.reshape(shards, capacity, packed.shape[1]), ROWS, s...  20.2 us
    all_to_all x2, starting transfers between devices, send(): lax.all_to_all(packed.reshape(shards, capacity, packed.shape[1]), ROWS, s...  19.5 us
    all_gather x1, blocking collectives, exclusive_prefix(): whole = lax.all_gather(start_state, pair, tiled=True)  10.3 us
    dot_general x5, matrix products, send(): jnp.dot(to_slot, v, preferred_element_type=jnp.float32).astype(jnp.bfloat16)  5.73 us
    dot_general x1, matrix products, inner_terms(): jnp.einsum('hts,shp->thp', affinity_logits, by_head, preferred_element_ty...  3.82 us
    dot_general x2, matrix products, place(): jnp.dot(to_place, values, preferred_element_type=jnp.float32)  3.34 us
  transfers between devices with their start and end apart: 2, of which 1 were waited for; matrix products, arithmetic and copies ran while one was open for 21% of the time, Pallas kernels for 0%

profile of v16, /device:TPU:1, one launch (start us, length us, event | category | flops | bytes accessed | tf_op | source)
XLA Modules:
  0.0 162.2 jit_solution(15223109769230698368)
XLA Ops:
  0.0 0.9 fusion.62
  0.9 1.2 reduce-window.24
  2.1 0.2 slice_reduce_fusion
  2.4 0.1 fusion.39
  2.5 0.7 fusion.63
  3.2 1.0 convolution_convert_fusion.7
  4.2 0.2 copy.65
  4.4 1.2 convolution_convert_fusion.5
  5.6 0.3 convolution_convert_fusion.6
  5.9 0.6 convolution_convert_fusion.4
  6.5 1.1 maximum_bitcast_fusion
  7.6 13.1 %all-to-all-start = ((bf16[64,8,1038]{2,1,0:T(8,128)(2,1)}), bf16[64,8,1038]{2,1,0:T(8,128)(2,1)S(1)}, u32[]{:S(2)}, u32[]{:S(2)}) async-start(bf16[64,8,1038]{2,1,0:T(8,128)(2,1)} %maximum_bitcast_fusion), calls=%async_computation | async-start | bytes 2359296 | tf_op jit(solution)/shard_map/all_to_all | solution.py:141
  20.8 0.2 reduce-window.31
  21.0 0.6 fusion.67
  21.7 0.7 slice.85
  23.7 0.5 fusion.73
  24.3 0.6 iota_compare_fusion.13
  24.8 0.5 iota_compare_fusion.17
  25.4 0.5 iota_compare_fusion.16
  25.9 2.6 %fusion.10 = bf16[64,8,768]{2,1,0:T(8,128)(2,1)} fusion(bf16[512,768]{1,0:T(8,128)(2,1)} %param.11, s32[512]{0:T(512)S(1)} %get-tuple-element.75), kind=kOutput, calls=%fused_computation.24 | convolution fusion | flops 403308544 | bytes 1574912 | tf_op jit(solution)/shard_map/dot_general | solution.py:136
  28.5 0.6 fusion.66
  29.1 0.6 iota_compare_fusion.15
  29.7 0.6 broadcast_and_fusion
  30.3 0.7 compare_convert_fusion.1
  31.0 0.9 fusion.14
  31.9 20.2 %all-to-all-done = bf16[64,8,1038]{2,1,0:T(8,128)(2,1)S(1)} async-done(((bf16[64,8,1038]{2,1,0:T(8,128)(2,1)}), bf16[64,8,1038]{2,1,0:T(8,128)(2,1)S(1)}, u32[]{:S(2)}, u32[]{:S(2)}) %all-to-all-start) | async-done | bytes 1062944 | tf_op jit(solution)/shard_map/all_to_all | solution.py:141
  52.1 6.4 %all-to-all-start.1 = ((bf16[64,8,768]{2,1,0:T(8,128)(2,1)}), bf16[64,8,768]{2,1,0:T(8,128)(2,1)}, u32[]{:S(2)}, u32[]{:S(2)}) async-start(bf16[64,8,768]{2,1,0:T(8,128)(2,1)} %fusion.10), calls=%async_computation.1 | async-start | bytes 1572864 | tf_op jit(solution)/shard_map/all_to_all | solution.py:141
  58.5 0.2 add_reduce_fusion
  58.7 0.8 convolution_convert_fusion.1
  59.6 0.9 copy-done.3
  60.6 1.2 reduce-window.32
  61.7 0.2 slice_reduce_fusion.1
  62.1 0.2 slice_reduce_fusion.2
  62.3 0.8 copy.68
  63.2 2.3 %fusion.13 = bf16[1,12,64,128]{3,2,1,0:T(8,128)(2,1)S(1)} fusion(bf16[512,12,64]{0,2,1:T(8,128)(2,1)S(1)} %bitcast.103, f32[12,512]{1,0:T(8,128)S(1)} %exponential_multiply_fusion.1, f32[512,128]{1,0:T(8,128)} %copy.68, f32[12]{0:T(128)S(1)} %get-tuple-element.76), kind=kOutput, calls=%fused_computation.30 | convolution fusion | flops 102432768 | bytes 1269808 | tf_op jit(solution)/shard_map/while/body/eval_jaxpr/hsn,shp->hpn/dot_general | solution.py:73
  65.7 2.3 %all_gather.15 = bf16[2,12,65,128]{3,2,1,0:T(8,128)(2,1)S(1)} all-gather(bf16[1,12,65,128]{3,2,1,0:T(8,128)(2,1)S(1)} %pad_maximum_fusion.1), channel_id=1, replica_groups=mesh['sx'=4,'sz'=8,'sc'=2,'head'=4] {'sc'}, dimensions={0}, use_global_device_ids=true | all-gather | bytes 599040 | tf_op jit(solution)/shard_map/all_gather | solution.py:38
  67.9 0.4 fusion.57
  68.3 0.1 select_reduce_fusion.5
  68.4 0.1 copy.75
  68.5 0.6 fusion.35
  69.4 25.6 %all_gather.16 = bf16[8,6,65,128]{3,2,1,0:T(8,128)(2,1)S(1)} all-gather(bf16[1,6,65,128]{3,2,1,0:T(8,128)(2,1)S(1)} %pad_maximum_fusion.2), channel_id=1, replica_groups=mesh['sx'=4,'sz'=8,'sc'=2,'head'=4] {'sz'}, dimensions={0}, use_global_device_ids=true | all-gather | bytes 898560 | tf_op jit(solution)/shard_map/all_gather | solution.py:38
  95.0 0.2 slice_reduce_fusion.3
  95.2 0.1 copy.90
  95.5 0.1 copy.86
  95.6 1.6 fusion.33
  97.2 0.8 copy.114
  98.1 0.3 select_reduce_fusion.1
  98.4 0.4 fusion.18
  98.8 0.4 fusion.20
  99.3 9.9 %all_gather.17 = bf16[4,6,65,128]{3,2,1,0:T(8,128)(2,1)S(1)} all-gather(bf16[1,6,65,128]{3,2,1,0:T(8,128)(2,1)S(1)} %pad_maximum_fusion.3), channel_id=1, replica_groups=mesh['sx'=4,'sz'=8,'sc'=2,'head'=4] {'sx'}, dimensions={0}, use_global_device_ids=true | all-gather | bytes 499200 | tf_op jit(solution)/shard_map/all_gather | solution.py:38
  109.2 0.1 fusion.56
  109.5 0.1 copy.81
  109.7 0.4 fusion.29
  110.2 10.3 %all_gather.18 = f32[12,64,128]{2,1,0:T(8,128)S(1)} all-gather(f32[6,64,128]{2,1,0:T(8,128)S(1)} %slice_add_fusion.2), channel_id=1, replica_groups=mesh['sx'=4,'sz'=8,'sc'=2,'head'=4] {'sc'}, dimensions={0}, use_global_device_ids=true | all-gather | bytes 589824 | tf_op jit(solution)/shard_map/all_gather | solution.py:58
  120.6 1.3 fusion.42
  121.9 3.8 %fusion = f32[12,64,512]{2,1,0:T(8,128)S(1)} fusion(bf16[512,12,64]{0,2,1:T(8,128)(2,1)S(1)} %bitcast.104, f32[12,512]{1,0:T(8,128)S(1)} %bitcast.116, f32[512,512]{1,0:T(8,128)S(1)} %fusion.42, pred[512,512]{1,0:T(8,128)(4,1)S(1)} %copy-done.6), kind=kOutput, calls=%fused_computation.1 | convolution fusion | flops 415236096 | bytes 3694592 | tf_op jit(solution)/shard_map/while/body/eval_jaxpr/hts,shp->thp/dot_general | solution.py:89
  125.8 3.1 %fusion.7 = f32[512,12,64]{0,2,1:T(8,128)} fusion(f32[12,64,512]{2,1,0:T(8,128)S(1)} %fusion, bf16[512,12,64]{0,2,1:T(8,128)(2,1)S(1)} %bitcast.105, f32[12]{0:T(128)S(1)} %copy-done.20, f32[512,12]{0,1:T(8,128)S(1)} %exponential_multiply_fusion, f32[12,65,128]{2,1,0:T(8,128)S(1)} %bitcast.107, f32[12,64,128]{2,1,0:T(8,128)S(1)} %all_gather.18, ...), kind=kOutput, calls=%fused_computation.16 | convolution fusion | flops 606142464 | bytes 4883456 | tf_op jit(solution)/shard_map/while/body/eval_jaxpr/tn,hpn->thp/dot_general | solution.py:94
  128.9 3.0 %copy.72 = f32[512,768]{1,0:T(8,128)} copy(f32[512,768]{0,1:T(8,128)} %bitcast.102) | data formatting | bytes 3145728 | tf_op jit(solution)/shard_map/reshape | solution.py:228
  131.9 2.5 %multiply_reduce_fusion = (f32[512]{0:T(512)S(1)}, f32[512,768]{1,0:T(8,128)S(1)}) fusion(f32[512,768]{1,0:T(8,128)} %copy.72, bf16[64,8,768]{2,1,0:T(8,128)(2,1)} %all-to-all-done.1, s32[512]{0:T(512)S(1)} %add_reduce_fusion), kind=kOutput, calls=%fused_computation.17 | convolution fusion | flops 406453760 | bytes 3936256 | tf_op jit(solution)/shard_map/dot_general | solution.py:162
  134.5 1.4 convolution_convert_fusion
  135.9 0.1 pad_maximum_fusion
  136.1 25.0 %all_to_all.15 = bf16[4,130,1536]{2,1,0:T(8,128)(2,1)S(1)} all-to-all(bf16[4,130,1536]{2,1,0:T(8,128)(2,1)S(1)} %pad_maximum_fusion), channel_id=1, replica_groups=mesh['sx'=4,'sz'=8,'sc'=2,'head'=4] {'head'}, dimensions={0} | all-to-all | bytes 3194880 | tf_op jit(solution)/shard_map/all_to_all | solution.py:244
  161.1 0.2 convert_reduce_fusion
  161.3 0.9 fusion.15
  (98 shorter events, 1.7 us)
Async XLA Ops:
  0.0 134.5 %copy-start = (bf16[768,1536]{1,0:T(8,128)(2,1)S(1)}, bf16[768,1536]{1,0:T(8,128)(2,1)}, u32[]{:S(2)}) copy-start(bf16[768,1536]{1,0:T(8,128)(2,1)} %param.19) | copy-start | bytes 7077892
  0.0 5.6 %copy-start.22 = (bf16[512,128]{1,0:T(8,128)(2,1)S(1)}, bf16[512,128]{1,0:T(8,128)(2,1)}, u32[]{:S(2)}) copy-start(bf16[512,128]{1,0:T(8,128)(2,1)} %param.12) | copy-start | bytes 393220
  0.0 5.9 %copy-start.21 = (bf16[512,768]{1,0:T(8,128)(2,1)S(1)}, bf16[512,768]{1,0:T(8,128)(2,1)}, u32[]{:S(2)}) copy-start(bf16[512,768]{1,0:T(8,128)(2,1)} %param.10) | copy-start | bytes 2359300
  7.6 13.2 %copy-start.9 = (s32[4]{0:T(128)S(1)}, s32[4]{0:T(128)}, u32[]{:S(2)}) copy-start(s32[4]{0:T(128)} %param.16) | copy-start | bytes 52
  7.6 44.5 %all-to-all-start = ((bf16[64,8,1038]{2,1,0:T(8,128)(2,1)}), bf16[64,8,1038]{2,1,0:T(8,128)(2,1)S(1)}, u32[]{:S(2)}, u32[]{:S(2)}) async-start(bf16[64,8,1038]{2,1,0:T(8,128)(2,1)} %maximum_bitcast_fusion), calls=%async_computation | async-start | bytes 2359296 | tf_op jit(solution)/shard_map/all_to_all | solution.py:141
  23.7 7.2 %copy-start.14 = (pred[2]{0:T(512)(128)(4,1)}, pred[2]{0:T(512)(128)(4,1)S(1)}, u32[]{:S(2)}) copy-start(pred[2]{0:T(512)(128)(4,1)S(1)} %iota_compare_fusion.18) | copy-start | bytes 10
  25.4 5.6 %copy-start.17 = (pred[8]{0:T(512)(128)(4,1)}, pred[8]{0:T(512)(128)(4,1)S(1)}, u32[]{:S(2)}) copy-start(pred[8]{0:T(512)(128)(4,1)S(1)} %get-tuple-element.92) | copy-start | bytes 28
  52.1 79.8 %all-to-all-start.1 = ((bf16[64,8,768]{2,1,0:T(8,128)(2,1)}), bf16[64,8,768]{2,1,0:T(8,128)(2,1)}, u32[]{:S(2)}, u32[]{:S(2)}) async-start(bf16[64,8,768]{2,1,0:T(8,128)(2,1)} %fusion.10), calls=%async_computation.1 | async-start | bytes 1572864 | tf_op jit(solution)/shard_map/all_to_all | solution.py:141
  59.5 1.0 copy-start.3
  59.6 5.9 %copy-start.1 = (bf16[512,768]{0,1:T(8,128)(2,1)}, bf16[512,768]{0,1:T(8,128)(2,1)S(1)}, u32[]{:S(2)}) copy-start(bf16[512,768]{0,1:T(8,128)(2,1)S(1)} %slice.100) | copy-start | bytes 2359300
  63.2 5.1 %copy-start.12 = (pred[2,2]{1,0:T(4,128)(4,1)S(1)}, pred[2,2]{1,0:T(4,128)(4,1)}, u32[]{:S(2)}) copy-start(pred[2,2]{1,0:T(4,128)(4,1)} %get-tuple-element.98) | copy-start | bytes 16
  63.2 5.1 %copy-start.13 = (pred[2,2]{1,0:T(4,128)(4,1)S(1)}, pred[2,2]{1,0:T(4,128)(4,1)}, u32[]{:S(2)}) copy-start(pred[2,2]{1,0:T(4,128)(4,1)} %get-tuple-element.99) | copy-start | bytes 16
  67.9 1.4 copy-start.5
  69.1 26.3 %copy-start.18 = (pred[8]{0:T(512)(128)(4,1)S(1)}, pred[8]{0:T(512)(128)(4,1)}, u32[]{:S(2)}) copy-start(pred[8]{0:T(512)(128)(4,1)} %copy-done.17) | copy-start | bytes 28
  69.1 26.3 %copy-start.16 = (f32[2]{0:T(128)S(1)}, f32[2]{0:T(128)}, u32[]{:S(2)}) copy-start(f32[2]{0:T(128)} %fusion.73) | copy-start | bytes 28
  69.4 28.7 %copy-start.7 = (pred[8,8]{1,0:T(8,128)(4,1)S(1)}, pred[8,8]{1,0:T(8,128)(4,1)}, u32[]{:S(2)}) copy-start(pred[8,8]{1,0:T(8,128)(4,1)} %iota_compare_fusion.13) | copy-start | bytes 196
  69.4 28.7 %copy-start.8 = (pred[8,8]{1,0:T(8,128)(4,1)S(1)}, pred[8,8]{1,0:T(8,128)(4,1)}, u32[]{:S(2)}) copy-start(pred[8,8]{1,0:T(8,128)(4,1)} %broadcast_and_fusion) | copy-start | bytes 196
  69.4 29.0 %copy-start.19 = (f32[8]{0:T(128)S(1)}, f32[8]{0:T(128)}, u32[]{:S(2)}) copy-start(f32[8]{0:T(128)} %get-tuple-element.94) | copy-start | bytes 100
  98.8 10.6 %copy-start.11 = (pred[4,4]{1,0:T(4,128)(4,1)S(1)}, pred[4,4]{1,0:T(4,128)(4,1)}, u32[]{:S(2)}) copy-start(pred[4,4]{1,0:T(4,128)(4,1)} %fusion.66) | copy-start | bytes 52
  98.8 10.7 %copy-start.10 = (f32[4]{0:T(128)S(1)}, f32[4]{0:T(128)}, u32[]{:S(2)}) copy-start(f32[4]{0:T(128)} %get-tuple-element.97) | copy-start | bytes 52
  99.3 21.2 %copy-start.15 = (pred[2]{0:T(512)(128)(4,1)S(1)}, pred[2]{0:T(512)(128)(4,1)}, u32[]{:S(2)}) copy-start(pred[2]{0:T(512)(128)(4,1)} %copy-done.14) | copy-start | bytes 10
  110.0 11.9 %copy-start.2 = (bf16[512,768]{0,1:T(8,128)(2,1)S(1)}, bf16[512,768]{0,1:T(8,128)(2,1)}, u32[]{:S(2)}) copy-start(bf16[512,768]{0,1:T(8,128)(2,1)} %copy-done.1) | copy-start | bytes 2359300
  110.0 11.9 %copy-start.6 = (pred[512,512]{1,0:T(8,128)(4,1)S(1)}, pred[512,512]{1,0:T(8,128)(4,1)}, u32[]{:S(2)}) copy-start(pred[512,512]{1,0:T(8,128)(4,1)} %fusion.14) | copy-start | bytes 786436
  121.9 3.8 %copy-start.4 = (f32[12,1,65,128]{3,2,0,1:T(8,128)S(1)}, f32[12,1,65,128]{3,2,0,1:T(8,128)}, u32[]{:S(2)}) copy-start(f32[12,1,65,128]{3,2,0,1:T(8,128)} %copy.114) | copy-start | bytes 1198084
  121.9 3.8 %copy-start.20 = (f32[12]{0:T(128)S(1)}, f32[12]{0:T(128)}, u32[]{:S(2)}) copy-start(f32[12]{0:T(128)} %param.17) | copy-start | bytes 148
  131.9 2.6 %copy-start.23 = (f32[768]{0:T(1024)S(1)}, f32[768]{0:T(1024)}, u32[]{:S(2)}) copy-start(f32[768]{0:T(1024)} %param.18) | copy-start | bytes 9220

commit v17 on v14

--- a/solution.py
+++ b/solution.py
@@ -86,15 +86,15 @@
     )
     products = jnp.einsum("tn,sn->ts", query_block, key_block, preferred_element_type=jnp.float32)
     affinity_logits = (products[None, :, :] * jnp.exp(decay_gaps)).astype(jnp.bfloat16)
-    return jnp.einsum("hts,shp->thp", affinity_logits, by_head, preferred_element_type=jnp.float32)
+    return jnp.einsum("hts,shp->htp", affinity_logits, by_head, preferred_element_type=jnp.float32)
 
 
 def entry_terms(query_block, carry_state, running, doc_block, before):
     entry_weight = jnp.exp(running) * (doc_block == before).astype(jnp.float32)[:, None]
     carried = jnp.einsum(
-        "tn,hpn->thp", query_block.astype(jnp.float32), carry_state, precision=lax.Precision.HIGHEST
-    )
-    return carried * entry_weight[:, :, None]
+        "tn,hpn->htp", query_block.astype(jnp.float32), carry_state, precision=lax.Precision.HIGHEST
+    )
+    return carried * entry_weight.T[:, :, None]
 
 
 def body(
@@ -207,7 +207,7 @@
         mixed_block = (
             inner_terms(by_head, key_block, query_block, running, doc_block)
             + carried
-            + skip_gain[None, :, None] * by_head.astype(jnp.float32)
+            + skip_gain[:, None, None] * by_head.astype(jnp.float32).transpose(1, 0, 2)
         )
         return (through[:, None, None] * carry_state + block_state, mixed_block)
 
@@ -225,14 +225,19 @@
             throughs,
         ),
     )
-    mixed = mixed.reshape(tok_dev, heads_here * width)
-    gate_rows = place(gate_moved)
+    mixed = mixed.transpose(1, 0, 2, 3).reshape(heads_here, tok_dev, width)
+    gate_rows = place(gate_moved).reshape(tok_dev, heads_here, width).transpose(1, 0, 2)
     gated = mixed * jax.nn.silu(gate_rows.astype(jnp.float32))
-    squares = jnp.sum(gated * gated, axis=1)
+    squares = jnp.sum(gated * gated, axis=(0, 2))
     square_hi = squares.astype(jnp.bfloat16)
     square_lo = (squares - square_hi.astype(jnp.float32)).astype(jnp.bfloat16)
-    unscaled = (gated * norm_gain[None, :]).astype(jnp.bfloat16)
-    partial = jnp.dot(unscaled, out_weight, preferred_element_type=jnp.float32).astype(jnp.bfloat16)
+    unscaled = (gated * norm_gain.reshape(heads_here, 1, width)).astype(jnp.bfloat16)
+    partial = jnp.einsum(
+        "htp,hpd->td",
+        unscaled,
+        out_weight.reshape(heads_here, width, out_weight.shape[1]),
+        preferred_element_type=jnp.float32,
+    ).astype(jnp.bfloat16)
     groups = lax.axis_size("head")
     chunk = tok_dev // groups
     d_model = partial.shape[1]

time: 163 us -> 167 us (1.025)
  local copies, waits for them, and re-layouts: 8.16 us -> 10.2 us
  other arithmetic: 15 us -> 17 us
    convert_element_type x0 -> x1, local copies, waits for them, and re-layouts: none -> 3.03 us  [body(): gated = mixed * jax.nn.silu(gate_rows.astype(jnp.float32))]
    reshape x1 -> x0, local copies, waits for them, and re-layouts: 3.03 us -> none  [body(): mixed = mixed.reshape(tok_dev, heads_here * width)]
  transfers between devices with their start and end apart: 2 -> 2, of which waited for: 1 -> 1; matrix products, arithmetic and copies ran while one was open for 21% -> 13% of each run, Pallas kernels for 0% -> 0%
where the time goes in v17:
time: 167 us; the launch traced here: 166 us
  blocking collectives  73.1 us (44%)
  matrix products  25.7 us (15%)
  starting transfers between devices  19.5 us (12%)
  waiting for transfers between devices  18.6 us (11%)
  other arithmetic  17 us (10%)
  local copies, waits for them, and re-layouts  10.2 us (6%)
  between operations  1.86 us (1%)
    all_gather x3, blocking collectives, gathered_level(): gathered = lax.all_gather(pack_state(kept, state), axis)  37.9 us
    all_to_all x1, blocking collectives, body(): lax.all_to_all(sent, 'head', split_axis=0, concat_axis=0, tiled=True)  25 us
    all_to_all x2, starting transfers between devices, send(): lax.all_to_all(packed.reshape(shards, capacity, packed.shape[1]), ROWS, s...  19.5 us
    all_to_all x2, waiting for transfers between devices, send(): lax.all_to_all(packed.reshape(shards, capacity, packed.shape[1]), ROWS, s...  18.6 us
    all_gather x1, blocking collectives, exclusive_prefix(): whole = lax.all_gather(start_state, pair, tiled=True)  10.2 us
    dot_general x5, matrix products, send(): jnp.dot(to_slot, v, preferred_element_type=jnp.float32).astype(jnp.bfloat16)  5.78 us
    dot_general x2, matrix products, place(): jnp.dot(to_place, values, preferred_element_type=jnp.float32)  3.67 us
    dot_general x1, matrix products, inner_terms(): jnp.einsum('hts,shp->htp', affinity_logits, by_head, preferred_element_ty...  3.49 us
  transfers between devices with their start and end apart: 2, of which 1 were waited for; matrix products, arithmetic and copies ran while one was open for 13% of the time, Pallas kernels for 0%

profile of v17, /device:TPU:1, one launch (start us, length us, event | category | flops | bytes accessed | tf_op | source)
XLA Modules:
  0.0 166.0 jit_solution(1590583134560178923)
XLA Ops:
  0.0 0.9 fusion.63
  0.9 1.2 reduce-window.24
  2.1 0.2 slice_reduce_fusion
  2.4 0.1 fusion.42
  2.5 0.7 fusion.64
  3.2 1.0 convolution_convert_fusion.6
  4.2 0.2 copy.65
  4.4 1.2 convolution_convert_fusion.4
  5.6 0.3 convolution_convert_fusion.5
  5.9 0.6 convolution_convert_fusion.3
  6.5 1.1 maximum_bitcast_fusion
  7.6 13.1 %all-to-all-start = ((bf16[64,8,1038]{2,1,0:T(8,128)(2,1)}), bf16[64,8,1038]{2,1,0:T(8,128)(2,1)S(1)}, u32[]{:S(2)}, u32[]{:S(2)}) async-start(bf16[64,8,1038]{2,1,0:T(8,128)(2,1)} %maximum_bitcast_fusion), calls=%async_computation | async-start | bytes 2359296 | tf_op jit(solution)/shard_map/all_to_all | solution.py:141
  20.8 0.7 reduce-window.31
  21.5 1.4 fusion.68
  22.9 0.6 slice.85
  24.8 0.7 mul.266
  25.5 0.5 fusion.74
  26.0 0.6 iota_compare_fusion.14
  26.6 0.5 iota_compare_fusion.18
  27.1 0.5 iota_compare_fusion.17
  27.6 2.6 %fusion.8 = bf16[64,8,768]{2,1,0:T(8,128)(2,1)} fusion(bf16[512,768]{1,0:T(8,128)(2,1)} %param.11, s32[512]{0:T(512)S(1)} %get-tuple-element.77), kind=kOutput, calls=%fused_computation.21 | convolution fusion | flops 403308544 | bytes 1574912 | tf_op jit(solution)/shard_map/dot_general | solution.py:136
  30.3 0.6 fusion.67
  30.9 0.5 iota_compare_fusion.16
  31.4 0.6 broadcast_and_fusion
  32.0 0.6 compare_convert_fusion.1
  32.6 0.9 fusion.12
  33.5 18.6 %all-to-all-done = bf16[64,8,1038]{2,1,0:T(8,128)(2,1)S(1)} async-done(((bf16[64,8,1038]{2,1,0:T(8,128)(2,1)}), bf16[64,8,1038]{2,1,0:T(8,128)(2,1)S(1)}, u32[]{:S(2)}, u32[]{:S(2)}) %all-to-all-start) | async-done | bytes 1062944 | tf_op jit(solution)/shard_map/all_to_all | solution.py:141
  52.1 6.4 %all-to-all-start.1 = ((bf16[64,8,768]{2,1,0:T(8,128)(2,1)}), bf16[64,8,768]{2,1,0:T(8,128)(2,1)}, u32[]{:S(2)}, u32[]{:S(2)}) async-start(bf16[64,8,768]{2,1,0:T(8,128)(2,1)} %fusion.8), calls=%async_computation.1 | async-start | bytes 1572864 | tf_op jit(solution)/shard_map/all_to_all | solution.py:141
  58.5 0.2 add_reduce_fusion
  58.7 0.8 convolution_convert_fusion
  59.6 0.9 copy-done.2
  60.6 1.2 reduce-window.32
  61.7 0.2 slice_reduce_fusion.1
  62.1 0.2 slice_reduce_fusion.2
  62.3 0.8 copy.68
  63.2 2.3 %fusion.11 = bf16[1,12,64,128]{3,2,1,0:T(8,128)(2,1)S(1)} fusion(bf16[512,12,64]{0,2,1:T(8,128)(2,1)S(1)} %bitcast.119, f32[12,512]{1,0:T(8,128)S(1)} %get-tuple-element.72, f32[512,128]{1,0:T(8,128)} %copy.68, f32[12]{0:T(128)S(1)} %get-tuple-element.78), kind=kOutput, calls=%fused_computation.27 | convolution fusion | flops 102432768 | bytes 1269808 | tf_op jit(solution)/shard_map/while/body/eval_jaxpr/hsn,shp->hpn/dot_general | solution.py:73
  65.7 2.3 %all_gather.15 = bf16[2,12,65,128]{3,2,1,0:T(8,128)(2,1)S(1)} all-gather(bf16[1,12,65,128]{3,2,1,0:T(8,128)(2,1)S(1)} %pad_maximum_fusion.1), channel_id=1, replica_groups=mesh['sx'=4,'sz'=8,'sc'=2,'head'=4] {'sc'}, dimensions={0}, use_global_device_ids=true | all-gather | bytes 599040 | tf_op jit(solution)/shard_map/all_gather | solution.py:38
  67.9 0.4 fusion.58
  68.5 0.6 fusion.36
  69.4 25.6 %all_gather.16 = bf16[8,6,65,128]{3,2,1,0:T(8,128)(2,1)S(1)} all-gather(bf16[1,6,65,128]{3,2,1,0:T(8,128)(2,1)S(1)} %pad_maximum_fusion.2), channel_id=1, replica_groups=mesh['sx'=4,'sz'=8,'sc'=2,'head'=4] {'sz'}, dimensions={0}, use_global_device_ids=true | all-gather | bytes 898560 | tf_op jit(solution)/shard_map/all_gather | solution.py:38
  95.0 0.2 slice_reduce_fusion.3
  95.2 0.1 copy.90
  95.5 2.3 %fusion.45 = f32[512,512]{1,0:T(8,128)} fusion(bf16[512,1038]{0,1:T(8,128)(2,1)} %copy-done.2), kind=kOutput, calls=%fused_computation.86 | convolution fusion | flops 67108864 | bytes 1310720 | tf_op jit(solution)/shard_map/while/body/eval_jaxpr/tn,sn->ts/dot_general | solution.py:87
  97.8 2.9 %fusion.7 = f32[512,768]{1,0:T(8,128)} fusion(bf16[64,8,768]{2,1,0:T(8,128)(2,1)} %all-to-all-done.1, s32[512]{0:T(512)S(1)} %add_reduce_fusion), kind=kOutput, calls=%fused_computation.18 | convolution fusion | flops 403701760 | bytes 2361344 | tf_op jit(solution)/shard_map/dot_general | solution.py:162
  100.7 3.0 %copy.72 = f32[512,768]{0,1:T(8,128)} copy(f32[512,768]{1,0:T(8,128)} %fusion.7) | data formatting | bytes 3145728 | tf_op jit(solution)/shard_map/convert_element_type | solution.py:230
  103.9 1.6 fusion.34
  105.5 0.8 copy.114
  106.4 0.3 select_reduce_fusion.1
  106.7 0.4 fusion.16
  107.1 0.7 copy.116
  107.8 0.4 fusion.18
  108.3 10.0 %all_gather.17 = bf16[4,6,65,128]{3,2,1,0:T(8,128)(2,1)S(1)} all-gather(bf16[1,6,65,128]{3,2,1,0:T(8,128)(2,1)S(1)} %pad_maximum_fusion.3), channel_id=1, replica_groups=mesh['sx'=4,'sz'=8,'sc'=2,'head'=4] {'sx'}, dimensions={0}, use_global_device_ids=true | all-gather | bytes 499200 | tf_op jit(solution)/shard_map/all_gather | solution.py:38
  118.3 0.8 copy-done.7
  119.1 0.1 fusion.57
  119.5 1.5 fusion.27
  121.0 1.0 slice_add_fusion.2
  122.0 10.2 %all_gather.18 = f32[12,64,128]{2,1,0:T(8,128)S(1)} all-gather(f32[6,64,128]{2,1,0:T(8,128)S(1)} %slice_add_fusion.2), channel_id=1, replica_groups=mesh['sx'=4,'sz'=8,'sc'=2,'head'=4] {'sc'}, dimensions={0}, use_global_device_ids=true | all-gather | bytes 589824 | tf_op jit(solution)/shard_map/all_gather | solution.py:58
  132.3 3.5 %fusion = f32[12,512,64]{1,2,0:T(8,128)S(1)} fusion(bf16[512,12,64]{0,2,1:T(8,128)(2,1)S(1)} %bitcast.120, f32[12,512]{1,0:T(8,128)S(1)} %bitcast.126, f32[512,512]{1,0:T(8,128)S(1)} %copy-done.3, pred[512,512]{1,0:T(8,128)(4,1)S(1)} %copy-done.9), kind=kOutput, calls=%fused_computation.1 | convolution fusion | flops 415236096 | bytes 3694592 | tf_op jit(solution)/shard_map/while/body/eval_jaxpr/hts,shp->htp/dot_general | solution.py:89
  135.8 2.3 %multiply_reduce_fusion = (f32[512]{0:T(512)S(1)}, f32[12,512,64]{1,2,0:T(8,128)S(1)}) fusion(f32[12,512,64]{1,2,0:T(8,128)S(1)} %bitcast.114, bf16[512,12,64]{0,2,1:T(8,128)(2,1)S(1)} %bitcast.121, f32[12]{0:T(128)S(1)} %copy-done.27, f32[12,512,64]{1,2,0:T(8,128)S(1)} %fusion, f32[12,512]{1,0:T(8,128)S(1)} %get-tuple-element.73, ...), kind=kOutput, calls=%fused_computation.13 | convolution fusion | flops 608894464 | bytes 6458368 | tf_op jit(solution)/shard_map/while/body/eval_jaxpr/tn,hpn->htp/dot_general | solution.py:94
  138.2 1.5 fusion.2
  139.7 0.1 pad_maximum_fusion
  139.9 25.0 %all_to_all.15 = bf16[4,136,1536]{2,1,0:T(8,128)(2,1)S(1)} all-to-all(bf16[4,136,1536]{2,1,0:T(8,128)(2,1)S(1)} %pad_maximum_fusion), channel_id=1, replica_groups=mesh['sx'=4,'sz'=8,'sc'=2,'head'=4] {'head'}, dimensions={0} | all-to-all | bytes 3342336 | tf_op jit(solution)/shard_map/all_to_all | solution.py:249
  164.9 0.2 convert_reduce_fusion
  165.1 0.9 fusion.13
  (106 shorter events, 2.0 us)
Async XLA Ops:
  0.0 138.2 %copy-start = (bf16[768,1536]{1,0:T(8,128)(2,1)S(1)}, bf16[768,1536]{1,0:T(8,128)(2,1)}, u32[]{:S(2)}) copy-start(bf16[768,1536]{1,0:T(8,128)(2,1)} %param.19) | copy-start | bytes 7077892
  0.0 5.6 %copy-start.26 = (bf16[512,128]{1,0:T(8,128)(2,1)S(1)}, bf16[512,128]{1,0:T(8,128)(2,1)}, u32[]{:S(2)}) copy-start(bf16[512,128]{1,0:T(8,128)(2,1)} %param.12) | copy-start | bytes 393220
  0.0 5.9 %copy-start.25 = (bf16[512,768]{1,0:T(8,128)(2,1)S(1)}, bf16[512,768]{1,0:T(8,128)(2,1)}, u32[]{:S(2)}) copy-start(bf16[512,768]{1,0:T(8,128)(2,1)} %param.10) | copy-start | bytes 2359300
  7.6 13.2 %copy-start.14 = (s32[4]{0:T(128)S(1)}, s32[4]{0:T(128)}, u32[]{:S(2)}) copy-start(s32[4]{0:T(128)} %param.16) | copy-start | bytes 52
  7.6 17.2 %copy-start.11 = (f32[768]{0:T(1024)S(1)}, f32[768]{0:T(1024)}, u32[]{:S(2)}) copy-start(f32[768]{0:T(1024)} %param.18) | copy-start | bytes 9220
  7.6 44.5 %all-to-all-start = ((bf16[64,8,1038]{2,1,0:T(8,128)(2,1)}), bf16[64,8,1038]{2,1,0:T(8,128)(2,1)S(1)}, u32[]{:S(2)}, u32[]{:S(2)}) async-start(bf16[64,8,1038]{2,1,0:T(8,128)(2,1)} %maximum_bitcast_fusion), calls=%async_computation | async-start | bytes 2359296 | tf_op jit(solution)/shard_map/all_to_all | solution.py:141
  25.5 5.9 %copy-start.20 = (pred[2]{0:T(512)(128)(4,1)}, pred[2]{0:T(512)(128)(4,1)S(1)}, u32[]{:S(2)}) copy-start(pred[2]{0:T(512)(128)(4,1)S(1)} %iota_compare_fusion.19) | copy-start | bytes 10
  27.1 5.5 %copy-start.22 = (pred[8]{0:T(512)(128)(4,1)}, pred[8]{0:T(512)(128)(4,1)S(1)}, u32[]{:S(2)}) copy-start(pred[8]{0:T(512)(128)(4,1)S(1)} %get-tuple-element.96) | copy-start | bytes 28
  52.1 45.7 %all-to-all-start.1 = ((bf16[64,8,768]{2,1,0:T(8,128)(2,1)}), bf16[64,8,768]{2,1,0:T(8,128)(2,1)}, u32[]{:S(2)}, u32[]{:S(2)}) async-start(bf16[64,8,768]{2,1,0:T(8,128)(2,1)} %fusion.8), calls=%async_computation.1 | async-start | bytes 1572864 | tf_op jit(solution)/shard_map/all_to_all | solution.py:141
  59.5 1.0 copy-start.2
  59.6 5.9 %copy-start.4 = (bf16[512,768]{0,1:T(8,128)(2,1)}, bf16[512,768]{0,1:T(8,128)(2,1)S(1)}, u32[]{:S(2)}) copy-start(bf16[512,768]{0,1:T(8,128)(2,1)S(1)} %slice.104) | copy-start | bytes 2359300
  63.2 5.1 %copy-start.17 = (pred[2,2]{1,0:T(4,128)(4,1)S(1)}, pred[2,2]{1,0:T(4,128)(4,1)}, u32[]{:S(2)}) copy-start(pred[2,2]{1,0:T(4,128)(4,1)} %get-tuple-element.100) | copy-start | bytes 16
  63.2 5.1 %copy-start.18 = (pred[2,2]{1,0:T(4,128)(4,1)S(1)}, pred[2,2]{1,0:T(4,128)(4,1)}, u32[]{:S(2)}) copy-start(pred[2,2]{1,0:T(4,128)(4,1)} %get-tuple-element.101) | copy-start | bytes 16
  67.9 1.4 copy-start.6
  69.1 26.2 %copy-start.21 = (pred[2]{0:T(512)(128)(4,1)S(1)}, pred[2]{0:T(512)(128)(4,1)}, u32[]{:S(2)}) copy-start(pred[2]{0:T(512)(128)(4,1)} %copy-done.20) | copy-start | bytes 10
  69.1 26.3 %copy-start.23 = (pred[8]{0:T(512)(128)(4,1)S(1)}, pred[8]{0:T(512)(128)(4,1)}, u32[]{:S(2)}) copy-start(pred[8]{0:T(512)(128)(4,1)} %copy-done.22) | copy-start | bytes 28
  100.7 3.0 %copy-start.19 = (f32[2]{0:T(128)S(1)}, f32[2]{0:T(128)}, u32[]{:S(2)}) copy-start(f32[2]{0:T(128)} %fusion.74) | copy-start | bytes 28
  103.7 2.7 %copy-start.12 = (pred[8,8]{1,0:T(8,128)(4,1)S(1)}, pred[8,8]{1,0:T(8,128)(4,1)}, u32[]{:S(2)}) copy-start(pred[8,8]{1,0:T(8,128)(4,1)} %iota_compare_fusion.14) | copy-start | bytes 196
  103.7 2.7 %copy-start.13 = (pred[8,8]{1,0:T(8,128)(4,1)S(1)}, pred[8,8]{1,0:T(8,128)(4,1)}, u32[]{:S(2)}) copy-start(pred[8,8]{1,0:T(8,128)(4,1)} %broadcast_and_fusion) | copy-start | bytes 196
  103.7 3.0 %copy-start.24 = (f32[8]{0:T(128)S(1)}, f32[8]{0:T(128)}, u32[]{:S(2)}) copy-start(f32[8]{0:T(128)} %get-tuple-element.97) | copy-start | bytes 100
  107.0 12.2 %copy-start.16 = (pred[4,4]{1,0:T(4,128)(4,1)S(1)}, pred[4,4]{1,0:T(4,128)(4,1)}, u32[]{:S(2)}) copy-start(pred[4,4]{1,0:T(4,128)(4,1)} %fusion.67) | copy-start | bytes 52
  107.0 12.3 %copy-start.15 = (f32[4]{0:T(128)S(1)}, f32[4]{0:T(128)}, u32[]{:S(2)}) copy-start(f32[4]{0:T(128)} %get-tuple-element.99) | copy-start | bytes 52
  108.2 24.0 %copy-start.3 = (f32[512,512]{1,0:T(8,128)S(1)}, f32[512,512]{1,0:T(8,128)}, u32[]{:S(2)}) copy-start(f32[512,512]{1,0:T(8,128)} %fusion.45) | copy-start | bytes 3145732
  118.3 0.8 copy-start.7
  119.5 12.7 %copy-start.5 = (bf16[512,768]{0,1:T(8,128)(2,1)S(1)}, bf16[512,768]{0,1:T(8,128)(2,1)}, u32[]{:S(2)}) copy-start(bf16[512,768]{0,1:T(8,128)(2,1)} %copy-done.4) | copy-start | bytes 2359300
  119.5 12.7 %copy-start.9 = (pred[512,512]{1,0:T(8,128)(4,1)S(1)}, pred[512,512]{1,0:T(8,128)(4,1)}, u32[]{:S(2)}) copy-start(pred[512,512]{1,0:T(8,128)(4,1)} %fusion.12) | copy-start | bytes 786436
  132.2 3.5 %copy-start.1 = (f32[512,768]{0,1:T(8,128)S(1)}, f32[512,768]{0,1:T(8,128)}, u32[]{:S(2)}) copy-start(f32[512,768]{0,1:T(8,128)} %copy.72) | copy-start | bytes 4718596
  132.2 3.5 %copy-start.8 = (f32[12,1,65,128]{3,2,0,1:T(8,128)S(1)}, f32[12,1,65,128]{3,2,0,1:T(8,128)}, u32[]{:S(2)}) copy-start(f32[12,1,65,128]{3,2,0,1:T(8,128)} %copy.114) | copy-start | bytes 1198084
  132.2 3.5 %copy-start.27 = (f32[12]{0:T(128)S(1)}, f32[12]{0:T(128)}, u32[]{:S(2)}) copy-start(f32[12]{0:T(128)} %param.17) | copy-start | bytes 148
  135.8 2.4 %copy-start.10 = (f32[12,64]{1,0:T(8,128)S(1)}, f32[12,64]{1,0:T(8,128)}, u32[]{:S(2)}) copy-start(f32[12,64]{1,0:T(8,128)} %mul.266) | copy-start | bytes 9220

commit v18 on v14

--- a/solution.py
+++ b/solution.py
@@ -92,7 +92,7 @@
 def entry_terms(query_block, carry_state, running, doc_block, before):
     entry_weight = jnp.exp(running) * (doc_block == before).astype(jnp.float32)[:, None]
     carried = jnp.einsum(
-        "tn,hpn->thp", query_block.astype(jnp.float32), carry_state, precision=lax.Precision.HIGHEST
+        "tn,hpn->thp", query_block.astype(jnp.float32), carry_state, precision=lax.Precision.HIGH
     )
     return carried * entry_weight[:, :, None]
 

time: 163 us -> 163 us (level)
  no operation moved by 1% of the time
where the time goes in v18:
time: 163 us; the launch traced here: 162 us
  blocking collectives  73.1 us (45%)
  matrix products  24 us (15%)
  waiting for transfers between devices  20.2 us (12%)
  starting transfers between devices  19.5 us (12%)
  other arithmetic  15 us (9%)
  local copies, waits for them, and re-layouts  8.16 us (5%)
  between operations  1.97 us (1%)
    all_gather x3, blocking collectives, gathered_level(): gathered = lax.all_gather(pack_state(kept, state), axis)  37.8 us
    all_to_all x1, blocking collectives, body(): lax.all_to_all(sent, 'head', split_axis=0, concat_axis=0, tiled=True)  25 us
    all_to_all x2, waiting for transfers between devices, send(): lax.all_to_all(packed.reshape(shards, capacity, packed.shape[1]), ROWS, s...  20.2 us
    all_to_all x2, starting transfers between devices, send(): lax.all_to_all(packed.reshape(shards, capacity, packed.shape[1]), ROWS, s...  19.5 us
    all_gather x1, blocking collectives, exclusive_prefix(): whole = lax.all_gather(start_state, pair, tiled=True)  10.3 us
    dot_general x5, matrix products, send(): jnp.dot(to_slot, v, preferred_element_type=jnp.float32).astype(jnp.bfloat16)  5.73 us
    dot_general x1, matrix products, inner_terms(): jnp.einsum('hts,shp->thp', affinity_logits, by_head, preferred_element_ty...  3.82 us
    dot_general x2, matrix products, place(): jnp.dot(to_place, values, preferred_element_type=jnp.float32)  3.34 us
  transfers between devices with their start and end apart: 2, of which 1 were waited for; matrix products, arithmetic and copies ran while one was open for 21% of the time, Pallas kernels for 0%

profile of v18, /device:TPU:1, one launch (start us, length us, event | category | flops | bytes accessed | tf_op | source)
XLA Modules:
  0.0 162.0 jit_solution(934749653761415243)
XLA Ops:
  0.0 0.9 fusion.65
  0.9 1.2 reduce-window.24
  2.1 0.2 slice_reduce_fusion
  2.4 0.1 fusion.44
  2.5 0.7 fusion.66
  3.2 1.0 convolution_convert_fusion.7
  4.2 0.2 copy.65
  4.4 1.2 convolution_convert_fusion.5
  5.6 0.3 convolution_convert_fusion.6
  5.9 0.6 convolution_convert_fusion.4
  6.5 1.1 maximum_bitcast_fusion
  7.6 13.1 %all-to-all-start = ((bf16[64,8,1038]{2,1,0:T(8,128)(2,1)}), bf16[64,8,1038]{2,1,0:T(8,128)(2,1)S(1)}, u32[]{:S(2)}, u32[]{:S(2)}) async-start(bf16[64,8,1038]{2,1,0:T(8,128)(2,1)} %maximum_bitcast_fusion), calls=%async_computation | async-start | bytes 2359296 | tf_op jit(solution)/shard_map/all_to_all | solution.py:141
  20.8 0.2 reduce-window.31
  21.0 0.6 fusion.70
  21.7 0.7 slice.85
  23.7 0.5 fusion.76
  24.3 0.6 iota_compare_fusion.14
  24.8 0.5 iota_compare_fusion.18
  25.4 0.5 iota_compare_fusion.17
  25.9 2.6 %fusion.10 = bf16[64,8,768]{2,1,0:T(8,128)(2,1)} fusion(bf16[512,768]{1,0:T(8,128)(2,1)} %param.11, s32[512]{0:T(512)S(1)} %get-tuple-element.75), kind=kOutput, calls=%fused_computation.24 | convolution fusion | flops 403308544 | bytes 1574912 | tf_op jit(solution)/shard_map/dot_general | solution.py:136
  28.5 0.6 fusion.69
  29.1 0.6 iota_compare_fusion.16
  29.7 0.6 broadcast_and_fusion
  30.3 0.7 compare_convert_fusion.1
  31.0 0.9 fusion.14
  31.9 20.2 %all-to-all-done = bf16[64,8,1038]{2,1,0:T(8,128)(2,1)S(1)} async-done(((bf16[64,8,1038]{2,1,0:T(8,128)(2,1)}), bf16[64,8,1038]{2,1,0:T(8,128)(2,1)S(1)}, u32[]{:S(2)}, u32[]{:S(2)}) %all-to-all-start) | async-done | bytes 1062944 | tf_op jit(solution)/shard_map/all_to_all | solution.py:141
  52.1 6.4 %all-to-all-start.1 = ((bf16[64,8,768]{2,1,0:T(8,128)(2,1)}), bf16[64,8,768]{2,1,0:T(8,128)(2,1)}, u32[]{:S(2)}, u32[]{:S(2)}) async-start(bf16[64,8,768]{2,1,0:T(8,128)(2,1)} %fusion.10), calls=%async_computation.1 | async-start | bytes 1572864 | tf_op jit(solution)/shard_map/all_to_all | solution.py:141
  58.5 0.2 add_reduce_fusion
  58.7 0.8 convolution_convert_fusion.1
  59.6 0.9 copy-done.3
  60.6 1.2 reduce-window.32
  61.7 0.2 slice_reduce_fusion.1
  62.1 0.2 slice_reduce_fusion.2
  62.3 0.8 copy.68
  63.2 2.3 %fusion.13 = bf16[1,12,64,128]{3,2,1,0:T(8,128)(2,1)S(1)} fusion(bf16[512,12,64]{0,2,1:T(8,128)(2,1)S(1)} %bitcast.103, f32[12,512]{1,0:T(8,128)S(1)} %exponential_multiply_fusion.1, f32[512,128]{1,0:T(8,128)} %copy.68, f32[12]{0:T(128)S(1)} %get-tuple-element.76), kind=kOutput, calls=%fused_computation.30 | convolution fusion | flops 102432768 | bytes 1269808 | tf_op jit(solution)/shard_map/while/body/eval_jaxpr/hsn,shp->hpn/dot_general | solution.py:73
  65.7 2.3 %all_gather.15 = bf16[2,12,65,128]{3,2,1,0:T(8,128)(2,1)S(1)} all-gather(bf16[1,12,65,128]{3,2,1,0:T(8,128)(2,1)S(1)} %pad_maximum_fusion.1), channel_id=1, replica_groups=mesh['sx'=4,'sz'=8,'sc'=2,'head'=4] {'sc'}, dimensions={0}, use_global_device_ids=true | all-gather | bytes 599040 | tf_op jit(solution)/shard_map/all_gather | solution.py:38
  67.9 0.4 fusion.60
  68.3 0.1 select_reduce_fusion.5
  68.4 0.1 copy.75
  68.5 0.6 fusion.38
  69.4 25.6 %all_gather.16 = bf16[8,6,65,128]{3,2,1,0:T(8,128)(2,1)S(1)} all-gather(bf16[1,6,65,128]{3,2,1,0:T(8,128)(2,1)S(1)} %pad_maximum_fusion.2), channel_id=1, replica_groups=mesh['sx'=4,'sz'=8,'sc'=2,'head'=4] {'sz'}, dimensions={0}, use_global_device_ids=true | all-gather | bytes 898560 | tf_op jit(solution)/shard_map/all_gather | solution.py:38
  95.0 0.2 slice_reduce_fusion.3
  95.2 0.1 copy.90
  95.5 0.1 copy.86
  95.6 1.6 fusion.36
  97.2 0.8 copy.114
  98.1 0.3 select_reduce_fusion.1
  98.4 0.4 fusion.18
  98.8 0.4 fusion.20
  99.3 9.9 %all_gather.17 = bf16[4,6,65,128]{3,2,1,0:T(8,128)(2,1)S(1)} all-gather(bf16[1,6,65,128]{3,2,1,0:T(8,128)(2,1)S(1)} %pad_maximum_fusion.3), channel_id=1, replica_groups=mesh['sx'=4,'sz'=8,'sc'=2,'head'=4] {'sx'}, dimensions={0}, use_global_device_ids=true | all-gather | bytes 499200 | tf_op jit(solution)/shard_map/all_gather | solution.py:38
  109.2 0.1 fusion.59
  109.5 0.1 copy.81
  109.7 0.4 fusion.29
  110.2 10.3 %all_gather.18 = f32[12,64,128]{2,1,0:T(8,128)S(1)} all-gather(f32[6,64,128]{2,1,0:T(8,128)S(1)} %slice_add_fusion.2), channel_id=1, replica_groups=mesh['sx'=4,'sz'=8,'sc'=2,'head'=4] {'sc'}, dimensions={0}, use_global_device_ids=true | all-gather | bytes 589824 | tf_op jit(solution)/shard_map/all_gather | solution.py:58
  120.6 1.3 fusion.47
  121.9 3.8 %fusion = f32[12,64,512]{2,1,0:T(8,128)S(1)} fusion(bf16[512,12,64]{0,2,1:T(8,128)(2,1)S(1)} %bitcast.104, f32[12,512]{1,0:T(8,128)S(1)} %bitcast.116, f32[512,512]{1,0:T(8,128)S(1)} %fusion.47, pred[512,512]{1,0:T(8,128)(4,1)S(1)} %copy-done.6), kind=kOutput, calls=%fused_computation.1 | convolution fusion | flops 415236096 | bytes 3694592 | tf_op jit(solution)/shard_map/while/body/eval_jaxpr/hts,shp->thp/dot_general | solution.py:89
  125.8 2.9 %fusion.7 = f32[512,12,64]{0,2,1:T(8,128)} fusion(f32[12,64,512]{2,1,0:T(8,128)S(1)} %fusion, bf16[512,12,64]{0,2,1:T(8,128)(2,1)S(1)} %bitcast.105, f32[12]{0:T(128)S(1)} %copy-done.20, f32[512,12]{0,1:T(8,128)S(1)} %exponential_multiply_fusion, f32[12,65,128]{2,1,0:T(8,128)S(1)} %bitcast.107, f32[12,64,128]{2,1,0:T(8,128)S(1)} %all_gather.18, ...), kind=kOutput, calls=%fused_computation.16 | convolution fusion | flops 304152576 | bytes 4883456 | tf_op jit(solution)/shard_map/while/body/eval_jaxpr/tn,hpn->thp/dot_general | solution.py:94
  128.7 3.0 %copy.72 = f32[512,768]{1,0:T(8,128)} copy(f32[512,768]{0,1:T(8,128)} %bitcast.102) | data formatting | bytes 3145728 | tf_op jit(solution)/shard_map/reshape | solution.py:228
  131.7 2.5 %multiply_reduce_fusion = (f32[512]{0:T(512)S(1)}, f32[512,768]{1,0:T(8,128)S(1)}) fusion(f32[512,768]{1,0:T(8,128)} %copy.72, bf16[64,8,768]{2,1,0:T(8,128)(2,1)} %all-to-all-done.1, s32[512]{0:T(512)S(1)} %add_reduce_fusion), kind=kOutput, calls=%fused_computation.17 | convolution fusion | flops 406453760 | bytes 3936256 | tf_op jit(solution)/shard_map/dot_general | solution.py:162
  134.3 1.4 convolution_convert_fusion
  135.7 0.1 pad_maximum_fusion
  135.9 25.0 %all_to_all.15 = bf16[4,136,1536]{2,1,0:T(8,128)(2,1)S(1)} all-to-all(bf16[4,136,1536]{2,1,0:T(8,128)(2,1)S(1)} %pad_maximum_fusion), channel_id=1, replica_groups=mesh['sx'=4,'sz'=8,'sc'=2,'head'=4] {'head'}, dimensions={0} | all-to-all | bytes 3342336 | tf_op jit(solution)/shard_map/all_to_all | solution.py:244
  160.8 0.2 convert_reduce_fusion
  161.1 0.9 fusion.15
  (98 shorter events, 1.7 us)
Async XLA Ops:
  0.0 134.3 %copy-start = (bf16[768,1536]{1,0:T(8,128)(2,1)S(1)}, bf16[768,1536]{1,0:T(8,128)(2,1)}, u32[]{:S(2)}) copy-start(bf16[768,1536]{1,0:T(8,128)(2,1)} %param.19) | copy-start | bytes 7077892
  0.0 5.6 %copy-start.22 = (bf16[512,128]{1,0:T(8,128)(2,1)S(1)}, bf16[512,128]{1,0:T(8,128)(2,1)}, u32[]{:S(2)}) copy-start(bf16[512,128]{1,0:T(8,128)(2,1)} %param.12) | copy-start | bytes 393220
  0.0 5.9 %copy-start.21 = (bf16[512,768]{1,0:T(8,128)(2,1)S(1)}, bf16[512,768]{1,0:T(8,128)(2,1)}, u32[]{:S(2)}) copy-start(bf16[512,768]{1,0:T(8,128)(2,1)} %param.10) | copy-start | bytes 2359300
  7.6 13.2 %copy-start.9 = (s32[4]{0:T(128)S(1)}, s32[4]{0:T(128)}, u32[]{:S(2)}) copy-start(s32[4]{0:T(128)} %param.16) | copy-start | bytes 52
  7.6 44.5 %all-to-all-start = ((bf16[64,8,1038]{2,1,0:T(8,128)(2,1)}), bf16[64,8,1038]{2,1,0:T(8,128)(2,1)S(1)}, u32[]{:S(2)}, u32[]{:S(2)}) async-start(bf16[64,8,1038]{2,1,0:T(8,128)(2,1)} %maximum_bitcast_fusion), calls=%async_computation | async-start | bytes 2359296 | tf_op jit(solution)/shard_map/all_to_all | solution.py:141
  23.7 7.2 %copy-start.14 = (pred[2]{0:T(512)(128)(4,1)}, pred[2]{0:T(512)(128)(4,1)S(1)}, u32[]{:S(2)}) copy-start(pred[2]{0:T(512)(128)(4,1)S(1)} %iota_compare_fusion.19) | copy-start | bytes 10
  25.4 5.6 %copy-start.17 = (pred[8]{0:T(512)(128)(4,1)}, pred[8]{0:T(512)(128)(4,1)S(1)}, u32[]{:S(2)}) copy-start(pred[8]{0:T(512)(128)(4,1)S(1)} %get-tuple-element.92) | copy-start | bytes 28
  52.1 79.6 %all-to-all-start.1 = ((bf16[64,8,768]{2,1,0:T(8,128)(2,1)}), bf16[64,8,768]{2,1,0:T(8,128)(2,1)}, u32[]{:S(2)}, u32[]{:S(2)}) async-start(bf16[64,8,768]{2,1,0:T(8,128)(2,1)} %fusion.10), calls=%async_computation.1 | async-start | bytes 1572864 | tf_op jit(solution)/shard_map/all_to_all | solution.py:141
  59.5 1.0 copy-start.3
  59.6 5.9 %copy-start.1 = (bf16[512,768]{0,1:T(8,128)(2,1)}, bf16[512,768]{0,1:T(8,128)(2,1)S(1)}, u32[]{:S(2)}) copy-start(bf16[512,768]{0,1:T(8,128)(2,1)S(1)} %slice.100) | copy-start | bytes 2359300
  63.2 5.1 %copy-start.12 = (pred[2,2]{1,0:T(4,128)(4,1)S(1)}, pred[2,2]{1,0:T(4,128)(4,1)}, u32[]{:S(2)}) copy-start(pred[2,2]{1,0:T(4,128)(4,1)} %get-tuple-element.98) | copy-start | bytes 16
  63.2 5.1 %copy-start.13 = (pred[2,2]{1,0:T(4,128)(4,1)S(1)}, pred[2,2]{1,0:T(4,128)(4,1)}, u32[]{:S(2)}) copy-start(pred[2,2]{1,0:T(4,128)(4,1)} %get-tuple-element.99) | copy-start | bytes 16
  67.9 1.4 copy-start.5
  69.1 26.3 %copy-start.18 = (pred[8]{0:T(512)(128)(4,1)S(1)}, pred[8]{0:T(512)(128)(4,1)}, u32[]{:S(2)}) copy-start(pred[8]{0:T(512)(128)(4,1)} %copy-done.17) | copy-start | bytes 28
  69.1 26.3 %copy-start.16 = (f32[2]{0:T(128)S(1)}, f32[2]{0:T(128)}, u32[]{:S(2)}) copy-start(f32[2]{0:T(128)} %fusion.76) | copy-start | bytes 28
  69.4 28.7 %copy-start.7 = (pred[8,8]{1,0:T(8,128)(4,1)S(1)}, pred[8,8]{1,0:T(8,128)(4,1)}, u32[]{:S(2)}) copy-start(pred[8,8]{1,0:T(8,128)(4,1)} %iota_compare_fusion.14) | copy-start | bytes 196
  69.4 28.7 %copy-start.8 = (pred[8,8]{1,0:T(8,128)(4,1)S(1)}, pred[8,8]{1,0:T(8,128)(4,1)}, u32[]{:S(2)}) copy-start(pred[8,8]{1,0:T(8,128)(4,1)} %broadcast_and_fusion) | copy-start | bytes 196
  69.4 29.0 %copy-start.19 = (f32[8]{0:T(128)S(1)}, f32[8]{0:T(128)}, u32[]{:S(2)}) copy-start(f32[8]{0:T(128)} %get-tuple-element.94) | copy-start | bytes 100
  98.8 10.6 %copy-start.11 = (pred[4,4]{1,0:T(4,128)(4,1)S(1)}, pred[4,4]{1,0:T(4,128)(4,1)}, u32[]{:S(2)}) copy-start(pred[4,4]{1,0:T(4,128)(4,1)} %fusion.69) | copy-start | bytes 52
  98.8 10.7 %copy-start.10 = (f32[4]{0:T(128)S(1)}, f32[4]{0:T(128)}, u32[]{:S(2)}) copy-start(f32[4]{0:T(128)} %get-tuple-element.97) | copy-start | bytes 52
  99.3 21.2 %copy-start.15 = (pred[2]{0:T(512)(128)(4,1)S(1)}, pred[2]{0:T(512)(128)(4,1)}, u32[]{:S(2)}) copy-start(pred[2]{0:T(512)(128)(4,1)} %copy-done.14) | copy-start | bytes 10
  110.0 11.9 %copy-start.2 = (bf16[512,768]{0,1:T(8,128)(2,1)S(1)}, bf16[512,768]{0,1:T(8,128)(2,1)}, u32[]{:S(2)}) copy-start(bf16[512,768]{0,1:T(8,128)(2,1)} %copy-done.1) | copy-start | bytes 2359300
  110.0 11.9 %copy-start.6 = (pred[512,512]{1,0:T(8,128)(4,1)S(1)}, pred[512,512]{1,0:T(8,128)(4,1)}, u32[]{:S(2)}) copy-start(pred[512,512]{1,0:T(8,128)(4,1)} %fusion.14) | copy-start | bytes 786436
  121.9 3.8 %copy-start.4 = (f32[12,1,65,128]{3,2,0,1:T(8,128)S(1)}, f32[12,1,65,128]{3,2,0,1:T(8,128)}, u32[]{:S(2)}) copy-start(f32[12,1,65,128]{3,2,0,1:T(8,128)} %copy.114) | copy-start | bytes 1198084
  121.9 3.8 %copy-start.20 = (f32[12]{0:T(128)S(1)}, f32[12]{0:T(128)}, u32[]{:S(2)}) copy-start(f32[12]{0:T(128)} %param.17) | copy-start | bytes 148
  131.7 2.6 %copy-start.23 = (f32[768]{0:T(1024)S(1)}, f32[768]{0:T(1024)}, u32[]{:S(2)}) copy-start(f32[768]{0:T(1024)} %param.18) | copy-start | bytes 9220

commit v19 on v18

--- a/solution.py
+++ b/solution.py
@@ -55,8 +55,8 @@
     )
     outer_before, _, _, _ = gathered_level(line_kept, line_total, lines)
     start_state = line_kept_before[:, None, None] * outer_before + line_before
-    whole = lax.all_gather(start_state, pair, tiled=True)
-    return pair_kept_before[:, None, None] * whole + pair_before
+    whole = lax.all_gather(start_state.astype(jnp.bfloat16), pair, tiled=True)
+    return pair_kept_before[:, None, None] * whole.astype(jnp.float32) + pair_before
 
 
 def doc_index(places, starts):
@@ -92,7 +92,10 @@
 def entry_terms(query_block, carry_state, running, doc_block, before):
     entry_weight = jnp.exp(running) * (doc_block == before).astype(jnp.float32)[:, None]
     carried = jnp.einsum(
-        "tn,hpn->thp", query_block.astype(jnp.float32), carry_state, precision=lax.Precision.HIGH
+        "tn,hpn->thp",
+        query_block,
+        carry_state.astype(jnp.bfloat16),
+        preferred_element_type=jnp.float32,
     )
     return carried * entry_weight[:, :, None]
 

time: 163 us -> 162 us (level)
  transfers between devices with their start and end apart: 2 -> 2, of which waited for: 1 -> 1; matrix products, arithmetic and copies ran while one was open for 21% -> 20% of each run, Pallas kernels for 0% -> 0%
where the time goes in v19:
time: 162 us; the launch traced here: 161 us
  blocking collectives  72.8 us (45%)
  matrix products  23.6 us (15%)
  waiting for transfers between devices  20.2 us (12%)
  starting transfers between devices  19.5 us (12%)
  other arithmetic  15 us (9%)
  local copies, waits for them, and re-layouts  8.16 us (5%)
  between operations  1.96 us (1%)
    all_gather x3, blocking collectives, gathered_level(): gathered = lax.all_gather(pack_state(kept, state), axis)  37.8 us
    all_to_all x1, blocking collectives, body(): lax.all_to_all(sent, 'head', split_axis=0, concat_axis=0, tiled=True)  25 us
    all_to_all x2, waiting for transfers between devices, send(): lax.all_to_all(packed.reshape(shards, capacity, packed.shape[1]), ROWS, s...  20.2 us
    all_to_all x2, starting transfers between devices, send(): lax.all_to_all(packed.reshape(shards, capacity, packed.shape[1]), ROWS, s...  19.5 us
    all_gather x1, blocking collectives, exclusive_prefix(): whole = lax.all_gather(start_state.astype(jnp.bfloat16), pair, tiled=True)  10.1 us
    dot_general x5, matrix products, send(): jnp.dot(to_slot, v, preferred_element_type=jnp.float32).astype(jnp.bfloat16)  5.73 us
    dot_general x1, matrix products, inner_terms(): jnp.einsum('hts,shp->thp', affinity_logits, by_head, preferred_element_ty...  3.82 us
    dot_general x2, matrix products, place(): jnp.dot(to_place, values, preferred_element_type=jnp.float32)  3.33 us
  transfers between devices with their start and end apart: 2, of which 1 were waited for; matrix products, arithmetic and copies ran while one was open for 20% of the time, Pallas kernels for 0%

profile of v19, /device:TPU:1, one launch (start us, length us, event | category | flops | bytes accessed | tf_op | source)
XLA Modules:
  0.0 161.3 jit_solution(17033192903691869683)
XLA Ops:
  0.0 0.9 fusion.67
  0.9 1.2 reduce-window.24
  2.1 0.2 slice_reduce_fusion
  2.4 0.1 fusion.46
  2.5 0.7 fusion.68
  3.2 1.0 convolution_convert_fusion.7
  4.2 0.2 copy.65
  4.4 1.2 convolution_convert_fusion.5
  5.6 0.3 convolution_convert_fusion.6
  5.9 0.6 convolution_convert_fusion.4
  6.5 1.1 maximum_bitcast_fusion
  7.6 13.1 %all-to-all-start = ((bf16[64,8,1038]{2,1,0:T(8,128)(2,1)}), bf16[64,8,1038]{2,1,0:T(8,128)(2,1)S(1)}, u32[]{:S(2)}, u32[]{:S(2)}) async-start(bf16[64,8,1038]{2,1,0:T(8,128)(2,1)} %maximum_bitcast_fusion), calls=%async_computation | async-start | bytes 2359296 | tf_op jit(solution)/shard_map/all_to_all | solution.py:144
  20.8 0.2 reduce-window.31
  21.0 0.6 fusion.72
  21.7 0.7 slice.85
  23.7 0.5 fusion.78
  24.3 0.6 iota_compare_fusion.14
  24.8 0.5 iota_compare_fusion.18
  25.4 0.5 iota_compare_fusion.17
  25.9 2.6 %fusion.10 = bf16[64,8,768]{2,1,0:T(8,128)(2,1)} fusion(bf16[512,768]{1,0:T(8,128)(2,1)} %param.11, s32[512]{0:T(512)S(1)} %get-tuple-element.75), kind=kOutput, calls=%fused_computation.24 | convolution fusion | flops 403308544 | bytes 1574912 | tf_op jit(solution)/shard_map/dot_general | solution.py:139
  28.5 0.6 fusion.71
  29.1 0.6 iota_compare_fusion.16
  29.7 0.6 broadcast_and_fusion
  30.3 0.7 compare_convert_fusion.1
  31.0 0.9 fusion.14
  31.9 20.2 %all-to-all-done = bf16[64,8,1038]{2,1,0:T(8,128)(2,1)S(1)} async-done(((bf16[64,8,1038]{2,1,0:T(8,128)(2,1)}), bf16[64,8,1038]{2,1,0:T(8,128)(2,1)S(1)}, u32[]{:S(2)}, u32[]{:S(2)}) %all-to-all-start) | async-done | bytes 1062944 | tf_op jit(solution)/shard_map/all_to_all | solution.py:144
  52.1 6.4 %all-to-all-start.1 = ((bf16[64,8,768]{2,1,0:T(8,128)(2,1)}), bf16[64,8,768]{2,1,0:T(8,128)(2,1)}, u32[]{:S(2)}, u32[]{:S(2)}) async-start(bf16[64,8,768]{2,1,0:T(8,128)(2,1)} %fusion.10), calls=%async_computation.1 | async-start | bytes 1572864 | tf_op jit(solution)/shard_map/all_to_all | solution.py:144
  58.5 0.2 add_reduce_fusion
  58.7 0.8 convolution_convert_fusion.1
  59.6 0.9 copy-done.3
  60.6 1.2 reduce-window.32
  61.7 0.2 slice_reduce_fusion.1
  62.1 0.2 slice_reduce_fusion.2
  62.3 0.8 copy.68
  63.2 2.3 %fusion.13 = bf16[1,12,64,128]{3,2,1,0:T(8,128)(2,1)S(1)} fusion(bf16[512,12,64]{0,2,1:T(8,128)(2,1)S(1)} %bitcast.103, f32[12,512]{1,0:T(8,128)S(1)} %exponential_multiply_fusion.1, f32[512,128]{1,0:T(8,128)} %copy.68, f32[12]{0:T(128)S(1)} %get-tuple-element.76), kind=kOutput, calls=%fused_computation.30 | convolution fusion | flops 102432768 | bytes 1269808 | tf_op jit(solution)/shard_map/while/body/eval_jaxpr/hsn,shp->hpn/dot_general | solution.py:73
  65.7 2.3 %all_gather.15 = bf16[2,12,65,128]{3,2,1,0:T(8,128)(2,1)S(1)} all-gather(bf16[1,12,65,128]{3,2,1,0:T(8,128)(2,1)S(1)} %pad_maximum_fusion.1), channel_id=1, replica_groups=mesh['sx'=4,'sz'=8,'sc'=2,'head'=4] {'sc'}, dimensions={0}, use_global_device_ids=true | all-gather | bytes 599040 | tf_op jit(solution)/shard_map/all_gather | solution.py:38
  67.9 0.4 fusion.62
  68.4 0.1 copy.75
  68.5 0.6 fusion.40
  69.4 25.6 %all_gather.16 = bf16[8,6,65,128]{3,2,1,0:T(8,128)(2,1)S(1)} all-gather(bf16[1,6,65,128]{3,2,1,0:T(8,128)(2,1)S(1)} %pad_maximum_fusion.2), channel_id=1, replica_groups=mesh['sx'=4,'sz'=8,'sc'=2,'head'=4] {'sz'}, dimensions={0}, use_global_device_ids=true | all-gather | bytes 898560 | tf_op jit(solution)/shard_map/all_gather | solution.py:38
  95.0 0.2 slice_reduce_fusion.3
  95.2 0.1 copy.90
  95.5 0.1 copy.86
  95.6 1.6 fusion.38
  97.2 0.8 copy.114
  98.1 0.3 select_reduce_fusion.1
  98.4 0.4 fusion.18
  98.8 0.4 fusion.20
  99.3 9.9 %all_gather.17 = bf16[4,6,65,128]{3,2,1,0:T(8,128)(2,1)S(1)} all-gather(bf16[1,6,65,128]{3,2,1,0:T(8,128)(2,1)S(1)} %pad_maximum_fusion.3), channel_id=1, replica_groups=mesh['sx'=4,'sz'=8,'sc'=2,'head'=4] {'sx'}, dimensions={0}, use_global_device_ids=true | all-gather | bytes 499200 | tf_op jit(solution)/shard_map/all_gather | solution.py:38
  109.2 0.1 fusion.61
  109.5 0.1 copy.81
  109.7 0.3 fusion.29
  110.0 0.1 fusion.36
  110.1 10.1 %all_gather.18 = bf16[12,64,128]{2,1,0:T(8,128)(2,1)S(1)} all-gather(bf16[6,64,128]{2,1,0:T(8,128)(2,1)S(1)} %fusion.36), channel_id=1, replica_groups=mesh['sx'=4,'sz'=8,'sc'=2,'head'=4] {'sc'}, dimensions={0}, use_global_device_ids=true | all-gather | bytes 294912 | tf_op jit(solution)/shard_map/all_gather | solution.py:58
  120.3 1.3 fusion.49
  121.7 3.8 %fusion = f32[12,64,512]{2,1,0:T(8,128)S(1)} fusion(bf16[512,12,64]{0,2,1:T(8,128)(2,1)S(1)} %bitcast.104, f32[12,512]{1,0:T(8,128)S(1)} %bitcast.116, f32[512,512]{1,0:T(8,128)S(1)} %fusion.49, pred[512,512]{1,0:T(8,128)(4,1)S(1)} %copy-done.6), kind=kOutput, calls=%fused_computation.1 | convolution fusion | flops 415236096 | bytes 3694592 | tf_op jit(solution)/shard_map/while/body/eval_jaxpr/hts,shp->thp/dot_general | solution.py:89
  125.5 2.5 %fusion.7 = f32[512,12,64]{0,2,1:T(8,128)} fusion(f32[12,64,512]{2,1,0:T(8,128)S(1)} %fusion, bf16[512,12,64]{0,2,1:T(8,128)(2,1)S(1)} %bitcast.105, f32[12]{0:T(128)S(1)} %copy-done.9, f32[512,12]{0,1:T(8,128)S(1)} %exponential_multiply_fusion, f32[12,65,128]{2,1,0:T(8,128)S(1)} %bitcast.107, bf16[12,64,128]{2,1,0:T(8,128)(2,1)S(1)} %all_gather.18, ...), kind=kOutput, calls=%fused_computation.16 | convolution fusion | flops 103022592 | bytes 4686848 | tf_op jit(solution)/shard_map/while/body/eval_jaxpr/tn,hpn->thp/dot_general | solution.py:94
  128.0 3.0 %copy.72 = f32[512,768]{1,0:T(8,128)} copy(f32[512,768]{0,1:T(8,128)} %bitcast.102) | data formatting | bytes 3145728 | tf_op jit(solution)/shard_map/reshape | solution.py:231
  131.1 2.5 %multiply_reduce_fusion = (f32[512]{0:T(512)S(1)}, f32[512,768]{1,0:T(8,128)S(1)}) fusion(f32[512,768]{1,0:T(8,128)} %copy.72, bf16[64,8,768]{2,1,0:T(8,128)(2,1)} %all-to-all-done.1, s32[512]{0:T(512)S(1)} %add_reduce_fusion), kind=kOutput, calls=%fused_computation.17 | convolution fusion | flops 406453760 | bytes 3936256 | tf_op jit(solution)/shard_map/dot_general | solution.py:165
  133.7 1.4 convolution_convert_fusion
  135.1 0.1 pad_maximum_fusion
  135.2 25.0 %all_to_all.15 = bf16[4,136,1536]{2,1,0:T(8,128)(2,1)S(1)} all-to-all(bf16[4,136,1536]{2,1,0:T(8,128)(2,1)S(1)} %pad_maximum_fusion), channel_id=1, replica_groups=mesh['sx'=4,'sz'=8,'sc'=2,'head'=4] {'head'}, dimensions={0} | all-to-all | bytes 3342336 | tf_op jit(solution)/shard_map/all_to_all | solution.py:247
  160.2 0.2 convert_reduce_fusion
  160.4 0.9 fusion.15
  (98 shorter events, 1.7 us)
Async XLA Ops:
  0.0 133.6 %copy-start = (bf16[768,1536]{1,0:T(8,128)(2,1)S(1)}, bf16[768,1536]{1,0:T(8,128)(2,1)}, u32[]{:S(2)}) copy-start(bf16[768,1536]{1,0:T(8,128)(2,1)} %param.19) | copy-start | bytes 7077892
  0.0 5.6 %copy-start.22 = (bf16[512,128]{1,0:T(8,128)(2,1)S(1)}, bf16[512,128]{1,0:T(8,128)(2,1)}, u32[]{:S(2)}) copy-start(bf16[512,128]{1,0:T(8,128)(2,1)} %param.12) | copy-start | bytes 393220
  0.0 5.9 %copy-start.21 = (bf16[512,768]{1,0:T(8,128)(2,1)S(1)}, bf16[512,768]{1,0:T(8,128)(2,1)}, u32[]{:S(2)}) copy-start(bf16[512,768]{1,0:T(8,128)(2,1)} %param.10) | copy-start | bytes 2359300
  7.6 13.2 %copy-start.10 = (s32[4]{0:T(128)S(1)}, s32[4]{0:T(128)}, u32[]{:S(2)}) copy-start(s32[4]{0:T(128)} %param.16) | copy-start | bytes 52
  7.6 44.5 %all-to-all-start = ((bf16[64,8,1038]{2,1,0:T(8,128)(2,1)}), bf16[64,8,1038]{2,1,0:T(8,128)(2,1)S(1)}, u32[]{:S(2)}, u32[]{:S(2)}) async-start(bf16[64,8,1038]{2,1,0:T(8,128)(2,1)} %maximum_bitcast_fusion), calls=%async_computation | async-start | bytes 2359296 | tf_op jit(solution)/shard_map/all_to_all | solution.py:144
  23.7 7.2 %copy-start.15 = (pred[2]{0:T(512)(128)(4,1)}, pred[2]{0:T(512)(128)(4,1)S(1)}, u32[]{:S(2)}) copy-start(pred[2]{0:T(512)(128)(4,1)S(1)} %iota_compare_fusion.19) | copy-start | bytes 10
  25.4 5.6 %copy-start.18 = (pred[8]{0:T(512)(128)(4,1)}, pred[8]{0:T(512)(128)(4,1)S(1)}, u32[]{:S(2)}) copy-start(pred[8]{0:T(512)(128)(4,1)S(1)} %get-tuple-element.92) | copy-start | bytes 28
  52.1 78.9 %all-to-all-start.1 = ((bf16[64,8,768]{2,1,0:T(8,128)(2,1)}), bf16[64,8,768]{2,1,0:T(8,128)(2,1)}, u32[]{:S(2)}, u32[]{:S(2)}) async-start(bf16[64,8,768]{2,1,0:T(8,128)(2,1)} %fusion.10), calls=%async_computation.1 | async-start | bytes 1572864 | tf_op jit(solution)/shard_map/all_to_all | solution.py:144
  59.5 1.0 copy-start.3
  59.6 5.9 %copy-start.1 = (bf16[512,768]{0,1:T(8,128)(2,1)}, bf16[512,768]{0,1:T(8,128)(2,1)S(1)}, u32[]{:S(2)}) copy-start(bf16[512,768]{0,1:T(8,128)(2,1)S(1)} %slice.100) | copy-start | bytes 2359300
  63.2 5.1 %copy-start.13 = (pred[2,2]{1,0:T(4,128)(4,1)S(1)}, pred[2,2]{1,0:T(4,128)(4,1)}, u32[]{:S(2)}) copy-start(pred[2,2]{1,0:T(4,128)(4,1)} %get-tuple-element.98) | copy-start | bytes 16
  63.2 5.1 %copy-start.14 = (pred[2,2]{1,0:T(4,128)(4,1)S(1)}, pred[2,2]{1,0:T(4,128)(4,1)}, u32[]{:S(2)}) copy-start(pred[2,2]{1,0:T(4,128)(4,1)} %get-tuple-element.99) | copy-start | bytes 16
  67.9 1.4 copy-start.5
  69.1 26.3 %copy-start.19 = (pred[8]{0:T(512)(128)(4,1)S(1)}, pred[8]{0:T(512)(128)(4,1)}, u32[]{:S(2)}) copy-start(pred[8]{0:T(512)(128)(4,1)} %copy-done.18) | copy-start | bytes 28
  69.1 26.3 %copy-start.17 = (f32[2]{0:T(128)S(1)}, f32[2]{0:T(128)}, u32[]{:S(2)}) copy-start(f32[2]{0:T(128)} %fusion.78) | copy-start | bytes 28
  69.4 28.7 %copy-start.7 = (pred[8,8]{1,0:T(8,128)(4,1)S(1)}, pred[8,8]{1,0:T(8,128)(4,1)}, u32[]{:S(2)}) copy-start(pred[8,8]{1,0:T(8,128)(4,1)} %iota_compare_fusion.14) | copy-start | bytes 196
  69.4 28.7 %copy-start.8 = (pred[8,8]{1,0:T(8,128)(4,1)S(1)}, pred[8,8]{1,0:T(8,128)(4,1)}, u32[]{:S(2)}) copy-start(pred[8,8]{1,0:T(8,128)(4,1)} %broadcast_and_fusion) | copy-start | bytes 196
  69.4 29.0 %copy-start.20 = (f32[8]{0:T(128)S(1)}, f32[8]{0:T(128)}, u32[]{:S(2)}) copy-start(f32[8]{0:T(128)} %get-tuple-element.94) | copy-start | bytes 100
  98.8 10.6 %copy-start.12 = (pred[4,4]{1,0:T(4,128)(4,1)S(1)}, pred[4,4]{1,0:T(4,128)(4,1)}, u32[]{:S(2)}) copy-start(pred[4,4]{1,0:T(4,128)(4,1)} %fusion.71) | copy-start | bytes 52
  98.8 10.7 %copy-start.11 = (f32[4]{0:T(128)S(1)}, f32[4]{0:T(128)}, u32[]{:S(2)}) copy-start(f32[4]{0:T(128)} %get-tuple-element.97) | copy-start | bytes 52
  99.2 21.0 %copy-start.16 = (pred[2]{0:T(512)(128)(4,1)S(1)}, pred[2]{0:T(512)(128)(4,1)}, u32[]{:S(2)}) copy-start(pred[2]{0:T(512)(128)(4,1)} %copy-done.15) | copy-start | bytes 10
  109.7 12.0 %copy-start.2 = (bf16[512,768]{0,1:T(8,128)(2,1)S(1)}, bf16[512,768]{0,1:T(8,128)(2,1)}, u32[]{:S(2)}) copy-start(bf16[512,768]{0,1:T(8,128)(2,1)} %copy-done.1) | copy-start | bytes 2359300
  109.7 12.0 %copy-start.6 = (pred[512,512]{1,0:T(8,128)(4,1)S(1)}, pred[512,512]{1,0:T(8,128)(4,1)}, u32[]{:S(2)}) copy-start(pred[512,512]{1,0:T(8,128)(4,1)} %fusion.14) | copy-start | bytes 786436
  121.6 3.8 %copy-start.4 = (f32[12,1,65,128]{3,2,0,1:T(8,128)S(1)}, f32[12,1,65,128]{3,2,0,1:T(8,128)}, u32[]{:S(2)}) copy-start(f32[12,1,65,128]{3,2,0,1:T(8,128)} %copy.114) | copy-start | bytes 1198084
  121.6 3.8 %copy-start.9 = (f32[12]{0:T(128)S(1)}, f32[12]{0:T(128)}, u32[]{:S(2)}) copy-start(f32[12]{0:T(128)} %param.17) | copy-start | bytes 148
  131.1 2.6 %copy-start.23 = (f32[768]{0:T(1024)S(1)}, f32[768]{0:T(1024)}, u32[]{:S(2)}) copy-start(f32[768]{0:T(1024)} %param.18) | copy-start | bytes 9220
